TPU v7x, 256 devices: a whole 4x4x8 slice. The times are simulated.
256 devices in a mesh: wide: 64 (over z, y, core), narrow: 4 (over x).
Axes of the slice: x: 4, y: 4, z: 8, core: 2. Of those that a mesh axis runs over, the one named last changes fastest.
Arguments:
- file_lengths: int32 [17], replicated, may hold values from 1 to 8, as said below
- queries: bfloat16 [32768, 4096], P('wide', 'narrow'), may hold values from -6 to 6
- out_grad: bfloat16 [32768, 4096], P('wide', 'narrow'), may hold values from -6 to 6
- mem_key: bfloat16 [8192, 1024], P('wide', 'narrow'), may hold values from -6 to 6
- memory_values: bfloat16 [8192, 1024], P('wide', 'narrow'), may hold values from -6 to 6
- enc_rows: bfloat16 [8192, 4096], P('wide'), may hold values from -16 to 16
- key_down: bfloat16 [4096, 128], replicated, may hold values from -0.09375 to 0.09375
- key_up: bfloat16 [128, 1024], P(None, 'narrow'), may hold values from -0.5 to 0.5
- value_down: bfloat16 [4096, 128], replicated, may hold values from -0.09375 to 0.09375
- value_up: bfloat16 [128, 1024], P(None, 'narrow'), may hold values from -0.5 to 0.5
Outputs:
- grad_key_down: float32 [4096, 128], P('wide')
- grad_value_down: float32 [4096, 128], P('wide')
- grad_key_up: float32 [128, 1024], P(None, 'narrow')
- grad_value_up: float32 [128, 1024], P(None, 'narrow')
Inputs may be any that keep to these rules, and one draw needn't show every extreme that they name: `file_lengths`: the lengths sum to 64; the last file has 8 stretches.
All inputs are finite; a program needn't handle non-finite values.
Results may differ from a plain program's by a relative error of at most 0.0056.
Values may be sent and summed in bfloat16 or wider, within the bound.
No kernel may reach another device: no remote copies, remote signals or barrier semaphores. Data moves between devices by JAX's collectives and lax.ppermute only.
A program may use at most 128 MiB of HBM per device.

v0:
```python
import jax
import jax.numpy as jnp
from jax import lax
from jax.sharding import PartitionSpec as P

HEAD_SIZE = 128
Q_PER_KV = 4


def passed_along(array, axis, by):
    devices = lax.axis_size(axis)
    pairs = [(i, i + by) for i in range(devices) if 0 <= i + by < devices]
    return lax.ppermute(array, axis, pairs)


def stretch_grads(query, dout, keys, values, valid):
    scale = HEAD_SIZE ** (-0.5)
    score = jnp.einsum("qgmd,kgd->gmqk", query, keys, preferred_element_type=jnp.float32) * scale
    mask = valid[None, None, None, :]
    expo = jnp.where(mask, jnp.exp(jnp.where(mask, score, 0.0)), 0.0)
    prob = expo / jnp.sum(expo, axis=-1, keepdims=True)
    prob_b = prob.astype(jnp.bfloat16)
    outp = jnp.einsum("gmqk,kgd->qgmd", prob_b, values, preferred_element_type=jnp.float32)
    delta = jnp.sum(dout.astype(jnp.float32) * outp, axis=-1)
    dprob = jnp.einsum("qgmd,kgd->gmqk", dout, values, preferred_element_type=jnp.float32)
    dscore = (prob * (dprob - jnp.transpose(delta, (1, 2, 0))[..., None])).astype(jnp.bfloat16)
    dkey = jnp.einsum("gmqk,qgmd->kgd", dscore, query, preferred_element_type=jnp.float32) * scale
    dval = jnp.einsum("gmqk,qgmd->kgd", prob_b, dout, preferred_element_type=jnp.float32)
    return (dkey, dval)


def on_device(
    file_lengths,
    queries,
    out_grad,
    mem_key,
    memory_values,
    enc_rows,
    key_down,
    key_up,
    value_down,
    value_up,
):
    wide_count = lax.axis_size("wide")
    span = min(8, wide_count // 2)
    rows = mem_key.shape[0]
    cols = mem_key.shape[1]
    local_heads = cols // HEAD_SIZE
    stretch = lax.axis_index("wide")
    starts = jnp.cumsum(file_lengths) - file_lengths
    first = jnp.max(jnp.where(starts <= stretch, starts, 0))
    position = stretch - first
    paired = jnp.stack([mem_key, memory_values])
    blocks = [paired]
    for offset in range(1, span):
        blocks.append(passed_along(paired, "wide", offset))
    window = jnp.stack(blocks)
    keys = window[:, 0].reshape(span * rows, local_heads, HEAD_SIZE)
    values = window[:, 1].reshape(span * rows, local_heads, HEAD_SIZE)
    valid = jnp.repeat(jnp.arange(span, dtype=jnp.int32) <= position, rows)
    query = queries.reshape(queries.shape[0], local_heads, Q_PER_KV, HEAD_SIZE)
    dout = out_grad.reshape(out_grad.shape[0], local_heads, Q_PER_KV, HEAD_SIZE)
    dkey, dval = stretch_grads(query, dout, keys, values, valid)
    contrib = jnp.stack([dkey.reshape(span, rows, cols), dval.reshape(span, rows, cols)], 1)
    total = contrib[0]
    for offset in range(1, span):
        total = total + passed_along(contrib[offset], "wide", -offset)
    key_grad = total[0].astype(jnp.bfloat16)
    value_grad = total[1].astype(jnp.bfloat16)
    u_key = jnp.dot(enc_rows, key_down, preferred_element_type=jnp.float32).astype(jnp.bfloat16)
    u_value = jnp.dot(enc_rows, value_down, preferred_element_type=jnp.float32).astype(jnp.bfloat16)
    part_key = jnp.dot(key_grad, key_up.T, preferred_element_type=jnp.float32)
    part_value = jnp.dot(value_grad, value_up.T, preferred_element_type=jnp.float32)
    h_key, h_value = lax.psum((part_key, part_value), "narrow")
    h_key = h_key.astype(jnp.bfloat16)
    h_value = h_value.astype(jnp.bfloat16)
    up_key = jnp.dot(u_key.T, key_grad, preferred_element_type=jnp.float32)
    up_value = jnp.dot(u_value.T, value_grad, preferred_element_type=jnp.float32)
    down_key = jnp.dot(enc_rows.T, h_key, preferred_element_type=jnp.float32)
    down_value = jnp.dot(enc_rows.T, h_value, preferred_element_type=jnp.float32)
    down_key, down_value, up_key, up_value = lax.psum(
        (down_key, down_value, up_key, up_value), "wide"
    )
    share = down_key.shape[0] // wide_count
    down_key = lax.dynamic_slice_in_dim(down_key, stretch * share, share, 0)
    down_value = lax.dynamic_slice_in_dim(down_value, stretch * share, share, 0)
    return (down_key, down_value, up_key, up_value)


def solution(mesh):
    placed = (
        P(),
        P("wide", "narrow"),
        P("wide", "narrow"),
        P("wide", "narrow"),
        P("wide", "narrow"),
        P("wide", None),
        P(),
        P(None, "narrow"),
        P(),
        P(None, "narrow"),
    )
    return jax.shard_map(
        on_device,
        mesh=mesh,
        in_specs=placed,
        out_specs=(P("wide", None), P("wide", None), P(None, "narrow"), P(None, "narrow")),
        check_vma=False,
    )
```

profile of v0, /device:TPU:1, one launch (start us, length us, event | category | flops | bytes accessed | tf_op | source)
XLA Modules:
  0.0 373.5 jit_solution(5158860478844453476)
XLA Ops:
  8.2 4.6 %collective-permute-start = (bf16[2,128,256]{2,1,0:T(8,128)(2,1)S(1)}, bf16[2,128,256]{2,1,0:T(8,128)(2,1)S(1)}, u32[]{:S(2)}, u32[]{:S(2)}) collective-permute-start(bf16[2,128,256]{2,1,0:T(8,128)(2,1)S(1)} %pad_maximum_fusion), channel_id=1, source_target_pairs={{0,4},{4,8},{8,12},{12,16},{16,20},{20,24},{24,28},{28,32},{32,36}... | collective-permute-start | bytes 393224 | tf_op jit(solution)/shard_map/ppermute | solution.py:13
  12.8 3.2 collective-permute-start.1
  16.0 3.5 collective-permute-start.2
  19.5 3.6 collective-permute-start.3
  23.2 5.2 %collective-permute-start.4 = (bf16[2,128,256]{2,1,0:T(8,128)(2,1)S(1)}, bf16[2,128,256]{2,1,0:T(8,128)(2,1)S(1)}, u32[]{:S(2)}, u32[]{:S(2)}) collective-permute-start(bf16[2,128,256]{2,1,0:T(8,128)(2,1)S(1)} %pad_maximum_fusion), channel_id=1, source_target_pairs={{0,20},{4,24},{8,28},{12,32},{16,36},{20,40},{24,44},{28,48},{32,5... | collective-permute-start | bytes 393224 | tf_op jit(solution)/shard_map/ppermute | solution.py:13
  31.3 2.6 reshape.47
  36.3 2.8 collective-permute-start.5
  39.1 4.9 %collective-permute-start.6 = (bf16[2,128,256]{2,1,0:T(8,128)(2,1)S(1)}, bf16[2,128,256]{2,1,0:T(8,128)(2,1)S(1)}, u32[]{:S(2)}, u32[]{:S(2)}) collective-permute-start(bf16[2,128,256]{2,1,0:T(8,128)(2,1)S(1)} %pad_maximum_fusion), channel_id=1, source_target_pairs={{0,28},{4,32},{8,36},{12,40},{16,44},{20,48},{24,52},{28,56},{32,6... | collective-permute-start | bytes 393224 | tf_op jit(solution)/shard_map/ppermute | solution.py:13
  47.6 5.7 %bitcast_reduce_fusion = (f32[2,4,512]{2,1,0:T(4,128)S(1)}, f32[2,1024,512,4]{2,1,3,0:T(8,128)S(1)}) fusion(pred[1024]{0:T(1024)(128)(4,1)S(1)} %broadcast_bitcast_fusion, bf16[512,2,4,128]{3,2,1,0:T(4,128)(2,1)} %reshape.47, bf16[1024,2,128,1]{2,1,0,3:T(2,128)(2,1)} %bitcast.134), kind=kOutput, calls=%fused_computation.4 | convolution fusion | flops 1090514944 | bytes 18367488 | tf_op jit(solution)/shard_map/qgmd,kgd->gmqk/dot_general | solution.py:18
  53.3 7.3 %bitcast_divide_fusion = f32[2,4,512,1024]{2,3,1,0:T(8,128)} fusion(f32[2,1024,512,4]{2,1,3,0:T(8,128)S(1)} %get-tuple-element.37, f32[2,4,512]{2,1,0:T(4,128)S(1)} %get-tuple-element.36, pred[1024]{0:T(1024)(128)(4,1)S(1)} %broadcast_bitcast_fusion), kind=kLoop, calls=%fused_computation.3 | loop fusion | flops 16777216 | bytes 33571840 | tf_op jit(solution)/shard_map/div | solution.py:21
  60.6 9.1 %fusion.14 = f32[1024,2,128]{2,0,1:T(8,128)} fusion(bf16[512,2,4,128]{0,3,2,1:T(8,128)(2,1)S(1)} %bitcast.124, f32[2,4,512,1024]{2,3,1,0:T(8,128)} %bitcast_divide_fusion), kind=kOutput, calls=%fused_computation.17 | convolution fusion | flops 1077936128 | bytes 18874368 | tf_op jit(solution)/shard_map/gmqk,qgmd->kgd/dot_general | solution.py:28
  69.7 7.1 %fusion.11 = f32[512,2,4]{0,2,1:T(4,128)S(1)} fusion(bf16[512,2,4,128]{0,3,2,1:T(8,128)(2,1)S(1)} %bitcast.125, bf16[1024,2,128,1]{0,2,3,1:T(8,128)(2,1)S(1)} %copy.85, f32[2,4,512,1024]{2,3,1,0:T(8,128)} %bitcast_divide_fusion), kind=kOutput, calls=%fused_computation.16 | convolution fusion | flops 1079504896 | bytes 18366464 | tf_op jit(solution)/shard_map/gmqk,kgd->qgmd/dot_general | solution.py:23
  77.2 9.4 %fusion.23 = f32[1024,2,128]{2,0,1:T(8,128)} fusion(f32[2,4,512,1024]{2,3,1,0:T(8,128)} %bitcast_divide_fusion, f32[2,4,512]{2,1,0:T(4,128)S(1)} %copy.70, bf16[1024,2,128,1]{0,2,3,1:T(8,128)(2,1)S(1)} %copy.85, bf16[512,2,4,128]{0,3,2,1:T(8,128)(2,1)S(1)} %bitcast.126, bf16[512,2,4,128]{3,2,1,0:T(4,128)(2,1)} %reshape.47), kind=kOutput, calls=%fused_computation.20 | convolution fusion | flops 2160328704 | bytes 20463616 | tf_op jit(solution)/shard_map/gmqk,qgmd->kgd/dot_general | solution.py:27
  88.4 2.5 copy.74
  92.5 1.8 fusion.37
  99.5 2.3 collective-permute-start.7
  101.8 2.6 collective-permute-done.10
  105.7 6.0 %collective-permute-done.11 = f32[2,128,256]{1,2,0:T(8,128)S(1)} collective-permute-done((f32[2,128,256]{1,2,0:T(8,128)S(1)}, f32[2,128,256]{1,2,0:T(8,128)S(1)}, u32[]{:S(2)}, u32[]{:S(2)}) %collective-permute-start.11) | collective-permute-done | bytes 262176 | tf_op jit(solution)/shard_map/ppermute | solution.py:13
  113.0 12.9 %collective-permute-done.13 = f32[2,128,256]{1,2,0:T(8,128)S(1)} collective-permute-done((f32[2,128,256]{1,2,0:T(8,128)S(1)}, f32[2,128,256]{1,2,0:T(8,128)S(1)}, u32[]{:S(2)}, u32[]{:S(2)}) %collective-permute-start.13) | collective-permute-done | bytes 262176 | tf_op jit(solution)/shard_map/ppermute | solution.py:13
  126.4 15.0 %all-reduce.6 = (bf16[128,128]{1,0:T(8,128)(2,1)S(1)}, bf16[128,128]{1,0:T(8,128)(2,1)S(1)}) all-reduce(f32[128,128]{1,0:T(8,128)S(1)} %fusion.32, f32[128,128]{1,0:T(8,128)S(1)} %fusion.33), channel_id=1, replica_groups=mesh['wide'=64,'narrow'=4] {'narrow'}, use_global_device_ids=true, to_apply=%region_4.5 | all-reduce | flops 32768 | bytes 196608 | tf_op jit(solution)/shard_map/psum | solution.py:74
  141.4 1.8 convolution_bitcast_fusion
  145.0 2.5 fusion.26
  147.5 2.5 fusion.27
  150.1 211.1 %all-reduce.5.cloned.1.call-done = (f32[4096,128]{0,1:T(8,128)}, f32[4096,128]{0,1:T(8,128)}, f32[128,256]{1,0:T(8,128)}, f32[128,256]{1,0:T(8,128)}) async-done(((f32[4096,128]{0,1:T(8,128)}, f32[4096,128]{0,1:T(8,128)}, f32[128,256]{1,0:T(8,128)}, f32[128,256]{1,0:T(8,128)}), (f32[4096,128]{0,1:T(8,128)}, f32[4096,128]{0,1:T(8,128)}, f32[128,256]{1,0:T(8,128)}, ...) | async-done | bytes 4456464 | tf_op jit(solution)/shard_map/psum | solution.py:81
  (61 shorter events, 28.4 us)
Async XLA Ops:
  7.2 134.3 %copy-start = (bf16[128,4096]{1,0:T(8,128)(2,1)S(1)}, bf16[128,4096]{1,0:T(8,128)(2,1)}, u32[]{:S(2)}) copy-start(bf16[128,4096]{1,0:T(8,128)(2,1)} %param.15) | copy-start | bytes 3145732
  7.2 354.0 %all-reduce.5.cloned.1.call-start = ((), (), s32[]{:S(2)}) async-start(), calls=%async_computation | async-start | bytes 8912896 | tf_op jit(solution)/shard_map/psum | solution.py:81
  8.2 28.1 %collective-permute-start = (bf16[2,128,256]{2,1,0:T(8,128)(2,1)S(1)}, bf16[2,128,256]{2,1,0:T(8,128)(2,1)S(1)}, u32[]{:S(2)}, u32[]{:S(2)}) collective-permute-start(bf16[2,128,256]{2,1,0:T(8,128)(2,1)S(1)} %pad_maximum_fusion), channel_id=1, source_target_pairs={{0,4},{4,8},{8,12},{12,16},{16,20},{20,24},{24,28},{28,32},{32,36}... | collective-permute-start | bytes 393224 | tf_op jit(solution)/shard_map/ppermute | solution.py:13
  12.8 26.3 %collective-permute-start.1 = (bf16[2,128,256]{2,1,0:T(8,128)(2,1)S(1)}, bf16[2,128,256]{2,1,0:T(8,128)(2,1)S(1)}, u32[]{:S(2)}, u32[]{:S(2)}) collective-permute-start(bf16[2,128,256]{2,1,0:T(8,128)(2,1)S(1)} %pad_maximum_fusion), channel_id=1, source_target_pairs={{0,8},{4,12},{8,16},{12,20},{16,24},{20,28},{24,32},{28,36},{32,40... | collective-permute-start | bytes 393224 | tf_op jit(solution)/shard_map/ppermute | solution.py:13
  16.0 28.1 %collective-permute-start.2 = (bf16[2,128,256]{2,1,0:T(8,128)(2,1)S(1)}, bf16[2,128,256]{2,1,0:T(8,128)(2,1)S(1)}, u32[]{:S(2)}, u32[]{:S(2)}) collective-permute-start(bf16[2,128,256]{2,1,0:T(8,128)(2,1)S(1)} %pad_maximum_fusion), channel_id=1, source_target_pairs={{0,12},{4,16},{8,20},{12,24},{16,28},{20,32},{24,36},{28,40},{32,4... | collective-permute-start | bytes 393224 | tf_op jit(solution)/shard_map/ppermute | solution.py:13
  19.5 24.6 %collective-permute-start.3 = (bf16[2,128,256]{2,1,0:T(8,128)(2,1)S(1)}, bf16[2,128,256]{2,1,0:T(8,128)(2,1)S(1)}, u32[]{:S(2)}, u32[]{:S(2)}) collective-permute-start(bf16[2,128,256]{2,1,0:T(8,128)(2,1)S(1)} %pad_maximum_fusion), channel_id=1, source_target_pairs={{0,16},{4,20},{8,24},{12,28},{16,32},{20,36},{24,40},{28,44},{32,4... | collective-permute-start | bytes 393224 | tf_op jit(solution)/shard_map/ppermute | solution.py:13
  23.2 21.0 %collective-permute-start.4 = (bf16[2,128,256]{2,1,0:T(8,128)(2,1)S(1)}, bf16[2,128,256]{2,1,0:T(8,128)(2,1)S(1)}, u32[]{:S(2)}, u32[]{:S(2)}) collective-permute-start(bf16[2,128,256]{2,1,0:T(8,128)(2,1)S(1)} %pad_maximum_fusion), channel_id=1, source_target_pairs={{0,20},{4,24},{8,28},{12,32},{16,36},{20,40},{24,44},{28,48},{32,5... | collective-permute-start | bytes 393224 | tf_op jit(solution)/shard_map/ppermute | solution.py:13
  36.3 7.9 %collective-permute-start.5 = (bf16[2,128,256]{2,1,0:T(8,128)(2,1)S(1)}, bf16[2,128,256]{2,1,0:T(8,128)(2,1)S(1)}, u32[]{:S(2)}, u32[]{:S(2)}) collective-permute-start(bf16[2,128,256]{2,1,0:T(8,128)(2,1)S(1)} %pad_maximum_fusion), channel_id=1, source_target_pairs={{0,24},{4,28},{8,32},{12,36},{16,40},{20,44},{24,48},{28,52},{32,5... | collective-permute-start | bytes 393224 | tf_op jit(solution)/shard_map/ppermute | solution.py:13
  39.1 6.9 %collective-permute-start.6 = (bf16[2,128,256]{2,1,0:T(8,128)(2,1)S(1)}, bf16[2,128,256]{2,1,0:T(8,128)(2,1)S(1)}, u32[]{:S(2)}, u32[]{:S(2)}) collective-permute-start(bf16[2,128,256]{2,1,0:T(8,128)(2,1)S(1)} %pad_maximum_fusion), channel_id=1, source_target_pairs={{0,28},{4,32},{8,36},{12,40},{16,44},{20,48},{24,52},{28,56},{32,6... | collective-permute-start | bytes 393224 | tf_op jit(solution)/shard_map/ppermute | solution.py:13
  77.2 48.8 %copy-start.1 = (bf16[128,256]{1,0:T(8,128)(2,1)S(1)}, bf16[128,256]{1,0:T(8,128)(2,1)}, u32[]{:S(2)}) copy-start(bf16[128,256]{1,0:T(8,128)(2,1)} %param.17) | copy-start | bytes 196612
  77.2 49.0 %copy-start.2 = (bf16[128,256]{1,0:T(8,128)(2,1)S(1)}, bf16[128,256]{1,0:T(8,128)(2,1)}, u32[]{:S(2)}) copy-start(bf16[128,256]{1,0:T(8,128)(2,1)} %param.19) | copy-start | bytes 196612
  94.3 10.1 %collective-permute-start.10 = (f32[2,128,256]{1,2,0:T(8,128)S(1)}, f32[2,128,256]{1,2,0:T(8,128)S(1)}, u32[]{:S(2)}, u32[]{:S(2)}) collective-permute-start(f32[2,128,256]{1,2,0:T(8,128)S(1)} %bitcast.141), channel_id=1, source_target_pairs={{16,0},{20,4},{24,8},{28,12},{32,16},{36,20},{40,24},{44,28},{48,3... | collective-permute-start | bytes 786440 | tf_op jit(solution)/shard_map/ppermute | solution.py:13
  95.6 16.1 %collective-permute-start.11 = (f32[2,128,256]{1,2,0:T(8,128)S(1)}, f32[2,128,256]{1,2,0:T(8,128)S(1)}, u32[]{:S(2)}, u32[]{:S(2)}) collective-permute-start(f32[2,128,256]{1,2,0:T(8,128)S(1)} %bitcast.140), channel_id=1, source_target_pairs={{20,0},{24,4},{28,8},{32,12},{36,16},{40,20},{44,24},{48,28},{52,3... | collective-permute-start | bytes 786440 | tf_op jit(solution)/shard_map/ppermute | solution.py:13
  96.9 16.1 %collective-permute-start.12 = (f32[2,128,256]{1,2,0:T(8,128)S(1)}, f32[2,128,256]{1,2,0:T(8,128)S(1)}, u32[]{:S(2)}, u32[]{:S(2)}) collective-permute-start(f32[2,128,256]{1,2,0:T(8,128)S(1)} %bitcast.139), channel_id=1, source_target_pairs={{24,0},{28,4},{32,8},{36,12},{40,16},{44,20},{48,24},{52,28},{56,3... | collective-permute-start | bytes 786440 | tf_op jit(solution)/shard_map/ppermute | solution.py:13
  98.2 27.7 %collective-permute-start.13 = (f32[2,128,256]{1,2,0:T(8,128)S(1)}, f32[2,128,256]{1,2,0:T(8,128)S(1)}, u32[]{:S(2)}, u32[]{:S(2)}) collective-permute-start(f32[2,128,256]{1,2,0:T(8,128)S(1)} %bitcast.138), channel_id=1, source_target_pairs={{28,0},{32,4},{36,8},{40,12},{44,16},{48,20},{52,24},{56,28},{60,3... | collective-permute-start | bytes 786440 | tf_op jit(solution)/shard_map/ppermute | solution.py:13
  99.5 26.4 %collective-permute-start.7 = (f32[2,128,256]{1,2,0:T(8,128)S(1)}, f32[2,128,256]{1,2,0:T(8,128)S(1)}, u32[]{:S(2)}, u32[]{:S(2)}) collective-permute-start(f32[2,128,256]{1,2,0:T(8,128)S(1)} %bitcast.137), channel_id=1, source_target_pairs={{4,0},{8,4},{12,8},{16,12},{20,16},{24,20},{28,24},{32,28},{36,32}... | collective-permute-start | bytes 786440 | tf_op jit(solution)/shard_map/ppermute | solution.py:13
  104.4 21.5 %collective-permute-start.8 = (f32[2,128,256]{1,2,0:T(8,128)S(1)}, f32[2,128,256]{1,2,0:T(8,128)S(1)}, u32[]{:S(2)}, u32[]{:S(2)}) collective-permute-start(f32[2,128,256]{1,2,0:T(8,128)S(1)} %bitcast.136), channel_id=1, source_target_pairs={{8,0},{12,4},{16,8},{20,12},{24,16},{28,20},{32,24},{36,28},{40,32... | collective-permute-start | bytes 786440 | tf_op jit(solution)/shard_map/ppermute | solution.py:13
  111.7 14.2 %collective-permute-start.9 = (f32[2,128,256]{1,2,0:T(8,128)S(1)}, f32[2,128,256]{1,2,0:T(8,128)S(1)}, u32[]{:S(2)}, u32[]{:S(2)}) collective-permute-start(f32[2,128,256]{1,2,0:T(8,128)S(1)} %bitcast.135), channel_id=1, source_target_pairs={{12,0},{16,4},{20,8},{24,12},{28,16},{32,20},{36,24},{40,28},{44,3... | collective-permute-start | bytes 786440 | tf_op jit(solution)/shard_map/ppermute | solution.py:13
Sparse Core Ops, SparseCore 0:
  150.2 210.9 all-reduce.4
where the time goes:
time: 375 us; the launch traced here: 374 us
  waiting for transfers between devices  234 us (62%)
  matrix products  40.2 us (11%)
  starting transfers between devices  37.9 us (10%)
  local copies, waits for them, and re-layouts  20.1 us (5%)
  between operations  15.1 us (4%)
  blocking collectives  15 us (4%)
  other arithmetic  10.7 us (3%)
    psum x1, waiting for transfers between devices, on_device(): lax.psum((down_key, down_value, up_key, up_value), 'wide')  211 us
    ppermute x14, starting transfers between devices, passed_along(): return lax.ppermute(array, axis, pairs)  37.9 us
    ppermute x14, waiting for transfers between devices, passed_along(): return lax.ppermute(array, axis, pairs)  23.4 us
    psum x1, blocking collectives, on_device(): h_key, h_value = lax.psum((part_key, part_value), 'narrow')  15 us
    dot_general x1, matrix products, stretch_grads(): jnp.einsum('gmqk,qgmd->kgd', dscore, query, preferred_element_type=jnp.fl...  9.35 us
    dot_general x1, matrix products, stretch_grads(): jnp.einsum('gmqk,qgmd->kgd', prob_b, dout, preferred_element_type=jnp.flo...  9.14 us
    unnamed x21, local copies, waits for them, and re-layouts  8.06 us
  transfers between devices with their start and end apart: 15, of which 5 were waited for; matrix products, arithmetic and copies ran while one was open for 2% of the time, Pallas kernels for 0%

commit v1 on v0

--- a/solution.py
+++ b/solution.py
@@ -71,19 +71,24 @@
     u_value = jnp.dot(enc_rows, value_down, preferred_element_type=jnp.float32).astype(jnp.bfloat16)
     part_key = jnp.dot(key_grad, key_up.T, preferred_element_type=jnp.float32)
     part_value = jnp.dot(value_grad, value_up.T, preferred_element_type=jnp.float32)
-    h_key, h_value = lax.psum((part_key, part_value), "narrow")
-    h_key = h_key.astype(jnp.bfloat16)
-    h_value = h_value.astype(jnp.bfloat16)
+    narrow_count = lax.axis_size("narrow")
+    rank = part_key.shape[1]
+    piece = rank // narrow_count
+    parts = jnp.stack(
+        [part_key.reshape(rows, narrow_count, piece), part_value.reshape(rows, narrow_count, piece)], 2
+    )
+    h_both = lax.psum_scatter(parts, "narrow", scatter_dimension=1, tiled=True)
+    h_both = h_both.reshape(rows, 2 * piece).astype(jnp.bfloat16)
     up_key = jnp.dot(u_key.T, key_grad, preferred_element_type=jnp.float32)
     up_value = jnp.dot(u_value.T, value_grad, preferred_element_type=jnp.float32)
-    down_key = jnp.dot(enc_rows.T, h_key, preferred_element_type=jnp.float32)
-    down_value = jnp.dot(enc_rows.T, h_value, preferred_element_type=jnp.float32)
-    down_key, down_value, up_key, up_value = lax.psum(
-        (down_key, down_value, up_key, up_value), "wide"
-    )
-    share = down_key.shape[0] // wide_count
-    down_key = lax.dynamic_slice_in_dim(down_key, stretch * share, share, 0)
-    down_value = lax.dynamic_slice_in_dim(down_value, stretch * share, share, 0)
+    down = jnp.dot(enc_rows.T, h_both, preferred_element_type=jnp.float32)
+    down = lax.psum_scatter(down, "wide", scatter_dimension=0, tiled=True)
+    up_key, up_value = lax.psum((up_key, up_value), "wide")
+    share = down.shape[0]
+    down = lax.all_gather(down.reshape(share, 2, piece), "narrow", axis=2, tiled=False)
+    down = down.reshape(share, 2, rank)
+    down_key = down[:, 0]
+    down_value = down[:, 1]
     return (down_key, down_value, up_key, up_value)
 
 

time: 375 us -> 501 us (1.34)
  waiting for transfers between devices: 234 us -> 344 us
  blocking collectives: 15 us -> 24.1 us
  local copies, waits for them, and re-layouts: 20.1 us -> 29.2 us
    unnamed x1 -> x3, waiting for transfers between devices: 0.02 us -> 148 us
    psum x1, waiting for transfers between devices: 211 us -> 174 us  [on_device(): up_key, up_value = lax.psum((up_key, up_value), 'wide')]
    psum x1 -> x0, blocking collectives: 15 us -> none  [on_device(): h_key, h_value = lax.psum((part_key, part_value), 'narrow')]
    unnamed x0 -> x1, blocking collectives: none -> 14.6 us
    another operation x1 -> x5, local copies, waits for them, and re-layouts: 0.07 us -> 11.3 us  [on_device(): jnp.stack([dkey.reshape(span, rows, cols), dval.reshape(span, rows, cols)...]
    all_gather x0 -> x1, blocking collectives: none -> 9.43 us  [on_device(): lax.all_gather(down.reshape(share, 2, piece), 'narrow', axis=2, tiled=False)]
    unnamed x21 -> x28, local copies, waits for them, and re-layouts: 8.06 us -> 11.1 us
  transfers between devices with their start and end apart: 15 -> 16, of which waited for: 5 -> 6; matrix products, arithmetic and copies ran while one was open for 2% -> 3% of each run, Pallas kernels for 0% -> 0%
where the time goes in v1:
time: 501 us; the launch traced here: 500 us
  waiting for transfers between devices  344 us (69%)
  starting transfers between devices  38 us (8%)
  matrix products  36.7 us (7%)
  local copies, waits for them, and re-layouts  29.2 us (6%)
  blocking collectives  24.1 us (5%)
  between operations  15.1 us (3%)
  other arithmetic  12.1 us (2%)
    psum x1, waiting for transfers between devices, on_device(): up_key, up_value = lax.psum((up_key, up_value), 'wide')  174 us
    unnamed x3, waiting for transfers between devices  148 us
    ppermute x14, starting transfers between devices, passed_along(): return lax.ppermute(array, axis, pairs)  37.9 us
    ppermute x14, waiting for transfers between devices, passed_along(): return lax.ppermute(array, axis, pairs)  22.9 us
    unnamed x1, blocking collectives  14.6 us
    another operation x5, local copies, waits for them, and re-layouts, on_device(): jnp.stack([dkey.reshape(span, rows, cols), dval.reshape(span, rows, cols)...  11.3 us
    unnamed x28, local copies, waits for them, and re-layouts  11.1 us
  transfers between devices with their start and end apart: 16, of which 6 were waited for; matrix products, arithmetic and copies ran while one was open for 3% of the time, Pallas kernels for 0%

profile of v1, /device:TPU:1, one launch (start us, length us, event | category | flops | bytes accessed | tf_op | source)
XLA Modules:
  0.0 499.5 jit_solution(16557086793061364701)
XLA Ops:
  8.2 4.6 collective-permute-start
  12.8 3.2 collective-permute-start.1
  16.0 3.5 collective-permute-start.2
  19.5 3.6 collective-permute-start.3
  23.2 5.2 %collective-permute-start.4 = (bf16[2,128,256]{2,1,0:T(8,128)(2,1)S(1)}, bf16[2,128,256]{2,1,0:T(8,128)(2,1)S(1)}, u32[]{:S(2)}, u32[]{:S(2)}) collective-permute-start(bf16[2,128,256]{2,1,0:T(8,128)(2,1)S(1)} %pad_maximum_fusion), channel_id=1, source_target_pairs={{0,20},{4,24},{8,28},{12,32},{16,36},{20,40},{24,44},{28,48},{32,5... | collective-permute-start | bytes 393224 | tf_op jit(solution)/shard_map/ppermute | solution.py:13
  31.3 2.6 reshape.66
  36.3 2.8 collective-permute-start.5
  39.1 4.9 collective-permute-start.6
  47.6 5.7 %bitcast_reduce_fusion = (f32[2,4,512]{2,1,0:T(4,128)S(1)}, f32[2,1024,512,4]{2,1,3,0:T(8,128)S(1)}) fusion(pred[1024]{0:T(1024)(128)(4,1)S(1)} %broadcast_bitcast_fusion, bf16[512,2,4,128]{3,2,1,0:T(4,128)(2,1)} %reshape.66, bf16[1024,2,128,1]{2,1,0,3:T(2,128)(2,1)} %bitcast.151), kind=kOutput, calls=%fused_computation.4 | convolution fusion | flops 1090514944 | bytes 18367488 | tf_op jit(solution)/shard_map/qgmd,kgd->gmqk/dot_general | solution.py:18
  53.3 7.2 %bitcast_divide_fusion = f32[2,4,512,1024]{2,3,1,0:T(8,128)} fusion(f32[2,1024,512,4]{2,1,3,0:T(8,128)S(1)} %get-tuple-element.30, f32[2,4,512]{2,1,0:T(4,128)S(1)} %get-tuple-element.29, pred[1024]{0:T(1024)(128)(4,1)S(1)} %broadcast_bitcast_fusion), kind=kLoop, calls=%fused_computation.3 | loop fusion | flops 16777216 | bytes 33571840 | tf_op jit(solution)/shard_map/div | solution.py:21
  60.6 9.1 %fusion.14 = f32[1024,2,128]{2,0,1:T(8,128)} fusion(bf16[512,2,4,128]{0,3,2,1:T(8,128)(2,1)S(1)} %bitcast.145, f32[2,4,512,1024]{2,3,1,0:T(8,128)} %bitcast_divide_fusion), kind=kOutput, calls=%fused_computation.16 | convolution fusion | flops 1077936128 | bytes 18874368 | tf_op jit(solution)/shard_map/gmqk,qgmd->kgd/dot_general | solution.py:28
  69.6 7.1 %fusion.11 = f32[512,2,4]{0,2,1:T(4,128)S(1)} fusion(bf16[512,2,4,128]{0,3,2,1:T(8,128)(2,1)S(1)} %bitcast.146, bf16[1024,2,128,1]{0,2,3,1:T(8,128)(2,1)S(1)} %copy.72, f32[2,4,512,1024]{2,3,1,0:T(8,128)} %bitcast_divide_fusion), kind=kOutput, calls=%fused_computation.15 | convolution fusion | flops 1079504896 | bytes 18366464 | tf_op jit(solution)/shard_map/gmqk,kgd->qgmd/dot_general | solution.py:23
  77.2 9.4 %fusion.23 = f32[1024,2,128]{2,0,1:T(8,128)} fusion(f32[2,4,512,1024]{2,3,1,0:T(8,128)} %bitcast_divide_fusion, f32[2,4,512]{2,1,0:T(4,128)S(1)} %copy.61, bf16[1024,2,128,1]{0,2,3,1:T(8,128)(2,1)S(1)} %copy.72, bf16[512,2,4,128]{0,3,2,1:T(8,128)(2,1)S(1)} %bitcast.147, bf16[512,2,4,128]{3,2,1,0:T(4,128)(2,1)} %reshape.66), kind=kOutput, calls=%fused_computation.19 | convolution fusion | flops 2160328704 | bytes 20463616 | tf_op jit(solution)/shard_map/gmqk,qgmd->kgd/dot_general | solution.py:27
  91.7 3.0 copy.90
  94.7 3.1 reshape.81
  107.6 2.6 collective-permute-done.10
  111.6 6.0 %collective-permute-done.11 = f32[2,128,256]{2,1,0:T(8,128)S(1)} collective-permute-done((f32[2,128,256]{2,1,0:T(8,128)S(1)}, f32[2,128,256]{2,1,0:T(8,128)S(1)}, u32[]{:S(2)}, u32[]{:S(2)}) %collective-permute-start.11) | collective-permute-done | bytes 262176 | tf_op jit(solution)/shard_map/ppermute | solution.py:13
  119.5 12.4 %collective-permute-done.13 = f32[2,128,256]{2,1,0:T(8,128)} collective-permute-done((f32[2,128,256]{2,1,0:T(8,128)}, f32[2,128,256]{2,1,0:T(8,128)}, u32[]{:S(2)}, u32[]{:S(2)}) %collective-permute-start.13) | collective-permute-done | bytes 262176 | tf_op jit(solution)/shard_map/ppermute | solution.py:13
  133.8 14.6 %all-reduce.6 = bf16[128,4,2,32]{0,3,1,2:T(8,128)(2,1)S(1)} all-reduce(f32[128,4,2,32]{0,3,1,2:T(8,128)S(1)} %pad_maximum_fusion.1), channel_id=2, replica_groups=mesh['wide'=64,'narrow'=4] {'narrow'}, use_global_device_ids=true, to_apply=%region_4.5.clone | all-reduce | flops 32768 | bytes 196608
  151.4 2.5 fusion.26
  154.0 2.5 fusion.27
  156.5 147.6 %reduce-scatter.7.cloned.1.call-done = f32[64,64]{1,0:T(8,128)} async-done(((f32[4096,64]{1,0:T(8,128)}), f32[64,64]{1,0:T(8,128)}) %reduce-scatter.7.cloned.1.call-update) | async-done | bytes 16400
  304.9 9.4 %all_gather.3 = f32[64,2,4,32]{0,3,2,1:T(8,128)S(1)} all-gather(f32[64,2,1,32]{0,3,2,1:T(8,128)S(1)} %bitcast.156), channel_id=1, replica_groups=mesh['wide'=64,'narrow'=4] {'narrow'}, dimensions={2}, use_global_device_ids=true | all-gather | bytes 81920 | tf_op jit(solution)/shard_map/all_gather | solution.py:88
  315.7 173.8 %all-reduce.5.cloned.1.call-done = (f32[128,256]{1,0:T(8,128)}, f32[128,256]{1,0:T(8,128)}) async-done(((f32[128,256]{1,0:T(8,128)}, f32[128,256]{1,0:T(8,128)}), (f32[128,256]{1,0:T(8,128)}, f32[128,256]{1,0:T(8,128)})) %all-reduce.5.cloned.1.call-update) | async-done | bytes 262160 | tf_op jit(solution)/shard_map/psum | solution.py:86
  (75 shorter events, 37.9 us)
Async XLA Ops:
  7.2 141.9 %copy-start = (bf16[128,4096]{1,0:T(8,128)(2,1)S(1)}, bf16[128,4096]{1,0:T(8,128)(2,1)}, u32[]{:S(2)}) copy-start(bf16[128,4096]{1,0:T(8,128)(2,1)} %param.15) | copy-start | bytes 3145732
  7.2 296.9 %reduce-scatter.7.cloned.1.call-start = ((), (), s32[]{:S(2)}) async-start(), calls=%async_computation.1 | async-start | bytes 2129920
  8.2 28.1 %collective-permute-start = (bf16[2,128,256]{2,1,0:T(8,128)(2,1)S(1)}, bf16[2,128,256]{2,1,0:T(8,128)(2,1)S(1)}, u32[]{:S(2)}, u32[]{:S(2)}) collective-permute-start(bf16[2,128,256]{2,1,0:T(8,128)(2,1)S(1)} %pad_maximum_fusion), channel_id=1, source_target_pairs={{0,4},{4,8},{8,12},{12,16},{16,20},{20,24},{24,28},{28,32},{32,36}... | collective-permute-start | bytes 393224 | tf_op jit(solution)/shard_map/ppermute | solution.py:13
  12.8 26.3 %collective-permute-start.1 = (bf16[2,128,256]{2,1,0:T(8,128)(2,1)S(1)}, bf16[2,128,256]{2,1,0:T(8,128)(2,1)S(1)}, u32[]{:S(2)}, u32[]{:S(2)}) collective-permute-start(bf16[2,128,256]{2,1,0:T(8,128)(2,1)S(1)} %pad_maximum_fusion), channel_id=1, source_target_pairs={{0,8},{4,12},{8,16},{12,20},{16,24},{20,28},{24,32},{28,36},{32,40... | collective-permute-start | bytes 393224 | tf_op jit(solution)/shard_map/ppermute | solution.py:13
  16.0 28.1 %collective-permute-start.2 = (bf16[2,128,256]{2,1,0:T(8,128)(2,1)S(1)}, bf16[2,128,256]{2,1,0:T(8,128)(2,1)S(1)}, u32[]{:S(2)}, u32[]{:S(2)}) collective-permute-start(bf16[2,128,256]{2,1,0:T(8,128)(2,1)S(1)} %pad_maximum_fusion), channel_id=1, source_target_pairs={{0,12},{4,16},{8,20},{12,24},{16,28},{20,32},{24,36},{28,40},{32,4... | collective-permute-start | bytes 393224 | tf_op jit(solution)/shard_map/ppermute | solution.py:13
  19.5 24.6 %collective-permute-start.3 = (bf16[2,128,256]{2,1,0:T(8,128)(2,1)S(1)}, bf16[2,128,256]{2,1,0:T(8,128)(2,1)S(1)}, u32[]{:S(2)}, u32[]{:S(2)}) collective-permute-start(bf16[2,128,256]{2,1,0:T(8,128)(2,1)S(1)} %pad_maximum_fusion), channel_id=1, source_target_pairs={{0,16},{4,20},{8,24},{12,28},{16,32},{20,36},{24,40},{28,44},{32,4... | collective-permute-start | bytes 393224 | tf_op jit(solution)/shard_map/ppermute | solution.py:13
  23.2 21.0 %collective-permute-start.4 = (bf16[2,128,256]{2,1,0:T(8,128)(2,1)S(1)}, bf16[2,128,256]{2,1,0:T(8,128)(2,1)S(1)}, u32[]{:S(2)}, u32[]{:S(2)}) collective-permute-start(bf16[2,128,256]{2,1,0:T(8,128)(2,1)S(1)} %pad_maximum_fusion), channel_id=1, source_target_pairs={{0,20},{4,24},{8,28},{12,32},{16,36},{20,40},{24,44},{28,48},{32,5... | collective-permute-start | bytes 393224 | tf_op jit(solution)/shard_map/ppermute | solution.py:13
  36.3 7.9 %collective-permute-start.5 = (bf16[2,128,256]{2,1,0:T(8,128)(2,1)S(1)}, bf16[2,128,256]{2,1,0:T(8,128)(2,1)S(1)}, u32[]{:S(2)}, u32[]{:S(2)}) collective-permute-start(bf16[2,128,256]{2,1,0:T(8,128)(2,1)S(1)} %pad_maximum_fusion), channel_id=1, source_target_pairs={{0,24},{4,28},{8,32},{12,36},{16,40},{20,44},{24,48},{28,52},{32,5... | collective-permute-start | bytes 393224 | tf_op jit(solution)/shard_map/ppermute | solution.py:13
  39.1 6.9 %collective-permute-start.6 = (bf16[2,128,256]{2,1,0:T(8,128)(2,1)S(1)}, bf16[2,128,256]{2,1,0:T(8,128)(2,1)S(1)}, u32[]{:S(2)}, u32[]{:S(2)}) collective-permute-start(bf16[2,128,256]{2,1,0:T(8,128)(2,1)S(1)} %pad_maximum_fusion), channel_id=1, source_target_pairs={{0,28},{4,32},{8,36},{12,40},{16,44},{20,48},{24,52},{28,56},{32,6... | collective-permute-start | bytes 393224 | tf_op jit(solution)/shard_map/ppermute | solution.py:13
  77.2 41.8 %copy-start.5 = (u32[256]{0:T(256)S(1)}, u32[256]{0:T(256)}, u32[]{:S(2)}) copy-start(u32[256]{0:T(256)} %constant.20) | copy-start | bytes 3076
  77.2 56.3 %copy-start.3 = (bf16[128,256]{1,0:T(8,128)(2,1)S(1)}, bf16[128,256]{1,0:T(8,128)(2,1)}, u32[]{:S(2)}) copy-start(bf16[128,256]{1,0:T(8,128)(2,1)} %param.19) | copy-start | bytes 196612
  77.2 56.5 %copy-start.4 = (bf16[128,256]{1,0:T(8,128)(2,1)S(1)}, bf16[128,256]{1,0:T(8,128)(2,1)}, u32[]{:S(2)}) copy-start(bf16[128,256]{1,0:T(8,128)(2,1)} %param.17) | copy-start | bytes 196612
  100.2 10.1 %collective-permute-start.10 = (f32[2,128,256]{2,1,0:T(8,128)S(1)}, f32[2,128,256]{2,1,0:T(8,128)S(1)}, u32[]{:S(2)}, u32[]{:S(2)}) collective-permute-start(f32[2,128,256]{2,1,0:T(8,128)S(1)} %get-tuple-element.22), channel_id=1, source_target_pairs={{16,0},{20,4},{24,8},{28,12},{32,16},{36,20},{40,24},{44,28},{48,3... | collective-permute-start | bytes 786440 | tf_op jit(solution)/shard_map/ppermute | solution.py:13
  101.5 16.1 %collective-permute-start.11 = (f32[2,128,256]{2,1,0:T(8,128)S(1)}, f32[2,128,256]{2,1,0:T(8,128)S(1)}, u32[]{:S(2)}, u32[]{:S(2)}) collective-permute-start(f32[2,128,256]{2,1,0:T(8,128)S(1)} %get-tuple-element.21), channel_id=1, source_target_pairs={{20,0},{24,4},{28,8},{32,12},{36,16},{40,20},{44,24},{48,28},{52,3... | collective-permute-start | bytes 786440 | tf_op jit(solution)/shard_map/ppermute | solution.py:13
  102.8 16.7 %collective-permute-start.12 = (f32[2,128,256]{2,1,0:T(8,128)}, f32[2,128,256]{2,1,0:T(8,128)}, u32[]{:S(2)}, u32[]{:S(2)}) collective-permute-start(f32[2,128,256]{2,1,0:T(8,128)} %get-tuple-element.20), channel_id=1, source_target_pairs={{24,0},{28,4},{32,8},{36,12},{40,16},{44,20},{48,24},{52,28},{56,3... | collective-permute-start | bytes 786440 | tf_op jit(solution)/shard_map/ppermute | solution.py:13
  104.1 27.8 %collective-permute-start.13 = (f32[2,128,256]{2,1,0:T(8,128)}, f32[2,128,256]{2,1,0:T(8,128)}, u32[]{:S(2)}, u32[]{:S(2)}) collective-permute-start(f32[2,128,256]{2,1,0:T(8,128)} %get-tuple-element.19), channel_id=1, source_target_pairs={{28,0},{32,4},{36,8},{40,12},{44,16},{48,20},{52,24},{56,28},{60,3... | collective-permute-start | bytes 786440 | tf_op jit(solution)/shard_map/ppermute | solution.py:13
  105.4 26.5 %collective-permute-start.7 = (f32[2,128,256]{2,1,0:T(8,128)}, f32[2,128,256]{2,1,0:T(8,128)}, u32[]{:S(2)}, u32[]{:S(2)}) collective-permute-start(f32[2,128,256]{2,1,0:T(8,128)} %get-tuple-element.18), channel_id=1, source_target_pairs={{4,0},{8,4},{12,8},{16,12},{20,16},{24,20},{28,24},{32,28},{36,32}... | collective-permute-start | bytes 786440 | tf_op jit(solution)/shard_map/ppermute | solution.py:13
  110.3 8.6 %copy-start.1 = (f32[2,128,256]{2,1,0:T(8,128)}, f32[2,128,256]{2,1,0:T(8,128)S(1)}, u32[]{:S(2)}) copy-start(f32[2,128,256]{2,1,0:T(8,128)S(1)} %collective-permute-done.10) | copy-start | bytes 786436
  110.3 21.6 %collective-permute-start.8 = (f32[2,128,256]{2,1,0:T(8,128)}, f32[2,128,256]{2,1,0:T(8,128)}, u32[]{:S(2)}, u32[]{:S(2)}) collective-permute-start(f32[2,128,256]{2,1,0:T(8,128)} %get-tuple-element.24), channel_id=1, source_target_pairs={{8,0},{12,4},{16,8},{20,12},{24,16},{28,20},{32,24},{36,28},{40,32... | collective-permute-start | bytes 786440 | tf_op jit(solution)/shard_map/ppermute | solution.py:13
  117.6 1.3 copy-start.2
  117.6 14.3 %collective-permute-start.9 = (f32[2,128,256]{2,1,0:T(8,128)S(1)}, f32[2,128,256]{2,1,0:T(8,128)}, u32[]{:S(2)}, u32[]{:S(2)}) collective-permute-start(f32[2,128,256]{2,1,0:T(8,128)S(1)} %get-tuple-element.23), channel_id=1, source_target_pairs={{12,0},{16,4},{20,8},{24,12},{28,16},{32,20},{36,24},{40,28},{44,3... | collective-permute-start | bytes 786440 | tf_op jit(solution)/shard_map/ppermute | solution.py:13
  151.4 338.2 %all-reduce.5.cloned.1.call-start = ((), (), s32[]{:S(2)}) async-start(), calls=%async_computation.2 | async-start | bytes 524288 | tf_op jit(solution)/shard_map/psum | solution.py:86
Sparse Core Ops, SparseCore 0:
  151.5 152.5 reduce-scatter.6
  308.2 181.3 all-reduce.4

commit v2 on v1

--- a/solution.py
+++ b/solution.py
@@ -11,6 +11,41 @@
     devices = lax.axis_size(axis)
     pairs = [(i, i + by) for i in range(devices) if 0 <= i + by < devices]
     return lax.ppermute(array, axis, pairs)
+
+
+def swapped(array, axis, bit):
+    devices = lax.axis_size(axis)
+    pairs = [(i, i ^ bit) for i in range(devices)]
+    return lax.ppermute(array, axis, pairs)
+
+
+def scattered_sum(x, axis):
+    devices = lax.axis_size(axis)
+    me = lax.axis_index(axis)
+    bit = 1
+    while bit < devices:
+        pair = x.reshape(x.shape[0] // 2, 2, *x.shape[1:])
+        mine = (me // bit) % 2
+        keep = lax.dynamic_index_in_dim(pair, mine, axis=1, keepdims=False)
+        give = lax.dynamic_index_in_dim(pair, 1 - mine, axis=1, keepdims=False)
+        x = keep + swapped(give, axis, bit)
+        bit *= 2
+    return x[0]
+
+
+def gathered(y, axis):
+    devices = lax.axis_size(axis)
+    me = lax.axis_index(axis)
+    y = y[None]
+    bit = devices // 2
+    while bit >= 1:
+        other = swapped(y, axis, bit)
+        first = (me // bit) % 2 == 0
+        low = jnp.where(first, y, other)
+        high = jnp.where(first, other, y)
+        y = jnp.stack([low, high], 1).reshape(y.shape[0] * 2, *y.shape[1:])
+        bit //= 2
+    return y
 
 
 def stretch_grads(query, dout, keys, values, valid):
@@ -42,7 +77,8 @@
     value_up,
 ):
     wide_count = lax.axis_size("wide")
-    span = min(8, wide_count // 2)
+    narrow_count = lax.axis_size("narrow")
+    span = 8
     rows = mem_key.shape[0]
     cols = mem_key.shape[1]
     local_heads = cols // HEAD_SIZE
@@ -50,11 +86,11 @@
     starts = jnp.cumsum(file_lengths) - file_lengths
     first = jnp.max(jnp.where(starts <= stretch, starts, 0))
     position = stretch - first
-    paired = jnp.stack([mem_key, memory_values])
-    blocks = [paired]
-    for offset in range(1, span):
-        blocks.append(passed_along(paired, "wide", offset))
-    window = jnp.stack(blocks)
+    window = jnp.stack([mem_key, memory_values])[None]
+    reach = 1
+    while reach < span:
+        window = jnp.concatenate([window, passed_along(window, "wide", reach)], 0)
+        reach *= 2
     keys = window[:, 0].reshape(span * rows, local_heads, HEAD_SIZE)
     values = window[:, 1].reshape(span * rows, local_heads, HEAD_SIZE)
     valid = jnp.repeat(jnp.arange(span, dtype=jnp.int32) <= position, rows)
@@ -62,34 +98,38 @@
     dout = out_grad.reshape(out_grad.shape[0], local_heads, Q_PER_KV, HEAD_SIZE)
     dkey, dval = stretch_grads(query, dout, keys, values, valid)
     contrib = jnp.stack([dkey.reshape(span, rows, cols), dval.reshape(span, rows, cols)], 1)
+    reach = span // 2
+    while reach >= 1:
+        contrib = contrib[:reach] + passed_along(contrib[reach : 2 * reach], "wide", -reach)
+        reach //= 2
     total = contrib[0]
-    for offset in range(1, span):
-        total = total + passed_along(contrib[offset], "wide", -offset)
     key_grad = total[0].astype(jnp.bfloat16)
     value_grad = total[1].astype(jnp.bfloat16)
     u_key = jnp.dot(enc_rows, key_down, preferred_element_type=jnp.float32).astype(jnp.bfloat16)
     u_value = jnp.dot(enc_rows, value_down, preferred_element_type=jnp.float32).astype(jnp.bfloat16)
     part_key = jnp.dot(key_grad, key_up.T, preferred_element_type=jnp.float32)
     part_value = jnp.dot(value_grad, value_up.T, preferred_element_type=jnp.float32)
-    narrow_count = lax.axis_size("narrow")
     rank = part_key.shape[1]
     piece = rank // narrow_count
-    parts = jnp.stack(
-        [part_key.reshape(rows, narrow_count, piece), part_value.reshape(rows, narrow_count, piece)], 2
+    parts = jnp.concatenate(
+        [
+            part_key.reshape(rows, narrow_count, piece).transpose(1, 0, 2),
+            part_value.reshape(rows, narrow_count, piece).transpose(1, 0, 2),
+        ],
+        2,
     )
-    h_both = lax.psum_scatter(parts, "narrow", scatter_dimension=1, tiled=True)
-    h_both = h_both.reshape(rows, 2 * piece).astype(jnp.bfloat16)
+    h_both = scattered_sum(parts, "narrow").astype(jnp.bfloat16)
     up_key = jnp.dot(u_key.T, key_grad, preferred_element_type=jnp.float32)
     up_value = jnp.dot(u_value.T, value_grad, preferred_element_type=jnp.float32)
     down = jnp.dot(enc_rows.T, h_both, preferred_element_type=jnp.float32)
-    down = lax.psum_scatter(down, "wide", scatter_dimension=0, tiled=True)
-    up_key, up_value = lax.psum((up_key, up_value), "wide")
-    share = down.shape[0]
-    down = lax.all_gather(down.reshape(share, 2, piece), "narrow", axis=2, tiled=False)
-    down = down.reshape(share, 2, rank)
-    down_key = down[:, 0]
-    down_value = down[:, 1]
-    return (down_key, down_value, up_key, up_value)
+    width = down.shape[0] // wide_count
+    up_both = jnp.stack([up_key, up_value]).reshape(wide_count, -1)
+    joined = jnp.concatenate([down.reshape(wide_count, width * 2 * piece), up_both], 1)
+    joined = scattered_sum(joined, "wide")
+    down = joined[: width * 2 * piece].reshape(width, 2, piece)
+    up_both = gathered(joined[width * 2 * piece :], "wide").reshape(2, rank, cols)
+    down = gathered(down, "narrow").transpose(1, 2, 0, 3).reshape(width, 2, rank)
+    return (down[:, 0], down[:, 1], up_both[0], up_both[1])
 
 
 def solution(mesh):

time: 501 us -> 232 us (0.46)
  waiting for transfers between devices: 344 us -> 78.4 us
  starting transfers between devices: 38 us -> 70 us
  blocking collectives: 24.1 us -> 0 us
  between operations: 15.1 us -> 2.06 us
    psum x1 -> x0, waiting for transfers between devices: 174 us -> none  [on_device(): up_key, up_value = lax.psum((up_key, up_value), 'wide')]
    unnamed x3 -> x0, waiting for transfers between devices: 148 us -> none
    ppermute x0 -> x16, starting transfers between devices: none -> 47.8 us  [swapped(): return lax.ppermute(array, axis, pairs)]
    ppermute x0 -> x16, waiting for transfers between devices: none -> 29.5 us  [swapped(): return lax.ppermute(array, axis, pairs)]
    ppermute x14 -> x6, waiting for transfers between devices: 22.9 us -> 48.9 us  [passed_along(): return lax.ppermute(array, axis, pairs)]
    ppermute x14 -> x6, starting transfers between devices: 37.9 us -> 22.2 us  [passed_along(): return lax.ppermute(array, axis, pairs)]
    unnamed x1 -> x0, blocking collectives: 14.6 us -> none
    all_gather x1 -> x0, blocking collectives: 9.43 us -> none  [on_device(): lax.all_gather(down.reshape(share, 2, piece), 'narrow', axis=2, tiled=False)]
  transfers between devices with their start and end apart: 16 -> 22, of which waited for: 6 -> 19; matrix products, arithmetic and copies ran while one was open for 3% -> 5% of each run, Pallas kernels for 0% -> 0%
where the time goes in v2:
time: 232 us; the launch traced here: 231 us
  waiting for transfers between devices  78.4 us (34%)
  starting transfers between devices  70 us (30%)
  matrix products  36.5 us (16%)
  local copies, waits for them, and re-layouts  31.7 us (14%)
  other arithmetic  12.5 us (5%)
    ppermute x6, waiting for transfers between devices, passed_along(): return lax.ppermute(array, axis, pairs)  48.9 us
    ppermute x16, starting transfers between devices, swapped(): return lax.ppermute(array, axis, pairs)  47.8 us
    ppermute x16, waiting for transfers between devices, swapped(): return lax.ppermute(array, axis, pairs)  29.5 us
    ppermute x6, starting transfers between devices, passed_along(): return lax.ppermute(array, axis, pairs)  22.2 us
    another operation x5, local copies, waits for them, and re-layouts, on_device(): jnp.stack([dkey.reshape(span, rows, cols), dval.reshape(span, rows, cols)...  11.2 us
    dot_general x1, matrix products, stretch_grads(): jnp.einsum('gmqk,qgmd->kgd', dscore, query, preferred_element_type=jnp.fl...  9.46 us
    dot_general x1, matrix products, stretch_grads(): jnp.einsum('gmqk,qgmd->kgd', prob_b, dout, preferred_element_type=jnp.flo...  9.09 us
    div x1, other arithmetic, stretch_grads(): prob = expo / jnp.sum(expo, axis=-1, keepdims=True)  7.28 us
  transfers between devices with their start and end apart: 22, of which 19 were waited for; matrix products, arithmetic and copies ran while one was open for 5% of the time, Pallas kernels for 0%

profile of v2, /device:TPU:1, one launch (start us, length us, event | category | flops | bytes accessed | tf_op | source)
XLA Modules:
  0.0 231.2 jit_solution(14209516264552329516)
XLA Ops:
  1.6 4.6 %collective-permute-start = (bf16[1,2,128,256]{3,2,1,0:T(8,128)(2,1)S(1)}, bf16[1,2,128,256]{3,2,1,0:T(8,128)(2,1)S(1)}, u32[]{:S(2)}, u32[]{:S(2)}) collective-permute-start(bf16[1,2,128,256]{3,2,1,0:T(8,128)(2,1)S(1)} %maximum_bitcast_fusion), channel_id=1, source_target_pairs={{0,4},{4,8},{8,12},{12,16},{16,20},{20,24},{24,28},{28,32},{32,36}... | collective-permute-start | bytes 393224 | tf_op jit(solution)/shard_map/ppermute | solution.py:13
  8.2 3.2 %collective-permute-start.1 = (bf16[2,2,128,256]{3,2,1,0:T(8,128)(2,1)S(1)}, bf16[2,2,128,256]{3,2,1,0:T(8,128)(2,1)S(1)}, u32[]{:S(2)}, u32[]{:S(2)}) collective-permute-start(bf16[2,2,128,256]{3,2,1,0:T(8,128)(2,1)S(1)} %pad_maximum_fusion.2), channel_id=1, source_target_pairs={{0,8},{4,12},{8,16},{12,20},{16,24},{20,28},{24,32},{28,36},{32,40... | collective-permute-start | bytes 786440 | tf_op jit(solution)/shard_map/ppermute | solution.py:13
  11.4 4.4 %collective-permute-done.1 = bf16[2,2,128,256]{3,2,1,0:T(8,128)(2,1)S(1)} collective-permute-done((bf16[2,2,128,256]{3,2,1,0:T(8,128)(2,1)S(1)}, bf16[2,2,128,256]{3,2,1,0:T(8,128)(2,1)S(1)}, u32[]{:S(2)}, u32[]{:S(2)}) %collective-permute-start.1) | collective-permute-done | bytes 262176 | tf_op jit(solution)/shard_map/ppermute | solution.py:13
  15.8 6.0 %collective-permute-start.2 = (bf16[4,2,128,256]{3,2,1,0:T(8,128)(2,1)S(1)}, bf16[4,2,128,256]{3,2,1,0:T(8,128)(2,1)}, u32[]{:S(2)}, u32[]{:S(2)}) collective-permute-start(bf16[4,2,128,256]{3,2,1,0:T(8,128)(2,1)S(1)} %pad_maximum_fusion.1), channel_id=1, source_target_pairs={{0,16},{4,20},{8,24},{12,28},{16,32},{20,36},{24,40},{28,44},{32,4... | collective-permute-start | bytes 1572872 | tf_op jit(solution)/shard_map/ppermute | solution.py:13
  32.5 5.7 %bitcast_reduce_fusion = (f32[2,4,512]{2,1,0:T(4,128)S(1)}, f32[2,1024,512,4]{2,1,3,0:T(8,128)S(1)}) fusion(pred[1024]{0:T(1024)(128)(4,1)S(1)} %broadcast_bitcast_fusion, bf16[512,2,4,128]{3,2,1,0:T(4,128)(2,1)} %reshape.122, bf16[1024,2,128,1]{2,1,0,3:T(2,128)(2,1)} %bitcast.171), kind=kOutput, calls=%fused_computation.4 | convolution fusion | flops 1090514944 | bytes 18367488 | tf_op jit(solution)/shard_map/qgmd,kgd->gmqk/dot_general | solution.py:53
  38.2 7.3 %bitcast_divide_fusion = f32[2,4,512,1024]{2,3,1,0:T(8,128)} fusion(f32[2,1024,512,4]{2,1,3,0:T(8,128)S(1)} %get-tuple-element.57, f32[2,4,512]{2,1,0:T(4,128)S(1)} %get-tuple-element.56, pred[1024]{0:T(1024)(128)(4,1)S(1)} %broadcast_bitcast_fusion), kind=kLoop, calls=%fused_computation.3 | loop fusion | flops 16777216 | bytes 33571840 | tf_op jit(solution)/shard_map/div | solution.py:56
  45.5 9.1 %fusion.14 = f32[1024,2,128]{2,0,1:T(8,128)} fusion(bf16[512,2,4,128]{0,3,2,1:T(8,128)(2,1)S(1)} %bitcast.163, f32[2,4,512,1024]{2,3,1,0:T(8,128)} %bitcast_divide_fusion), kind=kOutput, calls=%fused_computation.16 | convolution fusion | flops 1077936128 | bytes 18874368 | tf_op jit(solution)/shard_map/gmqk,qgmd->kgd/dot_general | solution.py:63
  54.6 7.1 %fusion.11 = f32[512,2,4]{0,2,1:T(4,128)S(1)} fusion(bf16[512,2,4,128]{0,3,2,1:T(8,128)(2,1)S(1)} %bitcast.164, bf16[1024,2,128,1]{0,2,3,1:T(8,128)(2,1)S(1)} %copy.143, f32[2,4,512,1024]{2,3,1,0:T(8,128)} %bitcast_divide_fusion), kind=kOutput, calls=%fused_computation.15 | convolution fusion | flops 1079504896 | bytes 18366464 | tf_op jit(solution)/shard_map/gmqk,kgd->qgmd/dot_general | solution.py:58
  61.7 9.5 %fusion.23 = f32[1024,2,128]{2,0,1:T(8,128)} fusion(f32[2,4,512,1024]{2,3,1,0:T(8,128)} %bitcast_divide_fusion, f32[2,4,512]{2,1,0:T(4,128)S(1)} %bitcast.179, bf16[1024,2,128,1]{0,2,3,1:T(8,128)(2,1)S(1)} %copy.143, bf16[512,2,4,128]{0,3,2,1:T(8,128)(2,1)S(1)} %bitcast.165, bf16[512,2,4,128]{3,2,1,0:T(4,128)(2,1)} %reshape.122), kind=kOutput, calls=%fused_computation.19 | convolution fusion | flops 2160328704 | bytes 20463616 | tf_op jit(solution)/shard_map/gmqk,qgmd->kgd/dot_general | solution.py:62
  76.4 3.0 %copy.161 = f32[1024,2,128]{2,1,0:T(2,128)} copy(f32[1024,2,128]{2,0,1:T(8,128)} %fusion.14) | data formatting | bytes 2097152 | tf_op jit(solution)/shard_map/stack;reshape | solution.py:100
  79.4 3.0 %reshape.147 = f32[8,1,128,256]{3,2,1,0:T(8,128)} reshape(f32[1024,2,128]{2,1,0:T(2,128)} %copy.161) | data formatting | bytes 2097152 | tf_op jit(solution)/shard_map/stack;reshape | solution.py:100
  85.2 24.7 %collective-permute-done.3 = f32[4,2,128,256]{3,2,1,0:T(8,128)S(1)} collective-permute-done((f32[4,2,128,256]{3,2,1,0:T(8,128)S(1)}, f32[4,2,128,256]{3,2,1,0:T(8,128)S(1)}, u32[]{:S(2)}, u32[]{:S(2)}) %collective-permute-start.3) | collective-permute-done | bytes 1048608 | tf_op jit(solution)/shard_map/ppermute | solution.py:13
  111.3 11.6 %collective-permute-done.4 = f32[2,2,128,256]{3,2,1,0:T(8,128)S(1)} collective-permute-done((f32[2,2,128,256]{3,2,1,0:T(8,128)S(1)}, f32[2,2,128,256]{3,2,1,0:T(8,128)S(1)}, u32[]{:S(2)}, u32[]{:S(2)}) %collective-permute-start.4) | collective-permute-done | bytes 524320 | tf_op jit(solution)/shard_map/ppermute | solution.py:13
  123.1 5.9 %collective-permute-start.5 = (f32[1,2,128,256]{3,2,1,0:T(8,128)S(1)}, f32[1,2,128,256]{3,2,1,0:T(8,128)S(1)}, u32[]{:S(2)}, u32[]{:S(2)}) collective-permute-start(f32[1,2,128,256]{3,2,1,0:T(8,128)S(1)} %slice.77), channel_id=1, source_target_pairs={{4,0},{8,4},{12,8},{16,12},{20,16},{24,20},{28,24},{32,28},{36,32}... | collective-permute-start | bytes 786440 | tf_op jit(solution)/shard_map/ppermute | solution.py:13
  129.1 5.2 %collective-permute-done.5 = f32[1,2,128,256]{3,2,1,0:T(8,128)S(1)} collective-permute-done((f32[1,2,128,256]{3,2,1,0:T(8,128)S(1)}, f32[1,2,128,256]{3,2,1,0:T(8,128)S(1)}, u32[]{:S(2)}, u32[]{:S(2)}) %collective-permute-start.5) | collective-permute-done | bytes 262176 | tf_op jit(solution)/shard_map/ppermute | solution.py:13
  157.2 7.9 %collective-permute-done.9 = f32[16,5120]{1,0:T(8,128)S(1)} collective-permute-done((f32[16,5120]{1,0:T(8,128)S(1)}, f32[16,5120]{1,0:T(8,128)S(1)}, u32[]{:S(2)}, u32[]{:S(2)}) %collective-permute-start.9) | collective-permute-done | bytes 327712 | tf_op jit(solution)/shard_map/ppermute | solution.py:19
  165.7 5.5 %collective-permute-start.10 = (f32[8,5120]{1,0:T(8,128)S(1)}, f32[8,5120]{1,0:T(8,128)S(1)}, u32[]{:S(2)}, u32[]{:S(2)}) collective-permute-start(f32[8,5120]{1,0:T(8,128)S(1)} %bitcast.173), channel_id=1, source_target_pairs={{0,16},{4,20},{8,24},{12,28},{16,0},{20,4},{24,8},{28,12},{32,48},... | collective-permute-start | bytes 491528 | tf_op jit(solution)/shard_map/ppermute | solution.py:19
  171.2 3.6 %collective-permute-done.10 = f32[8,5120]{1,0:T(8,128)S(1)} collective-permute-done((f32[8,5120]{1,0:T(8,128)S(1)}, f32[8,5120]{1,0:T(8,128)S(1)}, u32[]{:S(2)}, u32[]{:S(2)}) %collective-permute-start.10) | collective-permute-done | bytes 163872 | tf_op jit(solution)/shard_map/ppermute | solution.py:19
  178.9 7.9 %collective-permute-start.12 = (f32[2,5120]{1,0:T(2,128)S(1)}, f32[2,5120]{1,0:T(2,128)S(1)}, u32[]{:S(2)}, u32[]{:S(2)}) collective-permute-start(f32[2,5120]{1,0:T(2,128)S(1)} %bitcast.180), channel_id=1, source_target_pairs={{0,64},{4,68},{8,72},{12,76},{16,80},{20,84},{24,88},{28,92},{32,9... | collective-permute-start | bytes 122888 | tf_op jit(solution)/shard_map/ppermute | solution.py:19
  188.3 3.2 %collective-permute-start.13 = (f32[1,5120]{1,0:T(1,128)S(1)}, f32[1,5120]{1,0:T(1,128)S(1)}, u32[]{:S(2)}, u32[]{:S(2)}) collective-permute-start(f32[1,5120]{1,0:T(1,128)S(1)} %constant_dynamic-slice_fusion), channel_id=1, source_target_pairs={{0,128},{4,132},{8,136},{12,140},{16,144},{20,148},{24,152},{28,15... | collective-permute-start | bytes 61448 | tf_op jit(solution)/shard_map/ppermute | solution.py:19
  191.5 3.4 %collective-permute-done.13 = f32[1,5120]{1,0:T(1,128)S(1)} collective-permute-done((f32[1,5120]{1,0:T(1,128)S(1)}, f32[1,5120]{1,0:T(1,128)S(1)}, u32[]{:S(2)}, u32[]{:S(2)}) %collective-permute-start.13) | collective-permute-done | bytes 20512 | tf_op jit(solution)/shard_map/ppermute | solution.py:19
  195.0 3.2 %collective-permute-start.16 = (f32[1,1024]{1,0:T(1,128)S(1)}, f32[1,1024]{1,0:T(1,128)S(1)}, u32[]{:S(2)}, u32[]{:S(2)}) collective-permute-start(f32[1,1024]{1,0:T(1,128)S(1)} %slice.83), channel_id=1, source_target_pairs={{0,128},{4,132},{8,136},{12,140},{16,144},{20,148},{24,152},{28,15... | collective-permute-start | bytes 12296 | tf_op jit(solution)/shard_map/ppermute | solution.py:19
  198.2 3.3 %collective-permute-done.16 = f32[1,1024]{1,0:T(1,128)S(1)} collective-permute-done((f32[1,1024]{1,0:T(1,128)S(1)}, f32[1,1024]{1,0:T(1,128)S(1)}, u32[]{:S(2)}, u32[]{:S(2)}) %collective-permute-start.16) | collective-permute-done | bytes 4128 | tf_op jit(solution)/shard_map/ppermute | solution.py:19
  217.8 9.9 %collective-permute-start.21 = (f32[32,1024]{1,0:T(8,128)S(1)}, f32[32,1024]{1,0:T(8,128)S(1)}, u32[]{:S(2)}, u32[]{:S(2)}) collective-permute-start(f32[32,1024]{1,0:T(8,128)S(1)} %reshape.136), channel_id=1, source_target_pairs={{0,4},{4,0},{8,12},{12,8},{16,20},{20,16},{24,28},{28,24},{32,36},... | collective-permute-start | bytes 393224 | tf_op jit(solution)/shard_map/ppermute | solution.py:19
  (134 shorter events, 71.0 us)
Async XLA Ops:
  0.6 135.4 %copy-start = (bf16[128,4096]{1,0:T(8,128)(2,1)S(1)}, bf16[128,4096]{1,0:T(8,128)(2,1)}, u32[]{:S(2)}) copy-start(bf16[128,4096]{1,0:T(8,128)(2,1)} %param.15) | copy-start | bytes 3145732
  1.6 6.5 %collective-permute-start = (bf16[1,2,128,256]{3,2,1,0:T(8,128)(2,1)S(1)}, bf16[1,2,128,256]{3,2,1,0:T(8,128)(2,1)S(1)}, u32[]{:S(2)}, u32[]{:S(2)}) collective-permute-start(bf16[1,2,128,256]{3,2,1,0:T(8,128)(2,1)S(1)} %maximum_bitcast_fusion), channel_id=1, source_target_pairs={{0,4},{4,8},{8,12},{12,16},{16,20},{20,24},{24,28},{28,32},{32,36}... | collective-permute-start | bytes 393224 | tf_op jit(solution)/shard_map/ppermute | solution.py:13
  8.2 7.6 %collective-permute-start.1 = (bf16[2,2,128,256]{3,2,1,0:T(8,128)(2,1)S(1)}, bf16[2,2,128,256]{3,2,1,0:T(8,128)(2,1)S(1)}, u32[]{:S(2)}, u32[]{:S(2)}) collective-permute-start(bf16[2,2,128,256]{3,2,1,0:T(8,128)(2,1)S(1)} %pad_maximum_fusion.2), channel_id=1, source_target_pairs={{0,8},{4,12},{8,16},{12,20},{16,24},{20,28},{24,32},{28,36},{32,40... | collective-permute-start | bytes 786440 | tf_op jit(solution)/shard_map/ppermute | solution.py:13
  15.8 14.0 %collective-permute-start.2 = (bf16[4,2,128,256]{3,2,1,0:T(8,128)(2,1)S(1)}, bf16[4,2,128,256]{3,2,1,0:T(8,128)(2,1)}, u32[]{:S(2)}, u32[]{:S(2)}) collective-permute-start(bf16[4,2,128,256]{3,2,1,0:T(8,128)(2,1)S(1)} %pad_maximum_fusion.1), channel_id=1, source_target_pairs={{0,16},{4,20},{8,24},{12,28},{16,32},{20,36},{24,40},{28,44},{32,4... | collective-permute-start | bytes 1572872 | tf_op jit(solution)/shard_map/ppermute | solution.py:13
  61.7 72.8 %copy-start.2 = (bf16[128,256]{1,0:T(8,128)(2,1)S(1)}, bf16[128,256]{1,0:T(8,128)(2,1)}, u32[]{:S(2)}) copy-start(bf16[128,256]{1,0:T(8,128)(2,1)} %param.17) | copy-start | bytes 196612
  83.9 26.0 %collective-permute-start.3 = (f32[4,2,128,256]{3,2,1,0:T(8,128)S(1)}, f32[4,2,128,256]{3,2,1,0:T(8,128)S(1)}, u32[]{:S(2)}, u32[]{:S(2)}) collective-permute-start(f32[4,2,128,256]{3,2,1,0:T(8,128)S(1)} %slice.73), channel_id=1, source_target_pairs={{16,0},{20,4},{24,8},{28,12},{32,16},{36,20},{40,24},{44,28},{48,3... | collective-permute-start | bytes 3145736 | tf_op jit(solution)/shard_map/ppermute | solution.py:13
  110.0 12.9 %collective-permute-start.4 = (f32[2,2,128,256]{3,2,1,0:T(8,128)S(1)}, f32[2,2,128,256]{3,2,1,0:T(8,128)S(1)}, u32[]{:S(2)}, u32[]{:S(2)}) collective-permute-start(f32[2,2,128,256]{3,2,1,0:T(8,128)S(1)} %slice.75), channel_id=1, source_target_pairs={{8,0},{12,4},{16,8},{20,12},{24,16},{28,20},{32,24},{36,28},{40,32... | collective-permute-start | bytes 1572872 | tf_op jit(solution)/shard_map/ppermute | solution.py:13
  123.1 11.2 %collective-permute-start.5 = (f32[1,2,128,256]{3,2,1,0:T(8,128)S(1)}, f32[1,2,128,256]{3,2,1,0:T(8,128)S(1)}, u32[]{:S(2)}, u32[]{:S(2)}) collective-permute-start(f32[1,2,128,256]{3,2,1,0:T(8,128)S(1)} %slice.77), channel_id=1, source_target_pairs={{4,0},{8,4},{12,8},{16,12},{20,16},{24,20},{28,24},{32,28},{36,32}... | collective-permute-start | bytes 786440 | tf_op jit(solution)/shard_map/ppermute | solution.py:13
  134.7 5.0 %collective-permute-start.6 = (f32[2,128,64]{1,2,0:T(8,128)S(1)}, f32[2,128,64]{1,2,0:T(8,128)S(1)}, u32[]{:S(2)}, u32[]{:S(2)}) collective-permute-start(f32[2,128,64]{1,2,0:T(8,128)S(1)} %dynamic-slice_bitcast_fusion), channel_id=1, source_target_pairs={{0,1},{1,0},{2,3},{3,2},{4,5},{5,4},{6,7},{7,6},{8,9},{9,8},{10,11... | collective-permute-start | bytes 196616 | tf_op jit(solution)/shard_map/ppermute | solution.py:19
  139.8 4.6 %collective-permute-start.7 = (f32[1,128,64]{1,2,0:T(8,128)S(1)}, f32[1,128,64]{1,2,0:T(8,128)S(1)}, u32[]{:S(2)}, u32[]{:S(2)}) collective-permute-start(f32[1,128,64]{1,2,0:T(8,128)S(1)} %constant_dynamic-slice_fusion.11), channel_id=1, source_target_pairs={{0,2},{1,3},{2,0},{3,1},{4,6},{5,7},{6,4},{7,5},{8,10},{9,11},{10,... | collective-permute-start | bytes 98312 | tf_op jit(solution)/shard_map/ppermute | solution.py:19
  152.1 2.2 collective-permute-start.8
  155.5 9.6 %collective-permute-start.9 = (f32[16,5120]{1,0:T(8,128)S(1)}, f32[16,5120]{1,0:T(8,128)S(1)}, u32[]{:S(2)}, u32[]{:S(2)}) collective-permute-start(f32[16,5120]{1,0:T(8,128)S(1)} %bitcast.172), channel_id=1, source_target_pairs={{0,8},{4,12},{8,0},{12,4},{16,24},{20,28},{24,16},{28,20},{32,40},... | collective-permute-start | bytes 983048 | tf_op jit(solution)/shard_map/ppermute | solution.py:19
  165.7 9.1 %collective-permute-start.10 = (f32[8,5120]{1,0:T(8,128)S(1)}, f32[8,5120]{1,0:T(8,128)S(1)}, u32[]{:S(2)}, u32[]{:S(2)}) collective-permute-start(f32[8,5120]{1,0:T(8,128)S(1)} %bitcast.173), channel_id=1, source_target_pairs={{0,16},{4,20},{8,24},{12,28},{16,0},{20,4},{24,8},{28,12},{32,48},... | collective-permute-start | bytes 491528 | tf_op jit(solution)/shard_map/ppermute | solution.py:19
  175.2 3.5 %collective-permute-start.11 = (f32[4,5120]{1,0:T(4,128)S(1)}, f32[4,5120]{1,0:T(4,128)S(1)}, u32[]{:S(2)}, u32[]{:S(2)}) collective-permute-start(f32[4,5120]{1,0:T(4,128)S(1)} %bitcast.174), channel_id=1, source_target_pairs={{0,32},{4,36},{8,40},{12,44},{16,48},{20,52},{24,56},{28,60},{32,0... | collective-permute-start | bytes 245768 | tf_op jit(solution)/shard_map/ppermute | solution.py:19
  178.9 9.3 %collective-permute-start.12 = (f32[2,5120]{1,0:T(2,128)S(1)}, f32[2,5120]{1,0:T(2,128)S(1)}, u32[]{:S(2)}, u32[]{:S(2)}) collective-permute-start(f32[2,5120]{1,0:T(2,128)S(1)} %bitcast.180), channel_id=1, source_target_pairs={{0,64},{4,68},{8,72},{12,76},{16,80},{20,84},{24,88},{28,92},{32,9... | collective-permute-start | bytes 122888 | tf_op jit(solution)/shard_map/ppermute | solution.py:19
  188.3 6.6 %collective-permute-start.13 = (f32[1,5120]{1,0:T(1,128)S(1)}, f32[1,5120]{1,0:T(1,128)S(1)}, u32[]{:S(2)}, u32[]{:S(2)}) collective-permute-start(f32[1,5120]{1,0:T(1,128)S(1)} %constant_dynamic-slice_fusion), channel_id=1, source_target_pairs={{0,128},{4,132},{8,136},{12,140},{16,144},{20,148},{24,152},{28,15... | collective-permute-start | bytes 61448 | tf_op jit(solution)/shard_map/ppermute | solution.py:19
  195.0 6.5 %collective-permute-start.16 = (f32[1,1024]{1,0:T(1,128)S(1)}, f32[1,1024]{1,0:T(1,128)S(1)}, u32[]{:S(2)}, u32[]{:S(2)}) collective-permute-start(f32[1,1024]{1,0:T(1,128)S(1)} %slice.83), channel_id=1, source_target_pairs={{0,128},{4,132},{8,136},{12,140},{16,144},{20,148},{24,152},{28,15... | collective-permute-start | bytes 12296 | tf_op jit(solution)/shard_map/ppermute | solution.py:19
  201.5 5.2 %collective-permute-start.17 = (f32[2,1024]{1,0:T(2,128)S(1)}, f32[2,1024]{1,0:T(2,128)S(1)}, u32[]{:S(2)}, u32[]{:S(2)}) collective-permute-start(f32[2,1024]{1,0:T(2,128)S(1)} %maximum_bitcast_fusion.2), channel_id=1, source_target_pairs={{0,64},{4,68},{8,72},{12,76},{16,80},{20,84},{24,88},{28,92},{32,9... | collective-permute-start | bytes 24584 | tf_op jit(solution)/shard_map/ppermute | solution.py:19
  204.1 4.7 %collective-permute-start.14 = (f32[1,64,2,32]{3,2,1,0:T(2,128)S(1)}, f32[1,64,2,32]{3,2,1,0:T(2,128)S(1)}, u32[]{:S(2)}, u32[]{:S(2)}) collective-permute-start(f32[1,64,2,32]{3,2,1,0:T(2,128)S(1)} %broadcast_in_dim_reshape.4), channel_id=1, source_target_pairs={{0,2},{1,3},{2,0},{3,1},{4,6},{5,7},{6,4},{7,5},{8,10},{9,11},{10,... | collective-permute-start | bytes 49160 | tf_op jit(solution)/shard_map/ppermute | solution.py:19
  206.7 2.8 %collective-permute-start.18 = (f32[4,1024]{1,0:T(4,128)S(1)}, f32[4,1024]{1,0:T(4,128)S(1)}, u32[]{:S(2)}, u32[]{:S(2)}) collective-permute-start(f32[4,1024]{1,0:T(4,128)S(1)} %reshape.133), channel_id=1, source_target_pairs={{0,32},{4,36},{8,40},{12,44},{16,48},{20,52},{24,56},{28,60},{32,0... | collective-permute-start | bytes 49160 | tf_op jit(solution)/shard_map/ppermute | solution.py:19
  208.9 4.2 %collective-permute-start.15 = (f32[2,64,2,32]{3,2,1,0:T(2,128)S(1)}, f32[2,64,2,32]{3,2,1,0:T(2,128)S(1)}, u32[]{:S(2)}, u32[]{:S(2)}) collective-permute-start(f32[2,64,2,32]{3,2,1,0:T(2,128)S(1)} %maximum_bitcast_fusion.1), channel_id=1, source_target_pairs={{0,1},{1,0},{2,3},{3,2},{4,5},{5,4},{6,7},{7,6},{8,9},{9,8},{10,11... | collective-permute-start | bytes 98312 | tf_op jit(solution)/shard_map/ppermute | solution.py:19
  209.7 4.4 %collective-permute-start.19 = (f32[8,1024]{1,0:T(8,128)S(1)}, f32[8,1024]{1,0:T(8,128)S(1)}, u32[]{:S(2)}, u32[]{:S(2)}) collective-permute-start(f32[8,1024]{1,0:T(8,128)S(1)} %reshape.134), channel_id=1, source_target_pairs={{0,16},{4,20},{8,24},{12,28},{16,0},{20,4},{24,8},{28,12},{32,48},... | collective-permute-start | bytes 98312 | tf_op jit(solution)/shard_map/ppermute | solution.py:19
  214.3 3.2 %collective-permute-start.20 = (f32[16,1024]{1,0:T(8,128)S(1)}, f32[16,1024]{1,0:T(8,128)S(1)}, u32[]{:S(2)}, u32[]{:S(2)}) collective-permute-start(f32[16,1024]{1,0:T(8,128)S(1)} %reshape.135), channel_id=1, source_target_pairs={{0,8},{4,12},{8,0},{12,4},{16,24},{20,28},{24,16},{28,20},{32,40},... | collective-permute-start | bytes 196616 | tf_op jit(solution)/shard_map/ppermute | solution.py:19
  217.8 11.3 %collective-permute-start.21 = (f32[32,1024]{1,0:T(8,128)S(1)}, f32[32,1024]{1,0:T(8,128)S(1)}, u32[]{:S(2)}, u32[]{:S(2)}) collective-permute-start(f32[32,1024]{1,0:T(8,128)S(1)} %reshape.136), channel_id=1, source_target_pairs={{0,4},{4,0},{8,12},{12,8},{16,20},{20,16},{24,28},{28,24},{32,36},... | collective-permute-start | bytes 393224 | tf_op jit(solution)/shard_map/ppermute | solution.py:19
  (1 other events, 72.7 us)

commit v3 on v2

--- a/solution.py
+++ b/solution.py
@@ -31,6 +31,23 @@
         x = keep + swapped(give, axis, bit)
         bit *= 2
     return x[0]
+
+
+def scattered_sum_with(x, whole, axis):
+    devices = lax.axis_size(axis)
+    me = lax.axis_index(axis)
+    bit = 1
+    while bit < devices:
+        pair = x.reshape(x.shape[0] // 2, 2, *x.shape[1:])
+        mine = (me // bit) % 2
+        keep = lax.dynamic_index_in_dim(pair, mine, axis=1, keepdims=False)
+        give = lax.dynamic_index_in_dim(pair, 1 - mine, axis=1, keepdims=False)
+        message = jnp.concatenate([give.reshape(-1), whole.reshape(-1)])
+        back = swapped(message, axis, bit)
+        x = keep + back[: give.size].reshape(give.shape)
+        whole = whole + back[give.size :].reshape(whole.shape)
+        bit *= 2
+    return x[0], whole
 
 
 def gathered(y, axis):
@@ -123,11 +140,8 @@
     up_value = jnp.dot(u_value.T, value_grad, preferred_element_type=jnp.float32)
     down = jnp.dot(enc_rows.T, h_both, preferred_element_type=jnp.float32)
     width = down.shape[0] // wide_count
-    up_both = jnp.stack([up_key, up_value]).reshape(wide_count, -1)
-    joined = jnp.concatenate([down.reshape(wide_count, width * 2 * piece), up_both], 1)
-    joined = scattered_sum(joined, "wide")
-    down = joined[: width * 2 * piece].reshape(width, 2, piece)
-    up_both = gathered(joined[width * 2 * piece :], "wide").reshape(2, rank, cols)
+    down, up_both = scattered_sum_with(down.reshape(wide_count, width * 2 * piece), jnp.stack([up_key, up_value]), "wide")
+    down = down.reshape(width, 2, piece)
     down = gathered(down, "narrow").transpose(1, 2, 0, 3).reshape(width, 2, rank)
     return (down[:, 0], down[:, 1], up_both[0], up_both[1])
 

time: 232 us -> 250 us (1.078)
  waiting for transfers between devices: 78.4 us -> 112 us
  starting transfers between devices: 70 us -> 49.4 us
  local copies, waits for them, and re-layouts: 31.7 us -> 34.3 us
    ppermute x16 -> x10, waiting for transfers between devices: 29.5 us -> 63.3 us  [swapped(): return lax.ppermute(array, axis, pairs)]
    ppermute x16 -> x10, starting transfers between devices: 47.8 us -> 27.2 us  [swapped(): return lax.ppermute(array, axis, pairs)]
    slice x2 -> x20, local copies, waits for them, and re-layouts: 0.04 us -> 2.74 us  [the longest x12 1.47 us: scattered_sum_with(): x = keep + back[:give.size].reshape(give.shape)]
  transfers between devices with their start and end apart: 22 -> 16, of which waited for: 19 -> 15; matrix products, arithmetic and copies ran while one was open for 5% -> 5% of each run, Pallas kernels for 0% -> 0%
where the time goes in v3:
time: 250 us; the launch traced here: 248 us
  waiting for transfers between devices  112 us (45%)
  starting transfers between devices  49.4 us (20%)
  matrix products  36.5 us (15%)
  local copies, waits for them, and re-layouts  34.3 us (14%)
  other arithmetic  13.7 us (5%)
    ppermute x10, waiting for transfers between devices, swapped(): return lax.ppermute(array, axis, pairs)  63.3 us
    ppermute x6, waiting for transfers between devices, passed_along(): return lax.ppermute(array, axis, pairs)  48.9 us
    ppermute x10, starting transfers between devices, swapped(): return lax.ppermute(array, axis, pairs)  27.2 us
    ppermute x6, starting transfers between devices, passed_along(): return lax.ppermute(array, axis, pairs)  22.2 us
    another operation x5, local copies, waits for them, and re-layouts, on_device(): jnp.stack([dkey.reshape(span, rows, cols), dval.reshape(span, rows, cols)...  11.3 us
    dot_general x1, matrix products, stretch_grads(): jnp.einsum('gmqk,qgmd->kgd', dscore, query, preferred_element_type=jnp.fl...  9.47 us
    dot_general x1, matrix products, stretch_grads(): jnp.einsum('gmqk,qgmd->kgd', prob_b, dout, preferred_element_type=jnp.flo...  9.08 us
    div x1, other arithmetic, stretch_grads(): prob = expo / jnp.sum(expo, axis=-1, keepdims=True)  7.29 us
  transfers between devices with their start and end apart: 16, of which 15 were waited for; matrix products, arithmetic and copies ran while one was open for 5% of the time, Pallas kernels for 0%

profile of v3, /device:TPU:1, one launch (start us, length us, event | category | flops | bytes accessed | tf_op | source)
XLA Modules:
  0.0 248.2 jit_solution(16732173176821884634)
XLA Ops:
  1.6 4.6 %collective-permute-start = (bf16[1,2,128,256]{3,2,1,0:T(8,128)(2,1)S(1)}, bf16[1,2,128,256]{3,2,1,0:T(8,128)(2,1)S(1)}, u32[]{:S(2)}, u32[]{:S(2)}) collective-permute-start(bf16[1,2,128,256]{3,2,1,0:T(8,128)(2,1)S(1)} %maximum_bitcast_fusion), channel_id=1, source_target_pairs={{0,4},{4,8},{8,12},{12,16},{16,20},{20,24},{24,28},{28,32},{32,36}... | collective-permute-start | bytes 393224 | tf_op jit(solution)/shard_map/ppermute | solution.py:13
  8.2 3.2 %collective-permute-start.1 = (bf16[2,2,128,256]{3,2,1,0:T(8,128)(2,1)S(1)}, bf16[2,2,128,256]{3,2,1,0:T(8,128)(2,1)S(1)}, u32[]{:S(2)}, u32[]{:S(2)}) collective-permute-start(bf16[2,2,128,256]{3,2,1,0:T(8,128)(2,1)S(1)} %pad_maximum_fusion.8), channel_id=1, source_target_pairs={{0,8},{4,12},{8,16},{12,20},{16,24},{20,28},{24,32},{28,36},{32,40... | collective-permute-start | bytes 786440 | tf_op jit(solution)/shard_map/ppermute | solution.py:13
  11.4 4.4 %collective-permute-done.1 = bf16[2,2,128,256]{3,2,1,0:T(8,128)(2,1)S(1)} collective-permute-done((bf16[2,2,128,256]{3,2,1,0:T(8,128)(2,1)S(1)}, bf16[2,2,128,256]{3,2,1,0:T(8,128)(2,1)S(1)}, u32[]{:S(2)}, u32[]{:S(2)}) %collective-permute-start.1) | collective-permute-done | bytes 262176 | tf_op jit(solution)/shard_map/ppermute | solution.py:13
  15.8 5.9 %collective-permute-start.2 = (bf16[4,2,128,256]{3,2,1,0:T(8,128)(2,1)S(1)}, bf16[4,2,128,256]{3,2,1,0:T(8,128)(2,1)}, u32[]{:S(2)}, u32[]{:S(2)}) collective-permute-start(bf16[4,2,128,256]{3,2,1,0:T(8,128)(2,1)S(1)} %pad_maximum_fusion.2), channel_id=1, source_target_pairs={{0,16},{4,20},{8,24},{12,28},{16,32},{20,36},{24,40},{28,44},{32,4... | collective-permute-start | bytes 1572872 | tf_op jit(solution)/shard_map/ppermute | solution.py:13
  32.5 5.7 %bitcast_reduce_fusion = (f32[2,4,512]{2,1,0:T(4,128)S(1)}, f32[2,1024,512,4]{2,1,3,0:T(8,128)S(1)}) fusion(pred[1024]{0:T(1024)(128)(4,1)S(1)} %broadcast_bitcast_fusion, bf16[512,2,4,128]{3,2,1,0:T(4,128)(2,1)} %reshape.236, bf16[1024,2,128,1]{2,1,0,3:T(2,128)(2,1)} %bitcast.171), kind=kOutput, calls=%fused_computation.4 | convolution fusion | flops 1090514944 | bytes 18367488 | tf_op jit(solution)/shard_map/qgmd,kgd->gmqk/dot_general | solution.py:70
  38.2 7.3 %bitcast_divide_fusion = f32[2,4,512,1024]{2,3,1,0:T(8,128)} fusion(f32[2,1024,512,4]{2,1,3,0:T(8,128)S(1)} %get-tuple-element.49, f32[2,4,512]{2,1,0:T(4,128)S(1)} %get-tuple-element.48, pred[1024]{0:T(1024)(128)(4,1)S(1)} %broadcast_bitcast_fusion), kind=kLoop, calls=%fused_computation.3 | loop fusion | flops 16777216 | bytes 33571840 | tf_op jit(solution)/shard_map/div | solution.py:73
  45.5 9.1 %fusion.14 = f32[1024,2,128]{2,0,1:T(8,128)} fusion(bf16[512,2,4,128]{0,3,2,1:T(8,128)(2,1)S(1)} %bitcast.150, f32[2,4,512,1024]{2,3,1,0:T(8,128)} %bitcast_divide_fusion), kind=kOutput, calls=%fused_computation.16 | convolution fusion | flops 1077936128 | bytes 18874368 | tf_op jit(solution)/shard_map/gmqk,qgmd->kgd/dot_general | solution.py:80
  54.6 7.1 %fusion.11 = f32[512,2,4]{0,2,1:T(4,128)S(1)} fusion(bf16[512,2,4,128]{0,3,2,1:T(8,128)(2,1)S(1)} %bitcast.151, bf16[1024,2,128,1]{0,2,3,1:T(8,128)(2,1)S(1)} %copy.113, f32[2,4,512,1024]{2,3,1,0:T(8,128)} %bitcast_divide_fusion), kind=kOutput, calls=%fused_computation.15 | convolution fusion | flops 1079504896 | bytes 18366464 | tf_op jit(solution)/shard_map/gmqk,kgd->qgmd/dot_general | solution.py:75
  61.7 9.5 %fusion.23 = f32[1024,2,128]{2,0,1:T(8,128)} fusion(f32[2,4,512,1024]{2,3,1,0:T(8,128)} %bitcast_divide_fusion, f32[2,4,512]{2,1,0:T(4,128)S(1)} %bitcast.180, bf16[1024,2,128,1]{0,2,3,1:T(8,128)(2,1)S(1)} %copy.113, bf16[512,2,4,128]{0,3,2,1:T(8,128)(2,1)S(1)} %bitcast.152, bf16[512,2,4,128]{3,2,1,0:T(4,128)(2,1)} %reshape.236), kind=kOutput, calls=%fused_computation.19 | convolution fusion | flops 2160328704 | bytes 20463616 | tf_op jit(solution)/shard_map/gmqk,qgmd->kgd/dot_general | solution.py:79
  76.3 3.0 %copy.131 = f32[1024,2,128]{2,1,0:T(2,128)} copy(f32[1024,2,128]{2,0,1:T(8,128)} %fusion.14) | data formatting | bytes 2097152 | tf_op jit(solution)/shard_map/stack;reshape | solution.py:117
  79.4 3.1 %reshape.271 = f32[8,1,128,256]{3,2,1,0:T(8,128)} reshape(f32[1024,2,128]{2,1,0:T(2,128)} %copy.131) | data formatting | bytes 2097152 | tf_op jit(solution)/shard_map/stack;reshape | solution.py:117
  85.2 24.7 %collective-permute-done.3 = f32[4,2,128,256]{3,2,1,0:T(8,128)S(1)} collective-permute-done((f32[4,2,128,256]{3,2,1,0:T(8,128)S(1)}, f32[4,2,128,256]{3,2,1,0:T(8,128)S(1)}, u32[]{:S(2)}, u32[]{:S(2)}) %collective-permute-start.3) | collective-permute-done | bytes 1048608 | tf_op jit(solution)/shard_map/ppermute | solution.py:13
  111.3 11.6 %collective-permute-done.4 = f32[2,2,128,256]{3,2,1,0:T(8,128)S(1)} collective-permute-done((f32[2,2,128,256]{3,2,1,0:T(8,128)S(1)}, f32[2,2,128,256]{3,2,1,0:T(8,128)S(1)}, u32[]{:S(2)}, u32[]{:S(2)}) %collective-permute-start.4) | collective-permute-done | bytes 524320 | tf_op jit(solution)/shard_map/ppermute | solution.py:13
  123.1 5.9 %collective-permute-start.5 = (f32[1,2,128,256]{3,2,1,0:T(8,128)S(1)}, f32[1,2,128,256]{3,2,1,0:T(8,128)S(1)}, u32[]{:S(2)}, u32[]{:S(2)}) collective-permute-start(f32[1,2,128,256]{3,2,1,0:T(8,128)S(1)} %slice.210), channel_id=1, source_target_pairs={{4,0},{8,4},{12,8},{16,12},{20,16},{24,20},{28,24},{32,28},{36,32}... | collective-permute-start | bytes 786440 | tf_op jit(solution)/shard_map/ppermute | solution.py:13
  129.0 5.2 %collective-permute-done.5 = f32[1,2,128,256]{3,2,1,0:T(8,128)S(1)} collective-permute-done((f32[1,2,128,256]{3,2,1,0:T(8,128)S(1)}, f32[1,2,128,256]{3,2,1,0:T(8,128)S(1)}, u32[]{:S(2)}, u32[]{:S(2)}) %collective-permute-start.5) | collective-permute-done | bytes 262176 | tf_op jit(solution)/shard_map/ppermute | solution.py:13
  161.1 12.1 %collective-permute-done.9 = f32[131072]{0:T(1024)S(1)} collective-permute-done((f32[131072]{0:T(1024)S(1)}, f32[131072]{0:T(1024)S(1)}, u32[]{:S(2)}, u32[]{:S(2)}) %collective-permute-start.9) | collective-permute-done | bytes 524320 | tf_op jit(solution)/shard_map/ppermute | solution.py:19
  174.2 5.5 %collective-permute-start.10 = (f32[98304]{0:T(1024)S(1)}, f32[98304]{0:T(1024)S(1)}, u32[]{:S(2)}, u32[]{:S(2)}) collective-permute-start(f32[98304]{0:T(1024)S(1)} %pad_maximum_fusion.4), channel_id=1, source_target_pairs={{0,16},{4,20},{8,24},{12,28},{16,0},{20,4},{24,8},{28,12},{32,48},... | collective-permute-start | bytes 1179656 | tf_op jit(solution)/shard_map/ppermute | solution.py:19
  179.7 8.5 %collective-permute-done.10 = f32[98304]{0:T(1024)S(1)} collective-permute-done((f32[98304]{0:T(1024)S(1)}, f32[98304]{0:T(1024)S(1)}, u32[]{:S(2)}, u32[]{:S(2)}) %collective-permute-start.10) | collective-permute-done | bytes 393248 | tf_op jit(solution)/shard_map/ppermute | solution.py:19
  190.6 6.4 %collective-permute-done.11 = f32[81920]{0:T(1024)S(1)} collective-permute-done((f32[81920]{0:T(1024)S(1)}, f32[81920]{0:T(1024)S(1)}, u32[]{:S(2)}, u32[]{:S(2)}) %collective-permute-start.11) | collective-permute-done | bytes 327712 | tf_op jit(solution)/shard_map/ppermute | solution.py:19
  197.6 8.0 %collective-permute-start.12 = (f32[73728]{0:T(1024)S(1)}, f32[73728]{0:T(1024)S(1)}, u32[]{:S(2)}, u32[]{:S(2)}) collective-permute-start(f32[73728]{0:T(1024)S(1)} %pad_maximum_fusion.6), channel_id=1, source_target_pairs={{0,64},{4,68},{8,72},{12,76},{16,80},{20,84},{24,88},{28,92},{32,9... | collective-permute-start | bytes 884744 | tf_op jit(solution)/shard_map/ppermute | solution.py:19
  205.6 12.9 %collective-permute-done.12 = f32[73728]{0:T(1024)S(1)} collective-permute-done((f32[73728]{0:T(1024)S(1)}, f32[73728]{0:T(1024)S(1)}, u32[]{:S(2)}, u32[]{:S(2)}) %collective-permute-start.12) | collective-permute-done | bytes 294944 | tf_op jit(solution)/shard_map/ppermute | solution.py:19
  219.0 3.1 %collective-permute-start.13 = (f32[69632]{0:T(1024)S(1)}, f32[69632]{0:T(1024)S(1)}, u32[]{:S(2)}, u32[]{:S(2)}) collective-permute-start(f32[69632]{0:T(1024)S(1)} %pad_maximum_fusion.7), channel_id=1, source_target_pairs={{0,128},{4,132},{8,136},{12,140},{16,144},{20,148},{24,152},{28,15... | collective-permute-start | bytes 835592 | tf_op jit(solution)/shard_map/ppermute | solution.py:19
  222.3 15.2 %collective-permute-done.13 = f32[69632]{0:T(1024)S(1)} collective-permute-done((f32[69632]{0:T(1024)S(1)}, f32[69632]{0:T(1024)S(1)}, u32[]{:S(2)}, u32[]{:S(2)}) %collective-permute-start.13) | collective-permute-done | bytes 278560 | tf_op jit(solution)/shard_map/ppermute | solution.py:19
  243.5 2.9 %collective-permute-done.15 = f32[2,64,2,32]{3,2,1,0:T(2,128)S(1)} collective-permute-done((f32[2,64,2,32]{3,2,1,0:T(2,128)S(1)}, f32[2,64,2,32]{3,2,1,0:T(2,128)S(1)}, u32[]{:S(2)}, u32[]{:S(2)}) %collective-permute-start.15) | collective-permute-done | bytes 32800 | tf_op jit(solution)/shard_map/ppermute | solution.py:19
  (126 shorter events, 61.2 us)
Async XLA Ops:
  0.6 135.4 %copy-start = (bf16[128,4096]{1,0:T(8,128)(2,1)S(1)}, bf16[128,4096]{1,0:T(8,128)(2,1)}, u32[]{:S(2)}) copy-start(bf16[128,4096]{1,0:T(8,128)(2,1)} %param.15) | copy-start | bytes 3145732
  1.6 6.5 %collective-permute-start = (bf16[1,2,128,256]{3,2,1,0:T(8,128)(2,1)S(1)}, bf16[1,2,128,256]{3,2,1,0:T(8,128)(2,1)S(1)}, u32[]{:S(2)}, u32[]{:S(2)}) collective-permute-start(bf16[1,2,128,256]{3,2,1,0:T(8,128)(2,1)S(1)} %maximum_bitcast_fusion), channel_id=1, source_target_pairs={{0,4},{4,8},{8,12},{12,16},{16,20},{20,24},{24,28},{28,32},{32,36}... | collective-permute-start | bytes 393224 | tf_op jit(solution)/shard_map/ppermute | solution.py:13
  8.2 7.6 %collective-permute-start.1 = (bf16[2,2,128,256]{3,2,1,0:T(8,128)(2,1)S(1)}, bf16[2,2,128,256]{3,2,1,0:T(8,128)(2,1)S(1)}, u32[]{:S(2)}, u32[]{:S(2)}) collective-permute-start(bf16[2,2,128,256]{3,2,1,0:T(8,128)(2,1)S(1)} %pad_maximum_fusion.8), channel_id=1, source_target_pairs={{0,8},{4,12},{8,16},{12,20},{16,24},{20,28},{24,32},{28,36},{32,40... | collective-permute-start | bytes 786440 | tf_op jit(solution)/shard_map/ppermute | solution.py:13
  15.8 14.0 %collective-permute-start.2 = (bf16[4,2,128,256]{3,2,1,0:T(8,128)(2,1)S(1)}, bf16[4,2,128,256]{3,2,1,0:T(8,128)(2,1)}, u32[]{:S(2)}, u32[]{:S(2)}) collective-permute-start(bf16[4,2,128,256]{3,2,1,0:T(8,128)(2,1)S(1)} %pad_maximum_fusion.2), channel_id=1, source_target_pairs={{0,16},{4,20},{8,24},{12,28},{16,32},{20,36},{24,40},{28,44},{32,4... | collective-permute-start | bytes 1572872 | tf_op jit(solution)/shard_map/ppermute | solution.py:13
  61.7 72.7 %copy-start.1 = (bf16[128,256]{1,0:T(8,128)(2,1)S(1)}, bf16[128,256]{1,0:T(8,128)(2,1)}, u32[]{:S(2)}) copy-start(bf16[128,256]{1,0:T(8,128)(2,1)} %param.19) | copy-start | bytes 196612
  61.7 72.8 %copy-start.2 = (bf16[128,256]{1,0:T(8,128)(2,1)S(1)}, bf16[128,256]{1,0:T(8,128)(2,1)}, u32[]{:S(2)}) copy-start(bf16[128,256]{1,0:T(8,128)(2,1)} %param.17) | copy-start | bytes 196612
  83.9 26.0 %collective-permute-start.3 = (f32[4,2,128,256]{3,2,1,0:T(8,128)S(1)}, f32[4,2,128,256]{3,2,1,0:T(8,128)S(1)}, u32[]{:S(2)}, u32[]{:S(2)}) collective-permute-start(f32[4,2,128,256]{3,2,1,0:T(8,128)S(1)} %slice.206), channel_id=1, source_target_pairs={{16,0},{20,4},{24,8},{28,12},{32,16},{36,20},{40,24},{44,28},{48,3... | collective-permute-start | bytes 3145736 | tf_op jit(solution)/shard_map/ppermute | solution.py:13
  110.0 12.9 %collective-permute-start.4 = (f32[2,2,128,256]{3,2,1,0:T(8,128)S(1)}, f32[2,2,128,256]{3,2,1,0:T(8,128)S(1)}, u32[]{:S(2)}, u32[]{:S(2)}) collective-permute-start(f32[2,2,128,256]{3,2,1,0:T(8,128)S(1)} %slice.208), channel_id=1, source_target_pairs={{8,0},{12,4},{16,8},{20,12},{24,16},{28,20},{32,24},{36,28},{40,32... | collective-permute-start | bytes 1572872 | tf_op jit(solution)/shard_map/ppermute | solution.py:13
  123.1 11.2 %collective-permute-start.5 = (f32[1,2,128,256]{3,2,1,0:T(8,128)S(1)}, f32[1,2,128,256]{3,2,1,0:T(8,128)S(1)}, u32[]{:S(2)}, u32[]{:S(2)}) collective-permute-start(f32[1,2,128,256]{3,2,1,0:T(8,128)S(1)} %slice.210), channel_id=1, source_target_pairs={{4,0},{8,4},{12,8},{16,12},{20,16},{24,20},{28,24},{32,28},{36,32}... | collective-permute-start | bytes 786440 | tf_op jit(solution)/shard_map/ppermute | solution.py:13
  134.7 5.0 %collective-permute-start.6 = (f32[2,128,64]{1,2,0:T(8,128)S(1)}, f32[2,128,64]{1,2,0:T(8,128)S(1)}, u32[]{:S(2)}, u32[]{:S(2)}) collective-permute-start(f32[2,128,64]{1,2,0:T(8,128)S(1)} %dynamic-slice_bitcast_fusion), channel_id=1, source_target_pairs={{0,1},{1,0},{2,3},{3,2},{4,5},{5,4},{6,7},{7,6},{8,9},{9,8},{10,11... | collective-permute-start | bytes 196616 | tf_op jit(solution)/shard_map/ppermute | solution.py:19
  139.8 4.6 %collective-permute-start.7 = (f32[1,128,64]{1,2,0:T(8,128)S(1)}, f32[1,128,64]{1,2,0:T(8,128)S(1)}, u32[]{:S(2)}, u32[]{:S(2)}) collective-permute-start(f32[1,128,64]{1,2,0:T(8,128)S(1)} %constant_dynamic-slice_fusion.11), channel_id=1, source_target_pairs={{0,2},{1,3},{2,0},{3,1},{4,6},{5,7},{6,4},{7,5},{8,10},{9,11},{10,... | collective-permute-start | bytes 98312 | tf_op jit(solution)/shard_map/ppermute | solution.py:19
  153.2 2.5 %collective-permute-start.8 = (f32[196608]{0:T(1024)S(1)}, f32[196608]{0:T(1024)}, u32[]{:S(2)}, u32[]{:S(2)}) collective-permute-start(f32[196608]{0:T(1024)S(1)} %pad_maximum_fusion.1), channel_id=1, source_target_pairs={{0,4},{4,0},{8,12},{12,8},{16,20},{20,16},{24,28},{28,24},{32,36},... | collective-permute-start | bytes 2359304 | tf_op jit(solution)/shard_map/ppermute | solution.py:19
  159.4 13.8 %collective-permute-start.9 = (f32[131072]{0:T(1024)S(1)}, f32[131072]{0:T(1024)S(1)}, u32[]{:S(2)}, u32[]{:S(2)}) collective-permute-start(f32[131072]{0:T(1024)S(1)} %pad_maximum_fusion.3), channel_id=1, source_target_pairs={{0,8},{4,12},{8,0},{12,4},{16,24},{20,28},{24,16},{28,20},{32,40},... | collective-permute-start | bytes 1572872 | tf_op jit(solution)/shard_map/ppermute | solution.py:19
  174.2 14.0 %collective-permute-start.10 = (f32[98304]{0:T(1024)S(1)}, f32[98304]{0:T(1024)S(1)}, u32[]{:S(2)}, u32[]{:S(2)}) collective-permute-start(f32[98304]{0:T(1024)S(1)} %pad_maximum_fusion.4), channel_id=1, source_target_pairs={{0,16},{4,20},{8,24},{12,28},{16,0},{20,4},{24,8},{28,12},{32,48},... | collective-permute-start | bytes 1179656 | tf_op jit(solution)/shard_map/ppermute | solution.py:19
  188.9 8.1 %collective-permute-start.11 = (f32[81920]{0:T(1024)S(1)}, f32[81920]{0:T(1024)S(1)}, u32[]{:S(2)}, u32[]{:S(2)}) collective-permute-start(f32[81920]{0:T(1024)S(1)} %pad_maximum_fusion.5), channel_id=1, source_target_pairs={{0,32},{4,36},{8,40},{12,44},{16,48},{20,52},{24,56},{28,60},{32,0... | collective-permute-start | bytes 983048 | tf_op jit(solution)/shard_map/ppermute | solution.py:19
  197.6 20.9 %collective-permute-start.12 = (f32[73728]{0:T(1024)S(1)}, f32[73728]{0:T(1024)S(1)}, u32[]{:S(2)}, u32[]{:S(2)}) collective-permute-start(f32[73728]{0:T(1024)S(1)} %pad_maximum_fusion.6), channel_id=1, source_target_pairs={{0,64},{4,68},{8,72},{12,76},{16,80},{20,84},{24,88},{28,92},{32,9... | collective-permute-start | bytes 884744 | tf_op jit(solution)/shard_map/ppermute | solution.py:19
  219.0 18.5 %collective-permute-start.13 = (f32[69632]{0:T(1024)S(1)}, f32[69632]{0:T(1024)S(1)}, u32[]{:S(2)}, u32[]{:S(2)}) collective-permute-start(f32[69632]{0:T(1024)S(1)} %pad_maximum_fusion.7), channel_id=1, source_target_pairs={{0,128},{4,132},{8,136},{12,140},{16,144},{20,148},{24,152},{28,15... | collective-permute-start | bytes 835592 | tf_op jit(solution)/shard_map/ppermute | solution.py:19
  237.7 4.7 %collective-permute-start.14 = (f32[1,64,2,32]{3,2,1,0:T(2,128)S(1)}, f32[1,64,2,32]{3,2,1,0:T(2,128)S(1)}, u32[]{:S(2)}, u32[]{:S(2)}) collective-permute-start(f32[1,64,2,32]{3,2,1,0:T(2,128)S(1)} %add.195), channel_id=1, source_target_pairs={{0,2},{1,3},{2,0},{3,1},{4,6},{5,7},{6,4},{7,5},{8,10},{9,11},{10,... | collective-permute-start | bytes 49160 | tf_op jit(solution)/shard_map/ppermute | solution.py:19
  242.5 3.9 %collective-permute-start.15 = (f32[2,64,2,32]{3,2,1,0:T(2,128)S(1)}, f32[2,64,2,32]{3,2,1,0:T(2,128)S(1)}, u32[]{:S(2)}, u32[]{:S(2)}) collective-permute-start(f32[2,64,2,32]{3,2,1,0:T(2,128)S(1)} %maximum_bitcast_fusion.1), channel_id=1, source_target_pairs={{0,1},{1,0},{2,3},{3,2},{4,5},{5,4},{6,7},{7,6},{8,9},{9,8},{10,11... | collective-permute-start | bytes 98312 | tf_op jit(solution)/shard_map/ppermute | solution.py:19

commit v4 on v2

--- a/solution.py
+++ b/solution.py
@@ -1,6 +1,8 @@
 import jax
 import jax.numpy as jnp
 from jax import lax
+from jax.experimental import pallas as pl
+from jax.experimental.pallas import tpu as pltpu
 from jax.sharding import PartitionSpec as P
 
 HEAD_SIZE = 128
@@ -48,20 +50,63 @@
     return y
 
 
-def stretch_grads(query, dout, keys, values, valid):
+def attention_body(pos_ref, q_ref, do_ref, k_ref, v_ref, dk_ref, dv_ref):
+    m = pl.program_id(1)
     scale = HEAD_SIZE ** (-0.5)
-    score = jnp.einsum("qgmd,kgd->gmqk", query, keys, preferred_element_type=jnp.float32) * scale
-    mask = valid[None, None, None, :]
-    expo = jnp.where(mask, jnp.exp(jnp.where(mask, score, 0.0)), 0.0)
+    q = q_ref[...]
+    do = do_ref[...]
+    k = k_ref[...]
+    v = v_ref[...]
+    s = lax.dot_general(q, k, (((1,), (1,)), ((), ())), preferred_element_type=jnp.float32) * scale
+    block = lax.broadcasted_iota(jnp.int32, s.shape, 1) // 128
+    mask = block <= pos_ref[0]
+    expo = jnp.where(mask, jnp.exp(jnp.where(mask, s, 0.0)), 0.0)
     prob = expo / jnp.sum(expo, axis=-1, keepdims=True)
     prob_b = prob.astype(jnp.bfloat16)
-    outp = jnp.einsum("gmqk,kgd->qgmd", prob_b, values, preferred_element_type=jnp.float32)
-    delta = jnp.sum(dout.astype(jnp.float32) * outp, axis=-1)
-    dprob = jnp.einsum("qgmd,kgd->gmqk", dout, values, preferred_element_type=jnp.float32)
-    dscore = (prob * (dprob - jnp.transpose(delta, (1, 2, 0))[..., None])).astype(jnp.bfloat16)
-    dkey = jnp.einsum("gmqk,qgmd->kgd", dscore, query, preferred_element_type=jnp.float32) * scale
-    dval = jnp.einsum("gmqk,qgmd->kgd", prob_b, dout, preferred_element_type=jnp.float32)
-    return (dkey, dval)
+    outp = jnp.dot(prob_b, v, preferred_element_type=jnp.float32)
+    delta = jnp.sum(do.astype(jnp.float32) * outp, axis=-1, keepdims=True)
+    dprob = lax.dot_general(do, v, (((1,), (1,)), ((), ())), preferred_element_type=jnp.float32)
+    dscore = (prob * (dprob - delta)).astype(jnp.bfloat16)
+    dk = lax.dot_general(dscore, q, (((0,), (0,)), ((), ())), preferred_element_type=jnp.float32)
+    dv = lax.dot_general(prob_b, do, (((0,), (0,)), ((), ())), preferred_element_type=jnp.float32)
+
+    @pl.when(m == 0)
+    def _():
+        dk_ref[...] = dk
+        dv_ref[...] = dv
+
+    @pl.when(m > 0)
+    def _():
+        dk_ref[...] += dk
+        dv_ref[...] += dv
+
+
+def attention_grads(position, queries, out_grad, keys, values):
+    tokens = queries.shape[0]
+    window_rows, cols = keys.shape
+    heads = cols // HEAD_SIZE
+    scale = HEAD_SIZE ** (-0.5)
+    grid_spec = pltpu.PrefetchScalarGridSpec(
+        num_scalar_prefetch=1,
+        grid=(heads, Q_PER_KV),
+        in_specs=[
+            pl.BlockSpec((tokens, HEAD_SIZE), lambda g, m, p: (0, g * Q_PER_KV + m)),
+            pl.BlockSpec((tokens, HEAD_SIZE), lambda g, m, p: (0, g * Q_PER_KV + m)),
+            pl.BlockSpec((window_rows, HEAD_SIZE), lambda g, m, p: (0, g)),
+            pl.BlockSpec((window_rows, HEAD_SIZE), lambda g, m, p: (0, g)),
+        ],
+        out_specs=[
+            pl.BlockSpec((window_rows, HEAD_SIZE), lambda g, m, p: (0, g)),
+            pl.BlockSpec((window_rows, HEAD_SIZE), lambda g, m, p: (0, g)),
+        ],
+    )
+    dk, dv = pl.pallas_call(
+        attention_body,
+        grid_spec=grid_spec,
+        out_shape=[jax.ShapeDtypeStruct((window_rows, cols), jnp.float32)] * 2,
+        compiler_params=pltpu.CompilerParams(dimension_semantics=("arbitrary", "arbitrary")),
+    )(position.reshape(1).astype(jnp.int32), queries, out_grad, keys, values)
+    return dk * scale, dv
 
 
 def on_device(
@@ -91,12 +136,9 @@
     while reach < span:
         window = jnp.concatenate([window, passed_along(window, "wide", reach)], 0)
         reach *= 2
-    keys = window[:, 0].reshape(span * rows, local_heads, HEAD_SIZE)
-    values = window[:, 1].reshape(span * rows, local_heads, HEAD_SIZE)
-    valid = jnp.repeat(jnp.arange(span, dtype=jnp.int32) <= position, rows)
-    query = queries.reshape(queries.shape[0], local_heads, Q_PER_KV, HEAD_SIZE)
-    dout = out_grad.reshape(out_grad.shape[0], local_heads, Q_PER_KV, HEAD_SIZE)
-    dkey, dval = stretch_grads(query, dout, keys, values, valid)
+    keys = window[:, 0].reshape(span * rows, cols)
+    values = window[:, 1].reshape(span * rows, cols)
+    dkey, dval = attention_grads(position, queries, out_grad, keys, values)
     contrib = jnp.stack([dkey.reshape(span, rows, cols), dval.reshape(span, rows, cols)], 1)
     reach = span // 2
     while reach >= 1:

time: 232 us -> 200 us (0.86)
  matrix products: 36.5 us -> 3.99 us
  Pallas kernels: 0 us -> 20.1 us
  local copies, waits for them, and re-layouts: 31.7 us -> 13.9 us
  other arithmetic: 12.5 us -> 5.06 us
  waiting for transfers between devices: 78.4 us -> 84 us
    dot_general x4 -> x0, matrix products: 31.3 us -> none  [the longest x1 9.46 us: stretch_grads(): jnp.einsum('gmqk,qgmd->kgd', dscore, query, preferred_element_type=jnp.fl...]
    pallas_call x0 -> x1, Pallas kernels: none -> 20.1 us  [attention_grads(): pl.pallas_call(attention_body, grid_spec=grid_spec, out_shape=[jax.ShapeD...]
    another operation x9 -> x1, local copies, waits for them, and re-layouts: 13.5 us -> 0.1 us  [the longest x5 11.2 us: on_device(): jnp.stack([dkey.reshape(span, rows, cols), dval.reshape(span, rows, cols)...]
    div x1 -> x0, other arithmetic: 7.28 us -> none  [stretch_grads(): prob = expo / jnp.sum(expo, axis=-1, keepdims=True)]
    ppermute x6, waiting for transfers between devices: 48.9 us -> 54.8 us  [passed_along(): return lax.ppermute(array, axis, pairs)]
    unnamed x16 -> x20, local copies, waits for them, and re-layouts: 5.82 us -> 3.15 us
    reshape x1 -> x0, local copies, waits for them, and re-layouts: 2.57 us -> none  [on_device(): query = queries.reshape(queries.shape[0], local_heads, Q_PER_KV, HEAD_SIZE)]
  transfers between devices with their start and end apart: 22 -> 22, of which waited for: 19 -> 17; matrix products, arithmetic and copies ran while one was open for 5% -> 3% of each run, Pallas kernels for 0% -> 0%
where the time goes in v4:
time: 200 us
  waiting for transfers between devices  84 us (42%)
  starting transfers between devices  70.8 us (35%)
  Pallas kernels  20.1 us (10%)
  local copies, waits for them, and re-layouts  13.9 us (7%)
  other arithmetic  5.06 us (3%)
  matrix products  3.99 us (2%)
  between operations  2.04 us (1%)
    ppermute x6, waiting for transfers between devices, passed_along(): return lax.ppermute(array, axis, pairs)  54.8 us
    ppermute x16, starting transfers between devices, swapped(): return lax.ppermute(array, axis, pairs)  48.9 us
    ppermute x16, waiting for transfers between devices, swapped(): return lax.ppermute(array, axis, pairs)  29.2 us
    ppermute x6, starting transfers between devices, passed_along(): return lax.ppermute(array, axis, pairs)  21.9 us
    pallas_call x1, Pallas kernels, attention_grads(): pl.pallas_call(attention_body, grid_spec=grid_spec, out_shape=[jax.ShapeD...  20.1 us
  transfers between devices with their start and end apart: 22, of which 17 were waited for; matrix products, arithmetic and copies ran while one was open for 3% of the time, Pallas kernels for 0%

profile of v4, /device:TPU:1, one launch (start us, length us, event | category | flops | bytes accessed | tf_op | source)
XLA Modules:
  0.0 199.9 jit_solution(5099693847218932671)
XLA Ops:
  1.6 4.6 %collective-permute-start = (bf16[1,2,128,256]{3,2,1,0:T(8,128)(2,1)S(1)}, bf16[1,2,128,256]{3,2,1,0:T(8,128)(2,1)S(1)}, u32[]{:S(2)}, u32[]{:S(2)}) collective-permute-start(bf16[1,2,128,256]{3,2,1,0:T(8,128)(2,1)S(1)} %maximum_bitcast_fusion), channel_id=1, source_target_pairs={{0,4},{4,8},{8,12},{12,16},{16,20},{20,24},{24,28},{28,32},{32,36}... | collective-permute-start | bytes 393224 | tf_op jit(solution)/shard_map/ppermute | solution.py:15
  8.2 3.2 %collective-permute-start.1 = (bf16[2,2,128,256]{3,2,1,0:T(8,128)(2,1)S(1)}, bf16[2,2,128,256]{3,2,1,0:T(8,128)(2,1)S(1)}, u32[]{:S(2)}, u32[]{:S(2)}) collective-permute-start(bf16[2,2,128,256]{3,2,1,0:T(8,128)(2,1)S(1)} %pad_maximum_fusion.3), channel_id=1, source_target_pairs={{0,8},{4,12},{8,16},{12,20},{16,24},{20,28},{24,32},{28,36},{32,40... | collective-permute-start | bytes 786440 | tf_op jit(solution)/shard_map/ppermute | solution.py:15
  11.4 4.4 %collective-permute-done.1 = bf16[2,2,128,256]{3,2,1,0:T(8,128)(2,1)S(1)} collective-permute-done((bf16[2,2,128,256]{3,2,1,0:T(8,128)(2,1)S(1)}, bf16[2,2,128,256]{3,2,1,0:T(8,128)(2,1)S(1)}, u32[]{:S(2)}, u32[]{:S(2)}) %collective-permute-start.1) | collective-permute-done | bytes 262176 | tf_op jit(solution)/shard_map/ppermute | solution.py:15
  15.8 5.2 %collective-permute-start.2 = (bf16[4,2,128,256]{3,2,1,0:T(8,128)(2,1)S(1)}, bf16[4,2,128,256]{3,2,1,0:T(8,128)(2,1)S(1)}, u32[]{:S(2)}, u32[]{:S(2)}) collective-permute-start(bf16[4,2,128,256]{3,2,1,0:T(8,128)(2,1)S(1)} %pad_maximum_fusion.2), channel_id=1, source_target_pairs={{0,16},{4,20},{8,24},{12,28},{16,32},{20,36},{24,40},{28,44},{32,4... | collective-permute-start | bytes 1572872 | tf_op jit(solution)/shard_map/ppermute | solution.py:15
  22.6 7.3 %collective-permute-done.2 = bf16[4,2,128,256]{3,2,1,0:T(8,128)(2,1)S(1)} collective-permute-done((bf16[4,2,128,256]{3,2,1,0:T(8,128)(2,1)S(1)}, bf16[4,2,128,256]{3,2,1,0:T(8,128)(2,1)S(1)}, u32[]{:S(2)}, u32[]{:S(2)}) %collective-permute-start.2) | collective-permute-done | bytes 524320 | tf_op jit(solution)/shard_map/ppermute | solution.py:15
  31.0 20.1 %shard_map.129 = (f32[1024,256]{1,0:T(8,128)}, f32[1024,256]{1,0:T(8,128)}) custom-call(s32[1]{0:T(128)} %bitcast.1.pos_ref, bf16[512,1024]{1,0:T(8,128)(2,1)} %q_ref.1, bf16[512,1024]{1,0:T(8,128)(2,1)} %do_ref.1, bf16[1024,256]{1,0:T(8,128)(2,1)} %bitcast.128, bf16[1024,256]{1,0:T(8,128)(2,1)} %bitcast.127), custom_call_target="tpu_custom_call" | custom-call | tf_op jit(solution)/shard_map/pallas_call | solution.py:103
  54.0 24.6 %collective-permute-done.3 = f32[4,2,128,256]{3,2,1,0:T(8,128)S(1)} collective-permute-done((f32[4,2,128,256]{3,2,1,0:T(8,128)S(1)}, f32[4,2,128,256]{3,2,1,0:T(8,128)S(1)}, u32[]{:S(2)}, u32[]{:S(2)}) %collective-permute-start.3) | collective-permute-done | bytes 1048608 | tf_op jit(solution)/shard_map/ppermute | solution.py:15
  80.2 11.3 %collective-permute-done.4 = f32[2,2,128,256]{3,2,1,0:T(8,128)S(1)} collective-permute-done((f32[2,2,128,256]{3,2,1,0:T(8,128)S(1)}, f32[2,2,128,256]{3,2,1,0:T(8,128)S(1)}, u32[]{:S(2)}, u32[]{:S(2)}) %collective-permute-start.4) | collective-permute-done | bytes 524320 | tf_op jit(solution)/shard_map/ppermute | solution.py:15
  91.7 6.2 %collective-permute-start.5 = (f32[1,2,128,256]{3,2,1,0:T(8,128)S(1)}, f32[1,2,128,256]{3,2,1,0:T(8,128)S(1)}, u32[]{:S(2)}, u32[]{:S(2)}) collective-permute-start(f32[1,2,128,256]{3,2,1,0:T(8,128)S(1)} %slice.77), channel_id=1, source_target_pairs={{4,0},{8,4},{12,8},{16,12},{20,16},{24,20},{28,24},{32,28},{36,32}... | collective-permute-start | bytes 786440 | tf_op jit(solution)/shard_map/ppermute | solution.py:15
  98.0 5.4 %collective-permute-done.5 = f32[1,2,128,256]{3,2,1,0:T(8,128)S(1)} collective-permute-done((f32[1,2,128,256]{3,2,1,0:T(8,128)S(1)}, f32[1,2,128,256]{3,2,1,0:T(8,128)S(1)}, u32[]{:S(2)}, u32[]{:S(2)}) %collective-permute-start.5) | collective-permute-done | bytes 262176 | tf_op jit(solution)/shard_map/ppermute | solution.py:15
  107.6 2.5 %collective-permute-start.7 = (f32[1,128,64]{1,2,0:T(8,128)S(1)}, f32[1,128,64]{1,2,0:T(8,128)S(1)}, u32[]{:S(2)}, u32[]{:S(2)}) collective-permute-start(f32[1,128,64]{1,2,0:T(8,128)S(1)} %constant_dynamic-slice_fusion.11), channel_id=1, source_target_pairs={{0,2},{1,3},{2,0},{3,1},{4,6},{5,7},{6,4},{7,5},{8,10},{9,11},{10,... | collective-permute-start | bytes 98312 | tf_op jit(solution)/shard_map/ppermute | solution.py:21
  125.0 7.8 %collective-permute-done.9 = f32[16,5120]{1,0:T(8,128)S(1)} collective-permute-done((f32[16,5120]{1,0:T(8,128)S(1)}, f32[16,5120]{1,0:T(8,128)S(1)}, u32[]{:S(2)}, u32[]{:S(2)}) %collective-permute-start.9) | collective-permute-done | bytes 327712 | tf_op jit(solution)/shard_map/ppermute | solution.py:21
  133.4 5.6 %collective-permute-start.10 = (f32[8,5120]{1,0:T(8,128)S(1)}, f32[8,5120]{1,0:T(8,128)S(1)}, u32[]{:S(2)}, u32[]{:S(2)}) collective-permute-start(f32[8,5120]{1,0:T(8,128)S(1)} %bitcast.134), channel_id=1, source_target_pairs={{0,16},{4,20},{8,24},{12,28},{16,0},{20,4},{24,8},{28,12},{32,48},... | collective-permute-start | bytes 491528 | tf_op jit(solution)/shard_map/ppermute | solution.py:21
  139.0 3.6 %collective-permute-done.10 = f32[8,5120]{1,0:T(8,128)S(1)} collective-permute-done((f32[8,5120]{1,0:T(8,128)S(1)}, f32[8,5120]{1,0:T(8,128)S(1)}, u32[]{:S(2)}, u32[]{:S(2)}) %collective-permute-start.10) | collective-permute-done | bytes 163872 | tf_op jit(solution)/shard_map/ppermute | solution.py:21
  146.7 8.2 %collective-permute-start.12 = (f32[2,5120]{1,0:T(2,128)S(1)}, f32[2,5120]{1,0:T(2,128)S(1)}, u32[]{:S(2)}, u32[]{:S(2)}) collective-permute-start(f32[2,5120]{1,0:T(2,128)S(1)} %bitcast.140), channel_id=1, source_target_pairs={{0,64},{4,68},{8,72},{12,76},{16,80},{20,84},{24,88},{28,92},{32,9... | collective-permute-start | bytes 122888 | tf_op jit(solution)/shard_map/ppermute | solution.py:21
  156.3 3.4 %collective-permute-start.13 = (f32[1,5120]{1,0:T(1,128)S(1)}, f32[1,5120]{1,0:T(1,128)S(1)}, u32[]{:S(2)}, u32[]{:S(2)}) collective-permute-start(f32[1,5120]{1,0:T(1,128)S(1)} %constant_dynamic-slice_fusion), channel_id=1, source_target_pairs={{0,128},{4,132},{8,136},{12,140},{16,144},{20,148},{24,152},{28,15... | collective-permute-start | bytes 61448 | tf_op jit(solution)/shard_map/ppermute | solution.py:21
  159.7 3.2 %collective-permute-done.13 = f32[1,5120]{1,0:T(1,128)S(1)} collective-permute-done((f32[1,5120]{1,0:T(1,128)S(1)}, f32[1,5120]{1,0:T(1,128)S(1)}, u32[]{:S(2)}, u32[]{:S(2)}) %collective-permute-start.13) | collective-permute-done | bytes 20512 | tf_op jit(solution)/shard_map/ppermute | solution.py:21
  163.0 3.4 %collective-permute-start.16 = (f32[1,1024]{1,0:T(1,128)S(1)}, f32[1,1024]{1,0:T(1,128)S(1)}, u32[]{:S(2)}, u32[]{:S(2)}) collective-permute-start(f32[1,1024]{1,0:T(1,128)S(1)} %slice.83), channel_id=1, source_target_pairs={{0,128},{4,132},{8,136},{12,140},{16,144},{20,148},{24,152},{28,15... | collective-permute-start | bytes 12296 | tf_op jit(solution)/shard_map/ppermute | solution.py:21
  166.4 3.1 %collective-permute-done.16 = f32[1,1024]{1,0:T(1,128)S(1)} collective-permute-done((f32[1,1024]{1,0:T(1,128)S(1)}, f32[1,1024]{1,0:T(1,128)S(1)}, u32[]{:S(2)}, u32[]{:S(2)}) %collective-permute-start.16) | collective-permute-done | bytes 4128 | tf_op jit(solution)/shard_map/ppermute | solution.py:21
  169.5 2.5 %collective-permute-start.17 = (f32[2,1024]{1,0:T(2,128)S(1)}, f32[2,1024]{1,0:T(2,128)S(1)}, u32[]{:S(2)}, u32[]{:S(2)}) collective-permute-start(f32[2,1024]{1,0:T(2,128)S(1)} %maximum_bitcast_fusion.2), channel_id=1, source_target_pairs={{0,64},{4,68},{8,72},{12,76},{16,80},{20,84},{24,88},{28,92},{32,9... | collective-permute-start | bytes 24584 | tf_op jit(solution)/shard_map/ppermute | solution.py:21
  172.1 2.8 %collective-permute-start.14 = (f32[1,64,2,32]{3,2,1,0:T(2,128)S(1)}, f32[1,64,2,32]{3,2,1,0:T(2,128)S(1)}, u32[]{:S(2)}, u32[]{:S(2)}) collective-permute-start(f32[1,64,2,32]{3,2,1,0:T(2,128)S(1)} %broadcast_in_dim_reshape.3), channel_id=1, source_target_pairs={{0,2},{1,3},{2,0},{3,1},{4,6},{5,7},{6,4},{7,5},{8,10},{9,11},{10,... | collective-permute-start | bytes 49160 | tf_op jit(solution)/shard_map/ppermute | solution.py:21
  178.4 2.9 %collective-permute-start.19 = (f32[8,1024]{1,0:T(8,128)S(1)}, f32[8,1024]{1,0:T(8,128)S(1)}, u32[]{:S(2)}, u32[]{:S(2)}) collective-permute-start(f32[8,1024]{1,0:T(8,128)S(1)} %reshape.127), channel_id=1, source_target_pairs={{0,16},{4,20},{8,24},{12,28},{16,0},{20,4},{24,8},{28,12},{32,48},... | collective-permute-start | bytes 98312 | tf_op jit(solution)/shard_map/ppermute | solution.py:21
  183.6 2.8 %collective-permute-done.20 = f32[16,1024]{1,0:T(8,128)S(1)} collective-permute-done((f32[16,1024]{1,0:T(8,128)S(1)}, f32[16,1024]{1,0:T(8,128)S(1)}, u32[]{:S(2)}, u32[]{:S(2)}) %collective-permute-start.20) | collective-permute-done | bytes 65568 | tf_op jit(solution)/shard_map/ppermute | solution.py:21
  186.8 9.6 %collective-permute-start.21 = (f32[32,1024]{1,0:T(8,128)S(1)}, f32[32,1024]{1,0:T(8,128)S(1)}, u32[]{:S(2)}, u32[]{:S(2)}) collective-permute-start(f32[32,1024]{1,0:T(8,128)S(1)} %reshape.129), channel_id=1, source_target_pairs={{0,4},{4,0},{8,12},{12,8},{16,20},{20,16},{24,28},{28,24},{32,36},... | collective-permute-start | bytes 393224 | tf_op jit(solution)/shard_map/ppermute | solution.py:21
  (124 shorter events, 44.3 us)
Async XLA Ops:
  0.6 104.5 %copy-start = (bf16[128,4096]{1,0:T(8,128)(2,1)S(1)}, bf16[128,4096]{1,0:T(8,128)(2,1)}, u32[]{:S(2)}) copy-start(bf16[128,4096]{1,0:T(8,128)(2,1)} %param.15) | copy-start | bytes 3145732
  1.6 6.5 %collective-permute-start = (bf16[1,2,128,256]{3,2,1,0:T(8,128)(2,1)S(1)}, bf16[1,2,128,256]{3,2,1,0:T(8,128)(2,1)S(1)}, u32[]{:S(2)}, u32[]{:S(2)}) collective-permute-start(bf16[1,2,128,256]{3,2,1,0:T(8,128)(2,1)S(1)} %maximum_bitcast_fusion), channel_id=1, source_target_pairs={{0,4},{4,8},{8,12},{12,16},{16,20},{20,24},{24,28},{28,32},{32,36}... | collective-permute-start | bytes 393224 | tf_op jit(solution)/shard_map/ppermute | solution.py:15
  8.2 7.6 %collective-permute-start.1 = (bf16[2,2,128,256]{3,2,1,0:T(8,128)(2,1)S(1)}, bf16[2,2,128,256]{3,2,1,0:T(8,128)(2,1)S(1)}, u32[]{:S(2)}, u32[]{:S(2)}) collective-permute-start(bf16[2,2,128,256]{3,2,1,0:T(8,128)(2,1)S(1)} %pad_maximum_fusion.3), channel_id=1, source_target_pairs={{0,8},{4,12},{8,16},{12,20},{16,24},{20,28},{24,32},{28,36},{32,40... | collective-permute-start | bytes 786440 | tf_op jit(solution)/shard_map/ppermute | solution.py:15
  15.8 14.0 %collective-permute-start.2 = (bf16[4,2,128,256]{3,2,1,0:T(8,128)(2,1)S(1)}, bf16[4,2,128,256]{3,2,1,0:T(8,128)(2,1)S(1)}, u32[]{:S(2)}, u32[]{:S(2)}) collective-permute-start(bf16[4,2,128,256]{3,2,1,0:T(8,128)(2,1)S(1)} %pad_maximum_fusion.2), channel_id=1, source_target_pairs={{0,16},{4,20},{8,24},{12,28},{16,32},{20,36},{24,40},{28,44},{32,4... | collective-permute-start | bytes 1572872 | tf_op jit(solution)/shard_map/ppermute | solution.py:15
  52.7 25.9 %collective-permute-start.3 = (f32[4,2,128,256]{3,2,1,0:T(8,128)S(1)}, f32[4,2,128,256]{3,2,1,0:T(8,128)S(1)}, u32[]{:S(2)}, u32[]{:S(2)}) collective-permute-start(f32[4,2,128,256]{3,2,1,0:T(8,128)S(1)} %pad_maximum_fusion), channel_id=1, source_target_pairs={{16,0},{20,4},{24,8},{28,12},{32,16},{36,20},{40,24},{44,28},{48,3... | collective-permute-start | bytes 3145736 | tf_op jit(solution)/shard_map/ppermute | solution.py:15
  78.8 24.8 %copy-start.4 = (bf16[128,256]{1,0:T(8,128)(2,1)S(1)}, bf16[128,256]{1,0:T(8,128)(2,1)}, u32[]{:S(2)}) copy-start(bf16[128,256]{1,0:T(8,128)(2,1)} %param.17) | copy-start | bytes 196612
  78.8 12.8 %collective-permute-start.4 = (f32[2,2,128,256]{3,2,1,0:T(8,128)S(1)}, f32[2,2,128,256]{3,2,1,0:T(8,128)S(1)}, u32[]{:S(2)}, u32[]{:S(2)}) collective-permute-start(f32[2,2,128,256]{3,2,1,0:T(8,128)S(1)} %slice.75), channel_id=1, source_target_pairs={{8,0},{12,4},{16,8},{20,12},{24,16},{28,20},{32,24},{36,28},{40,32... | collective-permute-start | bytes 1572872 | tf_op jit(solution)/shard_map/ppermute | solution.py:15
  91.7 11.7 %collective-permute-start.5 = (f32[1,2,128,256]{3,2,1,0:T(8,128)S(1)}, f32[1,2,128,256]{3,2,1,0:T(8,128)S(1)}, u32[]{:S(2)}, u32[]{:S(2)}) collective-permute-start(f32[1,2,128,256]{3,2,1,0:T(8,128)S(1)} %slice.77), channel_id=1, source_target_pairs={{4,0},{8,4},{12,8},{16,12},{20,16},{24,20},{28,24},{32,28},{36,32}... | collective-permute-start | bytes 786440 | tf_op jit(solution)/shard_map/ppermute | solution.py:15
  103.8 3.8 %collective-permute-start.6 = (f32[2,128,64]{1,2,0:T(8,128)S(1)}, f32[2,128,64]{1,2,0:T(8,128)S(1)}, u32[]{:S(2)}, u32[]{:S(2)}) collective-permute-start(f32[2,128,64]{1,2,0:T(8,128)S(1)} %dynamic-slice_bitcast_fusion), channel_id=1, source_target_pairs={{0,1},{1,0},{2,3},{3,2},{4,5},{5,4},{6,7},{7,6},{8,9},{9,8},{10,11... | collective-permute-start | bytes 196616 | tf_op jit(solution)/shard_map/ppermute | solution.py:21
  107.6 4.4 %collective-permute-start.7 = (f32[1,128,64]{1,2,0:T(8,128)S(1)}, f32[1,128,64]{1,2,0:T(8,128)S(1)}, u32[]{:S(2)}, u32[]{:S(2)}) collective-permute-start(f32[1,128,64]{1,2,0:T(8,128)S(1)} %constant_dynamic-slice_fusion.11), channel_id=1, source_target_pairs={{0,2},{1,3},{2,0},{3,1},{4,6},{5,7},{6,4},{7,5},{8,10},{9,11},{10,... | collective-permute-start | bytes 98312 | tf_op jit(solution)/shard_map/ppermute | solution.py:21
  119.7 2.2 %collective-permute-start.8 = (f32[32,5120]{1,0:T(8,128)S(1)}, f32[32,5120]{1,0:T(8,128)S(1)}, u32[]{:S(2)}, u32[]{:S(2)}) collective-permute-start(f32[32,5120]{1,0:T(8,128)S(1)} %bitcast.129), channel_id=1, source_target_pairs={{0,4},{4,0},{8,12},{12,8},{16,20},{20,16},{24,28},{28,24},{32,36},... | collective-permute-start | bytes 1966088 | tf_op jit(solution)/shard_map/ppermute | solution.py:21
  123.1 9.7 %collective-permute-start.9 = (f32[16,5120]{1,0:T(8,128)S(1)}, f32[16,5120]{1,0:T(8,128)S(1)}, u32[]{:S(2)}, u32[]{:S(2)}) collective-permute-start(f32[16,5120]{1,0:T(8,128)S(1)} %bitcast.133), channel_id=1, source_target_pairs={{0,8},{4,12},{8,0},{12,4},{16,24},{20,28},{24,16},{28,20},{32,40},... | collective-permute-start | bytes 983048 | tf_op jit(solution)/shard_map/ppermute | solution.py:21
  133.4 9.1 %collective-permute-start.10 = (f32[8,5120]{1,0:T(8,128)S(1)}, f32[8,5120]{1,0:T(8,128)S(1)}, u32[]{:S(2)}, u32[]{:S(2)}) collective-permute-start(f32[8,5120]{1,0:T(8,128)S(1)} %bitcast.134), channel_id=1, source_target_pairs={{0,16},{4,20},{8,24},{12,28},{16,0},{20,4},{24,8},{28,12},{32,48},... | collective-permute-start | bytes 491528 | tf_op jit(solution)/shard_map/ppermute | solution.py:21
  142.9 3.6 %collective-permute-start.11 = (f32[4,5120]{1,0:T(4,128)S(1)}, f32[4,5120]{1,0:T(4,128)S(1)}, u32[]{:S(2)}, u32[]{:S(2)}) collective-permute-start(f32[4,5120]{1,0:T(4,128)S(1)} %bitcast.135), channel_id=1, source_target_pairs={{0,32},{4,36},{8,40},{12,44},{16,48},{20,52},{24,56},{28,60},{32,0... | collective-permute-start | bytes 245768 | tf_op jit(solution)/shard_map/ppermute | solution.py:21
  146.7 9.5 %collective-permute-start.12 = (f32[2,5120]{1,0:T(2,128)S(1)}, f32[2,5120]{1,0:T(2,128)S(1)}, u32[]{:S(2)}, u32[]{:S(2)}) collective-permute-start(f32[2,5120]{1,0:T(2,128)S(1)} %bitcast.140), channel_id=1, source_target_pairs={{0,64},{4,68},{8,72},{12,76},{16,80},{20,84},{24,88},{28,92},{32,9... | collective-permute-start | bytes 122888 | tf_op jit(solution)/shard_map/ppermute | solution.py:21
  156.3 6.6 %collective-permute-start.13 = (f32[1,5120]{1,0:T(1,128)S(1)}, f32[1,5120]{1,0:T(1,128)S(1)}, u32[]{:S(2)}, u32[]{:S(2)}) collective-permute-start(f32[1,5120]{1,0:T(1,128)S(1)} %constant_dynamic-slice_fusion), channel_id=1, source_target_pairs={{0,128},{4,132},{8,136},{12,140},{16,144},{20,148},{24,152},{28,15... | collective-permute-start | bytes 61448 | tf_op jit(solution)/shard_map/ppermute | solution.py:21
  163.0 6.5 %collective-permute-start.16 = (f32[1,1024]{1,0:T(1,128)S(1)}, f32[1,1024]{1,0:T(1,128)S(1)}, u32[]{:S(2)}, u32[]{:S(2)}) collective-permute-start(f32[1,1024]{1,0:T(1,128)S(1)} %slice.83), channel_id=1, source_target_pairs={{0,128},{4,132},{8,136},{12,140},{16,144},{20,148},{24,152},{28,15... | collective-permute-start | bytes 12296 | tf_op jit(solution)/shard_map/ppermute | solution.py:21
  169.5 5.5 %collective-permute-start.17 = (f32[2,1024]{1,0:T(2,128)S(1)}, f32[2,1024]{1,0:T(2,128)S(1)}, u32[]{:S(2)}, u32[]{:S(2)}) collective-permute-start(f32[2,1024]{1,0:T(2,128)S(1)} %maximum_bitcast_fusion.2), channel_id=1, source_target_pairs={{0,64},{4,68},{8,72},{12,76},{16,80},{20,84},{24,88},{28,92},{32,9... | collective-permute-start | bytes 24584 | tf_op jit(solution)/shard_map/ppermute | solution.py:21
  172.1 4.7 %collective-permute-start.14 = (f32[1,64,2,32]{3,2,1,0:T(2,128)S(1)}, f32[1,64,2,32]{3,2,1,0:T(2,128)S(1)}, u32[]{:S(2)}, u32[]{:S(2)}) collective-permute-start(f32[1,64,2,32]{3,2,1,0:T(2,128)S(1)} %broadcast_in_dim_reshape.3), channel_id=1, source_target_pairs={{0,2},{1,3},{2,0},{3,1},{4,6},{5,7},{6,4},{7,5},{8,10},{9,11},{10,... | collective-permute-start | bytes 49160 | tf_op jit(solution)/shard_map/ppermute | solution.py:21
  175.0 3.2 %collective-permute-start.18 = (f32[4,1024]{1,0:T(4,128)S(1)}, f32[4,1024]{1,0:T(4,128)S(1)}, u32[]{:S(2)}, u32[]{:S(2)}) collective-permute-start(f32[4,1024]{1,0:T(4,128)S(1)} %reshape.126), channel_id=1, source_target_pairs={{0,32},{4,36},{8,40},{12,44},{16,48},{20,52},{24,56},{28,60},{32,0... | collective-permute-start | bytes 49160 | tf_op jit(solution)/shard_map/ppermute | solution.py:21
  176.9 4.3 %collective-permute-start.15 = (f32[2,64,2,32]{3,2,1,0:T(2,128)S(1)}, f32[2,64,2,32]{3,2,1,0:T(2,128)S(1)}, u32[]{:S(2)}, u32[]{:S(2)}) collective-permute-start(f32[2,64,2,32]{3,2,1,0:T(2,128)S(1)} %maximum_bitcast_fusion.1), channel_id=1, source_target_pairs={{0,1},{1,0},{2,3},{3,2},{4,5},{5,4},{6,7},{7,6},{8,9},{9,8},{10,11... | collective-permute-start | bytes 98312 | tf_op jit(solution)/shard_map/ppermute | solution.py:21
  178.4 4.7 %collective-permute-start.19 = (f32[8,1024]{1,0:T(8,128)S(1)}, f32[8,1024]{1,0:T(8,128)S(1)}, u32[]{:S(2)}, u32[]{:S(2)}) collective-permute-start(f32[8,1024]{1,0:T(8,128)S(1)} %reshape.127), channel_id=1, source_target_pairs={{0,16},{4,20},{8,24},{12,28},{16,0},{20,4},{24,8},{28,12},{32,48},... | collective-permute-start | bytes 98312 | tf_op jit(solution)/shard_map/ppermute | solution.py:21
  183.2 3.2 %collective-permute-start.20 = (f32[16,1024]{1,0:T(8,128)S(1)}, f32[16,1024]{1,0:T(8,128)S(1)}, u32[]{:S(2)}, u32[]{:S(2)}) collective-permute-start(f32[16,1024]{1,0:T(8,128)S(1)} %reshape.128), channel_id=1, source_target_pairs={{0,8},{4,12},{8,0},{12,4},{16,24},{20,28},{24,16},{28,20},{32,40},... | collective-permute-start | bytes 196616 | tf_op jit(solution)/shard_map/ppermute | solution.py:21
  186.8 11.0 %collective-permute-start.21 = (f32[32,1024]{1,0:T(8,128)S(1)}, f32[32,1024]{1,0:T(8,128)S(1)}, u32[]{:S(2)}, u32[]{:S(2)}) collective-permute-start(f32[32,1024]{1,0:T(8,128)S(1)} %reshape.129), channel_id=1, source_target_pairs={{0,4},{4,0},{8,12},{12,8},{16,20},{20,16},{24,28},{28,24},{32,36},... | collective-permute-start | bytes 393224 | tf_op jit(solution)/shard_map/ppermute | solution.py:21
  (4 other events, 60.0 us)

commit v5 on v4

--- a/solution.py
+++ b/solution.py
@@ -15,38 +15,42 @@
     return lax.ppermute(array, axis, pairs)
 
 
-def swapped(array, axis, bit):
+def digit_steps(devices):
+    steps = []
+    low = 1
+    while low < devices:
+        radix = 4 if devices % (low * 4) == 0 else 2
+        steps.append((low, radix))
+        low *= radix
+    return steps
+
+
+def xor_partner(array, axis, mask):
     devices = lax.axis_size(axis)
-    pairs = [(i, i ^ bit) for i in range(devices)]
-    return lax.ppermute(array, axis, pairs)
+    return lax.ppermute(array, axis, [(i, i ^ mask) for i in range(devices)])
 
 
 def scattered_sum(x, axis):
-    devices = lax.axis_size(axis)
     me = lax.axis_index(axis)
-    bit = 1
-    while bit < devices:
-        pair = x.reshape(x.shape[0] // 2, 2, *x.shape[1:])
-        mine = (me // bit) % 2
-        keep = lax.dynamic_index_in_dim(pair, mine, axis=1, keepdims=False)
-        give = lax.dynamic_index_in_dim(pair, 1 - mine, axis=1, keepdims=False)
-        x = keep + swapped(give, axis, bit)
-        bit *= 2
+    for low, radix in digit_steps(lax.axis_size(axis)):
+        group = x.reshape(x.shape[0] // radix, radix, *x.shape[1:])
+        mine = (me // low) % radix
+        x = lax.dynamic_index_in_dim(group, mine, axis=1, keepdims=False)
+        for t in range(1, radix):
+            give = lax.dynamic_index_in_dim(group, jnp.bitwise_xor(mine, t), axis=1, keepdims=False)
+            x = x + xor_partner(give, axis, t * low)
     return x[0]
 
 
 def gathered(y, axis):
-    devices = lax.axis_size(axis)
     me = lax.axis_index(axis)
     y = y[None]
-    bit = devices // 2
-    while bit >= 1:
-        other = swapped(y, axis, bit)
-        first = (me // bit) % 2 == 0
-        low = jnp.where(first, y, other)
-        high = jnp.where(first, other, y)
-        y = jnp.stack([low, high], 1).reshape(y.shape[0] * 2, *y.shape[1:])
-        bit //= 2
+    for low, radix in reversed(digit_steps(lax.axis_size(axis))):
+        mine = (me // low) % radix
+        got = [y] + [xor_partner(y, axis, t * low) for t in range(1, radix)]
+        order = jnp.bitwise_xor(jnp.arange(radix, dtype=mine.dtype), mine)
+        y = jnp.take(jnp.stack(got, 1), order, axis=1)
+        y = y.reshape(y.shape[0] * radix, *y.shape[2:])
     return y
 
 

time: 200 us -> 200 us (level)
  starting transfers between devices: 70.8 us -> 68.7 us
    gather x0 -> x7, local copies, waits for them, and re-layouts: none -> 2.37 us  [gathered(): y = jnp.take(jnp.stack(got, 1), order, axis=1)]
    ppermute x16 -> x24, starting transfers between devices: 48.9 us -> 47.3 us  [xor_partner(): return lax.ppermute(array, axis, [(i, i ^ mask) for i in range(devices)])]
    ppermute x16 -> x24, waiting for transfers between devices: 29.2 us -> 30.5 us  [xor_partner(): return lax.ppermute(array, axis, [(i, i ^ mask) for i in range(devices)])]
  transfers between devices with their start and end apart: 22 -> 30, of which waited for: 17 -> 17; matrix products, arithmetic and copies ran while one was open for 3% -> 2% of each run, Pallas kernels for 0% -> 0%
where the time goes in v5:
time: 200 us; the launch traced here: 199 us
  waiting for transfers between devices  85 us (42%)
  starting transfers between devices  68.7 us (34%)
  Pallas kernels  20.1 us (10%)
  local copies, waits for them, and re-layouts  14.7 us (7%)
  other arithmetic  4.58 us (2%)
  matrix products  4.08 us (2%)
    ppermute x6, waiting for transfers between devices, passed_along(): return lax.ppermute(array, axis, pairs)  54.6 us
    ppermute x24, starting transfers between devices, xor_partner(): return lax.ppermute(array, axis, [(i, i ^ mask) for i in range(devices)])  47.3 us
    ppermute x24, waiting for transfers between devices, xor_partner(): return lax.ppermute(array, axis, [(i, i ^ mask) for i in range(devices)])  30.5 us
    ppermute x6, starting transfers between devices, passed_along(): return lax.ppermute(array, axis, pairs)  21.5 us
    pallas_call x1, Pallas kernels, attention_grads(): pl.pallas_call(attention_body, grid_spec=grid_spec, out_shape=[jax.ShapeD...  20.1 us
  transfers between devices with their start and end apart: 30, of which 17 were waited for; matrix products, arithmetic and copies ran while one was open for 2% of the time, Pallas kernels for 0%

profile of v5, /device:TPU:1, one launch (start us, length us, event | category | flops | bytes accessed | tf_op | source)
XLA Modules:
  0.0 199.2 jit_solution(10622387964522858575)
XLA Ops:
  1.6 4.6 %collective-permute-start = (bf16[1,2,128,256]{3,2,1,0:T(8,128)(2,1)S(1)}, bf16[1,2,128,256]{3,2,1,0:T(8,128)(2,1)S(1)}, u32[]{:S(2)}, u32[]{:S(2)}) collective-permute-start(bf16[1,2,128,256]{3,2,1,0:T(8,128)(2,1)S(1)} %maximum_bitcast_fusion), channel_id=1, source_target_pairs={{0,4},{4,8},{8,12},{12,16},{16,20},{20,24},{24,28},{28,32},{32,36}... | collective-permute-start | bytes 393224 | tf_op jit(solution)/shard_map/ppermute | solution.py:15
  8.2 3.2 %collective-permute-start.1 = (bf16[2,2,128,256]{3,2,1,0:T(8,128)(2,1)S(1)}, bf16[2,2,128,256]{3,2,1,0:T(8,128)(2,1)S(1)}, u32[]{:S(2)}, u32[]{:S(2)}) collective-permute-start(bf16[2,2,128,256]{3,2,1,0:T(8,128)(2,1)S(1)} %pad_maximum_fusion.3), channel_id=1, source_target_pairs={{0,8},{4,12},{8,16},{12,20},{16,24},{20,28},{24,32},{28,36},{32,40... | collective-permute-start | bytes 786440 | tf_op jit(solution)/shard_map/ppermute | solution.py:15
  11.4 4.4 %collective-permute-done.1 = bf16[2,2,128,256]{3,2,1,0:T(8,128)(2,1)S(1)} collective-permute-done((bf16[2,2,128,256]{3,2,1,0:T(8,128)(2,1)S(1)}, bf16[2,2,128,256]{3,2,1,0:T(8,128)(2,1)S(1)}, u32[]{:S(2)}, u32[]{:S(2)}) %collective-permute-start.1) | collective-permute-done | bytes 262176 | tf_op jit(solution)/shard_map/ppermute | solution.py:15
  15.8 5.2 %collective-permute-start.2 = (bf16[4,2,128,256]{3,2,1,0:T(8,128)(2,1)S(1)}, bf16[4,2,128,256]{3,2,1,0:T(8,128)(2,1)S(1)}, u32[]{:S(2)}, u32[]{:S(2)}) collective-permute-start(bf16[4,2,128,256]{3,2,1,0:T(8,128)(2,1)S(1)} %pad_maximum_fusion.2), channel_id=1, source_target_pairs={{0,16},{4,20},{8,24},{12,28},{16,32},{20,36},{24,40},{28,44},{32,4... | collective-permute-start | bytes 1572872 | tf_op jit(solution)/shard_map/ppermute | solution.py:15
  22.6 7.3 %collective-permute-done.2 = bf16[4,2,128,256]{3,2,1,0:T(8,128)(2,1)S(1)} collective-permute-done((bf16[4,2,128,256]{3,2,1,0:T(8,128)(2,1)S(1)}, bf16[4,2,128,256]{3,2,1,0:T(8,128)(2,1)S(1)}, u32[]{:S(2)}, u32[]{:S(2)}) %collective-permute-start.2) | collective-permute-done | bytes 524320 | tf_op jit(solution)/shard_map/ppermute | solution.py:15
  31.0 20.1 %shard_map.129 = (f32[1024,256]{1,0:T(8,128)}, f32[1024,256]{1,0:T(8,128)}) custom-call(s32[1]{0:T(128)} %bitcast.1.pos_ref, bf16[512,1024]{1,0:T(8,128)(2,1)} %q_ref.1, bf16[512,1024]{1,0:T(8,128)(2,1)} %do_ref.1, bf16[1024,256]{1,0:T(8,128)(2,1)} %bitcast.124, bf16[1024,256]{1,0:T(8,128)(2,1)} %bitcast.123), custom_call_target="tpu_custom_call" | custom-call | tf_op jit(solution)/shard_map/pallas_call | solution.py:107
  54.0 24.6 %collective-permute-done.3 = f32[4,2,128,256]{3,2,1,0:T(8,128)S(1)} collective-permute-done((f32[4,2,128,256]{3,2,1,0:T(8,128)S(1)}, f32[4,2,128,256]{3,2,1,0:T(8,128)S(1)}, u32[]{:S(2)}, u32[]{:S(2)}) %collective-permute-start.3) | collective-permute-done | bytes 1048608 | tf_op jit(solution)/shard_map/ppermute | solution.py:15
  80.2 11.5 %collective-permute-done.4 = f32[2,2,128,256]{3,2,1,0:T(8,128)S(1)} collective-permute-done((f32[2,2,128,256]{3,2,1,0:T(8,128)S(1)}, f32[2,2,128,256]{3,2,1,0:T(8,128)S(1)}, u32[]{:S(2)}, u32[]{:S(2)}) %collective-permute-start.4) | collective-permute-done | bytes 524320 | tf_op jit(solution)/shard_map/ppermute | solution.py:15
  91.8 5.9 %collective-permute-start.5 = (f32[1,2,128,256]{3,2,1,0:T(8,128)S(1)}, f32[1,2,128,256]{3,2,1,0:T(8,128)S(1)}, u32[]{:S(2)}, u32[]{:S(2)}) collective-permute-start(f32[1,2,128,256]{3,2,1,0:T(8,128)S(1)} %slice.85), channel_id=1, source_target_pairs={{4,0},{8,4},{12,8},{16,12},{20,16},{24,20},{28,24},{32,28},{36,32}... | collective-permute-start | bytes 786440 | tf_op jit(solution)/shard_map/ppermute | solution.py:15
  97.9 4.9 %collective-permute-done.5 = f32[1,2,128,256]{3,2,1,0:T(8,128)S(1)} collective-permute-done((f32[1,2,128,256]{3,2,1,0:T(8,128)S(1)}, f32[1,2,128,256]{3,2,1,0:T(8,128)S(1)}, u32[]{:S(2)}, u32[]{:S(2)}) %collective-permute-start.5) | collective-permute-done | bytes 262176 | tf_op jit(solution)/shard_map/ppermute | solution.py:15
  107.3 2.5 %collective-permute-start.7 = (f32[1,128,64]{1,2,0:T(8,128)S(1)}, f32[1,128,64]{1,2,0:T(8,128)S(1)}, u32[]{:S(2)}, u32[]{:S(2)}) collective-permute-start(f32[1,128,64]{1,2,0:T(8,128)S(1)} %get-tuple-element.31), channel_id=1, source_target_pairs={{0,2},{1,3},{2,0},{3,1},{4,6},{5,7},{6,4},{7,5},{8,10},{9,11},{10,... | collective-permute-start | bytes 98312 | tf_op jit(solution)/shard_map/ppermute | solution.py:30
  111.5 2.1 %collective-permute-done.8 = f32[1,128,64]{1,2,0:T(8,128)S(1)} collective-permute-done((f32[1,128,64]{1,2,0:T(8,128)S(1)}, f32[1,128,64]{1,2,0:T(8,128)S(1)}, u32[]{:S(2)}, u32[]{:S(2)}) %collective-permute-start.8) | collective-permute-done | bytes 32800 | tf_op jit(solution)/shard_map/ppermute | solution.py:30
  124.3 7.2 %collective-permute-done.10 = f32[16,5120]{1,0:T(8,128)S(1)} collective-permute-done((f32[16,5120]{1,0:T(8,128)S(1)}, f32[16,5120]{1,0:T(8,128)S(1)}, u32[]{:S(2)}, u32[]{:S(2)}) %collective-permute-start.10) | collective-permute-done | bytes 327712 | tf_op jit(solution)/shard_map/ppermute | solution.py:30
  131.5 7.0 %collective-permute-done.11 = f32[16,5120]{1,0:T(8,128)S(1)} collective-permute-done((f32[16,5120]{1,0:T(8,128)S(1)}, f32[16,5120]{1,0:T(8,128)S(1)}, u32[]{:S(2)}, u32[]{:S(2)}) %collective-permute-start.11) | collective-permute-done | bytes 327712 | tf_op jit(solution)/shard_map/ppermute | solution.py:30
  139.1 5.3 %collective-permute-start.12 = (f32[4,5120]{1,0:T(4,128)S(1)}, f32[4,5120]{1,0:T(4,128)S(1)}, u32[]{:S(2)}, u32[]{:S(2)}) collective-permute-start(f32[4,5120]{1,0:T(4,128)S(1)} %bitcast.130), channel_id=1, source_target_pairs={{0,16},{4,20},{8,24},{12,28},{16,0},{20,4},{24,8},{28,12},{32,48},... | collective-permute-start | bytes 245768 | tf_op jit(solution)/shard_map/ppermute | solution.py:30
  148.2 3.7 %collective-permute-done.14 = f32[4,5120]{1,0:T(4,128)S(1)} collective-permute-done((f32[4,5120]{1,0:T(4,128)S(1)}, f32[4,5120]{1,0:T(4,128)S(1)}, u32[]{:S(2)}, u32[]{:S(2)}) %collective-permute-start.14) | collective-permute-done | bytes 81952 | tf_op jit(solution)/shard_map/ppermute | solution.py:30
  152.0 7.9 %collective-permute-start.15 = (f32[1,5120]{1,0:T(1,128)S(1)}, f32[1,5120]{1,0:T(1,128)S(1)}, u32[]{:S(2)}, u32[]{:S(2)}) collective-permute-start(f32[1,5120]{1,0:T(1,128)S(1)} %get-tuple-element.33), channel_id=1, source_target_pairs={{0,64},{4,68},{8,72},{12,76},{16,80},{20,84},{24,88},{28,92},{32,9... | collective-permute-start | bytes 61448 | tf_op jit(solution)/shard_map/ppermute | solution.py:30
  159.9 3.4 %collective-permute-start.17 = (f32[1,5120]{1,0:T(1,128)S(1)}, f32[1,5120]{1,0:T(1,128)S(1)}, u32[]{:S(2)}, u32[]{:S(2)}) collective-permute-start(f32[1,5120]{1,0:T(1,128)S(1)} %get-tuple-element.34), channel_id=1, source_target_pairs={{0,192},{4,196},{8,200},{12,204},{16,208},{20,212},{24,216},{28,22... | collective-permute-start | bytes 61448 | tf_op jit(solution)/shard_map/ppermute | solution.py:30
  163.4 3.1 %collective-permute-done.16 = f32[1,5120]{1,0:T(1,128)S(1)} collective-permute-done((f32[1,5120]{1,0:T(1,128)S(1)}, f32[1,5120]{1,0:T(1,128)S(1)}, u32[]{:S(2)}, u32[]{:S(2)}) %collective-permute-start.16) | collective-permute-done | bytes 20512 | tf_op jit(solution)/shard_map/ppermute | solution.py:30
  167.1 3.2 %collective-permute-start.22 = (f32[1,1024]{1,0:T(1,128)S(1)}, f32[1,1024]{1,0:T(1,128)S(1)}, u32[]{:S(2)}, u32[]{:S(2)}) collective-permute-start(f32[1,1024]{1,0:T(1,128)S(1)} %get-tuple-element.37), channel_id=1, source_target_pairs={{0,128},{4,132},{8,136},{12,140},{16,144},{20,148},{24,152},{28,15... | collective-permute-start | bytes 12296 | tf_op jit(solution)/shard_map/ppermute | solution.py:30
  170.3 2.0 %collective-permute-start.23 = (f32[1,1024]{1,0:T(1,128)S(1)}, f32[1,1024]{1,0:T(1,128)S(1)}, u32[]{:S(2)}, u32[]{:S(2)}) collective-permute-start(f32[1,1024]{1,0:T(1,128)S(1)} %get-tuple-element.37), channel_id=1, source_target_pairs={{0,192},{4,196},{8,200},{12,204},{16,208},{20,212},{24,216},{28,22... | collective-permute-start | bytes 12296 | tf_op jit(solution)/shard_map/ppermute | solution.py:30
  174.2 2.5 %collective-permute-start.20 = (f32[1,64,2,32]{1,3,2,0:T(8,128)S(1)}, f32[1,64,2,32]{1,3,2,0:T(8,128)S(1)}, u32[]{:S(2)}, u32[]{:S(2)}) collective-permute-start(f32[1,64,2,32]{1,3,2,0:T(8,128)S(1)} %copy.36), channel_id=1, source_target_pairs={{0,3},{1,2},{2,1},{3,0},{4,7},{5,6},{6,5},{7,4},{8,11},{9,10},{10,... | collective-permute-start | bytes 49160 | tf_op jit(solution)/shard_map/ppermute | solution.py:30
  179.2 2.4 %collective-permute-start.26 = (f32[4,1024]{1,0:T(4,128)S(1)}, f32[4,1024]{1,0:T(4,128)S(1)}, u32[]{:S(2)}, u32[]{:S(2)}) collective-permute-start(f32[4,1024]{1,0:T(4,128)S(1)} %broadcast_select_fusion.2), channel_id=1, source_target_pairs={{0,48},{4,52},{8,56},{12,60},{16,32},{20,36},{24,40},{28,44},{32,1... | collective-permute-start | bytes 49160 | tf_op jit(solution)/shard_map/ppermute | solution.py:30
  185.0 6.6 %collective-permute-start.27 = (f32[16,1024]{1,0:T(8,128)S(1)}, f32[16,1024]{1,0:T(8,128)S(1)}, u32[]{:S(2)}, u32[]{:S(2)}) collective-permute-start(f32[16,1024]{1,0:T(8,128)S(1)} %broadcast_select_fusion), channel_id=1, source_target_pairs={{0,4},{4,0},{8,12},{12,8},{16,20},{20,16},{24,28},{28,24},{32,36},... | collective-permute-start | bytes 196616 | tf_op jit(solution)/shard_map/ppermute | solution.py:30
  (134 shorter events, 46.8 us)
Async XLA Ops:
  1.6 6.5 %collective-permute-start = (bf16[1,2,128,256]{3,2,1,0:T(8,128)(2,1)S(1)}, bf16[1,2,128,256]{3,2,1,0:T(8,128)(2,1)S(1)}, u32[]{:S(2)}, u32[]{:S(2)}) collective-permute-start(bf16[1,2,128,256]{3,2,1,0:T(8,128)(2,1)S(1)} %maximum_bitcast_fusion), channel_id=1, source_target_pairs={{0,4},{4,8},{8,12},{12,16},{16,20},{20,24},{24,28},{28,32},{32,36}... | collective-permute-start | bytes 393224 | tf_op jit(solution)/shard_map/ppermute | solution.py:15
  8.2 7.6 %collective-permute-start.1 = (bf16[2,2,128,256]{3,2,1,0:T(8,128)(2,1)S(1)}, bf16[2,2,128,256]{3,2,1,0:T(8,128)(2,1)S(1)}, u32[]{:S(2)}, u32[]{:S(2)}) collective-permute-start(bf16[2,2,128,256]{3,2,1,0:T(8,128)(2,1)S(1)} %pad_maximum_fusion.3), channel_id=1, source_target_pairs={{0,8},{4,12},{8,16},{12,20},{16,24},{20,28},{24,32},{28,36},{32,40... | collective-permute-start | bytes 786440 | tf_op jit(solution)/shard_map/ppermute | solution.py:15
  15.8 14.0 %collective-permute-start.2 = (bf16[4,2,128,256]{3,2,1,0:T(8,128)(2,1)S(1)}, bf16[4,2,128,256]{3,2,1,0:T(8,128)(2,1)S(1)}, u32[]{:S(2)}, u32[]{:S(2)}) collective-permute-start(bf16[4,2,128,256]{3,2,1,0:T(8,128)(2,1)S(1)} %pad_maximum_fusion.2), channel_id=1, source_target_pairs={{0,16},{4,20},{8,24},{12,28},{16,32},{20,36},{24,40},{28,44},{32,4... | collective-permute-start | bytes 1572872 | tf_op jit(solution)/shard_map/ppermute | solution.py:15
  52.7 25.9 %collective-permute-start.3 = (f32[4,2,128,256]{3,2,1,0:T(8,128)S(1)}, f32[4,2,128,256]{3,2,1,0:T(8,128)S(1)}, u32[]{:S(2)}, u32[]{:S(2)}) collective-permute-start(f32[4,2,128,256]{3,2,1,0:T(8,128)S(1)} %pad_maximum_fusion), channel_id=1, source_target_pairs={{16,0},{20,4},{24,8},{28,12},{32,16},{36,20},{40,24},{44,28},{48,3... | collective-permute-start | bytes 3145736 | tf_op jit(solution)/shard_map/ppermute | solution.py:15
  78.8 12.9 %collective-permute-start.4 = (f32[2,2,128,256]{3,2,1,0:T(8,128)S(1)}, f32[2,2,128,256]{3,2,1,0:T(8,128)S(1)}, u32[]{:S(2)}, u32[]{:S(2)}) collective-permute-start(f32[2,2,128,256]{3,2,1,0:T(8,128)S(1)} %slice.83), channel_id=1, source_target_pairs={{8,0},{12,4},{16,8},{20,12},{24,16},{28,20},{32,24},{36,28},{40,32... | collective-permute-start | bytes 1572872 | tf_op jit(solution)/shard_map/ppermute | solution.py:15
  91.8 11.0 %collective-permute-start.5 = (f32[1,2,128,256]{3,2,1,0:T(8,128)S(1)}, f32[1,2,128,256]{3,2,1,0:T(8,128)S(1)}, u32[]{:S(2)}, u32[]{:S(2)}) collective-permute-start(f32[1,2,128,256]{3,2,1,0:T(8,128)S(1)} %slice.85), channel_id=1, source_target_pairs={{4,0},{8,4},{12,8},{16,12},{20,16},{24,20},{28,24},{32,28},{36,32}... | collective-permute-start | bytes 786440 | tf_op jit(solution)/shard_map/ppermute | solution.py:15
  121.4 10.1 %collective-permute-start.10 = (f32[16,5120]{1,0:T(8,128)S(1)}, f32[16,5120]{1,0:T(8,128)S(1)}, u32[]{:S(2)}, u32[]{:S(2)}) collective-permute-start(f32[16,5120]{1,0:T(8,128)S(1)} %bitcast.126), channel_id=1, source_target_pairs={{0,8},{4,12},{8,0},{12,4},{16,24},{20,28},{24,16},{28,20},{32,40},... | collective-permute-start | bytes 983048 | tf_op jit(solution)/shard_map/ppermute | solution.py:30
  123.4 15.1 %collective-permute-start.11 = (f32[16,5120]{1,0:T(8,128)S(1)}, f32[16,5120]{1,0:T(8,128)S(1)}, u32[]{:S(2)}, u32[]{:S(2)}) collective-permute-start(f32[16,5120]{1,0:T(8,128)S(1)} %bitcast.127), channel_id=1, source_target_pairs={{0,12},{4,8},{8,4},{12,0},{16,28},{20,24},{24,20},{28,16},{32,44},... | collective-permute-start | bytes 983048 | tf_op jit(solution)/shard_map/ppermute | solution.py:30
  123.6 14.9 %collective-permute-start.9 = (f32[16,5120]{1,0:T(8,128)S(1)}, f32[16,5120]{1,0:T(8,128)S(1)}, u32[]{:S(2)}, u32[]{:S(2)}) collective-permute-start(f32[16,5120]{1,0:T(8,128)S(1)} %bitcast.128), channel_id=1, source_target_pairs={{0,4},{4,0},{8,12},{12,8},{16,20},{20,16},{24,28},{28,24},{32,36},... | collective-permute-start | bytes 983048 | tf_op jit(solution)/shard_map/ppermute | solution.py:30
  139.1 7.8 %collective-permute-start.12 = (f32[4,5120]{1,0:T(4,128)S(1)}, f32[4,5120]{1,0:T(4,128)S(1)}, u32[]{:S(2)}, u32[]{:S(2)}) collective-permute-start(f32[4,5120]{1,0:T(4,128)S(1)} %bitcast.130), channel_id=1, source_target_pairs={{0,16},{4,20},{8,24},{12,28},{16,0},{20,4},{24,8},{28,12},{32,48},... | collective-permute-start | bytes 245768 | tf_op jit(solution)/shard_map/ppermute | solution.py:30
  146.1 5.8 %collective-permute-start.14 = (f32[4,5120]{1,0:T(4,128)S(1)}, f32[4,5120]{1,0:T(4,128)S(1)}, u32[]{:S(2)}, u32[]{:S(2)}) collective-permute-start(f32[4,5120]{1,0:T(4,128)S(1)} %bitcast.132), channel_id=1, source_target_pairs={{0,48},{4,52},{8,56},{12,60},{16,32},{20,36},{24,40},{28,44},{32,1... | collective-permute-start | bytes 245768 | tf_op jit(solution)/shard_map/ppermute | solution.py:30
  152.0 11.4 %collective-permute-start.15 = (f32[1,5120]{1,0:T(1,128)S(1)}, f32[1,5120]{1,0:T(1,128)S(1)}, u32[]{:S(2)}, u32[]{:S(2)}) collective-permute-start(f32[1,5120]{1,0:T(1,128)S(1)} %get-tuple-element.33), channel_id=1, source_target_pairs={{0,64},{4,68},{8,72},{12,76},{16,80},{20,84},{24,88},{28,92},{32,9... | collective-permute-start | bytes 61448 | tf_op jit(solution)/shard_map/ppermute | solution.py:30
  159.9 6.6 %collective-permute-start.16 = (f32[1,5120]{1,0:T(1,128)S(1)}, f32[1,5120]{1,0:T(1,128)S(1)}, u32[]{:S(2)}, u32[]{:S(2)}) collective-permute-start(f32[1,5120]{1,0:T(1,128)S(1)} %get-tuple-element.35), channel_id=1, source_target_pairs={{0,128},{4,132},{8,136},{12,140},{16,144},{20,148},{24,152},{28,15... | collective-permute-start | bytes 61448 | tf_op jit(solution)/shard_map/ppermute | solution.py:30
  159.9 6.6 %collective-permute-start.17 = (f32[1,5120]{1,0:T(1,128)S(1)}, f32[1,5120]{1,0:T(1,128)S(1)}, u32[]{:S(2)}, u32[]{:S(2)}) collective-permute-start(f32[1,5120]{1,0:T(1,128)S(1)} %get-tuple-element.34), channel_id=1, source_target_pairs={{0,192},{4,196},{8,200},{12,204},{16,208},{20,212},{24,216},{28,22... | collective-permute-start | bytes 61448 | tf_op jit(solution)/shard_map/ppermute | solution.py:30
  166.6 7.6 %collective-permute-start.21 = (f32[1,1024]{1,0:T(1,128)S(1)}, f32[1,1024]{1,0:T(1,128)S(1)}, u32[]{:S(2)}, u32[]{:S(2)}) collective-permute-start(f32[1,1024]{1,0:T(1,128)S(1)} %get-tuple-element.37), channel_id=1, source_target_pairs={{0,64},{4,68},{8,72},{12,76},{16,80},{20,84},{24,88},{28,92},{32,9... | collective-permute-start | bytes 12296 | tf_op jit(solution)/shard_map/ppermute | solution.py:30
  167.1 9.6 %collective-permute-start.22 = (f32[1,1024]{1,0:T(1,128)S(1)}, f32[1,1024]{1,0:T(1,128)S(1)}, u32[]{:S(2)}, u32[]{:S(2)}) collective-permute-start(f32[1,1024]{1,0:T(1,128)S(1)} %get-tuple-element.37), channel_id=1, source_target_pairs={{0,128},{4,132},{8,136},{12,140},{16,144},{20,148},{24,152},{28,15... | collective-permute-start | bytes 12296 | tf_op jit(solution)/shard_map/ppermute | solution.py:30
  170.3 6.4 %collective-permute-start.23 = (f32[1,1024]{1,0:T(1,128)S(1)}, f32[1,1024]{1,0:T(1,128)S(1)}, u32[]{:S(2)}, u32[]{:S(2)}) collective-permute-start(f32[1,1024]{1,0:T(1,128)S(1)} %get-tuple-element.37), channel_id=1, source_target_pairs={{0,192},{4,196},{8,200},{12,204},{16,208},{20,212},{24,216},{28,22... | collective-permute-start | bytes 12296 | tf_op jit(solution)/shard_map/ppermute | solution.py:30
  172.6 6.6 %collective-permute-start.18 = (f32[1,64,2,32]{1,3,2,0:T(8,128)S(1)}, f32[1,64,2,32]{1,3,2,0:T(8,128)S(1)}, u32[]{:S(2)}, u32[]{:S(2)}) collective-permute-start(f32[1,64,2,32]{1,3,2,0:T(8,128)S(1)} %copy.36), channel_id=1, source_target_pairs={{0,1},{1,0},{2,3},{3,2},{4,5},{5,4},{6,7},{7,6},{8,9},{9,8},{10,11... | collective-permute-start | bytes 49160 | tf_op jit(solution)/shard_map/ppermute | solution.py:30
  172.6 9.0 %collective-permute-start.19 = (f32[1,64,2,32]{1,3,2,0:T(8,128)S(1)}, f32[1,64,2,32]{1,3,2,0:T(8,128)S(1)}, u32[]{:S(2)}, u32[]{:S(2)}) collective-permute-start(f32[1,64,2,32]{1,3,2,0:T(8,128)S(1)} %copy.36), channel_id=1, source_target_pairs={{0,2},{1,3},{2,0},{3,1},{4,6},{5,7},{6,4},{7,5},{8,10},{9,11},{10,... | collective-permute-start | bytes 49160 | tf_op jit(solution)/shard_map/ppermute | solution.py:30
  174.2 7.5 %collective-permute-start.20 = (f32[1,64,2,32]{1,3,2,0:T(8,128)S(1)}, f32[1,64,2,32]{1,3,2,0:T(8,128)S(1)}, u32[]{:S(2)}, u32[]{:S(2)}) collective-permute-start(f32[1,64,2,32]{1,3,2,0:T(8,128)S(1)} %copy.36), channel_id=1, source_target_pairs={{0,3},{1,2},{2,1},{3,0},{4,7},{5,6},{6,5},{7,4},{8,11},{9,10},{10,... | collective-permute-start | bytes 49160 | tf_op jit(solution)/shard_map/ppermute | solution.py:30
  177.4 6.3 %collective-permute-start.24 = (f32[4,1024]{1,0:T(4,128)S(1)}, f32[4,1024]{1,0:T(4,128)S(1)}, u32[]{:S(2)}, u32[]{:S(2)}) collective-permute-start(f32[4,1024]{1,0:T(4,128)S(1)} %broadcast_select_fusion.2), channel_id=1, source_target_pairs={{0,16},{4,20},{8,24},{12,28},{16,0},{20,4},{24,8},{28,12},{32,48},... | collective-permute-start | bytes 49160 | tf_op jit(solution)/shard_map/ppermute | solution.py:30
  178.6 5.1 %collective-permute-start.25 = (f32[4,1024]{1,0:T(4,128)S(1)}, f32[4,1024]{1,0:T(4,128)S(1)}, u32[]{:S(2)}, u32[]{:S(2)}) collective-permute-start(f32[4,1024]{1,0:T(4,128)S(1)} %broadcast_select_fusion.2), channel_id=1, source_target_pairs={{0,32},{4,36},{8,40},{12,44},{16,48},{20,52},{24,56},{28,60},{32,0... | collective-permute-start | bytes 49160 | tf_op jit(solution)/shard_map/ppermute | solution.py:30
  185.0 8.4 %collective-permute-start.27 = (f32[16,1024]{1,0:T(8,128)S(1)}, f32[16,1024]{1,0:T(8,128)S(1)}, u32[]{:S(2)}, u32[]{:S(2)}) collective-permute-start(f32[16,1024]{1,0:T(8,128)S(1)} %broadcast_select_fusion), channel_id=1, source_target_pairs={{0,4},{4,0},{8,12},{12,8},{16,20},{20,16},{24,28},{28,24},{32,36},... | collective-permute-start | bytes 196616 | tf_op jit(solution)/shard_map/ppermute | solution.py:30
  191.6 5.2 %collective-permute-start.29 = (f32[16,1024]{1,0:T(8,128)S(1)}, f32[16,1024]{1,0:T(8,128)S(1)}, u32[]{:S(2)}, u32[]{:S(2)}) collective-permute-start(f32[16,1024]{1,0:T(8,128)S(1)} %broadcast_select_fusion), channel_id=1, source_target_pairs={{0,12},{4,8},{8,4},{12,0},{16,28},{20,24},{24,20},{28,16},{32,44},... | collective-permute-start | bytes 196616 | tf_op jit(solution)/shard_map/ppermute | solution.py:30
  (12 other events, 152.6 us)

commit v6 on v5

--- a/solution.py
+++ b/solution.py
@@ -146,7 +146,8 @@
     contrib = jnp.stack([dkey.reshape(span, rows, cols), dval.reshape(span, rows, cols)], 1)
     reach = span // 2
     while reach >= 1:
-        contrib = contrib[:reach] + passed_along(contrib[reach : 2 * reach], "wide", -reach)
+        sent = passed_along(contrib[reach : 2 * reach].astype(jnp.bfloat16), "wide", -reach)
+        contrib = contrib[:reach] + sent.astype(jnp.float32)
         reach //= 2
     total = contrib[0]
     key_grad = total[0].astype(jnp.bfloat16)

time: 200 us -> 187 us (0.935)
  waiting for transfers between devices: 85 us -> 67.6 us
  other arithmetic: 4.58 us -> 7.37 us
    ppermute x6, waiting for transfers between devices: 54.6 us -> 37.1 us  [passed_along(): return lax.ppermute(array, axis, pairs)]
    add x3, other arithmetic: 0.24 us -> 2.28 us  [on_device(): contrib = contrib[:reach] + sent.astype(jnp.float32)]
    unnamed x21 -> x23, local copies, waits for them, and re-layouts: 3.34 us -> 4.12 us
where the time goes in v6:
time: 187 us; the launch traced here: 186 us
  starting transfers between devices  69.9 us (37%)
  waiting for transfers between devices  67.6 us (36%)
  Pallas kernels  20.1 us (11%)
  local copies, waits for them, and re-layouts  15.4 us (8%)
  other arithmetic  7.37 us (4%)
  matrix products  4.02 us (2%)
  between operations  2 us (1%)
    ppermute x24, starting transfers between devices, xor_partner(): return lax.ppermute(array, axis, [(i, i ^ mask) for i in range(devices)])  47.3 us
    ppermute x6, waiting for transfers between devices, passed_along(): return lax.ppermute(array, axis, pairs)  37.1 us
    ppermute x24, waiting for transfers between devices, xor_partner(): return lax.ppermute(array, axis, [(i, i ^ mask) for i in range(devices)])  30.5 us
    ppermute x6, starting transfers between devices, passed_along(): return lax.ppermute(array, axis, pairs)  22.6 us
    pallas_call x1, Pallas kernels, attention_grads(): pl.pallas_call(attention_body, grid_spec=grid_spec, out_shape=[jax.ShapeD...  20.1 us
    unnamed x23, local copies, waits for them, and re-layouts  4.12 us
  transfers between devices with their start and end apart: 30, of which 17 were waited for; matrix products, arithmetic and copies ran while one was open for 2% of the time, Pallas kernels for 0%

profile of v6, /device:TPU:1, one launch (start us, length us, event | category | flops | bytes accessed | tf_op | source)
XLA Modules:
  0.0 186.5 jit_solution(17481585155784288836)
XLA Ops:
  1.6 4.6 %collective-permute-start = (bf16[1,2,128,256]{3,2,1,0:T(8,128)(2,1)S(1)}, bf16[1,2,128,256]{3,2,1,0:T(8,128)(2,1)S(1)}, u32[]{:S(2)}, u32[]{:S(2)}) collective-permute-start(bf16[1,2,128,256]{3,2,1,0:T(8,128)(2,1)S(1)} %maximum_bitcast_fusion), channel_id=1, source_target_pairs={{0,4},{4,8},{8,12},{12,16},{16,20},{20,24},{24,28},{28,32},{32,36}... | collective-permute-start | bytes 393224 | tf_op jit(solution)/shard_map/ppermute | solution.py:15
  8.2 3.2 %collective-permute-start.1 = (bf16[2,2,128,256]{3,2,1,0:T(8,128)(2,1)S(1)}, bf16[2,2,128,256]{3,2,1,0:T(8,128)(2,1)S(1)}, u32[]{:S(2)}, u32[]{:S(2)}) collective-permute-start(bf16[2,2,128,256]{3,2,1,0:T(8,128)(2,1)S(1)} %pad_maximum_fusion.3), channel_id=1, source_target_pairs={{0,8},{4,12},{8,16},{12,20},{16,24},{20,28},{24,32},{28,36},{32,40... | collective-permute-start | bytes 786440 | tf_op jit(solution)/shard_map/ppermute | solution.py:15
  11.4 4.4 %collective-permute-done.1 = bf16[2,2,128,256]{3,2,1,0:T(8,128)(2,1)S(1)} collective-permute-done((bf16[2,2,128,256]{3,2,1,0:T(8,128)(2,1)S(1)}, bf16[2,2,128,256]{3,2,1,0:T(8,128)(2,1)S(1)}, u32[]{:S(2)}, u32[]{:S(2)}) %collective-permute-start.1) | collective-permute-done | bytes 262176 | tf_op jit(solution)/shard_map/ppermute | solution.py:15
  15.8 5.2 %collective-permute-start.2 = (bf16[4,2,128,256]{3,2,1,0:T(8,128)(2,1)S(1)}, bf16[4,2,128,256]{3,2,1,0:T(8,128)(2,1)S(1)}, u32[]{:S(2)}, u32[]{:S(2)}) collective-permute-start(bf16[4,2,128,256]{3,2,1,0:T(8,128)(2,1)S(1)} %pad_maximum_fusion.2), channel_id=1, source_target_pairs={{0,16},{4,20},{8,24},{12,28},{16,32},{20,36},{24,40},{28,44},{32,4... | collective-permute-start | bytes 1572872 | tf_op jit(solution)/shard_map/ppermute | solution.py:15
  22.6 7.3 %collective-permute-done.2 = bf16[4,2,128,256]{3,2,1,0:T(8,128)(2,1)S(1)} collective-permute-done((bf16[4,2,128,256]{3,2,1,0:T(8,128)(2,1)S(1)}, bf16[4,2,128,256]{3,2,1,0:T(8,128)(2,1)S(1)}, u32[]{:S(2)}, u32[]{:S(2)}) %collective-permute-start.2) | collective-permute-done | bytes 524320 | tf_op jit(solution)/shard_map/ppermute | solution.py:15
  31.0 20.1 %shard_map.129 = (f32[1024,256]{1,0:T(8,128)}, f32[1024,256]{1,0:T(8,128)}) custom-call(s32[1]{0:T(128)} %bitcast.1.pos_ref, bf16[512,1024]{1,0:T(8,128)(2,1)} %q_ref.1, bf16[512,1024]{1,0:T(8,128)(2,1)} %do_ref.1, bf16[1024,256]{1,0:T(8,128)(2,1)} %bitcast.124, bf16[1024,256]{1,0:T(8,128)(2,1)} %bitcast.123), custom_call_target="tpu_custom_call" | custom-call | tf_op jit(solution)/shard_map/pallas_call | solution.py:107
  54.8 13.6 %collective-permute-done.3 = bf16[4,2,128,256]{3,2,1,0:T(8,128)(2,1)} collective-permute-done((bf16[4,2,128,256]{3,2,1,0:T(8,128)(2,1)}, bf16[4,2,128,256]{3,2,1,0:T(8,128)(2,1)}, u32[]{:S(2)}, u32[]{:S(2)}) %collective-permute-start.3) | collective-permute-done | bytes 524320 | tf_op jit(solution)/shard_map/ppermute | solution.py:15
  72.1 5.7 %collective-permute-done.4 = bf16[2,2,128,256]{3,2,1,0:T(8,128)(2,1)S(1)} collective-permute-done((bf16[2,2,128,256]{3,2,1,0:T(8,128)(2,1)S(1)}, bf16[2,2,128,256]{3,2,1,0:T(8,128)(2,1)S(1)}, u32[]{:S(2)}, u32[]{:S(2)}) %collective-permute-start.4) | collective-permute-done | bytes 262176 | tf_op jit(solution)/shard_map/ppermute | solution.py:15
  79.0 6.9 %collective-permute-start.5 = (bf16[1,2,128,256]{3,2,1,0:T(8,128)(2,1)S(1)}, bf16[1,2,128,256]{3,2,1,0:T(8,128)(2,1)S(1)}, u32[]{:S(2)}, u32[]{:S(2)}) collective-permute-start(bf16[1,2,128,256]{3,2,1,0:T(8,128)(2,1)S(1)} %slice.128), channel_id=1, source_target_pairs={{4,0},{8,4},{12,8},{16,12},{20,16},{24,20},{28,24},{32,28},{36,32}... | collective-permute-start | bytes 393224 | tf_op jit(solution)/shard_map/ppermute | solution.py:15
  86.0 4.2 %collective-permute-done.5 = bf16[1,2,128,256]{3,2,1,0:T(8,128)(2,1)S(1)} collective-permute-done((bf16[1,2,128,256]{3,2,1,0:T(8,128)(2,1)S(1)}, bf16[1,2,128,256]{3,2,1,0:T(8,128)(2,1)S(1)}, u32[]{:S(2)}, u32[]{:S(2)}) %collective-permute-start.5) | collective-permute-done | bytes 131104 | tf_op jit(solution)/shard_map/ppermute | solution.py:15
  94.5 2.5 %collective-permute-start.7 = (f32[1,128,64]{1,2,0:T(8,128)S(1)}, f32[1,128,64]{1,2,0:T(8,128)S(1)}, u32[]{:S(2)}, u32[]{:S(2)}) collective-permute-start(f32[1,128,64]{1,2,0:T(8,128)S(1)} %get-tuple-element.31), channel_id=1, source_target_pairs={{0,2},{1,3},{2,0},{3,1},{4,6},{5,7},{6,4},{7,5},{8,10},{9,11},{10,... | collective-permute-start | bytes 98312 | tf_op jit(solution)/shard_map/ppermute | solution.py:30
  98.7 2.1 %collective-permute-done.8 = f32[1,128,64]{1,2,0:T(8,128)S(1)} collective-permute-done((f32[1,128,64]{1,2,0:T(8,128)S(1)}, f32[1,128,64]{1,2,0:T(8,128)S(1)}, u32[]{:S(2)}, u32[]{:S(2)}) %collective-permute-start.8) | collective-permute-done | bytes 32800 | tf_op jit(solution)/shard_map/ppermute | solution.py:30
  111.3 7.2 %collective-permute-done.10 = f32[16,5120]{1,0:T(8,128)S(1)} collective-permute-done((f32[16,5120]{1,0:T(8,128)S(1)}, f32[16,5120]{1,0:T(8,128)S(1)}, u32[]{:S(2)}, u32[]{:S(2)}) %collective-permute-start.10) | collective-permute-done | bytes 327712 | tf_op jit(solution)/shard_map/ppermute | solution.py:30
  118.5 7.0 %collective-permute-done.11 = f32[16,5120]{1,0:T(8,128)S(1)} collective-permute-done((f32[16,5120]{1,0:T(8,128)S(1)}, f32[16,5120]{1,0:T(8,128)S(1)}, u32[]{:S(2)}, u32[]{:S(2)}) %collective-permute-start.11) | collective-permute-done | bytes 327712 | tf_op jit(solution)/shard_map/ppermute | solution.py:30
  126.1 5.6 %collective-permute-start.12 = (f32[4,5120]{1,0:T(4,128)S(1)}, f32[4,5120]{1,0:T(4,128)S(1)}, u32[]{:S(2)}, u32[]{:S(2)}) collective-permute-start(f32[4,5120]{1,0:T(4,128)S(1)} %bitcast.130), channel_id=1, source_target_pairs={{0,16},{4,20},{8,24},{12,28},{16,0},{20,4},{24,8},{28,12},{32,48},... | collective-permute-start | bytes 245768 | tf_op jit(solution)/shard_map/ppermute | solution.py:30
  135.6 3.6 %collective-permute-done.14 = f32[4,5120]{1,0:T(4,128)S(1)} collective-permute-done((f32[4,5120]{1,0:T(4,128)S(1)}, f32[4,5120]{1,0:T(4,128)S(1)}, u32[]{:S(2)}, u32[]{:S(2)}) %collective-permute-start.14) | collective-permute-done | bytes 81952 | tf_op jit(solution)/shard_map/ppermute | solution.py:30
  139.3 7.9 %collective-permute-start.15 = (f32[1,5120]{1,0:T(1,128)S(1)}, f32[1,5120]{1,0:T(1,128)S(1)}, u32[]{:S(2)}, u32[]{:S(2)}) collective-permute-start(f32[1,5120]{1,0:T(1,128)S(1)} %get-tuple-element.33), channel_id=1, source_target_pairs={{0,64},{4,68},{8,72},{12,76},{16,80},{20,84},{24,88},{28,92},{32,9... | collective-permute-start | bytes 61448 | tf_op jit(solution)/shard_map/ppermute | solution.py:30
  147.2 3.4 %collective-permute-start.17 = (f32[1,5120]{1,0:T(1,128)S(1)}, f32[1,5120]{1,0:T(1,128)S(1)}, u32[]{:S(2)}, u32[]{:S(2)}) collective-permute-start(f32[1,5120]{1,0:T(1,128)S(1)} %get-tuple-element.34), channel_id=1, source_target_pairs={{0,192},{4,196},{8,200},{12,204},{16,208},{20,212},{24,216},{28,22... | collective-permute-start | bytes 61448 | tf_op jit(solution)/shard_map/ppermute | solution.py:30
  150.7 3.2 %collective-permute-done.16 = f32[1,5120]{1,0:T(1,128)S(1)} collective-permute-done((f32[1,5120]{1,0:T(1,128)S(1)}, f32[1,5120]{1,0:T(1,128)S(1)}, u32[]{:S(2)}, u32[]{:S(2)}) %collective-permute-start.16) | collective-permute-done | bytes 20512 | tf_op jit(solution)/shard_map/ppermute | solution.py:30
  154.4 3.2 %collective-permute-start.22 = (f32[1,1024]{1,0:T(1,128)S(1)}, f32[1,1024]{1,0:T(1,128)S(1)}, u32[]{:S(2)}, u32[]{:S(2)}) collective-permute-start(f32[1,1024]{1,0:T(1,128)S(1)} %get-tuple-element.37), channel_id=1, source_target_pairs={{0,128},{4,132},{8,136},{12,140},{16,144},{20,148},{24,152},{28,15... | collective-permute-start | bytes 12296 | tf_op jit(solution)/shard_map/ppermute | solution.py:30
  157.6 2.1 %collective-permute-start.23 = (f32[1,1024]{1,0:T(1,128)S(1)}, f32[1,1024]{1,0:T(1,128)S(1)}, u32[]{:S(2)}, u32[]{:S(2)}) collective-permute-start(f32[1,1024]{1,0:T(1,128)S(1)} %get-tuple-element.37), channel_id=1, source_target_pairs={{0,192},{4,196},{8,200},{12,204},{16,208},{20,212},{24,216},{28,22... | collective-permute-start | bytes 12296 | tf_op jit(solution)/shard_map/ppermute | solution.py:30
  161.6 2.5 %collective-permute-start.20 = (f32[1,64,2,32]{1,3,2,0:T(8,128)S(1)}, f32[1,64,2,32]{1,3,2,0:T(8,128)S(1)}, u32[]{:S(2)}, u32[]{:S(2)}) collective-permute-start(f32[1,64,2,32]{1,3,2,0:T(8,128)S(1)} %copy.36), channel_id=1, source_target_pairs={{0,3},{1,2},{2,1},{3,0},{4,7},{5,6},{6,5},{7,4},{8,11},{9,10},{10,... | collective-permute-start | bytes 49160 | tf_op jit(solution)/shard_map/ppermute | solution.py:30
  166.5 2.5 %collective-permute-start.26 = (f32[4,1024]{1,0:T(4,128)S(1)}, f32[4,1024]{1,0:T(4,128)S(1)}, u32[]{:S(2)}, u32[]{:S(2)}) collective-permute-start(f32[4,1024]{1,0:T(4,128)S(1)} %broadcast_select_fusion.2), channel_id=1, source_target_pairs={{0,48},{4,52},{8,56},{12,60},{16,32},{20,36},{24,40},{28,44},{32,1... | collective-permute-start | bytes 49160 | tf_op jit(solution)/shard_map/ppermute | solution.py:30
  172.3 6.5 %collective-permute-start.27 = (f32[16,1024]{1,0:T(8,128)S(1)}, f32[16,1024]{1,0:T(8,128)S(1)}, u32[]{:S(2)}, u32[]{:S(2)}) collective-permute-start(f32[16,1024]{1,0:T(8,128)S(1)} %broadcast_select_fusion), channel_id=1, source_target_pairs={{0,4},{4,0},{8,12},{12,8},{16,20},{20,16},{24,28},{28,24},{32,36},... | collective-permute-start | bytes 196616 | tf_op jit(solution)/shard_map/ppermute | solution.py:30
  (136 shorter events, 50.0 us)
Async XLA Ops:
  1.6 6.5 %collective-permute-start = (bf16[1,2,128,256]{3,2,1,0:T(8,128)(2,1)S(1)}, bf16[1,2,128,256]{3,2,1,0:T(8,128)(2,1)S(1)}, u32[]{:S(2)}, u32[]{:S(2)}) collective-permute-start(bf16[1,2,128,256]{3,2,1,0:T(8,128)(2,1)S(1)} %maximum_bitcast_fusion), channel_id=1, source_target_pairs={{0,4},{4,8},{8,12},{12,16},{16,20},{20,24},{24,28},{28,32},{32,36}... | collective-permute-start | bytes 393224 | tf_op jit(solution)/shard_map/ppermute | solution.py:15
  8.2 7.6 %collective-permute-start.1 = (bf16[2,2,128,256]{3,2,1,0:T(8,128)(2,1)S(1)}, bf16[2,2,128,256]{3,2,1,0:T(8,128)(2,1)S(1)}, u32[]{:S(2)}, u32[]{:S(2)}) collective-permute-start(bf16[2,2,128,256]{3,2,1,0:T(8,128)(2,1)S(1)} %pad_maximum_fusion.3), channel_id=1, source_target_pairs={{0,8},{4,12},{8,16},{12,20},{16,24},{20,28},{24,32},{28,36},{32,40... | collective-permute-start | bytes 786440 | tf_op jit(solution)/shard_map/ppermute | solution.py:15
  15.8 14.0 %collective-permute-start.2 = (bf16[4,2,128,256]{3,2,1,0:T(8,128)(2,1)S(1)}, bf16[4,2,128,256]{3,2,1,0:T(8,128)(2,1)S(1)}, u32[]{:S(2)}, u32[]{:S(2)}) collective-permute-start(bf16[4,2,128,256]{3,2,1,0:T(8,128)(2,1)S(1)} %pad_maximum_fusion.2), channel_id=1, source_target_pairs={{0,16},{4,20},{8,24},{12,28},{16,32},{20,36},{24,40},{28,44},{32,4... | collective-permute-start | bytes 1572872 | tf_op jit(solution)/shard_map/ppermute | solution.py:15
  53.5 14.9 %collective-permute-start.3 = (bf16[4,2,128,256]{3,2,1,0:T(8,128)(2,1)}, bf16[4,2,128,256]{3,2,1,0:T(8,128)(2,1)}, u32[]{:S(2)}, u32[]{:S(2)}) collective-permute-start(bf16[4,2,128,256]{3,2,1,0:T(8,128)(2,1)} %fusion.2), channel_id=1, source_target_pairs={{16,0},{20,4},{24,8},{28,12},{32,16},{36,20},{40,24},{44,28},{48,3... | collective-permute-start | bytes 1572872 | tf_op jit(solution)/shard_map/ppermute | solution.py:15
  70.6 7.2 %collective-permute-start.4 = (bf16[2,2,128,256]{3,2,1,0:T(8,128)(2,1)S(1)}, bf16[2,2,128,256]{3,2,1,0:T(8,128)(2,1)S(1)}, u32[]{:S(2)}, u32[]{:S(2)}) collective-permute-start(bf16[2,2,128,256]{3,2,1,0:T(8,128)(2,1)S(1)} %slice.127), channel_id=1, source_target_pairs={{8,0},{12,4},{16,8},{20,12},{24,16},{28,20},{32,24},{36,28},{40,32... | collective-permute-start | bytes 786440 | tf_op jit(solution)/shard_map/ppermute | solution.py:15
  79.0 11.2 %collective-permute-start.5 = (bf16[1,2,128,256]{3,2,1,0:T(8,128)(2,1)S(1)}, bf16[1,2,128,256]{3,2,1,0:T(8,128)(2,1)S(1)}, u32[]{:S(2)}, u32[]{:S(2)}) collective-permute-start(bf16[1,2,128,256]{3,2,1,0:T(8,128)(2,1)S(1)} %slice.128), channel_id=1, source_target_pairs={{4,0},{8,4},{12,8},{16,12},{20,16},{24,20},{28,24},{32,28},{36,32}... | collective-permute-start | bytes 393224 | tf_op jit(solution)/shard_map/ppermute | solution.py:15
  108.5 10.0 %collective-permute-start.10 = (f32[16,5120]{1,0:T(8,128)S(1)}, f32[16,5120]{1,0:T(8,128)S(1)}, u32[]{:S(2)}, u32[]{:S(2)}) collective-permute-start(f32[16,5120]{1,0:T(8,128)S(1)} %bitcast.126), channel_id=1, source_target_pairs={{0,8},{4,12},{8,0},{12,4},{16,24},{20,28},{24,16},{28,20},{32,40},... | collective-permute-start | bytes 983048 | tf_op jit(solution)/shard_map/ppermute | solution.py:30
  110.4 15.1 %collective-permute-start.11 = (f32[16,5120]{1,0:T(8,128)S(1)}, f32[16,5120]{1,0:T(8,128)S(1)}, u32[]{:S(2)}, u32[]{:S(2)}) collective-permute-start(f32[16,5120]{1,0:T(8,128)S(1)} %bitcast.127), channel_id=1, source_target_pairs={{0,12},{4,8},{8,4},{12,0},{16,28},{20,24},{24,20},{28,16},{32,44},... | collective-permute-start | bytes 983048 | tf_op jit(solution)/shard_map/ppermute | solution.py:30
  110.6 14.9 %collective-permute-start.9 = (f32[16,5120]{1,0:T(8,128)S(1)}, f32[16,5120]{1,0:T(8,128)S(1)}, u32[]{:S(2)}, u32[]{:S(2)}) collective-permute-start(f32[16,5120]{1,0:T(8,128)S(1)} %bitcast.128), channel_id=1, source_target_pairs={{0,4},{4,0},{8,12},{12,8},{16,20},{20,16},{24,28},{28,24},{32,36},... | collective-permute-start | bytes 983048 | tf_op jit(solution)/shard_map/ppermute | solution.py:30
  126.1 8.1 %collective-permute-start.12 = (f32[4,5120]{1,0:T(4,128)S(1)}, f32[4,5120]{1,0:T(4,128)S(1)}, u32[]{:S(2)}, u32[]{:S(2)}) collective-permute-start(f32[4,5120]{1,0:T(4,128)S(1)} %bitcast.130), channel_id=1, source_target_pairs={{0,16},{4,20},{8,24},{12,28},{16,0},{20,4},{24,8},{28,12},{32,48},... | collective-permute-start | bytes 245768 | tf_op jit(solution)/shard_map/ppermute | solution.py:30
  133.4 5.8 %collective-permute-start.14 = (f32[4,5120]{1,0:T(4,128)S(1)}, f32[4,5120]{1,0:T(4,128)S(1)}, u32[]{:S(2)}, u32[]{:S(2)}) collective-permute-start(f32[4,5120]{1,0:T(4,128)S(1)} %bitcast.132), channel_id=1, source_target_pairs={{0,48},{4,52},{8,56},{12,60},{16,32},{20,36},{24,40},{28,44},{32,1... | collective-permute-start | bytes 245768 | tf_op jit(solution)/shard_map/ppermute | solution.py:30
  139.3 11.4 %collective-permute-start.15 = (f32[1,5120]{1,0:T(1,128)S(1)}, f32[1,5120]{1,0:T(1,128)S(1)}, u32[]{:S(2)}, u32[]{:S(2)}) collective-permute-start(f32[1,5120]{1,0:T(1,128)S(1)} %get-tuple-element.33), channel_id=1, source_target_pairs={{0,64},{4,68},{8,72},{12,76},{16,80},{20,84},{24,88},{28,92},{32,9... | collective-permute-start | bytes 61448 | tf_op jit(solution)/shard_map/ppermute | solution.py:30
  147.2 6.7 %collective-permute-start.16 = (f32[1,5120]{1,0:T(1,128)S(1)}, f32[1,5120]{1,0:T(1,128)S(1)}, u32[]{:S(2)}, u32[]{:S(2)}) collective-permute-start(f32[1,5120]{1,0:T(1,128)S(1)} %get-tuple-element.35), channel_id=1, source_target_pairs={{0,128},{4,132},{8,136},{12,140},{16,144},{20,148},{24,152},{28,15... | collective-permute-start | bytes 61448 | tf_op jit(solution)/shard_map/ppermute | solution.py:30
  147.2 6.7 %collective-permute-start.17 = (f32[1,5120]{1,0:T(1,128)S(1)}, f32[1,5120]{1,0:T(1,128)S(1)}, u32[]{:S(2)}, u32[]{:S(2)}) collective-permute-start(f32[1,5120]{1,0:T(1,128)S(1)} %get-tuple-element.34), channel_id=1, source_target_pairs={{0,192},{4,196},{8,200},{12,204},{16,208},{20,212},{24,216},{28,22... | collective-permute-start | bytes 61448 | tf_op jit(solution)/shard_map/ppermute | solution.py:30
  154.0 7.6 %collective-permute-start.21 = (f32[1,1024]{1,0:T(1,128)S(1)}, f32[1,1024]{1,0:T(1,128)S(1)}, u32[]{:S(2)}, u32[]{:S(2)}) collective-permute-start(f32[1,1024]{1,0:T(1,128)S(1)} %get-tuple-element.37), channel_id=1, source_target_pairs={{0,64},{4,68},{8,72},{12,76},{16,80},{20,84},{24,88},{28,92},{32,9... | collective-permute-start | bytes 12296 | tf_op jit(solution)/shard_map/ppermute | solution.py:30
  154.4 9.7 %collective-permute-start.22 = (f32[1,1024]{1,0:T(1,128)S(1)}, f32[1,1024]{1,0:T(1,128)S(1)}, u32[]{:S(2)}, u32[]{:S(2)}) collective-permute-start(f32[1,1024]{1,0:T(1,128)S(1)} %get-tuple-element.37), channel_id=1, source_target_pairs={{0,128},{4,132},{8,136},{12,140},{16,144},{20,148},{24,152},{28,15... | collective-permute-start | bytes 12296 | tf_op jit(solution)/shard_map/ppermute | solution.py:30
  157.6 6.5 %collective-permute-start.23 = (f32[1,1024]{1,0:T(1,128)S(1)}, f32[1,1024]{1,0:T(1,128)S(1)}, u32[]{:S(2)}, u32[]{:S(2)}) collective-permute-start(f32[1,1024]{1,0:T(1,128)S(1)} %get-tuple-element.37), channel_id=1, source_target_pairs={{0,192},{4,196},{8,200},{12,204},{16,208},{20,212},{24,216},{28,22... | collective-permute-start | bytes 12296 | tf_op jit(solution)/shard_map/ppermute | solution.py:30
  160.0 6.6 %collective-permute-start.18 = (f32[1,64,2,32]{1,3,2,0:T(8,128)S(1)}, f32[1,64,2,32]{1,3,2,0:T(8,128)S(1)}, u32[]{:S(2)}, u32[]{:S(2)}) collective-permute-start(f32[1,64,2,32]{1,3,2,0:T(8,128)S(1)} %copy.36), channel_id=1, source_target_pairs={{0,1},{1,0},{2,3},{3,2},{4,5},{5,4},{6,7},{7,6},{8,9},{9,8},{10,11... | collective-permute-start | bytes 49160 | tf_op jit(solution)/shard_map/ppermute | solution.py:30
  160.0 9.0 %collective-permute-start.19 = (f32[1,64,2,32]{1,3,2,0:T(8,128)S(1)}, f32[1,64,2,32]{1,3,2,0:T(8,128)S(1)}, u32[]{:S(2)}, u32[]{:S(2)}) collective-permute-start(f32[1,64,2,32]{1,3,2,0:T(8,128)S(1)} %copy.36), channel_id=1, source_target_pairs={{0,2},{1,3},{2,0},{3,1},{4,6},{5,7},{6,4},{7,5},{8,10},{9,11},{10,... | collective-permute-start | bytes 49160 | tf_op jit(solution)/shard_map/ppermute | solution.py:30
  161.6 7.5 %collective-permute-start.20 = (f32[1,64,2,32]{1,3,2,0:T(8,128)S(1)}, f32[1,64,2,32]{1,3,2,0:T(8,128)S(1)}, u32[]{:S(2)}, u32[]{:S(2)}) collective-permute-start(f32[1,64,2,32]{1,3,2,0:T(8,128)S(1)} %copy.36), channel_id=1, source_target_pairs={{0,3},{1,2},{2,1},{3,0},{4,7},{5,6},{6,5},{7,4},{8,11},{9,10},{10,... | collective-permute-start | bytes 49160 | tf_op jit(solution)/shard_map/ppermute | solution.py:30
  164.8 6.3 %collective-permute-start.24 = (f32[4,1024]{1,0:T(4,128)S(1)}, f32[4,1024]{1,0:T(4,128)S(1)}, u32[]{:S(2)}, u32[]{:S(2)}) collective-permute-start(f32[4,1024]{1,0:T(4,128)S(1)} %broadcast_select_fusion.2), channel_id=1, source_target_pairs={{0,16},{4,20},{8,24},{12,28},{16,0},{20,4},{24,8},{28,12},{32,48},... | collective-permute-start | bytes 49160 | tf_op jit(solution)/shard_map/ppermute | solution.py:30
  165.9 5.2 %collective-permute-start.25 = (f32[4,1024]{1,0:T(4,128)S(1)}, f32[4,1024]{1,0:T(4,128)S(1)}, u32[]{:S(2)}, u32[]{:S(2)}) collective-permute-start(f32[4,1024]{1,0:T(4,128)S(1)} %broadcast_select_fusion.2), channel_id=1, source_target_pairs={{0,32},{4,36},{8,40},{12,44},{16,48},{20,52},{24,56},{28,60},{32,0... | collective-permute-start | bytes 49160 | tf_op jit(solution)/shard_map/ppermute | solution.py:30
  172.3 8.3 %collective-permute-start.27 = (f32[16,1024]{1,0:T(8,128)S(1)}, f32[16,1024]{1,0:T(8,128)S(1)}, u32[]{:S(2)}, u32[]{:S(2)}) collective-permute-start(f32[16,1024]{1,0:T(8,128)S(1)} %broadcast_select_fusion), channel_id=1, source_target_pairs={{0,4},{4,0},{8,12},{12,8},{16,20},{20,16},{24,28},{28,24},{32,36},... | collective-permute-start | bytes 196616 | tf_op jit(solution)/shard_map/ppermute | solution.py:30
  178.9 5.2 %collective-permute-start.29 = (f32[16,1024]{1,0:T(8,128)S(1)}, f32[16,1024]{1,0:T(8,128)S(1)}, u32[]{:S(2)}, u32[]{:S(2)}) collective-permute-start(f32[16,1024]{1,0:T(8,128)S(1)} %broadcast_select_fusion), channel_id=1, source_target_pairs={{0,12},{4,8},{8,4},{12,0},{16,28},{20,24},{24,20},{28,16},{32,44},... | collective-permute-start | bytes 196616 | tf_op jit(solution)/shard_map/ppermute | solution.py:30
  (13 other events, 161.0 us)

commit v7 on v5

--- a/solution.py
+++ b/solution.py
@@ -146,7 +146,10 @@
     contrib = jnp.stack([dkey.reshape(span, rows, cols), dval.reshape(span, rows, cols)], 1)
     reach = span // 2
     while reach >= 1:
-        contrib = contrib[:reach] + passed_along(contrib[reach : 2 * reach], "wide", -reach)
+        give = contrib[reach : 2 * reach]
+        if reach == span // 2:
+            give = give.astype(jnp.bfloat16)
+        contrib = contrib[:reach] + passed_along(give, "wide", -reach).astype(jnp.float32)
         reach //= 2
     total = contrib[0]
     key_grad = total[0].astype(jnp.bfloat16)

time: 200 us -> 188 us (0.940)
  waiting for transfers between devices: 85 us -> 73.8 us
    ppermute x6, waiting for transfers between devices: 54.6 us -> 43.3 us  [passed_along(): return lax.ppermute(array, axis, pairs)]
where the time goes in v7:
time: 188 us
  waiting for transfers between devices  73.8 us (39%)
  starting transfers between devices  68.7 us (37%)
  Pallas kernels  20.1 us (11%)
  local copies, waits for them, and re-layouts  14.7 us (8%)
  other arithmetic  4.52 us (2%)
  matrix products  4.08 us (2%)
  between operations  1.99 us (1%)
    ppermute x24, starting transfers between devices, xor_partner(): return lax.ppermute(array, axis, [(i, i ^ mask) for i in range(devices)])  47.3 us
    ppermute x6, waiting for transfers between devices, passed_along(): return lax.ppermute(array, axis, pairs)  43.3 us
    ppermute x24, waiting for transfers between devices, xor_partner(): return lax.ppermute(array, axis, [(i, i ^ mask) for i in range(devices)])  30.5 us
    ppermute x6, starting transfers between devices, passed_along(): return lax.ppermute(array, axis, pairs)  21.5 us
    pallas_call x1, Pallas kernels, attention_grads(): pl.pallas_call(attention_body, grid_spec=grid_spec, out_shape=[jax.ShapeD...  20.1 us
  transfers between devices with their start and end apart: 30, of which 17 were waited for; matrix products, arithmetic and copies ran while one was open for 2% of the time, Pallas kernels for 0%

profile of v7, /device:TPU:1, one launch (start us, length us, event | category | flops | bytes accessed | tf_op | source)
XLA Modules:
  0.0 187.9 jit_solution(16228924417385191472)
XLA Ops:
  1.6 4.6 %collective-permute-start = (bf16[1,2,128,256]{3,2,1,0:T(8,128)(2,1)S(1)}, bf16[1,2,128,256]{3,2,1,0:T(8,128)(2,1)S(1)}, u32[]{:S(2)}, u32[]{:S(2)}) collective-permute-start(bf16[1,2,128,256]{3,2,1,0:T(8,128)(2,1)S(1)} %maximum_bitcast_fusion), channel_id=1, source_target_pairs={{0,4},{4,8},{8,12},{12,16},{16,20},{20,24},{24,28},{28,32},{32,36}... | collective-permute-start | bytes 393224 | tf_op jit(solution)/shard_map/ppermute | solution.py:15
  8.2 3.2 %collective-permute-start.1 = (bf16[2,2,128,256]{3,2,1,0:T(8,128)(2,1)S(1)}, bf16[2,2,128,256]{3,2,1,0:T(8,128)(2,1)S(1)}, u32[]{:S(2)}, u32[]{:S(2)}) collective-permute-start(bf16[2,2,128,256]{3,2,1,0:T(8,128)(2,1)S(1)} %pad_maximum_fusion.3), channel_id=1, source_target_pairs={{0,8},{4,12},{8,16},{12,20},{16,24},{20,28},{24,32},{28,36},{32,40... | collective-permute-start | bytes 786440 | tf_op jit(solution)/shard_map/ppermute | solution.py:15
  11.4 4.4 %collective-permute-done.1 = bf16[2,2,128,256]{3,2,1,0:T(8,128)(2,1)S(1)} collective-permute-done((bf16[2,2,128,256]{3,2,1,0:T(8,128)(2,1)S(1)}, bf16[2,2,128,256]{3,2,1,0:T(8,128)(2,1)S(1)}, u32[]{:S(2)}, u32[]{:S(2)}) %collective-permute-start.1) | collective-permute-done | bytes 262176 | tf_op jit(solution)/shard_map/ppermute | solution.py:15
  15.8 5.2 %collective-permute-start.2 = (bf16[4,2,128,256]{3,2,1,0:T(8,128)(2,1)S(1)}, bf16[4,2,128,256]{3,2,1,0:T(8,128)(2,1)S(1)}, u32[]{:S(2)}, u32[]{:S(2)}) collective-permute-start(bf16[4,2,128,256]{3,2,1,0:T(8,128)(2,1)S(1)} %pad_maximum_fusion.2), channel_id=1, source_target_pairs={{0,16},{4,20},{8,24},{12,28},{16,32},{20,36},{24,40},{28,44},{32,4... | collective-permute-start | bytes 1572872 | tf_op jit(solution)/shard_map/ppermute | solution.py:15
  22.6 7.3 %collective-permute-done.2 = bf16[4,2,128,256]{3,2,1,0:T(8,128)(2,1)S(1)} collective-permute-done((bf16[4,2,128,256]{3,2,1,0:T(8,128)(2,1)S(1)}, bf16[4,2,128,256]{3,2,1,0:T(8,128)(2,1)S(1)}, u32[]{:S(2)}, u32[]{:S(2)}) %collective-permute-start.2) | collective-permute-done | bytes 524320 | tf_op jit(solution)/shard_map/ppermute | solution.py:15
  31.0 20.1 %shard_map.129 = (f32[1024,256]{1,0:T(8,128)}, f32[1024,256]{1,0:T(8,128)}) custom-call(s32[1]{0:T(128)} %bitcast.1.pos_ref, bf16[512,1024]{1,0:T(8,128)(2,1)} %q_ref.1, bf16[512,1024]{1,0:T(8,128)(2,1)} %do_ref.1, bf16[1024,256]{1,0:T(8,128)(2,1)} %bitcast.124, bf16[1024,256]{1,0:T(8,128)(2,1)} %bitcast.123), custom_call_target="tpu_custom_call" | custom-call | tf_op jit(solution)/shard_map/pallas_call | solution.py:107
  54.0 13.3 %collective-permute-done.3 = bf16[4,2,128,256]{3,2,1,0:T(8,128)(2,1)S(1)} collective-permute-done((bf16[4,2,128,256]{3,2,1,0:T(8,128)(2,1)S(1)}, bf16[4,2,128,256]{3,2,1,0:T(8,128)(2,1)S(1)}, u32[]{:S(2)}, u32[]{:S(2)}) %collective-permute-start.3) | collective-permute-done | bytes 524320 | tf_op jit(solution)/shard_map/ppermute | solution.py:15
  68.9 11.6 %collective-permute-done.4 = f32[2,2,128,256]{3,2,1,0:T(8,128)S(1)} collective-permute-done((f32[2,2,128,256]{3,2,1,0:T(8,128)S(1)}, f32[2,2,128,256]{3,2,1,0:T(8,128)S(1)}, u32[]{:S(2)}, u32[]{:S(2)}) %collective-permute-start.4) | collective-permute-done | bytes 524320 | tf_op jit(solution)/shard_map/ppermute | solution.py:15
  80.5 5.9 %collective-permute-start.5 = (f32[1,2,128,256]{3,2,1,0:T(8,128)S(1)}, f32[1,2,128,256]{3,2,1,0:T(8,128)S(1)}, u32[]{:S(2)}, u32[]{:S(2)}) collective-permute-start(f32[1,2,128,256]{3,2,1,0:T(8,128)S(1)} %slice.86), channel_id=1, source_target_pairs={{4,0},{8,4},{12,8},{16,12},{20,16},{24,20},{28,24},{32,28},{36,32}... | collective-permute-start | bytes 786440 | tf_op jit(solution)/shard_map/ppermute | solution.py:15
  86.6 4.9 %collective-permute-done.5 = f32[1,2,128,256]{3,2,1,0:T(8,128)S(1)} collective-permute-done((f32[1,2,128,256]{3,2,1,0:T(8,128)S(1)}, f32[1,2,128,256]{3,2,1,0:T(8,128)S(1)}, u32[]{:S(2)}, u32[]{:S(2)}) %collective-permute-start.5) | collective-permute-done | bytes 262176 | tf_op jit(solution)/shard_map/ppermute | solution.py:15
  96.0 2.5 %collective-permute-start.7 = (f32[1,128,64]{1,2,0:T(8,128)S(1)}, f32[1,128,64]{1,2,0:T(8,128)S(1)}, u32[]{:S(2)}, u32[]{:S(2)}) collective-permute-start(f32[1,128,64]{1,2,0:T(8,128)S(1)} %get-tuple-element.31), channel_id=1, source_target_pairs={{0,2},{1,3},{2,0},{3,1},{4,6},{5,7},{6,4},{7,5},{8,10},{9,11},{10,... | collective-permute-start | bytes 98312 | tf_op jit(solution)/shard_map/ppermute | solution.py:30
  100.3 2.1 %collective-permute-done.8 = f32[1,128,64]{1,2,0:T(8,128)S(1)} collective-permute-done((f32[1,128,64]{1,2,0:T(8,128)S(1)}, f32[1,128,64]{1,2,0:T(8,128)S(1)}, u32[]{:S(2)}, u32[]{:S(2)}) %collective-permute-start.8) | collective-permute-done | bytes 32800 | tf_op jit(solution)/shard_map/ppermute | solution.py:30
  113.0 7.2 %collective-permute-done.10 = f32[16,5120]{1,0:T(8,128)S(1)} collective-permute-done((f32[16,5120]{1,0:T(8,128)S(1)}, f32[16,5120]{1,0:T(8,128)S(1)}, u32[]{:S(2)}, u32[]{:S(2)}) %collective-permute-start.10) | collective-permute-done | bytes 327712 | tf_op jit(solution)/shard_map/ppermute | solution.py:30
  120.2 7.0 %collective-permute-done.11 = f32[16,5120]{1,0:T(8,128)S(1)} collective-permute-done((f32[16,5120]{1,0:T(8,128)S(1)}, f32[16,5120]{1,0:T(8,128)S(1)}, u32[]{:S(2)}, u32[]{:S(2)}) %collective-permute-start.11) | collective-permute-done | bytes 327712 | tf_op jit(solution)/shard_map/ppermute | solution.py:30
  127.8 5.3 %collective-permute-start.12 = (f32[4,5120]{1,0:T(4,128)S(1)}, f32[4,5120]{1,0:T(4,128)S(1)}, u32[]{:S(2)}, u32[]{:S(2)}) collective-permute-start(f32[4,5120]{1,0:T(4,128)S(1)} %bitcast.130), channel_id=1, source_target_pairs={{0,16},{4,20},{8,24},{12,28},{16,0},{20,4},{24,8},{28,12},{32,48},... | collective-permute-start | bytes 245768 | tf_op jit(solution)/shard_map/ppermute | solution.py:30
  136.9 3.7 %collective-permute-done.14 = f32[4,5120]{1,0:T(4,128)S(1)} collective-permute-done((f32[4,5120]{1,0:T(4,128)S(1)}, f32[4,5120]{1,0:T(4,128)S(1)}, u32[]{:S(2)}, u32[]{:S(2)}) %collective-permute-start.14) | collective-permute-done | bytes 81952 | tf_op jit(solution)/shard_map/ppermute | solution.py:30
  140.7 7.9 %collective-permute-start.15 = (f32[1,5120]{1,0:T(1,128)S(1)}, f32[1,5120]{1,0:T(1,128)S(1)}, u32[]{:S(2)}, u32[]{:S(2)}) collective-permute-start(f32[1,5120]{1,0:T(1,128)S(1)} %get-tuple-element.33), channel_id=1, source_target_pairs={{0,64},{4,68},{8,72},{12,76},{16,80},{20,84},{24,88},{28,92},{32,9... | collective-permute-start | bytes 61448 | tf_op jit(solution)/shard_map/ppermute | solution.py:30
  148.6 3.4 %collective-permute-start.17 = (f32[1,5120]{1,0:T(1,128)S(1)}, f32[1,5120]{1,0:T(1,128)S(1)}, u32[]{:S(2)}, u32[]{:S(2)}) collective-permute-start(f32[1,5120]{1,0:T(1,128)S(1)} %get-tuple-element.34), channel_id=1, source_target_pairs={{0,192},{4,196},{8,200},{12,204},{16,208},{20,212},{24,216},{28,22... | collective-permute-start | bytes 61448 | tf_op jit(solution)/shard_map/ppermute | solution.py:30
  152.1 3.2 %collective-permute-done.16 = f32[1,5120]{1,0:T(1,128)S(1)} collective-permute-done((f32[1,5120]{1,0:T(1,128)S(1)}, f32[1,5120]{1,0:T(1,128)S(1)}, u32[]{:S(2)}, u32[]{:S(2)}) %collective-permute-start.16) | collective-permute-done | bytes 20512 | tf_op jit(solution)/shard_map/ppermute | solution.py:30
  155.8 3.2 %collective-permute-start.22 = (f32[1,1024]{1,0:T(1,128)S(1)}, f32[1,1024]{1,0:T(1,128)S(1)}, u32[]{:S(2)}, u32[]{:S(2)}) collective-permute-start(f32[1,1024]{1,0:T(1,128)S(1)} %get-tuple-element.37), channel_id=1, source_target_pairs={{0,128},{4,132},{8,136},{12,140},{16,144},{20,148},{24,152},{28,15... | collective-permute-start | bytes 12296 | tf_op jit(solution)/shard_map/ppermute | solution.py:30
  159.0 2.1 %collective-permute-start.23 = (f32[1,1024]{1,0:T(1,128)S(1)}, f32[1,1024]{1,0:T(1,128)S(1)}, u32[]{:S(2)}, u32[]{:S(2)}) collective-permute-start(f32[1,1024]{1,0:T(1,128)S(1)} %get-tuple-element.37), channel_id=1, source_target_pairs={{0,192},{4,196},{8,200},{12,204},{16,208},{20,212},{24,216},{28,22... | collective-permute-start | bytes 12296 | tf_op jit(solution)/shard_map/ppermute | solution.py:30
  163.0 2.5 %collective-permute-start.20 = (f32[1,64,2,32]{1,3,2,0:T(8,128)S(1)}, f32[1,64,2,32]{1,3,2,0:T(8,128)S(1)}, u32[]{:S(2)}, u32[]{:S(2)}) collective-permute-start(f32[1,64,2,32]{1,3,2,0:T(8,128)S(1)} %copy.36), channel_id=1, source_target_pairs={{0,3},{1,2},{2,1},{3,0},{4,7},{5,6},{6,5},{7,4},{8,11},{9,10},{10,... | collective-permute-start | bytes 49160 | tf_op jit(solution)/shard_map/ppermute | solution.py:30
  167.9 2.5 %collective-permute-start.26 = (f32[4,1024]{1,0:T(4,128)S(1)}, f32[4,1024]{1,0:T(4,128)S(1)}, u32[]{:S(2)}, u32[]{:S(2)}) collective-permute-start(f32[4,1024]{1,0:T(4,128)S(1)} %broadcast_select_fusion.2), channel_id=1, source_target_pairs={{0,48},{4,52},{8,56},{12,60},{16,32},{20,36},{24,40},{28,44},{32,1... | collective-permute-start | bytes 49160 | tf_op jit(solution)/shard_map/ppermute | solution.py:30
  173.7 6.6 %collective-permute-start.27 = (f32[16,1024]{1,0:T(8,128)S(1)}, f32[16,1024]{1,0:T(8,128)S(1)}, u32[]{:S(2)}, u32[]{:S(2)}) collective-permute-start(f32[16,1024]{1,0:T(8,128)S(1)} %broadcast_select_fusion), channel_id=1, source_target_pairs={{0,4},{4,0},{8,12},{12,8},{16,20},{20,16},{24,28},{28,24},{32,36},... | collective-permute-start | bytes 196616 | tf_op jit(solution)/shard_map/ppermute | solution.py:30
  (134 shorter events, 46.3 us)
Async XLA Ops:
  1.6 6.5 %collective-permute-start = (bf16[1,2,128,256]{3,2,1,0:T(8,128)(2,1)S(1)}, bf16[1,2,128,256]{3,2,1,0:T(8,128)(2,1)S(1)}, u32[]{:S(2)}, u32[]{:S(2)}) collective-permute-start(bf16[1,2,128,256]{3,2,1,0:T(8,128)(2,1)S(1)} %maximum_bitcast_fusion), channel_id=1, source_target_pairs={{0,4},{4,8},{8,12},{12,16},{16,20},{20,24},{24,28},{28,32},{32,36}... | collective-permute-start | bytes 393224 | tf_op jit(solution)/shard_map/ppermute | solution.py:15
  8.2 7.6 %collective-permute-start.1 = (bf16[2,2,128,256]{3,2,1,0:T(8,128)(2,1)S(1)}, bf16[2,2,128,256]{3,2,1,0:T(8,128)(2,1)S(1)}, u32[]{:S(2)}, u32[]{:S(2)}) collective-permute-start(bf16[2,2,128,256]{3,2,1,0:T(8,128)(2,1)S(1)} %pad_maximum_fusion.3), channel_id=1, source_target_pairs={{0,8},{4,12},{8,16},{12,20},{16,24},{20,28},{24,32},{28,36},{32,40... | collective-permute-start | bytes 786440 | tf_op jit(solution)/shard_map/ppermute | solution.py:15
  15.8 14.0 %collective-permute-start.2 = (bf16[4,2,128,256]{3,2,1,0:T(8,128)(2,1)S(1)}, bf16[4,2,128,256]{3,2,1,0:T(8,128)(2,1)S(1)}, u32[]{:S(2)}, u32[]{:S(2)}) collective-permute-start(bf16[4,2,128,256]{3,2,1,0:T(8,128)(2,1)S(1)} %pad_maximum_fusion.2), channel_id=1, source_target_pairs={{0,16},{4,20},{8,24},{12,28},{16,32},{20,36},{24,40},{28,44},{32,4... | collective-permute-start | bytes 1572872 | tf_op jit(solution)/shard_map/ppermute | solution.py:15
  52.7 14.6 %collective-permute-start.3 = (bf16[4,2,128,256]{3,2,1,0:T(8,128)(2,1)S(1)}, bf16[4,2,128,256]{3,2,1,0:T(8,128)(2,1)S(1)}, u32[]{:S(2)}, u32[]{:S(2)}) collective-permute-start(bf16[4,2,128,256]{3,2,1,0:T(8,128)(2,1)S(1)} %fusion.2), channel_id=1, source_target_pairs={{16,0},{20,4},{24,8},{28,12},{32,16},{36,20},{40,24},{44,28},{48,3... | collective-permute-start | bytes 1572872 | tf_op jit(solution)/shard_map/ppermute | solution.py:15
  67.5 13.0 %collective-permute-start.4 = (f32[2,2,128,256]{3,2,1,0:T(8,128)S(1)}, f32[2,2,128,256]{3,2,1,0:T(8,128)S(1)}, u32[]{:S(2)}, u32[]{:S(2)}) collective-permute-start(f32[2,2,128,256]{3,2,1,0:T(8,128)S(1)} %slice.84), channel_id=1, source_target_pairs={{8,0},{12,4},{16,8},{20,12},{24,16},{28,20},{32,24},{36,28},{40,32... | collective-permute-start | bytes 1572872 | tf_op jit(solution)/shard_map/ppermute | solution.py:15
  80.5 10.9 %collective-permute-start.5 = (f32[1,2,128,256]{3,2,1,0:T(8,128)S(1)}, f32[1,2,128,256]{3,2,1,0:T(8,128)S(1)}, u32[]{:S(2)}, u32[]{:S(2)}) collective-permute-start(f32[1,2,128,256]{3,2,1,0:T(8,128)S(1)} %slice.86), channel_id=1, source_target_pairs={{4,0},{8,4},{12,8},{16,12},{20,16},{24,20},{28,24},{32,28},{36,32}... | collective-permute-start | bytes 786440 | tf_op jit(solution)/shard_map/ppermute | solution.py:15
  110.1 10.1 %collective-permute-start.10 = (f32[16,5120]{1,0:T(8,128)S(1)}, f32[16,5120]{1,0:T(8,128)S(1)}, u32[]{:S(2)}, u32[]{:S(2)}) collective-permute-start(f32[16,5120]{1,0:T(8,128)S(1)} %bitcast.126), channel_id=1, source_target_pairs={{0,8},{4,12},{8,0},{12,4},{16,24},{20,28},{24,16},{28,20},{32,40},... | collective-permute-start | bytes 983048 | tf_op jit(solution)/shard_map/ppermute | solution.py:30
  112.1 15.1 %collective-permute-start.11 = (f32[16,5120]{1,0:T(8,128)S(1)}, f32[16,5120]{1,0:T(8,128)S(1)}, u32[]{:S(2)}, u32[]{:S(2)}) collective-permute-start(f32[16,5120]{1,0:T(8,128)S(1)} %bitcast.127), channel_id=1, source_target_pairs={{0,12},{4,8},{8,4},{12,0},{16,28},{20,24},{24,20},{28,16},{32,44},... | collective-permute-start | bytes 983048 | tf_op jit(solution)/shard_map/ppermute | solution.py:30
  112.3 14.9 %collective-permute-start.9 = (f32[16,5120]{1,0:T(8,128)S(1)}, f32[16,5120]{1,0:T(8,128)S(1)}, u32[]{:S(2)}, u32[]{:S(2)}) collective-permute-start(f32[16,5120]{1,0:T(8,128)S(1)} %bitcast.128), channel_id=1, source_target_pairs={{0,4},{4,0},{8,12},{12,8},{16,20},{20,16},{24,28},{28,24},{32,36},... | collective-permute-start | bytes 983048 | tf_op jit(solution)/shard_map/ppermute | solution.py:30
  127.8 7.8 %collective-permute-start.12 = (f32[4,5120]{1,0:T(4,128)S(1)}, f32[4,5120]{1,0:T(4,128)S(1)}, u32[]{:S(2)}, u32[]{:S(2)}) collective-permute-start(f32[4,5120]{1,0:T(4,128)S(1)} %bitcast.130), channel_id=1, source_target_pairs={{0,16},{4,20},{8,24},{12,28},{16,0},{20,4},{24,8},{28,12},{32,48},... | collective-permute-start | bytes 245768 | tf_op jit(solution)/shard_map/ppermute | solution.py:30
  134.8 5.8 %collective-permute-start.14 = (f32[4,5120]{1,0:T(4,128)S(1)}, f32[4,5120]{1,0:T(4,128)S(1)}, u32[]{:S(2)}, u32[]{:S(2)}) collective-permute-start(f32[4,5120]{1,0:T(4,128)S(1)} %bitcast.132), channel_id=1, source_target_pairs={{0,48},{4,52},{8,56},{12,60},{16,32},{20,36},{24,40},{28,44},{32,1... | collective-permute-start | bytes 245768 | tf_op jit(solution)/shard_map/ppermute | solution.py:30
  140.7 11.4 %collective-permute-start.15 = (f32[1,5120]{1,0:T(1,128)S(1)}, f32[1,5120]{1,0:T(1,128)S(1)}, u32[]{:S(2)}, u32[]{:S(2)}) collective-permute-start(f32[1,5120]{1,0:T(1,128)S(1)} %get-tuple-element.33), channel_id=1, source_target_pairs={{0,64},{4,68},{8,72},{12,76},{16,80},{20,84},{24,88},{28,92},{32,9... | collective-permute-start | bytes 61448 | tf_op jit(solution)/shard_map/ppermute | solution.py:30
  148.6 6.7 %collective-permute-start.16 = (f32[1,5120]{1,0:T(1,128)S(1)}, f32[1,5120]{1,0:T(1,128)S(1)}, u32[]{:S(2)}, u32[]{:S(2)}) collective-permute-start(f32[1,5120]{1,0:T(1,128)S(1)} %get-tuple-element.35), channel_id=1, source_target_pairs={{0,128},{4,132},{8,136},{12,140},{16,144},{20,148},{24,152},{28,15... | collective-permute-start | bytes 61448 | tf_op jit(solution)/shard_map/ppermute | solution.py:30
  148.6 6.7 %collective-permute-start.17 = (f32[1,5120]{1,0:T(1,128)S(1)}, f32[1,5120]{1,0:T(1,128)S(1)}, u32[]{:S(2)}, u32[]{:S(2)}) collective-permute-start(f32[1,5120]{1,0:T(1,128)S(1)} %get-tuple-element.34), channel_id=1, source_target_pairs={{0,192},{4,196},{8,200},{12,204},{16,208},{20,212},{24,216},{28,22... | collective-permute-start | bytes 61448 | tf_op jit(solution)/shard_map/ppermute | solution.py:30
  155.4 7.6 %collective-permute-start.21 = (f32[1,1024]{1,0:T(1,128)S(1)}, f32[1,1024]{1,0:T(1,128)S(1)}, u32[]{:S(2)}, u32[]{:S(2)}) collective-permute-start(f32[1,1024]{1,0:T(1,128)S(1)} %get-tuple-element.37), channel_id=1, source_target_pairs={{0,64},{4,68},{8,72},{12,76},{16,80},{20,84},{24,88},{28,92},{32,9... | collective-permute-start | bytes 12296 | tf_op jit(solution)/shard_map/ppermute | solution.py:30
  155.8 9.7 %collective-permute-start.22 = (f32[1,1024]{1,0:T(1,128)S(1)}, f32[1,1024]{1,0:T(1,128)S(1)}, u32[]{:S(2)}, u32[]{:S(2)}) collective-permute-start(f32[1,1024]{1,0:T(1,128)S(1)} %get-tuple-element.37), channel_id=1, source_target_pairs={{0,128},{4,132},{8,136},{12,140},{16,144},{20,148},{24,152},{28,15... | collective-permute-start | bytes 12296 | tf_op jit(solution)/shard_map/ppermute | solution.py:30
  159.0 6.5 %collective-permute-start.23 = (f32[1,1024]{1,0:T(1,128)S(1)}, f32[1,1024]{1,0:T(1,128)S(1)}, u32[]{:S(2)}, u32[]{:S(2)}) collective-permute-start(f32[1,1024]{1,0:T(1,128)S(1)} %get-tuple-element.37), channel_id=1, source_target_pairs={{0,192},{4,196},{8,200},{12,204},{16,208},{20,212},{24,216},{28,22... | collective-permute-start | bytes 12296 | tf_op jit(solution)/shard_map/ppermute | solution.py:30
  161.4 6.5 %collective-permute-start.18 = (f32[1,64,2,32]{1,3,2,0:T(8,128)S(1)}, f32[1,64,2,32]{1,3,2,0:T(8,128)S(1)}, u32[]{:S(2)}, u32[]{:S(2)}) collective-permute-start(f32[1,64,2,32]{1,3,2,0:T(8,128)S(1)} %copy.36), channel_id=1, source_target_pairs={{0,1},{1,0},{2,3},{3,2},{4,5},{5,4},{6,7},{7,6},{8,9},{9,8},{10,11... | collective-permute-start | bytes 49160 | tf_op jit(solution)/shard_map/ppermute | solution.py:30
  161.4 9.0 %collective-permute-start.19 = (f32[1,64,2,32]{1,3,2,0:T(8,128)S(1)}, f32[1,64,2,32]{1,3,2,0:T(8,128)S(1)}, u32[]{:S(2)}, u32[]{:S(2)}) collective-permute-start(f32[1,64,2,32]{1,3,2,0:T(8,128)S(1)} %copy.36), channel_id=1, source_target_pairs={{0,2},{1,3},{2,0},{3,1},{4,6},{5,7},{6,4},{7,5},{8,10},{9,11},{10,... | collective-permute-start | bytes 49160 | tf_op jit(solution)/shard_map/ppermute | solution.py:30
  163.0 7.5 %collective-permute-start.20 = (f32[1,64,2,32]{1,3,2,0:T(8,128)S(1)}, f32[1,64,2,32]{1,3,2,0:T(8,128)S(1)}, u32[]{:S(2)}, u32[]{:S(2)}) collective-permute-start(f32[1,64,2,32]{1,3,2,0:T(8,128)S(1)} %copy.36), channel_id=1, source_target_pairs={{0,3},{1,2},{2,1},{3,0},{4,7},{5,6},{6,5},{7,4},{8,11},{9,10},{10,... | collective-permute-start | bytes 49160 | tf_op jit(solution)/shard_map/ppermute | solution.py:30
  166.3 6.3 %collective-permute-start.24 = (f32[4,1024]{1,0:T(4,128)S(1)}, f32[4,1024]{1,0:T(4,128)S(1)}, u32[]{:S(2)}, u32[]{:S(2)}) collective-permute-start(f32[4,1024]{1,0:T(4,128)S(1)} %broadcast_select_fusion.2), channel_id=1, source_target_pairs={{0,16},{4,20},{8,24},{12,28},{16,0},{20,4},{24,8},{28,12},{32,48},... | collective-permute-start | bytes 49160 | tf_op jit(solution)/shard_map/ppermute | solution.py:30
  167.3 5.3 %collective-permute-start.25 = (f32[4,1024]{1,0:T(4,128)S(1)}, f32[4,1024]{1,0:T(4,128)S(1)}, u32[]{:S(2)}, u32[]{:S(2)}) collective-permute-start(f32[4,1024]{1,0:T(4,128)S(1)} %broadcast_select_fusion.2), channel_id=1, source_target_pairs={{0,32},{4,36},{8,40},{12,44},{16,48},{20,52},{24,56},{28,60},{32,0... | collective-permute-start | bytes 49160 | tf_op jit(solution)/shard_map/ppermute | solution.py:30
  173.7 8.4 %collective-permute-start.27 = (f32[16,1024]{1,0:T(8,128)S(1)}, f32[16,1024]{1,0:T(8,128)S(1)}, u32[]{:S(2)}, u32[]{:S(2)}) collective-permute-start(f32[16,1024]{1,0:T(8,128)S(1)} %broadcast_select_fusion), channel_id=1, source_target_pairs={{0,4},{4,0},{8,12},{12,8},{16,20},{20,16},{24,28},{28,24},{32,36},... | collective-permute-start | bytes 196616 | tf_op jit(solution)/shard_map/ppermute | solution.py:30
  180.3 5.2 %collective-permute-start.29 = (f32[16,1024]{1,0:T(8,128)S(1)}, f32[16,1024]{1,0:T(8,128)S(1)}, u32[]{:S(2)}, u32[]{:S(2)}) collective-permute-start(f32[16,1024]{1,0:T(8,128)S(1)} %broadcast_select_fusion), channel_id=1, source_target_pairs={{0,12},{4,8},{8,4},{12,0},{16,28},{20,24},{24,20},{28,16},{32,44},... | collective-permute-start | bytes 196616 | tf_op jit(solution)/shard_map/ppermute | solution.py:30
  (12 other events, 141.4 us)

commit v8 on v7

--- a/solution.py
+++ b/solution.py
@@ -62,10 +62,9 @@
     k = k_ref[...]
     v = v_ref[...]
     s = lax.dot_general(q, k, (((1,), (1,)), ((), ())), preferred_element_type=jnp.float32) * scale
-    block = lax.broadcasted_iota(jnp.int32, s.shape, 1) // 128
-    mask = block <= pos_ref[0]
-    expo = jnp.where(mask, jnp.exp(jnp.where(mask, s, 0.0)), 0.0)
-    prob = expo / jnp.sum(expo, axis=-1, keepdims=True)
+    block = lax.broadcasted_iota(jnp.int32, (1, s.shape[1]), 1) // 128
+    expo = jnp.exp(jnp.where(block <= pos_ref[0], s, -jnp.inf))
+    prob = expo * (1.0 / jnp.sum(expo, axis=-1, keepdims=True))
     prob_b = prob.astype(jnp.bfloat16)
     outp = jnp.dot(prob_b, v, preferred_element_type=jnp.float32)
     delta = jnp.sum(do.astype(jnp.float32) * outp, axis=-1, keepdims=True)

time: 188 us -> 188 us (level)
  no operation moved by 1% of the time
where the time goes in v8:
time: 188 us; the launch traced here: 187 us
  waiting for transfers between devices  73.8 us (39%)
  starting transfers between devices  68.7 us (37%)
  Pallas kernels  19.5 us (10%)
  local copies, waits for them, and re-layouts  14.7 us (8%)
  other arithmetic  4.52 us (2%)
  matrix products  4.08 us (2%)
  between operations  1.99 us (1%)
    ppermute x24, starting transfers between devices, xor_partner(): return lax.ppermute(array, axis, [(i, i ^ mask) for i in range(devices)])  47.2 us
    ppermute x6, waiting for transfers between devices, passed_along(): return lax.ppermute(array, axis, pairs)  43.3 us
    ppermute x24, waiting for transfers between devices, xor_partner(): return lax.ppermute(array, axis, [(i, i ^ mask) for i in range(devices)])  30.5 us
    ppermute x6, starting transfers between devices, passed_along(): return lax.ppermute(array, axis, pairs)  21.4 us
    pallas_call x1, Pallas kernels, attention_grads(): pl.pallas_call(attention_body, grid_spec=grid_spec, out_shape=[jax.ShapeD...  19.5 us
  transfers between devices with their start and end apart: 30, of which 17 were waited for; matrix products, arithmetic and copies ran while one was open for 2% of the time, Pallas kernels for 0%

profile of v8, /device:TPU:1, one launch (start us, length us, event | category | flops | bytes accessed | tf_op | source)
XLA Modules:
  0.0 187.3 jit_solution(2024511776095700723)
XLA Ops:
  1.6 4.6 %collective-permute-start = (bf16[1,2,128,256]{3,2,1,0:T(8,128)(2,1)S(1)}, bf16[1,2,128,256]{3,2,1,0:T(8,128)(2,1)S(1)}, u32[]{:S(2)}, u32[]{:S(2)}) collective-permute-start(bf16[1,2,128,256]{3,2,1,0:T(8,128)(2,1)S(1)} %maximum_bitcast_fusion), channel_id=1, source_target_pairs={{0,4},{4,8},{8,12},{12,16},{16,20},{20,24},{24,28},{28,32},{32,36}... | collective-permute-start | bytes 393224 | tf_op jit(solution)/shard_map/ppermute | solution.py:15
  8.2 3.2 %collective-permute-start.1 = (bf16[2,2,128,256]{3,2,1,0:T(8,128)(2,1)S(1)}, bf16[2,2,128,256]{3,2,1,0:T(8,128)(2,1)S(1)}, u32[]{:S(2)}, u32[]{:S(2)}) collective-permute-start(bf16[2,2,128,256]{3,2,1,0:T(8,128)(2,1)S(1)} %pad_maximum_fusion.3), channel_id=1, source_target_pairs={{0,8},{4,12},{8,16},{12,20},{16,24},{20,28},{24,32},{28,36},{32,40... | collective-permute-start | bytes 786440 | tf_op jit(solution)/shard_map/ppermute | solution.py:15
  11.4 4.4 %collective-permute-done.1 = bf16[2,2,128,256]{3,2,1,0:T(8,128)(2,1)S(1)} collective-permute-done((bf16[2,2,128,256]{3,2,1,0:T(8,128)(2,1)S(1)}, bf16[2,2,128,256]{3,2,1,0:T(8,128)(2,1)S(1)}, u32[]{:S(2)}, u32[]{:S(2)}) %collective-permute-start.1) | collective-permute-done | bytes 262176 | tf_op jit(solution)/shard_map/ppermute | solution.py:15
  15.8 5.2 %collective-permute-start.2 = (bf16[4,2,128,256]{3,2,1,0:T(8,128)(2,1)S(1)}, bf16[4,2,128,256]{3,2,1,0:T(8,128)(2,1)S(1)}, u32[]{:S(2)}, u32[]{:S(2)}) collective-permute-start(bf16[4,2,128,256]{3,2,1,0:T(8,128)(2,1)S(1)} %pad_maximum_fusion.2), channel_id=1, source_target_pairs={{0,16},{4,20},{8,24},{12,28},{16,32},{20,36},{24,40},{28,44},{32,4... | collective-permute-start | bytes 1572872 | tf_op jit(solution)/shard_map/ppermute | solution.py:15
  22.6 7.3 %collective-permute-done.2 = bf16[4,2,128,256]{3,2,1,0:T(8,128)(2,1)S(1)} collective-permute-done((bf16[4,2,128,256]{3,2,1,0:T(8,128)(2,1)S(1)}, bf16[4,2,128,256]{3,2,1,0:T(8,128)(2,1)S(1)}, u32[]{:S(2)}, u32[]{:S(2)}) %collective-permute-start.2) | collective-permute-done | bytes 524320 | tf_op jit(solution)/shard_map/ppermute | solution.py:15
  31.0 19.5 %shard_map.129 = (f32[1024,256]{1,0:T(8,128)}, f32[1024,256]{1,0:T(8,128)}) custom-call(s32[1]{0:T(128)} %bitcast.1.pos_ref, bf16[512,1024]{1,0:T(8,128)(2,1)} %q_ref.1, bf16[512,1024]{1,0:T(8,128)(2,1)} %do_ref.1, bf16[1024,256]{1,0:T(8,128)(2,1)} %bitcast.124, bf16[1024,256]{1,0:T(8,128)(2,1)} %bitcast.123), custom_call_target="tpu_custom_call" | custom-call | tf_op jit(solution)/shard_map/pallas_call | solution.py:106
  53.4 13.3 %collective-permute-done.3 = bf16[4,2,128,256]{3,2,1,0:T(8,128)(2,1)S(1)} collective-permute-done((bf16[4,2,128,256]{3,2,1,0:T(8,128)(2,1)S(1)}, bf16[4,2,128,256]{3,2,1,0:T(8,128)(2,1)S(1)}, u32[]{:S(2)}, u32[]{:S(2)}) %collective-permute-start.3) | collective-permute-done | bytes 524320 | tf_op jit(solution)/shard_map/ppermute | solution.py:15
  68.3 11.6 %collective-permute-done.4 = f32[2,2,128,256]{3,2,1,0:T(8,128)S(1)} collective-permute-done((f32[2,2,128,256]{3,2,1,0:T(8,128)S(1)}, f32[2,2,128,256]{3,2,1,0:T(8,128)S(1)}, u32[]{:S(2)}, u32[]{:S(2)}) %collective-permute-start.4) | collective-permute-done | bytes 524320 | tf_op jit(solution)/shard_map/ppermute | solution.py:15
  80.0 5.9 %collective-permute-start.5 = (f32[1,2,128,256]{3,2,1,0:T(8,128)S(1)}, f32[1,2,128,256]{3,2,1,0:T(8,128)S(1)}, u32[]{:S(2)}, u32[]{:S(2)}) collective-permute-start(f32[1,2,128,256]{3,2,1,0:T(8,128)S(1)} %slice.86), channel_id=1, source_target_pairs={{4,0},{8,4},{12,8},{16,12},{20,16},{24,20},{28,24},{32,28},{36,32}... | collective-permute-start | bytes 786440 | tf_op jit(solution)/shard_map/ppermute | solution.py:15
  86.0 4.9 %collective-permute-done.5 = f32[1,2,128,256]{3,2,1,0:T(8,128)S(1)} collective-permute-done((f32[1,2,128,256]{3,2,1,0:T(8,128)S(1)}, f32[1,2,128,256]{3,2,1,0:T(8,128)S(1)}, u32[]{:S(2)}, u32[]{:S(2)}) %collective-permute-start.5) | collective-permute-done | bytes 262176 | tf_op jit(solution)/shard_map/ppermute | solution.py:15
  95.4 2.5 %collective-permute-start.7 = (f32[1,128,64]{1,2,0:T(8,128)S(1)}, f32[1,128,64]{1,2,0:T(8,128)S(1)}, u32[]{:S(2)}, u32[]{:S(2)}) collective-permute-start(f32[1,128,64]{1,2,0:T(8,128)S(1)} %get-tuple-element.31), channel_id=1, source_target_pairs={{0,2},{1,3},{2,0},{3,1},{4,6},{5,7},{6,4},{7,5},{8,10},{9,11},{10,... | collective-permute-start | bytes 98312 | tf_op jit(solution)/shard_map/ppermute | solution.py:30
  99.7 2.1 %collective-permute-done.8 = f32[1,128,64]{1,2,0:T(8,128)S(1)} collective-permute-done((f32[1,128,64]{1,2,0:T(8,128)S(1)}, f32[1,128,64]{1,2,0:T(8,128)S(1)}, u32[]{:S(2)}, u32[]{:S(2)}) %collective-permute-start.8) | collective-permute-done | bytes 32800 | tf_op jit(solution)/shard_map/ppermute | solution.py:30
  112.4 7.2 %collective-permute-done.10 = f32[16,5120]{1,0:T(8,128)S(1)} collective-permute-done((f32[16,5120]{1,0:T(8,128)S(1)}, f32[16,5120]{1,0:T(8,128)S(1)}, u32[]{:S(2)}, u32[]{:S(2)}) %collective-permute-start.10) | collective-permute-done | bytes 327712 | tf_op jit(solution)/shard_map/ppermute | solution.py:30
  119.6 7.0 %collective-permute-done.11 = f32[16,5120]{1,0:T(8,128)S(1)} collective-permute-done((f32[16,5120]{1,0:T(8,128)S(1)}, f32[16,5120]{1,0:T(8,128)S(1)}, u32[]{:S(2)}, u32[]{:S(2)}) %collective-permute-start.11) | collective-permute-done | bytes 327712 | tf_op jit(solution)/shard_map/ppermute | solution.py:30
  127.2 5.3 %collective-permute-start.12 = (f32[4,5120]{1,0:T(4,128)S(1)}, f32[4,5120]{1,0:T(4,128)S(1)}, u32[]{:S(2)}, u32[]{:S(2)}) collective-permute-start(f32[4,5120]{1,0:T(4,128)S(1)} %bitcast.130), channel_id=1, source_target_pairs={{0,16},{4,20},{8,24},{12,28},{16,0},{20,4},{24,8},{28,12},{32,48},... | collective-permute-start | bytes 245768 | tf_op jit(solution)/shard_map/ppermute | solution.py:30
  136.4 3.7 %collective-permute-done.14 = f32[4,5120]{1,0:T(4,128)S(1)} collective-permute-done((f32[4,5120]{1,0:T(4,128)S(1)}, f32[4,5120]{1,0:T(4,128)S(1)}, u32[]{:S(2)}, u32[]{:S(2)}) %collective-permute-start.14) | collective-permute-done | bytes 81952 | tf_op jit(solution)/shard_map/ppermute | solution.py:30
  140.1 7.9 %collective-permute-start.15 = (f32[1,5120]{1,0:T(1,128)S(1)}, f32[1,5120]{1,0:T(1,128)S(1)}, u32[]{:S(2)}, u32[]{:S(2)}) collective-permute-start(f32[1,5120]{1,0:T(1,128)S(1)} %get-tuple-element.33), channel_id=1, source_target_pairs={{0,64},{4,68},{8,72},{12,76},{16,80},{20,84},{24,88},{28,92},{32,9... | collective-permute-start | bytes 61448 | tf_op jit(solution)/shard_map/ppermute | solution.py:30
  148.0 3.4 %collective-permute-start.17 = (f32[1,5120]{1,0:T(1,128)S(1)}, f32[1,5120]{1,0:T(1,128)S(1)}, u32[]{:S(2)}, u32[]{:S(2)}) collective-permute-start(f32[1,5120]{1,0:T(1,128)S(1)} %get-tuple-element.34), channel_id=1, source_target_pairs={{0,192},{4,196},{8,200},{12,204},{16,208},{20,212},{24,216},{28,22... | collective-permute-start | bytes 61448 | tf_op jit(solution)/shard_map/ppermute | solution.py:30
  151.5 3.2 %collective-permute-done.16 = f32[1,5120]{1,0:T(1,128)S(1)} collective-permute-done((f32[1,5120]{1,0:T(1,128)S(1)}, f32[1,5120]{1,0:T(1,128)S(1)}, u32[]{:S(2)}, u32[]{:S(2)}) %collective-permute-start.16) | collective-permute-done | bytes 20512 | tf_op jit(solution)/shard_map/ppermute | solution.py:30
  155.2 3.2 %collective-permute-start.22 = (f32[1,1024]{1,0:T(1,128)S(1)}, f32[1,1024]{1,0:T(1,128)S(1)}, u32[]{:S(2)}, u32[]{:S(2)}) collective-permute-start(f32[1,1024]{1,0:T(1,128)S(1)} %get-tuple-element.37), channel_id=1, source_target_pairs={{0,128},{4,132},{8,136},{12,140},{16,144},{20,148},{24,152},{28,15... | collective-permute-start | bytes 12296 | tf_op jit(solution)/shard_map/ppermute | solution.py:30
  158.4 2.1 %collective-permute-start.23 = (f32[1,1024]{1,0:T(1,128)S(1)}, f32[1,1024]{1,0:T(1,128)S(1)}, u32[]{:S(2)}, u32[]{:S(2)}) collective-permute-start(f32[1,1024]{1,0:T(1,128)S(1)} %get-tuple-element.37), channel_id=1, source_target_pairs={{0,192},{4,196},{8,200},{12,204},{16,208},{20,212},{24,216},{28,22... | collective-permute-start | bytes 12296 | tf_op jit(solution)/shard_map/ppermute | solution.py:30
  162.4 2.5 %collective-permute-start.20 = (f32[1,64,2,32]{1,3,2,0:T(8,128)S(1)}, f32[1,64,2,32]{1,3,2,0:T(8,128)S(1)}, u32[]{:S(2)}, u32[]{:S(2)}) collective-permute-start(f32[1,64,2,32]{1,3,2,0:T(8,128)S(1)} %copy.36), channel_id=1, source_target_pairs={{0,3},{1,2},{2,1},{3,0},{4,7},{5,6},{6,5},{7,4},{8,11},{9,10},{10,... | collective-permute-start | bytes 49160 | tf_op jit(solution)/shard_map/ppermute | solution.py:30
  167.3 2.5 %collective-permute-start.26 = (f32[4,1024]{1,0:T(4,128)S(1)}, f32[4,1024]{1,0:T(4,128)S(1)}, u32[]{:S(2)}, u32[]{:S(2)}) collective-permute-start(f32[4,1024]{1,0:T(4,128)S(1)} %broadcast_select_fusion.2), channel_id=1, source_target_pairs={{0,48},{4,52},{8,56},{12,60},{16,32},{20,36},{24,40},{28,44},{32,1... | collective-permute-start | bytes 49160 | tf_op jit(solution)/shard_map/ppermute | solution.py:30
  173.1 6.6 %collective-permute-start.27 = (f32[16,1024]{1,0:T(8,128)S(1)}, f32[16,1024]{1,0:T(8,128)S(1)}, u32[]{:S(2)}, u32[]{:S(2)}) collective-permute-start(f32[16,1024]{1,0:T(8,128)S(1)} %broadcast_select_fusion), channel_id=1, source_target_pairs={{0,4},{4,0},{8,12},{12,8},{16,20},{20,16},{24,28},{28,24},{32,36},... | collective-permute-start | bytes 196616 | tf_op jit(solution)/shard_map/ppermute | solution.py:30
  (134 shorter events, 46.3 us)
Async XLA Ops:
  1.6 6.5 %collective-permute-start = (bf16[1,2,128,256]{3,2,1,0:T(8,128)(2,1)S(1)}, bf16[1,2,128,256]{3,2,1,0:T(8,128)(2,1)S(1)}, u32[]{:S(2)}, u32[]{:S(2)}) collective-permute-start(bf16[1,2,128,256]{3,2,1,0:T(8,128)(2,1)S(1)} %maximum_bitcast_fusion), channel_id=1, source_target_pairs={{0,4},{4,8},{8,12},{12,16},{16,20},{20,24},{24,28},{28,32},{32,36}... | collective-permute-start | bytes 393224 | tf_op jit(solution)/shard_map/ppermute | solution.py:15
  8.2 7.6 %collective-permute-start.1 = (bf16[2,2,128,256]{3,2,1,0:T(8,128)(2,1)S(1)}, bf16[2,2,128,256]{3,2,1,0:T(8,128)(2,1)S(1)}, u32[]{:S(2)}, u32[]{:S(2)}) collective-permute-start(bf16[2,2,128,256]{3,2,1,0:T(8,128)(2,1)S(1)} %pad_maximum_fusion.3), channel_id=1, source_target_pairs={{0,8},{4,12},{8,16},{12,20},{16,24},{20,28},{24,32},{28,36},{32,40... | collective-permute-start | bytes 786440 | tf_op jit(solution)/shard_map/ppermute | solution.py:15
  15.8 14.0 %collective-permute-start.2 = (bf16[4,2,128,256]{3,2,1,0:T(8,128)(2,1)S(1)}, bf16[4,2,128,256]{3,2,1,0:T(8,128)(2,1)S(1)}, u32[]{:S(2)}, u32[]{:S(2)}) collective-permute-start(bf16[4,2,128,256]{3,2,1,0:T(8,128)(2,1)S(1)} %pad_maximum_fusion.2), channel_id=1, source_target_pairs={{0,16},{4,20},{8,24},{12,28},{16,32},{20,36},{24,40},{28,44},{32,4... | collective-permute-start | bytes 1572872 | tf_op jit(solution)/shard_map/ppermute | solution.py:15
  52.1 14.6 %collective-permute-start.3 = (bf16[4,2,128,256]{3,2,1,0:T(8,128)(2,1)S(1)}, bf16[4,2,128,256]{3,2,1,0:T(8,128)(2,1)S(1)}, u32[]{:S(2)}, u32[]{:S(2)}) collective-permute-start(bf16[4,2,128,256]{3,2,1,0:T(8,128)(2,1)S(1)} %fusion.2), channel_id=1, source_target_pairs={{16,0},{20,4},{24,8},{28,12},{32,16},{36,20},{40,24},{44,28},{48,3... | collective-permute-start | bytes 1572872 | tf_op jit(solution)/shard_map/ppermute | solution.py:15
  66.9 13.0 %collective-permute-start.4 = (f32[2,2,128,256]{3,2,1,0:T(8,128)S(1)}, f32[2,2,128,256]{3,2,1,0:T(8,128)S(1)}, u32[]{:S(2)}, u32[]{:S(2)}) collective-permute-start(f32[2,2,128,256]{3,2,1,0:T(8,128)S(1)} %slice.84), channel_id=1, source_target_pairs={{8,0},{12,4},{16,8},{20,12},{24,16},{28,20},{32,24},{36,28},{40,32... | collective-permute-start | bytes 1572872 | tf_op jit(solution)/shard_map/ppermute | solution.py:15
  80.0 10.9 %collective-permute-start.5 = (f32[1,2,128,256]{3,2,1,0:T(8,128)S(1)}, f32[1,2,128,256]{3,2,1,0:T(8,128)S(1)}, u32[]{:S(2)}, u32[]{:S(2)}) collective-permute-start(f32[1,2,128,256]{3,2,1,0:T(8,128)S(1)} %slice.86), channel_id=1, source_target_pairs={{4,0},{8,4},{12,8},{16,12},{20,16},{24,20},{28,24},{32,28},{36,32}... | collective-permute-start | bytes 786440 | tf_op jit(solution)/shard_map/ppermute | solution.py:15
  109.5 10.1 %collective-permute-start.10 = (f32[16,5120]{1,0:T(8,128)S(1)}, f32[16,5120]{1,0:T(8,128)S(1)}, u32[]{:S(2)}, u32[]{:S(2)}) collective-permute-start(f32[16,5120]{1,0:T(8,128)S(1)} %bitcast.126), channel_id=1, source_target_pairs={{0,8},{4,12},{8,0},{12,4},{16,24},{20,28},{24,16},{28,20},{32,40},... | collective-permute-start | bytes 983048 | tf_op jit(solution)/shard_map/ppermute | solution.py:30
  111.5 15.1 %collective-permute-start.11 = (f32[16,5120]{1,0:T(8,128)S(1)}, f32[16,5120]{1,0:T(8,128)S(1)}, u32[]{:S(2)}, u32[]{:S(2)}) collective-permute-start(f32[16,5120]{1,0:T(8,128)S(1)} %bitcast.127), channel_id=1, source_target_pairs={{0,12},{4,8},{8,4},{12,0},{16,28},{20,24},{24,20},{28,16},{32,44},... | collective-permute-start | bytes 983048 | tf_op jit(solution)/shard_map/ppermute | solution.py:30
  111.7 14.9 %collective-permute-start.9 = (f32[16,5120]{1,0:T(8,128)S(1)}, f32[16,5120]{1,0:T(8,128)S(1)}, u32[]{:S(2)}, u32[]{:S(2)}) collective-permute-start(f32[16,5120]{1,0:T(8,128)S(1)} %bitcast.128), channel_id=1, source_target_pairs={{0,4},{4,0},{8,12},{12,8},{16,20},{20,16},{24,28},{28,24},{32,36},... | collective-permute-start | bytes 983048 | tf_op jit(solution)/shard_map/ppermute | solution.py:30
  127.2 7.8 %collective-permute-start.12 = (f32[4,5120]{1,0:T(4,128)S(1)}, f32[4,5120]{1,0:T(4,128)S(1)}, u32[]{:S(2)}, u32[]{:S(2)}) collective-permute-start(f32[4,5120]{1,0:T(4,128)S(1)} %bitcast.130), channel_id=1, source_target_pairs={{0,16},{4,20},{8,24},{12,28},{16,0},{20,4},{24,8},{28,12},{32,48},... | collective-permute-start | bytes 245768 | tf_op jit(solution)/shard_map/ppermute | solution.py:30
  134.3 5.8 %collective-permute-start.14 = (f32[4,5120]{1,0:T(4,128)S(1)}, f32[4,5120]{1,0:T(4,128)S(1)}, u32[]{:S(2)}, u32[]{:S(2)}) collective-permute-start(f32[4,5120]{1,0:T(4,128)S(1)} %bitcast.132), channel_id=1, source_target_pairs={{0,48},{4,52},{8,56},{12,60},{16,32},{20,36},{24,40},{28,44},{32,1... | collective-permute-start | bytes 245768 | tf_op jit(solution)/shard_map/ppermute | solution.py:30
  140.1 11.4 %collective-permute-start.15 = (f32[1,5120]{1,0:T(1,128)S(1)}, f32[1,5120]{1,0:T(1,128)S(1)}, u32[]{:S(2)}, u32[]{:S(2)}) collective-permute-start(f32[1,5120]{1,0:T(1,128)S(1)} %get-tuple-element.33), channel_id=1, source_target_pairs={{0,64},{4,68},{8,72},{12,76},{16,80},{20,84},{24,88},{28,92},{32,9... | collective-permute-start | bytes 61448 | tf_op jit(solution)/shard_map/ppermute | solution.py:30
  148.0 6.7 %collective-permute-start.16 = (f32[1,5120]{1,0:T(1,128)S(1)}, f32[1,5120]{1,0:T(1,128)S(1)}, u32[]{:S(2)}, u32[]{:S(2)}) collective-permute-start(f32[1,5120]{1,0:T(1,128)S(1)} %get-tuple-element.35), channel_id=1, source_target_pairs={{0,128},{4,132},{8,136},{12,140},{16,144},{20,148},{24,152},{28,15... | collective-permute-start | bytes 61448 | tf_op jit(solution)/shard_map/ppermute | solution.py:30
  148.0 6.7 %collective-permute-start.17 = (f32[1,5120]{1,0:T(1,128)S(1)}, f32[1,5120]{1,0:T(1,128)S(1)}, u32[]{:S(2)}, u32[]{:S(2)}) collective-permute-start(f32[1,5120]{1,0:T(1,128)S(1)} %get-tuple-element.34), channel_id=1, source_target_pairs={{0,192},{4,196},{8,200},{12,204},{16,208},{20,212},{24,216},{28,22... | collective-permute-start | bytes 61448 | tf_op jit(solution)/shard_map/ppermute | solution.py:30
  154.8 7.6 %collective-permute-start.21 = (f32[1,1024]{1,0:T(1,128)S(1)}, f32[1,1024]{1,0:T(1,128)S(1)}, u32[]{:S(2)}, u32[]{:S(2)}) collective-permute-start(f32[1,1024]{1,0:T(1,128)S(1)} %get-tuple-element.37), channel_id=1, source_target_pairs={{0,64},{4,68},{8,72},{12,76},{16,80},{20,84},{24,88},{28,92},{32,9... | collective-permute-start | bytes 12296 | tf_op jit(solution)/shard_map/ppermute | solution.py:30
  155.2 9.7 %collective-permute-start.22 = (f32[1,1024]{1,0:T(1,128)S(1)}, f32[1,1024]{1,0:T(1,128)S(1)}, u32[]{:S(2)}, u32[]{:S(2)}) collective-permute-start(f32[1,1024]{1,0:T(1,128)S(1)} %get-tuple-element.37), channel_id=1, source_target_pairs={{0,128},{4,132},{8,136},{12,140},{16,144},{20,148},{24,152},{28,15... | collective-permute-start | bytes 12296 | tf_op jit(solution)/shard_map/ppermute | solution.py:30
  158.4 6.5 %collective-permute-start.23 = (f32[1,1024]{1,0:T(1,128)S(1)}, f32[1,1024]{1,0:T(1,128)S(1)}, u32[]{:S(2)}, u32[]{:S(2)}) collective-permute-start(f32[1,1024]{1,0:T(1,128)S(1)} %get-tuple-element.37), channel_id=1, source_target_pairs={{0,192},{4,196},{8,200},{12,204},{16,208},{20,212},{24,216},{28,22... | collective-permute-start | bytes 12296 | tf_op jit(solution)/shard_map/ppermute | solution.py:30
  160.8 6.5 %collective-permute-start.18 = (f32[1,64,2,32]{1,3,2,0:T(8,128)S(1)}, f32[1,64,2,32]{1,3,2,0:T(8,128)S(1)}, u32[]{:S(2)}, u32[]{:S(2)}) collective-permute-start(f32[1,64,2,32]{1,3,2,0:T(8,128)S(1)} %copy.36), channel_id=1, source_target_pairs={{0,1},{1,0},{2,3},{3,2},{4,5},{5,4},{6,7},{7,6},{8,9},{9,8},{10,11... | collective-permute-start | bytes 49160 | tf_op jit(solution)/shard_map/ppermute | solution.py:30
  160.9 9.0 %collective-permute-start.19 = (f32[1,64,2,32]{1,3,2,0:T(8,128)S(1)}, f32[1,64,2,32]{1,3,2,0:T(8,128)S(1)}, u32[]{:S(2)}, u32[]{:S(2)}) collective-permute-start(f32[1,64,2,32]{1,3,2,0:T(8,128)S(1)} %copy.36), channel_id=1, source_target_pairs={{0,2},{1,3},{2,0},{3,1},{4,6},{5,7},{6,4},{7,5},{8,10},{9,11},{10,... | collective-permute-start | bytes 49160 | tf_op jit(solution)/shard_map/ppermute | solution.py:30
  162.4 7.4 %collective-permute-start.20 = (f32[1,64,2,32]{1,3,2,0:T(8,128)S(1)}, f32[1,64,2,32]{1,3,2,0:T(8,128)S(1)}, u32[]{:S(2)}, u32[]{:S(2)}) collective-permute-start(f32[1,64,2,32]{1,3,2,0:T(8,128)S(1)} %copy.36), channel_id=1, source_target_pairs={{0,3},{1,2},{2,1},{3,0},{4,7},{5,6},{6,5},{7,4},{8,11},{9,10},{10,... | collective-permute-start | bytes 49160 | tf_op jit(solution)/shard_map/ppermute | solution.py:30
  165.7 6.3 %collective-permute-start.24 = (f32[4,1024]{1,0:T(4,128)S(1)}, f32[4,1024]{1,0:T(4,128)S(1)}, u32[]{:S(2)}, u32[]{:S(2)}) collective-permute-start(f32[4,1024]{1,0:T(4,128)S(1)} %broadcast_select_fusion.2), channel_id=1, source_target_pairs={{0,16},{4,20},{8,24},{12,28},{16,0},{20,4},{24,8},{28,12},{32,48},... | collective-permute-start | bytes 49160 | tf_op jit(solution)/shard_map/ppermute | solution.py:30
  166.7 5.3 %collective-permute-start.25 = (f32[4,1024]{1,0:T(4,128)S(1)}, f32[4,1024]{1,0:T(4,128)S(1)}, u32[]{:S(2)}, u32[]{:S(2)}) collective-permute-start(f32[4,1024]{1,0:T(4,128)S(1)} %broadcast_select_fusion.2), channel_id=1, source_target_pairs={{0,32},{4,36},{8,40},{12,44},{16,48},{20,52},{24,56},{28,60},{32,0... | collective-permute-start | bytes 49160 | tf_op jit(solution)/shard_map/ppermute | solution.py:30
  173.1 8.4 %collective-permute-start.27 = (f32[16,1024]{1,0:T(8,128)S(1)}, f32[16,1024]{1,0:T(8,128)S(1)}, u32[]{:S(2)}, u32[]{:S(2)}) collective-permute-start(f32[16,1024]{1,0:T(8,128)S(1)} %broadcast_select_fusion), channel_id=1, source_target_pairs={{0,4},{4,0},{8,12},{12,8},{16,20},{20,16},{24,28},{28,24},{32,36},... | collective-permute-start | bytes 196616 | tf_op jit(solution)/shard_map/ppermute | solution.py:30
  179.7 5.2 %collective-permute-start.29 = (f32[16,1024]{1,0:T(8,128)S(1)}, f32[16,1024]{1,0:T(8,128)S(1)}, u32[]{:S(2)}, u32[]{:S(2)}) collective-permute-start(f32[16,1024]{1,0:T(8,128)S(1)} %broadcast_select_fusion), channel_id=1, source_target_pairs={{0,12},{4,8},{8,4},{12,0},{16,28},{20,24},{24,20},{28,16},{32,44},... | collective-permute-start | bytes 196616 | tf_op jit(solution)/shard_map/ppermute | solution.py:30
  (12 other events, 140.8 us)

commit v9 on v8

--- a/solution.py
+++ b/solution.py
@@ -30,15 +30,17 @@
     return lax.ppermute(array, axis, [(i, i ^ mask) for i in range(devices)])
 
 
-def scattered_sum(x, axis):
+def scattered_sum(x, axis, first_kind=None):
     me = lax.axis_index(axis)
-    for low, radix in digit_steps(lax.axis_size(axis)):
+    for step, (low, radix) in enumerate(digit_steps(lax.axis_size(axis))):
         group = x.reshape(x.shape[0] // radix, radix, *x.shape[1:])
         mine = (me // low) % radix
         x = lax.dynamic_index_in_dim(group, mine, axis=1, keepdims=False)
         for t in range(1, radix):
             give = lax.dynamic_index_in_dim(group, jnp.bitwise_xor(mine, t), axis=1, keepdims=False)
-            x = x + xor_partner(give, axis, t * low)
+            if step == 0 and first_kind is not None:
+                give = give.astype(first_kind)
+            x = x + xor_partner(give, axis, t * low).astype(x.dtype)
     return x[0]
 
 
@@ -173,7 +175,7 @@
     width = down.shape[0] // wide_count
     up_both = jnp.stack([up_key, up_value]).reshape(wide_count, -1)
     joined = jnp.concatenate([down.reshape(wide_count, width * 2 * piece), up_both], 1)
-    joined = scattered_sum(joined, "wide")
+    joined = scattered_sum(joined, "wide", jnp.bfloat16)
     down = joined[: width * 2 * piece].reshape(width, 2, piece)
     up_both = gathered(joined[width * 2 * piece :], "wide").reshape(2, rank, cols)
     down = gathered(down, "narrow").transpose(1, 2, 0, 3).reshape(width, 2, rank)

time: 188 us -> 182 us (0.968)
  waiting for transfers between devices: 73.8 us -> 66.3 us
    ppermute x24, waiting for transfers between devices: 30.5 us -> 23.4 us  [xor_partner(): return lax.ppermute(array, axis, [(i, i ^ mask) for i in range(devices)])]
  transfers between devices with their start and end apart: 30 -> 30, of which waited for: 17 -> 17; matrix products, arithmetic and copies ran while one was open for 2% -> 3% of each run, Pallas kernels for 0% -> 0%
where the time goes in v9:
time: 182 us
  starting transfers between devices  69.2 us (38%)
  waiting for transfers between devices  66.3 us (36%)
  Pallas kernels  19.5 us (11%)
  local copies, waits for them, and re-layouts  14.5 us (8%)
  other arithmetic  6.33 us (3%)
  matrix products  4.02 us (2%)
  between operations  2.01 us (1%)
    ppermute x24, starting transfers between devices, xor_partner(): return lax.ppermute(array, axis, [(i, i ^ mask) for i in range(devices)])  47.1 us
    ppermute x6, waiting for transfers between devices, passed_along(): return lax.ppermute(array, axis, pairs)  42.9 us
    ppermute x24, waiting for transfers between devices, xor_partner(): return lax.ppermute(array, axis, [(i, i ^ mask) for i in range(devices)])  23.4 us
    ppermute x6, starting transfers between devices, passed_along(): return lax.ppermute(array, axis, pairs)  22.2 us
    pallas_call x1, Pallas kernels, attention_grads(): pl.pallas_call(attention_body, grid_spec=grid_spec, out_shape=[jax.ShapeD...  19.5 us
  transfers between devices with their start and end apart: 30, of which 17 were waited for; matrix products, arithmetic and copies ran while one was open for 3% of the time, Pallas kernels for 0%

profile of v9, /device:TPU:1, one launch (start us, length us, event | category | flops | bytes accessed | tf_op | source)
XLA Modules:
  0.0 181.8 jit_solution(5890111448885509415)
XLA Ops:
  1.6 4.6 %collective-permute-start = (bf16[1,2,128,256]{3,2,1,0:T(8,128)(2,1)S(1)}, bf16[1,2,128,256]{3,2,1,0:T(8,128)(2,1)S(1)}, u32[]{:S(2)}, u32[]{:S(2)}) collective-permute-start(bf16[1,2,128,256]{3,2,1,0:T(8,128)(2,1)S(1)} %maximum_bitcast_fusion), channel_id=1, source_target_pairs={{0,4},{4,8},{8,12},{12,16},{16,20},{20,24},{24,28},{28,32},{32,36}... | collective-permute-start | bytes 393224 | tf_op jit(solution)/shard_map/ppermute | solution.py:15
  8.2 3.2 %collective-permute-start.1 = (bf16[2,2,128,256]{3,2,1,0:T(8,128)(2,1)S(1)}, bf16[2,2,128,256]{3,2,1,0:T(8,128)(2,1)S(1)}, u32[]{:S(2)}, u32[]{:S(2)}) collective-permute-start(bf16[2,2,128,256]{3,2,1,0:T(8,128)(2,1)S(1)} %pad_maximum_fusion.3), channel_id=1, source_target_pairs={{0,8},{4,12},{8,16},{12,20},{16,24},{20,28},{24,32},{28,36},{32,40... | collective-permute-start | bytes 786440 | tf_op jit(solution)/shard_map/ppermute | solution.py:15
  11.4 4.4 %collective-permute-done.1 = bf16[2,2,128,256]{3,2,1,0:T(8,128)(2,1)S(1)} collective-permute-done((bf16[2,2,128,256]{3,2,1,0:T(8,128)(2,1)S(1)}, bf16[2,2,128,256]{3,2,1,0:T(8,128)(2,1)S(1)}, u32[]{:S(2)}, u32[]{:S(2)}) %collective-permute-start.1) | collective-permute-done | bytes 262176 | tf_op jit(solution)/shard_map/ppermute | solution.py:15
  15.8 5.2 %collective-permute-start.2 = (bf16[4,2,128,256]{3,2,1,0:T(8,128)(2,1)S(1)}, bf16[4,2,128,256]{3,2,1,0:T(8,128)(2,1)S(1)}, u32[]{:S(2)}, u32[]{:S(2)}) collective-permute-start(bf16[4,2,128,256]{3,2,1,0:T(8,128)(2,1)S(1)} %pad_maximum_fusion.2), channel_id=1, source_target_pairs={{0,16},{4,20},{8,24},{12,28},{16,32},{20,36},{24,40},{28,44},{32,4... | collective-permute-start | bytes 1572872 | tf_op jit(solution)/shard_map/ppermute | solution.py:15
  22.6 7.3 %collective-permute-done.2 = bf16[4,2,128,256]{3,2,1,0:T(8,128)(2,1)S(1)} collective-permute-done((bf16[4,2,128,256]{3,2,1,0:T(8,128)(2,1)S(1)}, bf16[4,2,128,256]{3,2,1,0:T(8,128)(2,1)S(1)}, u32[]{:S(2)}, u32[]{:S(2)}) %collective-permute-start.2) | collective-permute-done | bytes 524320 | tf_op jit(solution)/shard_map/ppermute | solution.py:15
  31.0 19.5 %shard_map.129 = (f32[1024,256]{1,0:T(8,128)}, f32[1024,256]{1,0:T(8,128)}) custom-call(s32[1]{0:T(128)} %bitcast.1.pos_ref, bf16[512,1024]{1,0:T(8,128)(2,1)} %q_ref.1, bf16[512,1024]{1,0:T(8,128)(2,1)} %do_ref.1, bf16[1024,256]{1,0:T(8,128)(2,1)} %bitcast.124, bf16[1024,256]{1,0:T(8,128)(2,1)} %bitcast.123), custom_call_target="tpu_custom_call" | custom-call | tf_op jit(solution)/shard_map/pallas_call | solution.py:108
  54.2 13.6 %collective-permute-done.3 = bf16[4,2,128,256]{3,2,1,0:T(8,128)(2,1)} collective-permute-done((bf16[4,2,128,256]{3,2,1,0:T(8,128)(2,1)}, bf16[4,2,128,256]{3,2,1,0:T(8,128)(2,1)}, u32[]{:S(2)}, u32[]{:S(2)}) %collective-permute-start.3) | collective-permute-done | bytes 524320 | tf_op jit(solution)/shard_map/ppermute | solution.py:15
  70.4 10.2 %collective-permute-done.4 = f32[2,2,128,256]{3,2,1,0:T(8,128)S(1)} collective-permute-done((f32[2,2,128,256]{3,2,1,0:T(8,128)S(1)}, f32[2,2,128,256]{3,2,1,0:T(8,128)S(1)}, u32[]{:S(2)}, u32[]{:S(2)}) %collective-permute-start.4) | collective-permute-done | bytes 524320 | tf_op jit(solution)/shard_map/ppermute | solution.py:15
  80.7 6.6 %collective-permute-start.5 = (f32[1,2,128,256]{3,2,1,0:T(8,128)S(1)}, f32[1,2,128,256]{3,2,1,0:T(8,128)S(1)}, u32[]{:S(2)}, u32[]{:S(2)}) collective-permute-start(f32[1,2,128,256]{3,2,1,0:T(8,128)S(1)} %slice.86), channel_id=1, source_target_pairs={{4,0},{8,4},{12,8},{16,12},{20,16},{24,20},{28,24},{32,28},{36,32}... | collective-permute-start | bytes 786440 | tf_op jit(solution)/shard_map/ppermute | solution.py:15
  87.4 5.6 %collective-permute-done.5 = f32[1,2,128,256]{3,2,1,0:T(8,128)S(1)} collective-permute-done((f32[1,2,128,256]{3,2,1,0:T(8,128)S(1)}, f32[1,2,128,256]{3,2,1,0:T(8,128)S(1)}, u32[]{:S(2)}, u32[]{:S(2)}) %collective-permute-start.5) | collective-permute-done | bytes 262176 | tf_op jit(solution)/shard_map/ppermute | solution.py:15
  97.3 2.5 %collective-permute-start.7 = (f32[1,128,64]{1,2,0:T(8,128)S(1)}, f32[1,128,64]{1,2,0:T(8,128)S(1)}, u32[]{:S(2)}, u32[]{:S(2)}) collective-permute-start(f32[1,128,64]{1,2,0:T(8,128)S(1)} %get-tuple-element.34), channel_id=1, source_target_pairs={{0,2},{1,3},{2,0},{3,1},{4,6},{5,7},{6,4},{7,5},{8,10},{9,11},{10,... | collective-permute-start | bytes 98312 | tf_op jit(solution)/shard_map/ppermute | solution.py:30
  101.5 2.2 %collective-permute-done.8 = f32[1,128,64]{1,2,0:T(8,128)S(1)} collective-permute-done((f32[1,128,64]{1,2,0:T(8,128)S(1)}, f32[1,128,64]{1,2,0:T(8,128)S(1)}, u32[]{:S(2)}, u32[]{:S(2)}) %collective-permute-start.8) | collective-permute-done | bytes 32800 | tf_op jit(solution)/shard_map/ppermute | solution.py:30
  114.3 3.4 %collective-permute-done.10 = bf16[16,5120]{1,0:T(8,128)(2,1)S(1)} collective-permute-done((bf16[16,5120]{1,0:T(8,128)(2,1)S(1)}, bf16[16,5120]{1,0:T(8,128)(2,1)S(1)}, u32[]{:S(2)}, u32[]{:S(2)}) %collective-permute-start.10) | collective-permute-done | bytes 163872 | tf_op jit(solution)/shard_map/ppermute | solution.py:30
  117.7 3.5 %collective-permute-done.11 = bf16[16,5120]{1,0:T(8,128)(2,1)S(1)} collective-permute-done((bf16[16,5120]{1,0:T(8,128)(2,1)S(1)}, bf16[16,5120]{1,0:T(8,128)(2,1)S(1)}, u32[]{:S(2)}, u32[]{:S(2)}) %collective-permute-start.11) | collective-permute-done | bytes 163872 | tf_op jit(solution)/shard_map/ppermute | solution.py:30
  121.7 5.3 %collective-permute-start.12 = (f32[4,5120]{1,0:T(4,128)S(1)}, f32[4,5120]{1,0:T(4,128)S(1)}, u32[]{:S(2)}, u32[]{:S(2)}) collective-permute-start(f32[4,5120]{1,0:T(4,128)S(1)} %bitcast.130), channel_id=1, source_target_pairs={{0,16},{4,20},{8,24},{12,28},{16,0},{20,4},{24,8},{28,12},{32,48},... | collective-permute-start | bytes 245768 | tf_op jit(solution)/shard_map/ppermute | solution.py:30
  130.9 3.7 %collective-permute-done.14 = f32[4,5120]{1,0:T(4,128)S(1)} collective-permute-done((f32[4,5120]{1,0:T(4,128)S(1)}, f32[4,5120]{1,0:T(4,128)S(1)}, u32[]{:S(2)}, u32[]{:S(2)}) %collective-permute-start.14) | collective-permute-done | bytes 81952 | tf_op jit(solution)/shard_map/ppermute | solution.py:30
  134.7 7.9 %collective-permute-start.15 = (f32[1,5120]{1,0:T(1,128)S(1)}, f32[1,5120]{1,0:T(1,128)S(1)}, u32[]{:S(2)}, u32[]{:S(2)}) collective-permute-start(f32[1,5120]{1,0:T(1,128)S(1)} %get-tuple-element.36), channel_id=1, source_target_pairs={{0,64},{4,68},{8,72},{12,76},{16,80},{20,84},{24,88},{28,92},{32,9... | collective-permute-start | bytes 61448 | tf_op jit(solution)/shard_map/ppermute | solution.py:30
  142.6 3.4 %collective-permute-start.17 = (f32[1,5120]{1,0:T(1,128)S(1)}, f32[1,5120]{1,0:T(1,128)S(1)}, u32[]{:S(2)}, u32[]{:S(2)}) collective-permute-start(f32[1,5120]{1,0:T(1,128)S(1)} %get-tuple-element.37), channel_id=1, source_target_pairs={{0,192},{4,196},{8,200},{12,204},{16,208},{20,212},{24,216},{28,22... | collective-permute-start | bytes 61448 | tf_op jit(solution)/shard_map/ppermute | solution.py:30
  146.1 3.2 %collective-permute-done.16 = f32[1,5120]{1,0:T(1,128)S(1)} collective-permute-done((f32[1,5120]{1,0:T(1,128)S(1)}, f32[1,5120]{1,0:T(1,128)S(1)}, u32[]{:S(2)}, u32[]{:S(2)}) %collective-permute-start.16) | collective-permute-done | bytes 20512 | tf_op jit(solution)/shard_map/ppermute | solution.py:30
  149.8 3.2 %collective-permute-start.22 = (f32[1,1024]{1,0:T(1,128)S(1)}, f32[1,1024]{1,0:T(1,128)S(1)}, u32[]{:S(2)}, u32[]{:S(2)}) collective-permute-start(f32[1,1024]{1,0:T(1,128)S(1)} %get-tuple-element.40), channel_id=1, source_target_pairs={{0,128},{4,132},{8,136},{12,140},{16,144},{20,148},{24,152},{28,15... | collective-permute-start | bytes 12296 | tf_op jit(solution)/shard_map/ppermute | solution.py:30
  152.9 2.1 %collective-permute-start.23 = (f32[1,1024]{1,0:T(1,128)S(1)}, f32[1,1024]{1,0:T(1,128)S(1)}, u32[]{:S(2)}, u32[]{:S(2)}) collective-permute-start(f32[1,1024]{1,0:T(1,128)S(1)} %get-tuple-element.40), channel_id=1, source_target_pairs={{0,192},{4,196},{8,200},{12,204},{16,208},{20,212},{24,216},{28,22... | collective-permute-start | bytes 12296 | tf_op jit(solution)/shard_map/ppermute | solution.py:30
  156.9 2.5 %collective-permute-start.20 = (f32[1,64,2,32]{1,3,2,0:T(8,128)S(1)}, f32[1,64,2,32]{1,3,2,0:T(8,128)S(1)}, u32[]{:S(2)}, u32[]{:S(2)}) collective-permute-start(f32[1,64,2,32]{1,3,2,0:T(8,128)S(1)} %copy.54), channel_id=1, source_target_pairs={{0,3},{1,2},{2,1},{3,0},{4,7},{5,6},{6,5},{7,4},{8,11},{9,10},{10,... | collective-permute-start | bytes 49160 | tf_op jit(solution)/shard_map/ppermute | solution.py:30
  162.0 2.4 %collective-permute-start.26 = (f32[4,1024]{1,0:T(4,128)S(1)}, f32[4,1024]{1,0:T(4,128)S(1)}, u32[]{:S(2)}, u32[]{:S(2)}) collective-permute-start(f32[4,1024]{1,0:T(4,128)S(1)} %broadcast_select_fusion.2), channel_id=1, source_target_pairs={{0,48},{4,52},{8,56},{12,60},{16,32},{20,36},{24,40},{28,44},{32,1... | collective-permute-start | bytes 49160 | tf_op jit(solution)/shard_map/ppermute | solution.py:30
  167.8 6.4 %collective-permute-start.27 = (f32[16,1024]{1,0:T(8,128)S(1)}, f32[16,1024]{1,0:T(8,128)S(1)}, u32[]{:S(2)}, u32[]{:S(2)}) collective-permute-start(f32[16,1024]{1,0:T(8,128)S(1)} %broadcast_select_fusion), channel_id=1, source_target_pairs={{0,4},{4,0},{8,12},{12,8},{16,20},{20,16},{24,28},{28,24},{32,36},... | collective-permute-start | bytes 196616 | tf_op jit(solution)/shard_map/ppermute | solution.py:30
  (135 shorter events, 48.2 us)
Async XLA Ops:
  1.6 6.5 %collective-permute-start = (bf16[1,2,128,256]{3,2,1,0:T(8,128)(2,1)S(1)}, bf16[1,2,128,256]{3,2,1,0:T(8,128)(2,1)S(1)}, u32[]{:S(2)}, u32[]{:S(2)}) collective-permute-start(bf16[1,2,128,256]{3,2,1,0:T(8,128)(2,1)S(1)} %maximum_bitcast_fusion), channel_id=1, source_target_pairs={{0,4},{4,8},{8,12},{12,16},{16,20},{20,24},{24,28},{28,32},{32,36}... | collective-permute-start | bytes 393224 | tf_op jit(solution)/shard_map/ppermute | solution.py:15
  8.2 7.6 %collective-permute-start.1 = (bf16[2,2,128,256]{3,2,1,0:T(8,128)(2,1)S(1)}, bf16[2,2,128,256]{3,2,1,0:T(8,128)(2,1)S(1)}, u32[]{:S(2)}, u32[]{:S(2)}) collective-permute-start(bf16[2,2,128,256]{3,2,1,0:T(8,128)(2,1)S(1)} %pad_maximum_fusion.3), channel_id=1, source_target_pairs={{0,8},{4,12},{8,16},{12,20},{16,24},{20,28},{24,32},{28,36},{32,40... | collective-permute-start | bytes 786440 | tf_op jit(solution)/shard_map/ppermute | solution.py:15
  15.8 14.0 %collective-permute-start.2 = (bf16[4,2,128,256]{3,2,1,0:T(8,128)(2,1)S(1)}, bf16[4,2,128,256]{3,2,1,0:T(8,128)(2,1)S(1)}, u32[]{:S(2)}, u32[]{:S(2)}) collective-permute-start(bf16[4,2,128,256]{3,2,1,0:T(8,128)(2,1)S(1)} %pad_maximum_fusion.2), channel_id=1, source_target_pairs={{0,16},{4,20},{8,24},{12,28},{16,32},{20,36},{24,40},{28,44},{32,4... | collective-permute-start | bytes 1572872 | tf_op jit(solution)/shard_map/ppermute | solution.py:15
  52.9 14.9 %collective-permute-start.3 = (bf16[4,2,128,256]{3,2,1,0:T(8,128)(2,1)}, bf16[4,2,128,256]{3,2,1,0:T(8,128)(2,1)}, u32[]{:S(2)}, u32[]{:S(2)}) collective-permute-start(bf16[4,2,128,256]{3,2,1,0:T(8,128)(2,1)} %fusion.2), channel_id=1, source_target_pairs={{16,0},{20,4},{24,8},{28,12},{32,16},{36,20},{40,24},{44,28},{48,3... | collective-permute-start | bytes 1572872 | tf_op jit(solution)/shard_map/ppermute | solution.py:15
  69.0 11.5 %collective-permute-start.4 = (f32[2,2,128,256]{3,2,1,0:T(8,128)S(1)}, f32[2,2,128,256]{3,2,1,0:T(8,128)S(1)}, u32[]{:S(2)}, u32[]{:S(2)}) collective-permute-start(f32[2,2,128,256]{3,2,1,0:T(8,128)S(1)} %slice.84), channel_id=1, source_target_pairs={{8,0},{12,4},{16,8},{20,12},{24,16},{28,20},{32,24},{36,28},{40,32... | collective-permute-start | bytes 1572872 | tf_op jit(solution)/shard_map/ppermute | solution.py:15
  80.7 12.3 %collective-permute-start.5 = (f32[1,2,128,256]{3,2,1,0:T(8,128)S(1)}, f32[1,2,128,256]{3,2,1,0:T(8,128)S(1)}, u32[]{:S(2)}, u32[]{:S(2)}) collective-permute-start(f32[1,2,128,256]{3,2,1,0:T(8,128)S(1)} %slice.86), channel_id=1, source_target_pairs={{4,0},{8,4},{12,8},{16,12},{20,16},{24,20},{28,24},{32,28},{36,32}... | collective-permute-start | bytes 786440 | tf_op jit(solution)/shard_map/ppermute | solution.py:15
  111.1 6.6 %collective-permute-start.10 = (bf16[16,5120]{1,0:T(8,128)(2,1)S(1)}, bf16[16,5120]{1,0:T(8,128)(2,1)S(1)}, u32[]{:S(2)}, u32[]{:S(2)}) collective-permute-start(bf16[16,5120]{1,0:T(8,128)(2,1)S(1)} %bitcast.127), channel_id=1, source_target_pairs={{0,8},{4,12},{8,0},{12,4},{16,24},{20,28},{24,16},{28,20},{32,40},... | collective-permute-start | bytes 491528 | tf_op jit(solution)/shard_map/ppermute | solution.py:30
  113.1 8.1 %collective-permute-start.11 = (bf16[16,5120]{1,0:T(8,128)(2,1)S(1)}, bf16[16,5120]{1,0:T(8,128)(2,1)S(1)}, u32[]{:S(2)}, u32[]{:S(2)}) collective-permute-start(bf16[16,5120]{1,0:T(8,128)(2,1)S(1)} %bitcast.128), channel_id=1, source_target_pairs={{0,12},{4,8},{8,4},{12,0},{16,28},{20,24},{24,20},{28,16},{32,44},... | collective-permute-start | bytes 491528 | tf_op jit(solution)/shard_map/ppermute | solution.py:30
  113.3 7.9 %collective-permute-start.9 = (bf16[16,5120]{1,0:T(8,128)(2,1)S(1)}, bf16[16,5120]{1,0:T(8,128)(2,1)S(1)}, u32[]{:S(2)}, u32[]{:S(2)}) collective-permute-start(bf16[16,5120]{1,0:T(8,128)(2,1)S(1)} %bitcast.129), channel_id=1, source_target_pairs={{0,4},{4,0},{8,12},{12,8},{16,20},{20,16},{24,28},{28,24},{32,36},... | collective-permute-start | bytes 491528 | tf_op jit(solution)/shard_map/ppermute | solution.py:30
  121.7 7.8 %collective-permute-start.12 = (f32[4,5120]{1,0:T(4,128)S(1)}, f32[4,5120]{1,0:T(4,128)S(1)}, u32[]{:S(2)}, u32[]{:S(2)}) collective-permute-start(f32[4,5120]{1,0:T(4,128)S(1)} %bitcast.130), channel_id=1, source_target_pairs={{0,16},{4,20},{8,24},{12,28},{16,0},{20,4},{24,8},{28,12},{32,48},... | collective-permute-start | bytes 245768 | tf_op jit(solution)/shard_map/ppermute | solution.py:30
  128.8 5.8 %collective-permute-start.14 = (f32[4,5120]{1,0:T(4,128)S(1)}, f32[4,5120]{1,0:T(4,128)S(1)}, u32[]{:S(2)}, u32[]{:S(2)}) collective-permute-start(f32[4,5120]{1,0:T(4,128)S(1)} %bitcast.132), channel_id=1, source_target_pairs={{0,48},{4,52},{8,56},{12,60},{16,32},{20,36},{24,40},{28,44},{32,1... | collective-permute-start | bytes 245768 | tf_op jit(solution)/shard_map/ppermute | solution.py:30
  134.7 11.4 %collective-permute-start.15 = (f32[1,5120]{1,0:T(1,128)S(1)}, f32[1,5120]{1,0:T(1,128)S(1)}, u32[]{:S(2)}, u32[]{:S(2)}) collective-permute-start(f32[1,5120]{1,0:T(1,128)S(1)} %get-tuple-element.36), channel_id=1, source_target_pairs={{0,64},{4,68},{8,72},{12,76},{16,80},{20,84},{24,88},{28,92},{32,9... | collective-permute-start | bytes 61448 | tf_op jit(solution)/shard_map/ppermute | solution.py:30
  142.6 6.7 %collective-permute-start.16 = (f32[1,5120]{1,0:T(1,128)S(1)}, f32[1,5120]{1,0:T(1,128)S(1)}, u32[]{:S(2)}, u32[]{:S(2)}) collective-permute-start(f32[1,5120]{1,0:T(1,128)S(1)} %get-tuple-element.38), channel_id=1, source_target_pairs={{0,128},{4,132},{8,136},{12,140},{16,144},{20,148},{24,152},{28,15... | collective-permute-start | bytes 61448 | tf_op jit(solution)/shard_map/ppermute | solution.py:30
  142.6 6.7 %collective-permute-start.17 = (f32[1,5120]{1,0:T(1,128)S(1)}, f32[1,5120]{1,0:T(1,128)S(1)}, u32[]{:S(2)}, u32[]{:S(2)}) collective-permute-start(f32[1,5120]{1,0:T(1,128)S(1)} %get-tuple-element.37), channel_id=1, source_target_pairs={{0,192},{4,196},{8,200},{12,204},{16,208},{20,212},{24,216},{28,22... | collective-permute-start | bytes 61448 | tf_op jit(solution)/shard_map/ppermute | solution.py:30
  149.3 7.6 %collective-permute-start.21 = (f32[1,1024]{1,0:T(1,128)S(1)}, f32[1,1024]{1,0:T(1,128)S(1)}, u32[]{:S(2)}, u32[]{:S(2)}) collective-permute-start(f32[1,1024]{1,0:T(1,128)S(1)} %get-tuple-element.40), channel_id=1, source_target_pairs={{0,64},{4,68},{8,72},{12,76},{16,80},{20,84},{24,88},{28,92},{32,9... | collective-permute-start | bytes 12296 | tf_op jit(solution)/shard_map/ppermute | solution.py:30
  149.8 9.7 %collective-permute-start.22 = (f32[1,1024]{1,0:T(1,128)S(1)}, f32[1,1024]{1,0:T(1,128)S(1)}, u32[]{:S(2)}, u32[]{:S(2)}) collective-permute-start(f32[1,1024]{1,0:T(1,128)S(1)} %get-tuple-element.40), channel_id=1, source_target_pairs={{0,128},{4,132},{8,136},{12,140},{16,144},{20,148},{24,152},{28,15... | collective-permute-start | bytes 12296 | tf_op jit(solution)/shard_map/ppermute | solution.py:30
  152.9 6.5 %collective-permute-start.23 = (f32[1,1024]{1,0:T(1,128)S(1)}, f32[1,1024]{1,0:T(1,128)S(1)}, u32[]{:S(2)}, u32[]{:S(2)}) collective-permute-start(f32[1,1024]{1,0:T(1,128)S(1)} %get-tuple-element.40), channel_id=1, source_target_pairs={{0,192},{4,196},{8,200},{12,204},{16,208},{20,212},{24,216},{28,22... | collective-permute-start | bytes 12296 | tf_op jit(solution)/shard_map/ppermute | solution.py:30
  155.3 6.7 %collective-permute-start.18 = (f32[1,64,2,32]{1,3,2,0:T(8,128)S(1)}, f32[1,64,2,32]{1,3,2,0:T(8,128)S(1)}, u32[]{:S(2)}, u32[]{:S(2)}) collective-permute-start(f32[1,64,2,32]{1,3,2,0:T(8,128)S(1)} %copy.54), channel_id=1, source_target_pairs={{0,1},{1,0},{2,3},{3,2},{4,5},{5,4},{6,7},{7,6},{8,9},{9,8},{10,11... | collective-permute-start | bytes 49160 | tf_op jit(solution)/shard_map/ppermute | solution.py:30
  155.4 9.0 %collective-permute-start.19 = (f32[1,64,2,32]{1,3,2,0:T(8,128)S(1)}, f32[1,64,2,32]{1,3,2,0:T(8,128)S(1)}, u32[]{:S(2)}, u32[]{:S(2)}) collective-permute-start(f32[1,64,2,32]{1,3,2,0:T(8,128)S(1)} %copy.54), channel_id=1, source_target_pairs={{0,2},{1,3},{2,0},{3,1},{4,6},{5,7},{6,4},{7,5},{8,10},{9,11},{10,... | collective-permute-start | bytes 49160 | tf_op jit(solution)/shard_map/ppermute | solution.py:30
  156.9 7.4 %collective-permute-start.20 = (f32[1,64,2,32]{1,3,2,0:T(8,128)S(1)}, f32[1,64,2,32]{1,3,2,0:T(8,128)S(1)}, u32[]{:S(2)}, u32[]{:S(2)}) collective-permute-start(f32[1,64,2,32]{1,3,2,0:T(8,128)S(1)} %copy.54), channel_id=1, source_target_pairs={{0,3},{1,2},{2,1},{3,0},{4,7},{5,6},{6,5},{7,4},{8,11},{9,10},{10,... | collective-permute-start | bytes 49160 | tf_op jit(solution)/shard_map/ppermute | solution.py:30
  160.2 6.3 %collective-permute-start.24 = (f32[4,1024]{1,0:T(4,128)S(1)}, f32[4,1024]{1,0:T(4,128)S(1)}, u32[]{:S(2)}, u32[]{:S(2)}) collective-permute-start(f32[4,1024]{1,0:T(4,128)S(1)} %broadcast_select_fusion.2), channel_id=1, source_target_pairs={{0,16},{4,20},{8,24},{12,28},{16,0},{20,4},{24,8},{28,12},{32,48},... | collective-permute-start | bytes 49160 | tf_op jit(solution)/shard_map/ppermute | solution.py:30
  161.2 5.3 %collective-permute-start.25 = (f32[4,1024]{1,0:T(4,128)S(1)}, f32[4,1024]{1,0:T(4,128)S(1)}, u32[]{:S(2)}, u32[]{:S(2)}) collective-permute-start(f32[4,1024]{1,0:T(4,128)S(1)} %broadcast_select_fusion.2), channel_id=1, source_target_pairs={{0,32},{4,36},{8,40},{12,44},{16,48},{20,52},{24,56},{28,60},{32,0... | collective-permute-start | bytes 49160 | tf_op jit(solution)/shard_map/ppermute | solution.py:30
  167.8 8.2 %collective-permute-start.27 = (f32[16,1024]{1,0:T(8,128)S(1)}, f32[16,1024]{1,0:T(8,128)S(1)}, u32[]{:S(2)}, u32[]{:S(2)}) collective-permute-start(f32[16,1024]{1,0:T(8,128)S(1)} %broadcast_select_fusion), channel_id=1, source_target_pairs={{0,4},{4,0},{8,12},{12,8},{16,20},{20,16},{24,28},{28,24},{32,36},... | collective-permute-start | bytes 196616 | tf_op jit(solution)/shard_map/ppermute | solution.py:30
  174.2 5.2 %collective-permute-start.29 = (f32[16,1024]{1,0:T(8,128)S(1)}, f32[16,1024]{1,0:T(8,128)S(1)}, u32[]{:S(2)}, u32[]{:S(2)}) collective-permute-start(f32[16,1024]{1,0:T(8,128)S(1)} %broadcast_select_fusion), channel_id=1, source_target_pairs={{0,12},{4,8},{8,4},{12,0},{16,28},{20,24},{24,20},{28,16},{32,44},... | collective-permute-start | bytes 196616 | tf_op jit(solution)/shard_map/ppermute | solution.py:30
  (12 other events, 165.7 us)

commit v10 on v9

--- a/solution.py
+++ b/solution.py
@@ -42,6 +42,44 @@
                 give = give.astype(first_kind)
             x = x + xor_partner(give, axis, t * low).astype(x.dtype)
     return x[0]
+
+
+def wide_sums(parted, whole, axis):
+    me = lax.axis_index(axis)
+    steps = digit_steps(lax.axis_size(axis))
+    low, radix = steps[0]
+    split = parted.shape[1]
+    x = jnp.concatenate([parted, whole], 1)
+    group = x.reshape(x.shape[0] // radix, radix, *x.shape[1:])
+    first = (me // low) % radix
+    x = lax.dynamic_index_in_dim(group, first, axis=1, keepdims=False)
+    for t in range(1, radix):
+        give = lax.dynamic_index_in_dim(group, jnp.bitwise_xor(first, t), axis=1, keepdims=False)
+        x = x + xor_partner(give.astype(jnp.bfloat16), axis, t * low).astype(x.dtype)
+    parted = x[:, :split]
+    whole = x[:, split:]
+    for low, radix in steps[1:]:
+        group = parted.reshape(parted.shape[0] // radix, radix, *parted.shape[1:])
+        mine = (me // low) % radix
+        parted = lax.dynamic_index_in_dim(group, mine, axis=1, keepdims=False)
+        size = parted.size
+        wholes = [whole]
+        for t in range(1, radix):
+            give = lax.dynamic_index_in_dim(group, jnp.bitwise_xor(mine, t), axis=1, keepdims=False)
+            back = xor_partner(jnp.concatenate([give.reshape(-1), whole.reshape(-1)]), axis, t * low)
+            parted = parted + back[:size].reshape(parted.shape)
+            wholes.append(back[size:].reshape(whole.shape))
+        order = jnp.bitwise_xor(jnp.arange(radix, dtype=mine.dtype), mine)
+        ranked = jnp.take(jnp.stack(wholes), order, axis=0)
+        whole = ranked[0]
+        for d in range(1, radix):
+            whole = whole + ranked[d]
+    low, radix = steps[0]
+    got = [whole] + [xor_partner(whole, axis, t * low) for t in range(1, radix)]
+    order = jnp.bitwise_xor(jnp.arange(radix, dtype=first.dtype), first)
+    whole = jnp.take(jnp.stack(got, 1), order, axis=1)
+    whole = whole.reshape(whole.shape[0] * radix, *whole.shape[2:])
+    return parted[0], whole
 
 
 def gathered(y, axis):
@@ -174,10 +212,9 @@
     down = jnp.dot(enc_rows.T, h_both, preferred_element_type=jnp.float32)
     width = down.shape[0] // wide_count
     up_both = jnp.stack([up_key, up_value]).reshape(wide_count, -1)
-    joined = jnp.concatenate([down.reshape(wide_count, width * 2 * piece), up_both], 1)
-    joined = scattered_sum(joined, "wide", jnp.bfloat16)
-    down = joined[: width * 2 * piece].reshape(width, 2, piece)
-    up_both = gathered(joined[width * 2 * piece :], "wide").reshape(2, rank, cols)
+    down, up_both = wide_sums(down.reshape(wide_count, width * 2 * piece), up_both, "wide")
+    down = down.reshape(width, 2, piece)
+    up_both = up_both.reshape(2, rank, cols)
     down = gathered(down, "narrow").transpose(1, 2, 0, 3).reshape(width, 2, rank)
     return (down[:, 0], down[:, 1], up_both[0], up_both[1])
 

time: 182 us -> 169 us (0.929)
  starting transfers between devices: 69.2 us -> 56.3 us
  local copies, waits for them, and re-layouts: 14.5 us -> 16.9 us
  other arithmetic: 6.33 us -> 4.5 us
    ppermute x24 -> x18, starting transfers between devices: 47.1 us -> 34.8 us  [xor_partner(): return lax.ppermute(array, axis, [(i, i ^ mask) for i in range(devices)])]
    ppermute x24 -> x18, waiting for transfers between devices: 23.4 us -> 22.1 us  [xor_partner(): return lax.ppermute(array, axis, [(i, i ^ mask) for i in range(devices)])]
  transfers between devices with their start and end apart: 30 -> 24, of which waited for: 17 -> 15; matrix products, arithmetic and copies ran while one was open for 3% -> 3% of each run, Pallas kernels for 0% -> 0%
where the time goes in v10:
time: 169 us
  waiting for transfers between devices  65.4 us (39%)
  starting transfers between devices  56.3 us (33%)
  Pallas kernels  19.5 us (12%)
  local copies, waits for them, and re-layouts  16.9 us (10%)
  other arithmetic  4.5 us (3%)
  matrix products  4.08 us (2%)
  between operations  2.18 us (1%)
    ppermute x6, waiting for transfers between devices, passed_along(): return lax.ppermute(array, axis, pairs)  43.3 us
    ppermute x18, starting transfers between devices, xor_partner(): return lax.ppermute(array, axis, [(i, i ^ mask) for i in range(devices)])  34.8 us
    ppermute x18, waiting for transfers between devices, xor_partner(): return lax.ppermute(array, axis, [(i, i ^ mask) for i in range(devices)])  22.1 us
    ppermute x6, starting transfers between devices, passed_along(): return lax.ppermute(array, axis, pairs)  21.4 us
    pallas_call x1, Pallas kernels, attention_grads(): pl.pallas_call(attention_body, grid_spec=grid_spec, out_shape=[jax.ShapeD...  19.5 us
  transfers between devices with their start and end apart: 24, of which 15 were waited for; matrix products, arithmetic and copies ran while one was open for 3% of the time, Pallas kernels for 0%

profile of v10, /device:TPU:1, one launch (start us, length us, event | category | flops | bytes accessed | tf_op | source)
XLA Modules:
  0.0 168.8 jit_solution(12472333063960920088)
XLA Ops:
  1.6 4.6 %collective-permute-start = (bf16[1,2,128,256]{3,2,1,0:T(8,128)(2,1)S(1)}, bf16[1,2,128,256]{3,2,1,0:T(8,128)(2,1)S(1)}, u32[]{:S(2)}, u32[]{:S(2)}) collective-permute-start(bf16[1,2,128,256]{3,2,1,0:T(8,128)(2,1)S(1)} %maximum_bitcast_fusion), channel_id=1, source_target_pairs={{0,4},{4,8},{8,12},{12,16},{16,20},{20,24},{24,28},{28,32},{32,36}... | collective-permute-start | bytes 393224 | tf_op jit(solution)/shard_map/ppermute | solution.py:15
  8.2 3.2 %collective-permute-start.1 = (bf16[2,2,128,256]{3,2,1,0:T(8,128)(2,1)S(1)}, bf16[2,2,128,256]{3,2,1,0:T(8,128)(2,1)S(1)}, u32[]{:S(2)}, u32[]{:S(2)}) collective-permute-start(bf16[2,2,128,256]{3,2,1,0:T(8,128)(2,1)S(1)} %pad_maximum_fusion.3), channel_id=1, source_target_pairs={{0,8},{4,12},{8,16},{12,20},{16,24},{20,28},{24,32},{28,36},{32,40... | collective-permute-start | bytes 786440 | tf_op jit(solution)/shard_map/ppermute | solution.py:15
  11.4 4.4 %collective-permute-done.1 = bf16[2,2,128,256]{3,2,1,0:T(8,128)(2,1)S(1)} collective-permute-done((bf16[2,2,128,256]{3,2,1,0:T(8,128)(2,1)S(1)}, bf16[2,2,128,256]{3,2,1,0:T(8,128)(2,1)S(1)}, u32[]{:S(2)}, u32[]{:S(2)}) %collective-permute-start.1) | collective-permute-done | bytes 262176 | tf_op jit(solution)/shard_map/ppermute | solution.py:15
  15.8 5.2 %collective-permute-start.2 = (bf16[4,2,128,256]{3,2,1,0:T(8,128)(2,1)S(1)}, bf16[4,2,128,256]{3,2,1,0:T(8,128)(2,1)S(1)}, u32[]{:S(2)}, u32[]{:S(2)}) collective-permute-start(bf16[4,2,128,256]{3,2,1,0:T(8,128)(2,1)S(1)} %pad_maximum_fusion.2), channel_id=1, source_target_pairs={{0,16},{4,20},{8,24},{12,28},{16,32},{20,36},{24,40},{28,44},{32,4... | collective-permute-start | bytes 1572872 | tf_op jit(solution)/shard_map/ppermute | solution.py:15
  22.6 7.3 %collective-permute-done.2 = bf16[4,2,128,256]{3,2,1,0:T(8,128)(2,1)S(1)} collective-permute-done((bf16[4,2,128,256]{3,2,1,0:T(8,128)(2,1)S(1)}, bf16[4,2,128,256]{3,2,1,0:T(8,128)(2,1)S(1)}, u32[]{:S(2)}, u32[]{:S(2)}) %collective-permute-start.2) | collective-permute-done | bytes 524320 | tf_op jit(solution)/shard_map/ppermute | solution.py:15
  31.0 19.5 %shard_map.129 = (f32[1024,256]{1,0:T(8,128)}, f32[1024,256]{1,0:T(8,128)}) custom-call(s32[1]{0:T(128)} %bitcast.1.pos_ref, bf16[512,1024]{1,0:T(8,128)(2,1)} %q_ref.1, bf16[512,1024]{1,0:T(8,128)(2,1)} %do_ref.1, bf16[1024,256]{1,0:T(8,128)(2,1)} %bitcast.116, bf16[1024,256]{1,0:T(8,128)(2,1)} %bitcast.115), custom_call_target="tpu_custom_call" | custom-call | tf_op jit(solution)/shard_map/pallas_call | solution.py:146
  53.4 13.3 %collective-permute-done.3 = bf16[4,2,128,256]{3,2,1,0:T(8,128)(2,1)S(1)} collective-permute-done((bf16[4,2,128,256]{3,2,1,0:T(8,128)(2,1)S(1)}, bf16[4,2,128,256]{3,2,1,0:T(8,128)(2,1)S(1)}, u32[]{:S(2)}, u32[]{:S(2)}) %collective-permute-start.3) | collective-permute-done | bytes 524320 | tf_op jit(solution)/shard_map/ppermute | solution.py:15
  68.3 11.6 %collective-permute-done.4 = f32[2,2,128,256]{3,2,1,0:T(8,128)S(1)} collective-permute-done((f32[2,2,128,256]{3,2,1,0:T(8,128)S(1)}, f32[2,2,128,256]{3,2,1,0:T(8,128)S(1)}, u32[]{:S(2)}, u32[]{:S(2)}) %collective-permute-start.4) | collective-permute-done | bytes 524320 | tf_op jit(solution)/shard_map/ppermute | solution.py:15
  80.0 5.9 %collective-permute-start.5 = (f32[1,2,128,256]{3,2,1,0:T(8,128)S(1)}, f32[1,2,128,256]{3,2,1,0:T(8,128)S(1)}, u32[]{:S(2)}, u32[]{:S(2)}) collective-permute-start(f32[1,2,128,256]{3,2,1,0:T(8,128)S(1)} %slice.284), channel_id=1, source_target_pairs={{4,0},{8,4},{12,8},{16,12},{20,16},{24,20},{28,24},{32,28},{36,32}... | collective-permute-start | bytes 786440 | tf_op jit(solution)/shard_map/ppermute | solution.py:15
  86.0 4.9 %collective-permute-done.5 = f32[1,2,128,256]{3,2,1,0:T(8,128)S(1)} collective-permute-done((f32[1,2,128,256]{3,2,1,0:T(8,128)S(1)}, f32[1,2,128,256]{3,2,1,0:T(8,128)S(1)}, u32[]{:S(2)}, u32[]{:S(2)}) %collective-permute-start.5) | collective-permute-done | bytes 262176 | tf_op jit(solution)/shard_map/ppermute | solution.py:15
  90.9 1.9 %convolution_bitcast_fusion.1 = f32[1,128,256]{2,1,0:T(8,128)S(1)} fusion(bf16[128,4096]{1,0:T(8,128)(2,1)S(1)} %copy-done, bf16[4096,128]{1,0:T(8,128)(2,1)} %param.20, bf16[1,2,128,256]{3,2,1,0:T(8,128)(2,1)S(1)} %slice_add_fusion.1), kind=kOutput, calls=%fused_computation.7 | convolution fusion | flops 142622720 | bytes 2293760 | tf_op jit(solution)/shard_map/dot_general | solution.py:211
  95.4 2.4 %collective-permute-start.7 = (f32[1,128,64]{1,2,0:T(8,128)S(1)}, f32[1,128,64]{1,2,0:T(8,128)S(1)}, u32[]{:S(2)}, u32[]{:S(2)}) collective-permute-start(f32[1,128,64]{1,2,0:T(8,128)S(1)} %get-tuple-element.45), channel_id=1, source_target_pairs={{0,2},{1,3},{2,0},{3,1},{4,6},{5,7},{6,4},{7,5},{8,10},{9,11},{10,... | collective-permute-start | bytes 98312 | tf_op jit(solution)/shard_map/ppermute | solution.py:30
  99.7 2.1 %collective-permute-done.8 = f32[1,128,64]{1,2,0:T(8,128)S(1)} collective-permute-done((f32[1,128,64]{1,2,0:T(8,128)S(1)}, f32[1,128,64]{1,2,0:T(8,128)S(1)}, u32[]{:S(2)}, u32[]{:S(2)}) %collective-permute-start.8) | collective-permute-done | bytes 32800 | tf_op jit(solution)/shard_map/ppermute | solution.py:30
  109.1 2.0 %collective-permute-start.10 = (bf16[16,5120]{1,0:T(8,128)(2,1)S(1)}, bf16[16,5120]{1,0:T(8,128)(2,1)S(1)}, u32[]{:S(2)}, u32[]{:S(2)}) collective-permute-start(bf16[16,5120]{1,0:T(8,128)(2,1)S(1)} %bitcast.123), channel_id=1, source_target_pairs={{0,8},{4,12},{8,0},{12,4},{16,24},{20,28},{24,16},{28,20},{32,40},... | collective-permute-start | bytes 491528 | tf_op jit(solution)/shard_map/ppermute | solution.py:30
  112.4 3.4 %collective-permute-done.10 = bf16[16,5120]{1,0:T(8,128)(2,1)S(1)} collective-permute-done((bf16[16,5120]{1,0:T(8,128)(2,1)S(1)}, bf16[16,5120]{1,0:T(8,128)(2,1)S(1)}, u32[]{:S(2)}, u32[]{:S(2)}) %collective-permute-start.10) | collective-permute-done | bytes 163872 | tf_op jit(solution)/shard_map/ppermute | solution.py:30
  115.7 3.5 %collective-permute-done.11 = bf16[16,5120]{1,0:T(8,128)(2,1)S(1)} collective-permute-done((bf16[16,5120]{1,0:T(8,128)(2,1)S(1)}, bf16[16,5120]{1,0:T(8,128)(2,1)S(1)}, u32[]{:S(2)}, u32[]{:S(2)}) %collective-permute-start.11) | collective-permute-done | bytes 163872 | tf_op jit(solution)/shard_map/ppermute | solution.py:30
  119.8 5.3 %collective-permute-start.12 = (f32[32768]{0:T(1024)S(1)}, f32[32768]{0:T(1024)S(1)}, u32[]{:S(2)}, u32[]{:S(2)}) collective-permute-start(f32[32768]{0:T(1024)S(1)} %get-tuple-element.55), channel_id=1, source_target_pairs={{0,16},{4,20},{8,24},{12,28},{16,0},{20,4},{24,8},{28,12},{32,48},... | collective-permute-start | bytes 393224 | tf_op jit(solution)/shard_map/ppermute | solution.py:30
  130.1 3.3 %collective-permute-done.14 = f32[32768]{0:T(1024)S(1)} collective-permute-done((f32[32768]{0:T(1024)S(1)}, f32[32768]{0:T(1024)S(1)}, u32[]{:S(2)}, u32[]{:S(2)}) %collective-permute-start.14) | collective-permute-done | bytes 131104 | tf_op jit(solution)/shard_map/ppermute | solution.py:30
  135.7 7.9 %collective-permute-start.15 = (f32[20480]{0:T(1024)S(1)}, f32[20480]{0:T(1024)S(1)}, u32[]{:S(2)}, u32[]{:S(2)}) collective-permute-start(f32[20480]{0:T(1024)S(1)} %get-tuple-element.47), channel_id=1, source_target_pairs={{0,64},{4,68},{8,72},{12,76},{16,80},{20,84},{24,88},{28,92},{32,9... | collective-permute-start | bytes 245768 | tf_op jit(solution)/shard_map/ppermute | solution.py:30
  143.7 3.3 %collective-permute-start.17 = (f32[20480]{0:T(1024)S(1)}, f32[20480]{0:T(1024)S(1)}, u32[]{:S(2)}, u32[]{:S(2)}) collective-permute-start(f32[20480]{0:T(1024)S(1)} %get-tuple-element.49), channel_id=1, source_target_pairs={{0,192},{4,196},{8,200},{12,204},{16,208},{20,212},{24,216},{28,22... | collective-permute-start | bytes 245768 | tf_op jit(solution)/shard_map/ppermute | solution.py:30
  147.5 4.3 %collective-permute-done.16 = f32[20480]{0:T(1024)S(1)} collective-permute-done((f32[20480]{0:T(1024)S(1)}, f32[20480]{0:T(1024)S(1)}, u32[]{:S(2)}, u32[]{:S(2)}) %collective-permute-start.16) | collective-permute-done | bytes 81952 | tf_op jit(solution)/shard_map/ppermute | solution.py:30
  152.5 3.2 %collective-permute-start.21 = (f32[16,1024]{1,0:T(8,128)S(1)}, f32[16,1024]{1,0:T(8,128)S(1)}, u32[]{:S(2)}, u32[]{:S(2)}) collective-permute-start(f32[16,1024]{1,0:T(8,128)S(1)} %fusion.40), channel_id=1, source_target_pairs={{0,4},{4,0},{8,12},{12,8},{16,20},{20,16},{24,28},{28,24},{32,36},... | collective-permute-start | bytes 196616 | tf_op jit(solution)/shard_map/ppermute | solution.py:30
  158.8 2.1 %collective-permute-start.20 = (f32[1,64,2,32]{1,3,2,0:T(8,128)S(1)}, f32[1,64,2,32]{1,3,2,0:T(8,128)S(1)}, u32[]{:S(2)}, u32[]{:S(2)}) collective-permute-start(f32[1,64,2,32]{1,3,2,0:T(8,128)S(1)} %add_add_fusion), channel_id=1, source_target_pairs={{0,3},{1,2},{2,1},{3,0},{4,7},{5,6},{6,5},{7,4},{8,11},{9,10},{10,... | collective-permute-start | bytes 49160 | tf_op jit(solution)/shard_map/ppermute | solution.py:30
  161.2 2.4 %collective-permute-start.23 = (f32[16,1024]{1,0:T(8,128)S(1)}, f32[16,1024]{1,0:T(8,128)S(1)}, u32[]{:S(2)}, u32[]{:S(2)}) collective-permute-start(f32[16,1024]{1,0:T(8,128)S(1)} %fusion.40), channel_id=1, source_target_pairs={{0,12},{4,8},{8,4},{12,0},{16,28},{20,24},{24,20},{28,16},{32,44},... | collective-permute-start | bytes 196616 | tf_op jit(solution)/shard_map/ppermute | solution.py:30
  (152 shorter events, 39.8 us)
Async XLA Ops:
  1.6 6.5 %collective-permute-start = (bf16[1,2,128,256]{3,2,1,0:T(8,128)(2,1)S(1)}, bf16[1,2,128,256]{3,2,1,0:T(8,128)(2,1)S(1)}, u32[]{:S(2)}, u32[]{:S(2)}) collective-permute-start(bf16[1,2,128,256]{3,2,1,0:T(8,128)(2,1)S(1)} %maximum_bitcast_fusion), channel_id=1, source_target_pairs={{0,4},{4,8},{8,12},{12,16},{16,20},{20,24},{24,28},{28,32},{32,36}... | collective-permute-start | bytes 393224 | tf_op jit(solution)/shard_map/ppermute | solution.py:15
  8.2 7.6 %collective-permute-start.1 = (bf16[2,2,128,256]{3,2,1,0:T(8,128)(2,1)S(1)}, bf16[2,2,128,256]{3,2,1,0:T(8,128)(2,1)S(1)}, u32[]{:S(2)}, u32[]{:S(2)}) collective-permute-start(bf16[2,2,128,256]{3,2,1,0:T(8,128)(2,1)S(1)} %pad_maximum_fusion.3), channel_id=1, source_target_pairs={{0,8},{4,12},{8,16},{12,20},{16,24},{20,28},{24,32},{28,36},{32,40... | collective-permute-start | bytes 786440 | tf_op jit(solution)/shard_map/ppermute | solution.py:15
  15.8 14.0 %collective-permute-start.2 = (bf16[4,2,128,256]{3,2,1,0:T(8,128)(2,1)S(1)}, bf16[4,2,128,256]{3,2,1,0:T(8,128)(2,1)S(1)}, u32[]{:S(2)}, u32[]{:S(2)}) collective-permute-start(bf16[4,2,128,256]{3,2,1,0:T(8,128)(2,1)S(1)} %pad_maximum_fusion.2), channel_id=1, source_target_pairs={{0,16},{4,20},{8,24},{12,28},{16,32},{20,36},{24,40},{28,44},{32,4... | collective-permute-start | bytes 1572872 | tf_op jit(solution)/shard_map/ppermute | solution.py:15
  52.1 14.6 %collective-permute-start.3 = (bf16[4,2,128,256]{3,2,1,0:T(8,128)(2,1)S(1)}, bf16[4,2,128,256]{3,2,1,0:T(8,128)(2,1)S(1)}, u32[]{:S(2)}, u32[]{:S(2)}) collective-permute-start(bf16[4,2,128,256]{3,2,1,0:T(8,128)(2,1)S(1)} %fusion.2), channel_id=1, source_target_pairs={{16,0},{20,4},{24,8},{28,12},{32,16},{36,20},{40,24},{44,28},{48,3... | collective-permute-start | bytes 1572872 | tf_op jit(solution)/shard_map/ppermute | solution.py:15
  66.9 13.0 %collective-permute-start.4 = (f32[2,2,128,256]{3,2,1,0:T(8,128)S(1)}, f32[2,2,128,256]{3,2,1,0:T(8,128)S(1)}, u32[]{:S(2)}, u32[]{:S(2)}) collective-permute-start(f32[2,2,128,256]{3,2,1,0:T(8,128)S(1)} %slice.282), channel_id=1, source_target_pairs={{8,0},{12,4},{16,8},{20,12},{24,16},{28,20},{32,24},{36,28},{40,32... | collective-permute-start | bytes 1572872 | tf_op jit(solution)/shard_map/ppermute | solution.py:15
  80.0 10.9 %collective-permute-start.5 = (f32[1,2,128,256]{3,2,1,0:T(8,128)S(1)}, f32[1,2,128,256]{3,2,1,0:T(8,128)S(1)}, u32[]{:S(2)}, u32[]{:S(2)}) collective-permute-start(f32[1,2,128,256]{3,2,1,0:T(8,128)S(1)} %slice.284), channel_id=1, source_target_pairs={{4,0},{8,4},{12,8},{16,12},{20,16},{24,20},{28,24},{32,28},{36,32}... | collective-permute-start | bytes 786440 | tf_op jit(solution)/shard_map/ppermute | solution.py:15
  94.1 4.1 %collective-permute-start.6 = (f32[1,128,64]{1,2,0:T(8,128)S(1)}, f32[1,128,64]{1,2,0:T(8,128)S(1)}, u32[]{:S(2)}, u32[]{:S(2)}) collective-permute-start(f32[1,128,64]{1,2,0:T(8,128)S(1)} %get-tuple-element.44), channel_id=1, source_target_pairs={{0,1},{1,0},{2,3},{3,2},{4,5},{5,4},{6,7},{7,6},{8,9},{9,8},{10,11... | collective-permute-start | bytes 98312 | tf_op jit(solution)/shard_map/ppermute | solution.py:30
  95.4 4.3 %collective-permute-start.7 = (f32[1,128,64]{1,2,0:T(8,128)S(1)}, f32[1,128,64]{1,2,0:T(8,128)S(1)}, u32[]{:S(2)}, u32[]{:S(2)}) collective-permute-start(f32[1,128,64]{1,2,0:T(8,128)S(1)} %get-tuple-element.45), channel_id=1, source_target_pairs={{0,2},{1,3},{2,0},{3,1},{4,6},{5,7},{6,4},{7,5},{8,10},{9,11},{10,... | collective-permute-start | bytes 98312 | tf_op jit(solution)/shard_map/ppermute | solution.py:30
  97.8 4.0 %collective-permute-start.8 = (f32[1,128,64]{1,2,0:T(8,128)S(1)}, f32[1,128,64]{1,2,0:T(8,128)S(1)}, u32[]{:S(2)}, u32[]{:S(2)}) collective-permute-start(f32[1,128,64]{1,2,0:T(8,128)S(1)} %get-tuple-element.46), channel_id=1, source_target_pairs={{0,3},{1,2},{2,1},{3,0},{4,7},{5,6},{6,5},{7,4},{8,11},{9,10},{10,... | collective-permute-start | bytes 98312 | tf_op jit(solution)/shard_map/ppermute | solution.py:30
  109.1 6.6 %collective-permute-start.10 = (bf16[16,5120]{1,0:T(8,128)(2,1)S(1)}, bf16[16,5120]{1,0:T(8,128)(2,1)S(1)}, u32[]{:S(2)}, u32[]{:S(2)}) collective-permute-start(bf16[16,5120]{1,0:T(8,128)(2,1)S(1)} %bitcast.123), channel_id=1, source_target_pairs={{0,8},{4,12},{8,0},{12,4},{16,24},{20,28},{24,16},{28,20},{32,40},... | collective-permute-start | bytes 491528 | tf_op jit(solution)/shard_map/ppermute | solution.py:30
  111.2 8.0 %collective-permute-start.11 = (bf16[16,5120]{1,0:T(8,128)(2,1)S(1)}, bf16[16,5120]{1,0:T(8,128)(2,1)S(1)}, u32[]{:S(2)}, u32[]{:S(2)}) collective-permute-start(bf16[16,5120]{1,0:T(8,128)(2,1)S(1)} %bitcast.124), channel_id=1, source_target_pairs={{0,12},{4,8},{8,4},{12,0},{16,28},{20,24},{24,20},{28,16},{32,44},... | collective-permute-start | bytes 491528 | tf_op jit(solution)/shard_map/ppermute | solution.py:30
  111.4 7.9 %collective-permute-start.9 = (bf16[16,5120]{1,0:T(8,128)(2,1)S(1)}, bf16[16,5120]{1,0:T(8,128)(2,1)S(1)}, u32[]{:S(2)}, u32[]{:S(2)}) collective-permute-start(bf16[16,5120]{1,0:T(8,128)(2,1)S(1)} %bitcast.125), channel_id=1, source_target_pairs={{0,4},{4,0},{8,12},{12,8},{16,20},{20,16},{24,28},{28,24},{32,36},... | collective-permute-start | bytes 491528 | tf_op jit(solution)/shard_map/ppermute | solution.py:30
  119.8 8.9 %collective-permute-start.12 = (f32[32768]{0:T(1024)S(1)}, f32[32768]{0:T(1024)S(1)}, u32[]{:S(2)}, u32[]{:S(2)}) collective-permute-start(f32[32768]{0:T(1024)S(1)} %get-tuple-element.55), channel_id=1, source_target_pairs={{0,16},{4,20},{8,24},{12,28},{16,0},{20,4},{24,8},{28,12},{32,48},... | collective-permute-start | bytes 393224 | tf_op jit(solution)/shard_map/ppermute | solution.py:30
  125.1 4.9 %collective-permute-start.13 = (f32[32768]{0:T(1024)S(1)}, f32[32768]{0:T(1024)S(1)}, u32[]{:S(2)}, u32[]{:S(2)}) collective-permute-start(f32[32768]{0:T(1024)S(1)} %get-tuple-element.56), channel_id=1, source_target_pairs={{0,32},{4,36},{8,40},{12,44},{16,48},{20,52},{24,56},{28,60},{32,0... | collective-permute-start | bytes 393224 | tf_op jit(solution)/shard_map/ppermute | solution.py:30
  126.9 6.6 %collective-permute-start.14 = (f32[32768]{0:T(1024)S(1)}, f32[32768]{0:T(1024)S(1)}, u32[]{:S(2)}, u32[]{:S(2)}) collective-permute-start(f32[32768]{0:T(1024)S(1)} %get-tuple-element.57), channel_id=1, source_target_pairs={{0,48},{4,52},{8,56},{12,60},{16,32},{20,36},{24,40},{28,44},{32,1... | collective-permute-start | bytes 393224 | tf_op jit(solution)/shard_map/ppermute | solution.py:30
  135.7 11.7 %collective-permute-start.15 = (f32[20480]{0:T(1024)S(1)}, f32[20480]{0:T(1024)S(1)}, u32[]{:S(2)}, u32[]{:S(2)}) collective-permute-start(f32[20480]{0:T(1024)S(1)} %get-tuple-element.47), channel_id=1, source_target_pairs={{0,64},{4,68},{8,72},{12,76},{16,80},{20,84},{24,88},{28,92},{32,9... | collective-permute-start | bytes 245768 | tf_op jit(solution)/shard_map/ppermute | solution.py:30
  143.6 8.1 %collective-permute-start.16 = (f32[20480]{0:T(1024)S(1)}, f32[20480]{0:T(1024)S(1)}, u32[]{:S(2)}, u32[]{:S(2)}) collective-permute-start(f32[20480]{0:T(1024)S(1)} %get-tuple-element.48), channel_id=1, source_target_pairs={{0,128},{4,132},{8,136},{12,140},{16,144},{20,148},{24,152},{28,15... | collective-permute-start | bytes 245768 | tf_op jit(solution)/shard_map/ppermute | solution.py:30
  143.7 8.1 %collective-permute-start.17 = (f32[20480]{0:T(1024)S(1)}, f32[20480]{0:T(1024)S(1)}, u32[]{:S(2)}, u32[]{:S(2)}) collective-permute-start(f32[20480]{0:T(1024)S(1)} %get-tuple-element.49), channel_id=1, source_target_pairs={{0,192},{4,196},{8,200},{12,204},{16,208},{20,212},{24,216},{28,22... | collective-permute-start | bytes 245768 | tf_op jit(solution)/shard_map/ppermute | solution.py:30
  152.5 13.1 %collective-permute-start.21 = (f32[16,1024]{1,0:T(8,128)S(1)}, f32[16,1024]{1,0:T(8,128)S(1)}, u32[]{:S(2)}, u32[]{:S(2)}) collective-permute-start(f32[16,1024]{1,0:T(8,128)S(1)} %fusion.40), channel_id=1, source_target_pairs={{0,4},{4,0},{8,12},{12,8},{16,20},{20,16},{24,28},{28,24},{32,36},... | collective-permute-start | bytes 196616 | tf_op jit(solution)/shard_map/ppermute | solution.py:30
  155.7 10.0 %collective-permute-start.22 = (f32[16,1024]{1,0:T(8,128)S(1)}, f32[16,1024]{1,0:T(8,128)S(1)}, u32[]{:S(2)}, u32[]{:S(2)}) collective-permute-start(f32[16,1024]{1,0:T(8,128)S(1)} %fusion.40), channel_id=1, source_target_pairs={{0,8},{4,12},{8,0},{12,4},{16,24},{20,28},{24,16},{28,20},{32,40},... | collective-permute-start | bytes 196616 | tf_op jit(solution)/shard_map/ppermute | solution.py:30
  157.0 4.2 %collective-permute-start.18 = (f32[1,64,2,32]{1,3,2,0:T(8,128)S(1)}, f32[1,64,2,32]{1,3,2,0:T(8,128)S(1)}, u32[]{:S(2)}, u32[]{:S(2)}) collective-permute-start(f32[1,64,2,32]{1,3,2,0:T(8,128)S(1)} %add_add_fusion), channel_id=1, source_target_pairs={{0,1},{1,0},{2,3},{3,2},{4,5},{5,4},{6,7},{7,6},{8,9},{9,8},{10,11... | collective-permute-start | bytes 49160 | tf_op jit(solution)/shard_map/ppermute | solution.py:30
  157.1 6.5 %collective-permute-start.19 = (f32[1,64,2,32]{1,3,2,0:T(8,128)S(1)}, f32[1,64,2,32]{1,3,2,0:T(8,128)S(1)}, u32[]{:S(2)}, u32[]{:S(2)}) collective-permute-start(f32[1,64,2,32]{1,3,2,0:T(8,128)S(1)} %add_add_fusion), channel_id=1, source_target_pairs={{0,2},{1,3},{2,0},{3,1},{4,6},{5,7},{6,4},{7,5},{8,10},{9,11},{10,... | collective-permute-start | bytes 49160 | tf_op jit(solution)/shard_map/ppermute | solution.py:30
  158.8 4.8 %collective-permute-start.20 = (f32[1,64,2,32]{1,3,2,0:T(8,128)S(1)}, f32[1,64,2,32]{1,3,2,0:T(8,128)S(1)}, u32[]{:S(2)}, u32[]{:S(2)}) collective-permute-start(f32[1,64,2,32]{1,3,2,0:T(8,128)S(1)} %add_add_fusion), channel_id=1, source_target_pairs={{0,3},{1,2},{2,1},{3,0},{4,7},{5,6},{6,5},{7,4},{8,11},{9,10},{10,... | collective-permute-start | bytes 49160 | tf_op jit(solution)/shard_map/ppermute | solution.py:30
  161.2 5.3 %collective-permute-start.23 = (f32[16,1024]{1,0:T(8,128)S(1)}, f32[16,1024]{1,0:T(8,128)S(1)}, u32[]{:S(2)}, u32[]{:S(2)}) collective-permute-start(f32[16,1024]{1,0:T(8,128)S(1)} %fusion.40), channel_id=1, source_target_pairs={{0,12},{4,8},{8,4},{12,0},{16,28},{20,24},{24,20},{28,16},{32,44},... | collective-permute-start | bytes 196616 | tf_op jit(solution)/shard_map/ppermute | solution.py:30
  (6 other events, 116.0 us)

commit v11 on v10

--- a/solution.py
+++ b/solution.py
@@ -102,7 +102,8 @@
     k = k_ref[...]
     v = v_ref[...]
     s = lax.dot_general(q, k, (((1,), (1,)), ((), ())), preferred_element_type=jnp.float32) * scale
-    block = lax.broadcasted_iota(jnp.int32, (1, s.shape[1]), 1) // 128
+    place = lax.broadcasted_iota(jnp.int32, (1, s.shape[1]), 1) // 128
+    block = (place % 2) * 4 + ((place // 2) % 2) * 2 + place // 4
     expo = jnp.exp(jnp.where(block <= pos_ref[0], s, -jnp.inf))
     prob = expo * (1.0 / jnp.sum(expo, axis=-1, keepdims=True))
     prob_b = prob.astype(jnp.bfloat16)
@@ -175,21 +176,21 @@
     first = jnp.max(jnp.where(starts <= stretch, starts, 0))
     position = stretch - first
     window = jnp.stack([mem_key, memory_values])[None]
-    reach = 1
-    while reach < span:
+    reach = span // 2
+    while reach >= 1:
         window = jnp.concatenate([window, passed_along(window, "wide", reach)], 0)
-        reach *= 2
+        reach //= 2
     keys = window[:, 0].reshape(span * rows, cols)
     values = window[:, 1].reshape(span * rows, cols)
     dkey, dval = attention_grads(position, queries, out_grad, keys, values)
     contrib = jnp.stack([dkey.reshape(span, rows, cols), dval.reshape(span, rows, cols)], 1)
-    reach = span // 2
-    while reach >= 1:
-        give = contrib[reach : 2 * reach]
-        if reach == span // 2:
+    half = span // 2
+    while half >= 1:
+        give = contrib[half : 2 * half]
+        if half == span // 2:
             give = give.astype(jnp.bfloat16)
-        contrib = contrib[:reach] + passed_along(give, "wide", -reach).astype(jnp.float32)
-        reach //= 2
+        contrib = contrib[:half] + passed_along(give, "wide", -(span // (2 * half))).astype(jnp.float32)
+        half //= 2
     total = contrib[0]
     key_grad = total[0].astype(jnp.bfloat16)
     value_grad = total[1].astype(jnp.bfloat16)

time: 169 us -> 169 us (level)
    ppermute x18, starting transfers between devices: 34.8 us -> 37.5 us  [xor_partner(): return lax.ppermute(array, axis, [(i, i ^ mask) for i in range(devices)])]
    ppermute x6, starting transfers between devices: 21.4 us -> 19.6 us  [passed_along(): return lax.ppermute(array, axis, pairs)]
  transfers between devices with their start and end apart: 24 -> 24, of which waited for: 15 -> 17; matrix products, arithmetic and copies ran while one was open for 3% -> 3% of each run, Pallas kernels for 0% -> 0%
where the time goes in v11:
time: 169 us; the launch traced here: 168 us
  waiting for transfers between devices  63.9 us (38%)
  starting transfers between devices  57.1 us (34%)
  Pallas kernels  19.5 us (12%)
  local copies, waits for them, and re-layouts  16.9 us (10%)
  other arithmetic  4.5 us (3%)
  matrix products  4.08 us (2%)
  between operations  2.16 us (1%)
    ppermute x6, waiting for transfers between devices, passed_along(): return lax.ppermute(array, axis, pairs)  42 us
    ppermute x18, starting transfers between devices, xor_partner(): return lax.ppermute(array, axis, [(i, i ^ mask) for i in range(devices)])  37.5 us
    ppermute x18, waiting for transfers between devices, xor_partner(): return lax.ppermute(array, axis, [(i, i ^ mask) for i in range(devices)])  21.9 us
    ppermute x6, starting transfers between devices, passed_along(): return lax.ppermute(array, axis, pairs)  19.6 us
    pallas_call x1, Pallas kernels, attention_grads(): pl.pallas_call(attention_body, grid_spec=grid_spec, out_shape=[jax.ShapeD...  19.5 us
  transfers between devices with their start and end apart: 24, of which 17 were waited for; matrix products, arithmetic and copies ran while one was open for 3% of the time, Pallas kernels for 0%

profile of v11, /device:TPU:1, one launch (start us, length us, event | category | flops | bytes accessed | tf_op | source)
XLA Modules:
  0.0 168.2 jit_solution(12513183863972541500)
XLA Ops:
  1.6 5.6 %collective-permute-start = (bf16[1,2,128,256]{3,2,1,0:T(8,128)(2,1)S(1)}, bf16[1,2,128,256]{3,2,1,0:T(8,128)(2,1)S(1)}, u32[]{:S(2)}, u32[]{:S(2)}) collective-permute-start(bf16[1,2,128,256]{3,2,1,0:T(8,128)(2,1)S(1)} %maximum_bitcast_fusion), channel_id=1, source_target_pairs={{0,16},{4,20},{8,24},{12,28},{16,32},{20,36},{24,40},{28,44},{32,4... | collective-permute-start | bytes 393224 | tf_op jit(solution)/shard_map/ppermute | solution.py:15
  7.3 2.2 %collective-permute-done = bf16[1,2,128,256]{3,2,1,0:T(8,128)(2,1)S(1)} collective-permute-done((bf16[1,2,128,256]{3,2,1,0:T(8,128)(2,1)S(1)}, bf16[1,2,128,256]{3,2,1,0:T(8,128)(2,1)S(1)}, u32[]{:S(2)}, u32[]{:S(2)}) %collective-permute-start) | collective-permute-done | bytes 131104 | tf_op jit(solution)/shard_map/ppermute | solution.py:15
  9.5 2.3 %collective-permute-start.1 = (bf16[2,2,128,256]{3,2,1,0:T(8,128)(2,1)S(1)}, bf16[2,2,128,256]{3,2,1,0:T(8,128)(2,1)S(1)}, u32[]{:S(2)}, u32[]{:S(2)}) collective-permute-start(bf16[2,2,128,256]{3,2,1,0:T(8,128)(2,1)S(1)} %pad_maximum_fusion.3), channel_id=1, source_target_pairs={{0,8},{4,12},{8,16},{12,20},{16,24},{20,28},{24,32},{28,36},{32,40... | collective-permute-start | bytes 786440 | tf_op jit(solution)/shard_map/ppermute | solution.py:15
  11.8 4.1 %collective-permute-done.1 = bf16[2,2,128,256]{3,2,1,0:T(8,128)(2,1)S(1)} collective-permute-done((bf16[2,2,128,256]{3,2,1,0:T(8,128)(2,1)S(1)}, bf16[2,2,128,256]{3,2,1,0:T(8,128)(2,1)S(1)}, u32[]{:S(2)}, u32[]{:S(2)}) %collective-permute-start.1) | collective-permute-done | bytes 262176 | tf_op jit(solution)/shard_map/ppermute | solution.py:15
  16.0 7.2 %collective-permute-start.2 = (bf16[4,2,128,256]{3,2,1,0:T(8,128)(2,1)S(1)}, bf16[4,2,128,256]{3,2,1,0:T(8,128)(2,1)S(1)}, u32[]{:S(2)}, u32[]{:S(2)}) collective-permute-start(bf16[4,2,128,256]{3,2,1,0:T(8,128)(2,1)S(1)} %pad_maximum_fusion.2), channel_id=1, source_target_pairs={{0,4},{4,8},{8,12},{12,16},{16,20},{20,24},{24,28},{28,32},{32,36}... | collective-permute-start | bytes 1572872 | tf_op jit(solution)/shard_map/ppermute | solution.py:15
  24.7 4.5 %collective-permute-done.2 = bf16[4,2,128,256]{3,2,1,0:T(8,128)(2,1)S(1)} collective-permute-done((bf16[4,2,128,256]{3,2,1,0:T(8,128)(2,1)S(1)}, bf16[4,2,128,256]{3,2,1,0:T(8,128)(2,1)S(1)}, u32[]{:S(2)}, u32[]{:S(2)}) %collective-permute-start.2) | collective-permute-done | bytes 524320 | tf_op jit(solution)/shard_map/ppermute | solution.py:15
  30.4 19.5 %shard_map.129 = (f32[1024,256]{1,0:T(8,128)}, f32[1024,256]{1,0:T(8,128)}) custom-call(s32[1]{0:T(128)} %bitcast.1.pos_ref, bf16[512,1024]{1,0:T(8,128)(2,1)} %q_ref.1, bf16[512,1024]{1,0:T(8,128)(2,1)} %do_ref.1, bf16[1024,256]{1,0:T(8,128)(2,1)} %bitcast.116, bf16[1024,256]{1,0:T(8,128)(2,1)} %bitcast.115), custom_call_target="tpu_custom_call" | custom-call | tf_op jit(solution)/shard_map/pallas_call | solution.py:147
  51.5 1.9 %collective-permute-start.3 = (bf16[4,2,128,256]{3,2,1,0:T(8,128)(2,1)S(1)}, bf16[4,2,128,256]{3,2,1,0:T(8,128)(2,1)S(1)}, u32[]{:S(2)}, u32[]{:S(2)}) collective-permute-start(bf16[4,2,128,256]{3,2,1,0:T(8,128)(2,1)S(1)} %fusion.2), channel_id=1, source_target_pairs={{4,0},{8,4},{12,8},{16,12},{20,16},{24,20},{28,24},{32,28},{36,32}... | collective-permute-start | bytes 1572872 | tf_op jit(solution)/shard_map/ppermute | solution.py:15
  53.5 9.3 %collective-permute-done.3 = bf16[4,2,128,256]{3,2,1,0:T(8,128)(2,1)S(1)} collective-permute-done((bf16[4,2,128,256]{3,2,1,0:T(8,128)(2,1)S(1)}, bf16[4,2,128,256]{3,2,1,0:T(8,128)(2,1)S(1)}, u32[]{:S(2)}, u32[]{:S(2)}) %collective-permute-start.3) | collective-permute-done | bytes 524320 | tf_op jit(solution)/shard_map/ppermute | solution.py:15
  64.4 12.8 %collective-permute-done.4 = f32[2,2,128,256]{3,2,1,0:T(8,128)S(1)} collective-permute-done((f32[2,2,128,256]{3,2,1,0:T(8,128)S(1)}, f32[2,2,128,256]{3,2,1,0:T(8,128)S(1)}, u32[]{:S(2)}, u32[]{:S(2)}) %collective-permute-start.4) | collective-permute-done | bytes 524320 | tf_op jit(solution)/shard_map/ppermute | solution.py:15
  78.7 9.1 %collective-permute-done.5 = f32[1,2,128,256]{3,2,1,0:T(8,128)S(1)} collective-permute-done((f32[1,2,128,256]{3,2,1,0:T(8,128)S(1)}, f32[1,2,128,256]{3,2,1,0:T(8,128)S(1)}, u32[]{:S(2)}, u32[]{:S(2)}) %collective-permute-start.5) | collective-permute-done | bytes 262176 | tf_op jit(solution)/shard_map/ppermute | solution.py:15
  87.8 1.9 %convolution_bitcast_fusion.1 = f32[1,128,256]{2,1,0:T(8,128)S(1)} fusion(bf16[128,4096]{1,0:T(8,128)(2,1)S(1)} %copy-done, bf16[4096,128]{1,0:T(8,128)(2,1)} %param.20, bf16[1,2,128,256]{3,2,1,0:T(8,128)(2,1)S(1)} %slice_add_fusion.1), kind=kOutput, calls=%fused_computation.7 | convolution fusion | flops 142622720 | bytes 2293760 | tf_op jit(solution)/shard_map/dot_general | solution.py:212
  92.3 2.5 %collective-permute-start.7 = (f32[1,128,64]{1,2,0:T(8,128)S(1)}, f32[1,128,64]{1,2,0:T(8,128)S(1)}, u32[]{:S(2)}, u32[]{:S(2)}) collective-permute-start(f32[1,128,64]{1,2,0:T(8,128)S(1)} %get-tuple-element.45), channel_id=1, source_target_pairs={{0,2},{1,3},{2,0},{3,1},{4,6},{5,7},{6,4},{7,5},{8,10},{9,11},{10,... | collective-permute-start | bytes 98312 | tf_op jit(solution)/shard_map/ppermute | solution.py:30
  96.5 2.2 %collective-permute-done.8 = f32[1,128,64]{1,2,0:T(8,128)S(1)} collective-permute-done((f32[1,128,64]{1,2,0:T(8,128)S(1)}, f32[1,128,64]{1,2,0:T(8,128)S(1)}, u32[]{:S(2)}, u32[]{:S(2)}) %collective-permute-start.8) | collective-permute-done | bytes 32800 | tf_op jit(solution)/shard_map/ppermute | solution.py:30
  106.0 4.8 %collective-permute-start.10 = (bf16[16,5120]{1,0:T(8,128)(2,1)S(1)}, bf16[16,5120]{1,0:T(8,128)(2,1)S(1)}, u32[]{:S(2)}, u32[]{:S(2)}) collective-permute-start(bf16[16,5120]{1,0:T(8,128)(2,1)S(1)} %bitcast.123), channel_id=1, source_target_pairs={{0,8},{4,12},{8,0},{12,4},{16,24},{20,28},{24,16},{28,20},{32,40},... | collective-permute-start | bytes 491528 | tf_op jit(solution)/shard_map/ppermute | solution.py:30
  112.1 3.5 %collective-permute-done.10 = bf16[16,5120]{1,0:T(8,128)(2,1)S(1)} collective-permute-done((bf16[16,5120]{1,0:T(8,128)(2,1)S(1)}, bf16[16,5120]{1,0:T(8,128)(2,1)S(1)}, u32[]{:S(2)}, u32[]{:S(2)}) %collective-permute-start.10) | collective-permute-done | bytes 163872 | tf_op jit(solution)/shard_map/ppermute | solution.py:30
  115.6 3.5 %collective-permute-done.11 = bf16[16,5120]{1,0:T(8,128)(2,1)S(1)} collective-permute-done((bf16[16,5120]{1,0:T(8,128)(2,1)S(1)}, bf16[16,5120]{1,0:T(8,128)(2,1)S(1)}, u32[]{:S(2)}, u32[]{:S(2)}) %collective-permute-start.11) | collective-permute-done | bytes 163872 | tf_op jit(solution)/shard_map/ppermute | solution.py:30
  119.7 4.6 %collective-permute-start.12 = (f32[32768]{0:T(1024)S(1)}, f32[32768]{0:T(1024)S(1)}, u32[]{:S(2)}, u32[]{:S(2)}) collective-permute-start(f32[32768]{0:T(1024)S(1)} %get-tuple-element.55), channel_id=1, source_target_pairs={{0,16},{4,20},{8,24},{12,28},{16,0},{20,4},{24,8},{28,12},{32,48},... | collective-permute-start | bytes 393224 | tf_op jit(solution)/shard_map/ppermute | solution.py:30
  129.6 3.3 %collective-permute-done.14 = f32[32768]{0:T(1024)S(1)} collective-permute-done((f32[32768]{0:T(1024)S(1)}, f32[32768]{0:T(1024)S(1)}, u32[]{:S(2)}, u32[]{:S(2)}) %collective-permute-start.14) | collective-permute-done | bytes 131104 | tf_op jit(solution)/shard_map/ppermute | solution.py:30
  135.1 6.9 %collective-permute-start.15 = (f32[20480]{0:T(1024)S(1)}, f32[20480]{0:T(1024)S(1)}, u32[]{:S(2)}, u32[]{:S(2)}) collective-permute-start(f32[20480]{0:T(1024)S(1)} %get-tuple-element.47), channel_id=1, source_target_pairs={{0,64},{4,68},{8,72},{12,76},{16,80},{20,84},{24,88},{28,92},{32,9... | collective-permute-start | bytes 245768 | tf_op jit(solution)/shard_map/ppermute | solution.py:30
  143.0 2.4 %collective-permute-start.17 = (f32[20480]{0:T(1024)S(1)}, f32[20480]{0:T(1024)S(1)}, u32[]{:S(2)}, u32[]{:S(2)}) collective-permute-start(f32[20480]{0:T(1024)S(1)} %get-tuple-element.49), channel_id=1, source_target_pairs={{0,192},{4,196},{8,200},{12,204},{16,208},{20,212},{24,216},{28,22... | collective-permute-start | bytes 245768 | tf_op jit(solution)/shard_map/ppermute | solution.py:30
  145.9 3.6 %collective-permute-done.16 = f32[20480]{0:T(1024)S(1)} collective-permute-done((f32[20480]{0:T(1024)S(1)}, f32[20480]{0:T(1024)S(1)}, u32[]{:S(2)}, u32[]{:S(2)}) %collective-permute-start.16) | collective-permute-done | bytes 81952 | tf_op jit(solution)/shard_map/ppermute | solution.py:30
  150.9 4.2 %collective-permute-start.21 = (f32[16,1024]{1,0:T(8,128)S(1)}, f32[16,1024]{1,0:T(8,128)S(1)}, u32[]{:S(2)}, u32[]{:S(2)}) collective-permute-start(f32[16,1024]{1,0:T(8,128)S(1)} %fusion.40), channel_id=1, source_target_pairs={{0,4},{4,0},{8,12},{12,8},{16,20},{20,16},{24,28},{28,24},{32,36},... | collective-permute-start | bytes 196616 | tf_op jit(solution)/shard_map/ppermute | solution.py:30
  158.8 2.6 %collective-permute-start.20 = (f32[1,64,2,32]{1,3,2,0:T(8,128)S(1)}, f32[1,64,2,32]{1,3,2,0:T(8,128)S(1)}, u32[]{:S(2)}, u32[]{:S(2)}) collective-permute-start(f32[1,64,2,32]{1,3,2,0:T(8,128)S(1)} %add_add_fusion), channel_id=1, source_target_pairs={{0,3},{1,2},{2,1},{3,0},{4,7},{5,6},{6,5},{7,4},{8,11},{9,10},{10,... | collective-permute-start | bytes 49160 | tf_op jit(solution)/shard_map/ppermute | solution.py:30
  (152 shorter events, 41.6 us)
Async XLA Ops:
  1.6 7.8 %collective-permute-start = (bf16[1,2,128,256]{3,2,1,0:T(8,128)(2,1)S(1)}, bf16[1,2,128,256]{3,2,1,0:T(8,128)(2,1)S(1)}, u32[]{:S(2)}, u32[]{:S(2)}) collective-permute-start(bf16[1,2,128,256]{3,2,1,0:T(8,128)(2,1)S(1)} %maximum_bitcast_fusion), channel_id=1, source_target_pairs={{0,16},{4,20},{8,24},{12,28},{16,32},{20,36},{24,40},{28,44},{32,4... | collective-permute-start | bytes 393224 | tf_op jit(solution)/shard_map/ppermute | solution.py:15
  9.5 6.4 %collective-permute-start.1 = (bf16[2,2,128,256]{3,2,1,0:T(8,128)(2,1)S(1)}, bf16[2,2,128,256]{3,2,1,0:T(8,128)(2,1)S(1)}, u32[]{:S(2)}, u32[]{:S(2)}) collective-permute-start(bf16[2,2,128,256]{3,2,1,0:T(8,128)(2,1)S(1)} %pad_maximum_fusion.3), channel_id=1, source_target_pairs={{0,8},{4,12},{8,16},{12,20},{16,24},{20,28},{24,32},{28,36},{32,40... | collective-permute-start | bytes 786440 | tf_op jit(solution)/shard_map/ppermute | solution.py:15
  16.0 13.3 %collective-permute-start.2 = (bf16[4,2,128,256]{3,2,1,0:T(8,128)(2,1)S(1)}, bf16[4,2,128,256]{3,2,1,0:T(8,128)(2,1)S(1)}, u32[]{:S(2)}, u32[]{:S(2)}) collective-permute-start(bf16[4,2,128,256]{3,2,1,0:T(8,128)(2,1)S(1)} %pad_maximum_fusion.2), channel_id=1, source_target_pairs={{0,4},{4,8},{8,12},{12,16},{16,20},{20,24},{24,28},{28,32},{32,36}... | collective-permute-start | bytes 1572872 | tf_op jit(solution)/shard_map/ppermute | solution.py:15
  51.5 11.2 %collective-permute-start.3 = (bf16[4,2,128,256]{3,2,1,0:T(8,128)(2,1)S(1)}, bf16[4,2,128,256]{3,2,1,0:T(8,128)(2,1)S(1)}, u32[]{:S(2)}, u32[]{:S(2)}) collective-permute-start(bf16[4,2,128,256]{3,2,1,0:T(8,128)(2,1)S(1)} %fusion.2), channel_id=1, source_target_pairs={{4,0},{8,4},{12,8},{16,12},{20,16},{24,20},{28,24},{32,28},{36,32}... | collective-permute-start | bytes 1572872 | tf_op jit(solution)/shard_map/ppermute | solution.py:15
  62.9 14.2 %collective-permute-start.4 = (f32[2,2,128,256]{3,2,1,0:T(8,128)S(1)}, f32[2,2,128,256]{3,2,1,0:T(8,128)S(1)}, u32[]{:S(2)}, u32[]{:S(2)}) collective-permute-start(f32[2,2,128,256]{3,2,1,0:T(8,128)S(1)} %slice.282), channel_id=1, source_target_pairs={{8,0},{12,4},{16,8},{20,12},{24,16},{28,20},{32,24},{36,28},{40,32... | collective-permute-start | bytes 1572872 | tf_op jit(solution)/shard_map/ppermute | solution.py:15
  77.3 10.5 %collective-permute-start.5 = (f32[1,2,128,256]{3,2,1,0:T(8,128)S(1)}, f32[1,2,128,256]{3,2,1,0:T(8,128)S(1)}, u32[]{:S(2)}, u32[]{:S(2)}) collective-permute-start(f32[1,2,128,256]{3,2,1,0:T(8,128)S(1)} %slice.284), channel_id=1, source_target_pairs={{16,0},{20,4},{24,8},{28,12},{32,16},{36,20},{40,24},{44,28},{48,3... | collective-permute-start | bytes 786440 | tf_op jit(solution)/shard_map/ppermute | solution.py:15
  91.0 4.1 %collective-permute-start.6 = (f32[1,128,64]{1,2,0:T(8,128)S(1)}, f32[1,128,64]{1,2,0:T(8,128)S(1)}, u32[]{:S(2)}, u32[]{:S(2)}) collective-permute-start(f32[1,128,64]{1,2,0:T(8,128)S(1)} %get-tuple-element.44), channel_id=1, source_target_pairs={{0,1},{1,0},{2,3},{3,2},{4,5},{5,4},{6,7},{7,6},{8,9},{9,8},{10,11... | collective-permute-start | bytes 98312 | tf_op jit(solution)/shard_map/ppermute | solution.py:30
  92.3 4.3 %collective-permute-start.7 = (f32[1,128,64]{1,2,0:T(8,128)S(1)}, f32[1,128,64]{1,2,0:T(8,128)S(1)}, u32[]{:S(2)}, u32[]{:S(2)}) collective-permute-start(f32[1,128,64]{1,2,0:T(8,128)S(1)} %get-tuple-element.45), channel_id=1, source_target_pairs={{0,2},{1,3},{2,0},{3,1},{4,6},{5,7},{6,4},{7,5},{8,10},{9,11},{10,... | collective-permute-start | bytes 98312 | tf_op jit(solution)/shard_map/ppermute | solution.py:30
  94.7 4.0 %collective-permute-start.8 = (f32[1,128,64]{1,2,0:T(8,128)S(1)}, f32[1,128,64]{1,2,0:T(8,128)S(1)}, u32[]{:S(2)}, u32[]{:S(2)}) collective-permute-start(f32[1,128,64]{1,2,0:T(8,128)S(1)} %get-tuple-element.46), channel_id=1, source_target_pairs={{0,3},{1,2},{2,1},{3,0},{4,7},{5,6},{6,5},{7,4},{8,11},{9,10},{10,... | collective-permute-start | bytes 98312 | tf_op jit(solution)/shard_map/ppermute | solution.py:30
  106.0 9.6 %collective-permute-start.10 = (bf16[16,5120]{1,0:T(8,128)(2,1)S(1)}, bf16[16,5120]{1,0:T(8,128)(2,1)S(1)}, u32[]{:S(2)}, u32[]{:S(2)}) collective-permute-start(bf16[16,5120]{1,0:T(8,128)(2,1)S(1)} %bitcast.123), channel_id=1, source_target_pairs={{0,8},{4,12},{8,0},{12,4},{16,24},{20,28},{24,16},{28,20},{32,40},... | collective-permute-start | bytes 491528 | tf_op jit(solution)/shard_map/ppermute | solution.py:30
  110.9 8.2 %collective-permute-start.11 = (bf16[16,5120]{1,0:T(8,128)(2,1)S(1)}, bf16[16,5120]{1,0:T(8,128)(2,1)S(1)}, u32[]{:S(2)}, u32[]{:S(2)}) collective-permute-start(bf16[16,5120]{1,0:T(8,128)(2,1)S(1)} %bitcast.124), channel_id=1, source_target_pairs={{0,12},{4,8},{8,4},{12,0},{16,28},{20,24},{24,20},{28,16},{32,44},... | collective-permute-start | bytes 491528 | tf_op jit(solution)/shard_map/ppermute | solution.py:30
  111.1 8.0 %collective-permute-start.9 = (bf16[16,5120]{1,0:T(8,128)(2,1)S(1)}, bf16[16,5120]{1,0:T(8,128)(2,1)S(1)}, u32[]{:S(2)}, u32[]{:S(2)}) collective-permute-start(bf16[16,5120]{1,0:T(8,128)(2,1)S(1)} %bitcast.125), channel_id=1, source_target_pairs={{0,4},{4,0},{8,12},{12,8},{16,20},{20,16},{24,28},{28,24},{32,36},... | collective-permute-start | bytes 491528 | tf_op jit(solution)/shard_map/ppermute | solution.py:30
  119.7 8.5 %collective-permute-start.12 = (f32[32768]{0:T(1024)S(1)}, f32[32768]{0:T(1024)S(1)}, u32[]{:S(2)}, u32[]{:S(2)}) collective-permute-start(f32[32768]{0:T(1024)S(1)} %get-tuple-element.55), channel_id=1, source_target_pairs={{0,16},{4,20},{8,24},{12,28},{16,0},{20,4},{24,8},{28,12},{32,48},... | collective-permute-start | bytes 393224 | tf_op jit(solution)/shard_map/ppermute | solution.py:30
  124.3 5.2 %collective-permute-start.13 = (f32[32768]{0:T(1024)S(1)}, f32[32768]{0:T(1024)S(1)}, u32[]{:S(2)}, u32[]{:S(2)}) collective-permute-start(f32[32768]{0:T(1024)S(1)} %get-tuple-element.56), channel_id=1, source_target_pairs={{0,32},{4,36},{8,40},{12,44},{16,48},{20,52},{24,56},{28,60},{32,0... | collective-permute-start | bytes 393224 | tf_op jit(solution)/shard_map/ppermute | solution.py:30
  126.0 6.9 %collective-permute-start.14 = (f32[32768]{0:T(1024)S(1)}, f32[32768]{0:T(1024)S(1)}, u32[]{:S(2)}, u32[]{:S(2)}) collective-permute-start(f32[32768]{0:T(1024)S(1)} %get-tuple-element.57), channel_id=1, source_target_pairs={{0,48},{4,52},{8,56},{12,60},{16,32},{20,36},{24,40},{28,44},{32,1... | collective-permute-start | bytes 393224 | tf_op jit(solution)/shard_map/ppermute | solution.py:30
  135.1 10.7 %collective-permute-start.15 = (f32[20480]{0:T(1024)S(1)}, f32[20480]{0:T(1024)S(1)}, u32[]{:S(2)}, u32[]{:S(2)}) collective-permute-start(f32[20480]{0:T(1024)S(1)} %get-tuple-element.47), channel_id=1, source_target_pairs={{0,64},{4,68},{8,72},{12,76},{16,80},{20,84},{24,88},{28,92},{32,9... | collective-permute-start | bytes 245768 | tf_op jit(solution)/shard_map/ppermute | solution.py:30
  142.0 7.5 %collective-permute-start.16 = (f32[20480]{0:T(1024)S(1)}, f32[20480]{0:T(1024)S(1)}, u32[]{:S(2)}, u32[]{:S(2)}) collective-permute-start(f32[20480]{0:T(1024)S(1)} %get-tuple-element.48), channel_id=1, source_target_pairs={{0,128},{4,132},{8,136},{12,140},{16,144},{20,148},{24,152},{28,15... | collective-permute-start | bytes 245768 | tf_op jit(solution)/shard_map/ppermute | solution.py:30
  143.0 7.1 %collective-permute-start.17 = (f32[20480]{0:T(1024)S(1)}, f32[20480]{0:T(1024)S(1)}, u32[]{:S(2)}, u32[]{:S(2)}) collective-permute-start(f32[20480]{0:T(1024)S(1)} %get-tuple-element.49), channel_id=1, source_target_pairs={{0,192},{4,196},{8,200},{12,204},{16,208},{20,212},{24,216},{28,22... | collective-permute-start | bytes 245768 | tf_op jit(solution)/shard_map/ppermute | solution.py:30
  150.9 14.3 %collective-permute-start.21 = (f32[16,1024]{1,0:T(8,128)S(1)}, f32[16,1024]{1,0:T(8,128)S(1)}, u32[]{:S(2)}, u32[]{:S(2)}) collective-permute-start(f32[16,1024]{1,0:T(8,128)S(1)} %fusion.40), channel_id=1, source_target_pairs={{0,4},{4,0},{8,12},{12,8},{16,20},{20,16},{24,28},{28,24},{32,36},... | collective-permute-start | bytes 196616 | tf_op jit(solution)/shard_map/ppermute | solution.py:30
  155.0 10.1 %collective-permute-start.22 = (f32[16,1024]{1,0:T(8,128)S(1)}, f32[16,1024]{1,0:T(8,128)S(1)}, u32[]{:S(2)}, u32[]{:S(2)}) collective-permute-start(f32[16,1024]{1,0:T(8,128)S(1)} %fusion.40), channel_id=1, source_target_pairs={{0,8},{4,12},{8,0},{12,4},{16,24},{20,28},{24,16},{28,20},{32,40},... | collective-permute-start | bytes 196616 | tf_op jit(solution)/shard_map/ppermute | solution.py:30
  157.4 4.2 %collective-permute-start.18 = (f32[1,64,2,32]{1,3,2,0:T(8,128)S(1)}, f32[1,64,2,32]{1,3,2,0:T(8,128)S(1)}, u32[]{:S(2)}, u32[]{:S(2)}) collective-permute-start(f32[1,64,2,32]{1,3,2,0:T(8,128)S(1)} %add_add_fusion), channel_id=1, source_target_pairs={{0,1},{1,0},{2,3},{3,2},{4,5},{5,4},{6,7},{7,6},{8,9},{9,8},{10,11... | collective-permute-start | bytes 49160 | tf_op jit(solution)/shard_map/ppermute | solution.py:30
  157.5 5.4 %collective-permute-start.19 = (f32[1,64,2,32]{1,3,2,0:T(8,128)S(1)}, f32[1,64,2,32]{1,3,2,0:T(8,128)S(1)}, u32[]{:S(2)}, u32[]{:S(2)}) collective-permute-start(f32[1,64,2,32]{1,3,2,0:T(8,128)S(1)} %add_add_fusion), channel_id=1, source_target_pairs={{0,2},{1,3},{2,0},{3,1},{4,6},{5,7},{6,4},{7,5},{8,10},{9,11},{10,... | collective-permute-start | bytes 49160 | tf_op jit(solution)/shard_map/ppermute | solution.py:30
  158.8 4.3 %collective-permute-start.20 = (f32[1,64,2,32]{1,3,2,0:T(8,128)S(1)}, f32[1,64,2,32]{1,3,2,0:T(8,128)S(1)}, u32[]{:S(2)}, u32[]{:S(2)}) collective-permute-start(f32[1,64,2,32]{1,3,2,0:T(8,128)S(1)} %add_add_fusion), channel_id=1, source_target_pairs={{0,3},{1,2},{2,1},{3,0},{4,7},{5,6},{6,5},{7,4},{8,11},{9,10},{10,... | collective-permute-start | bytes 49160 | tf_op jit(solution)/shard_map/ppermute | solution.py:30
  161.7 4.2 %collective-permute-start.23 = (f32[16,1024]{1,0:T(8,128)S(1)}, f32[16,1024]{1,0:T(8,128)S(1)}, u32[]{:S(2)}, u32[]{:S(2)}) collective-permute-start(f32[16,1024]{1,0:T(8,128)S(1)} %fusion.40), channel_id=1, source_target_pairs={{0,12},{4,8},{8,4},{12,0},{16,28},{20,24},{24,20},{28,16},{32,44},... | collective-permute-start | bytes 196616 | tf_op jit(solution)/shard_map/ppermute | solution.py:30
  (6 other events, 115.0 us)

commit v12 on v10

--- a/solution.py
+++ b/solution.py
@@ -174,41 +174,34 @@
     starts = jnp.cumsum(file_lengths) - file_lengths
     first = jnp.max(jnp.where(starts <= stretch, starts, 0))
     position = stretch - first
-    window = jnp.stack([mem_key, memory_values])[None]
+    u_key = jnp.dot(enc_rows, key_down, preferred_element_type=jnp.float32).astype(jnp.bfloat16)
+    u_value = jnp.dot(enc_rows, value_down, preferred_element_type=jnp.float32).astype(jnp.bfloat16)
+    rank = u_key.shape[1]
+    piece = rank // narrow_count
+    window = jnp.concatenate([jnp.stack([mem_key, memory_values]), jnp.stack([u_key, u_value])], 2)[None]
     reach = 1
     while reach < span:
         window = jnp.concatenate([window, passed_along(window, "wide", reach)], 0)
         reach *= 2
-    keys = window[:, 0].reshape(span * rows, cols)
-    values = window[:, 1].reshape(span * rows, cols)
+    keys = window[:, 0, :, :cols].reshape(span * rows, cols)
+    values = window[:, 1, :, :cols].reshape(span * rows, cols)
+    u_window = window[:, :, :, cols:].astype(jnp.float32)
     dkey, dval = attention_grads(position, queries, out_grad, keys, values)
-    contrib = jnp.stack([dkey.reshape(span, rows, cols), dval.reshape(span, rows, cols)], 1)
+    dkey = dkey.reshape(span, rows, cols)
+    dval = dval.reshape(span, rows, cols)
+    exact = lax.Precision.HIGHEST
+    up_key = jnp.einsum("jrk,jrc->kc", u_window[:, 0], dkey, precision=exact)
+    up_value = jnp.einsum("jrk,jrc->kc", u_window[:, 1], dval, precision=exact)
+    part_key = jnp.einsum("jrc,kc->jrk", dkey, key_up.astype(jnp.float32), precision=exact)
+    part_value = jnp.einsum("jrc,kc->jrk", dval, value_up.astype(jnp.float32), precision=exact)
+    parts = jnp.stack([part_key, part_value], 1).reshape(span, 2, rows, narrow_count, piece)
+    contrib = scattered_sum(parts.transpose(3, 0, 1, 2, 4), "narrow")
     reach = span // 2
     while reach >= 1:
-        give = contrib[reach : 2 * reach]
-        if reach == span // 2:
-            give = give.astype(jnp.bfloat16)
-        contrib = contrib[:reach] + passed_along(give, "wide", -reach).astype(jnp.float32)
+        contrib = contrib[:reach] + passed_along(contrib[reach : 2 * reach], "wide", -reach)
         reach //= 2
     total = contrib[0]
-    key_grad = total[0].astype(jnp.bfloat16)
-    value_grad = total[1].astype(jnp.bfloat16)
-    u_key = jnp.dot(enc_rows, key_down, preferred_element_type=jnp.float32).astype(jnp.bfloat16)
-    u_value = jnp.dot(enc_rows, value_down, preferred_element_type=jnp.float32).astype(jnp.bfloat16)
-    part_key = jnp.dot(key_grad, key_up.T, preferred_element_type=jnp.float32)
-    part_value = jnp.dot(value_grad, value_up.T, preferred_element_type=jnp.float32)
-    rank = part_key.shape[1]
-    piece = rank // narrow_count
-    parts = jnp.concatenate(
-        [
-            part_key.reshape(rows, narrow_count, piece).transpose(1, 0, 2),
-            part_value.reshape(rows, narrow_count, piece).transpose(1, 0, 2),
-        ],
-        2,
-    )
-    h_both = scattered_sum(parts, "narrow").astype(jnp.bfloat16)
-    up_key = jnp.dot(u_key.T, key_grad, preferred_element_type=jnp.float32)
-    up_value = jnp.dot(u_value.T, value_grad, preferred_element_type=jnp.float32)
+    h_both = jnp.concatenate([total[0], total[1]], 1).astype(jnp.bfloat16)
     down = jnp.dot(enc_rows.T, h_both, preferred_element_type=jnp.float32)
     width = down.shape[0] // wide_count
     up_both = jnp.stack([up_key, up_value]).reshape(wide_count, -1)

time: 169 us -> 181 us (1.071)
  local copies, waits for them, and re-layouts: 16.9 us -> 23.6 us
  starting transfers between devices: 56.3 us -> 60.5 us
  waiting for transfers between devices: 65.4 us -> 63.3 us
  matrix products: 4.08 us -> 5.98 us
    ppermute x6, waiting for transfers between devices: 43.3 us -> 36.4 us  [passed_along(): return lax.ppermute(array, axis, pairs)]
    ppermute x18, waiting for transfers between devices: 22.1 us -> 26.9 us  [xor_partner(): return lax.ppermute(array, axis, [(i, i ^ mask) for i in range(devices)])]
    ppermute x18, starting transfers between devices: 34.8 us -> 39.2 us  [xor_partner(): return lax.ppermute(array, axis, [(i, i ^ mask) for i in range(devices)])]
    slice x3 -> x6, local copies, waits for them, and re-layouts: 1.14 us -> 3.94 us  [the longest x1 2.05 us: on_device(): keys = window[:, 0, :, :cols].reshape(span * rows, cols)]
    another operation x3 -> x6, local copies, waits for them, and re-layouts: 1.35 us -> 3.52 us
    dot_general x4 -> x6, matrix products: 2.81 us -> 4.7 us  [the longest x1 1.75 us: on_device(): jnp.dot(enc_rows, key_down, preferred_element_type=jnp.float32)]
    unnamed x20 -> x28, local copies, waits for them, and re-layouts: 3.27 us -> 4.99 us
  transfers between devices with their start and end apart: 24 -> 24, of which waited for: 15 -> 16; matrix products, arithmetic and copies ran while one was open for 3% -> 4% of each run, Pallas kernels for 0% -> 0%
where the time goes in v12:
time: 181 us; the launch traced here: 180 us
  waiting for transfers between devices  63.3 us (35%)
  starting transfers between devices  60.5 us (33%)
  local copies, waits for them, and re-layouts  23.6 us (13%)
  Pallas kernels  19.5 us (11%)
  matrix products  5.98 us (3%)
  other arithmetic  5.4 us (3%)
  between operations  2.25 us (1%)
    ppermute x18, starting transfers between devices, xor_partner(): return lax.ppermute(array, axis, [(i, i ^ mask) for i in range(devices)])  39.2 us
    ppermute x6, waiting for transfers between devices, passed_along(): return lax.ppermute(array, axis, pairs)  36.4 us
    ppermute x18, waiting for transfers between devices, xor_partner(): return lax.ppermute(array, axis, [(i, i ^ mask) for i in range(devices)])  26.9 us
    ppermute x6, starting transfers between devices, passed_along(): return lax.ppermute(array, axis, pairs)  21.3 us
    pallas_call x1, Pallas kernels, attention_grads(): pl.pallas_call(attention_body, grid_spec=grid_spec, out_shape=[jax.ShapeD...  19.5 us
    unnamed x28, local copies, waits for them, and re-layouts  4.99 us
  transfers between devices with their start and end apart: 24, of which 16 were waited for; matrix products, arithmetic and copies ran while one was open for 4% of the time, Pallas kernels for 0%

profile of v12, /device:TPU:1, one launch (start us, length us, event | category | flops | bytes accessed | tf_op | source)
XLA Modules:
  0.0 180.5 jit_solution(17845257104961324575)
XLA Ops:
  5.1 4.6 %collective-permute-start = (bf16[1,2,128,384]{2,3,0,1:T(8,128)(2,1)S(1)}, bf16[1,2,128,384]{2,3,0,1:T(8,128)(2,1)S(1)}, u32[]{:S(2)}, u32[]{:S(2)}) collective-permute-start(bf16[1,2,128,384]{2,3,0,1:T(8,128)(2,1)S(1)} %maximum_bitcast_fusion.4), channel_id=1, source_target_pairs={{0,4},{4,8},{8,12},{12,16},{16,20},{20,24},{24,28},{28,32},{32,36}... | collective-permute-start | bytes 589832 | tf_op jit(solution)/shard_map/ppermute | solution.py:15
  9.6 2.6 %collective-permute-done = bf16[1,2,128,384]{2,3,0,1:T(8,128)(2,1)S(1)} collective-permute-done((bf16[1,2,128,384]{2,3,0,1:T(8,128)(2,1)S(1)}, bf16[1,2,128,384]{2,3,0,1:T(8,128)(2,1)S(1)}, u32[]{:S(2)}, u32[]{:S(2)}) %collective-permute-start) | collective-permute-done | bytes 196640 | tf_op jit(solution)/shard_map/ppermute | solution.py:15
  12.3 3.2 %collective-permute-start.1 = (bf16[2,2,128,384]{2,3,0,1:T(8,128)(2,1)S(1)}, bf16[2,2,128,384]{2,3,0,1:T(8,128)(2,1)S(1)}, u32[]{:S(2)}, u32[]{:S(2)}) collective-permute-start(bf16[2,2,128,384]{2,3,0,1:T(8,128)(2,1)S(1)} %pad_maximum_fusion.2), channel_id=1, source_target_pairs={{0,8},{4,12},{8,16},{12,20},{16,24},{20,28},{24,32},{28,36},{32,40... | collective-permute-start | bytes 1179656 | tf_op jit(solution)/shard_map/ppermute | solution.py:15
  15.5 7.1 %collective-permute-done.1 = bf16[2,2,128,384]{2,3,0,1:T(8,128)(2,1)S(1)} collective-permute-done((bf16[2,2,128,384]{2,3,0,1:T(8,128)(2,1)S(1)}, bf16[2,2,128,384]{2,3,0,1:T(8,128)(2,1)S(1)}, u32[]{:S(2)}, u32[]{:S(2)}) %collective-permute-start.1) | collective-permute-done | bytes 393248 | tf_op jit(solution)/shard_map/ppermute | solution.py:15
  22.7 5.2 %collective-permute-start.2 = (bf16[4,2,128,384]{2,3,0,1:T(8,128)(2,1)S(1)}, bf16[4,2,128,384]{2,3,0,1:T(8,128)(2,1)S(1)}, u32[]{:S(2)}, u32[]{:S(2)}) collective-permute-start(bf16[4,2,128,384]{2,3,0,1:T(8,128)(2,1)S(1)} %pad_maximum_fusion.1), channel_id=1, source_target_pairs={{0,16},{4,20},{8,24},{12,28},{16,32},{20,36},{24,40},{28,44},{32,4... | collective-permute-start | bytes 2359304 | tf_op jit(solution)/shard_map/ppermute | solution.py:15
  29.7 12.6 %collective-permute-done.2 = bf16[4,2,128,384]{2,3,0,1:T(8,128)(2,1)S(1)} collective-permute-done((bf16[4,2,128,384]{2,3,0,1:T(8,128)(2,1)S(1)}, bf16[4,2,128,384]{2,3,0,1:T(8,128)(2,1)S(1)}, u32[]{:S(2)}, u32[]{:S(2)}) %collective-permute-start.2) | collective-permute-done | bytes 786464 | tf_op jit(solution)/shard_map/ppermute | solution.py:15
  46.4 19.5 %shard_map.129 = (f32[1024,256]{1,0:T(8,128)}, f32[1024,256]{1,0:T(8,128)}) custom-call(s32[1]{0:T(128)} %bitcast.1.pos_ref, bf16[512,1024]{1,0:T(8,128)(2,1)} %q_ref.1, bf16[512,1024]{1,0:T(8,128)(2,1)} %do_ref.1, bf16[1024,256]{1,0:T(8,128)(2,1)} %bitcast.147, bf16[1024,256]{1,0:T(8,128)(2,1)} %bitcast.148), custom_call_target="tpu_custom_call" | custom-call | tf_op jit(solution)/shard_map/pallas_call | solution.py:146
  72.2 2.4 %collective-permute-start.4 = (f32[1,8,2,128,32]{3,4,2,1,0:T(8,128)}, f32[1,8,2,128,32]{3,4,2,1,0:T(8,128)}, u32[]{:S(2)}, u32[]{:S(2)}) collective-permute-start(f32[1,8,2,128,32]{3,4,2,1,0:T(8,128)} %bitcast.138), channel_id=1, source_target_pairs={{0,2},{1,3},{2,0},{3,1},{4,6},{5,7},{6,4},{7,5},{8,10},{9,11},{10,... | collective-permute-start | bytes 786440 | tf_op jit(solution)/shard_map/ppermute | solution.py:30
  75.8 6.9 %collective-permute-done.4 = f32[1,8,2,128,32]{3,4,2,1,0:T(8,128)} collective-permute-done((f32[1,8,2,128,32]{3,4,2,1,0:T(8,128)}, f32[1,8,2,128,32]{3,4,2,1,0:T(8,128)}, u32[]{:S(2)}, u32[]{:S(2)}) %collective-permute-start.4) | collective-permute-done | bytes 262176 | tf_op jit(solution)/shard_map/ppermute | solution.py:30
  82.7 4.4 %collective-permute-done.5 = f32[1,8,2,128,32]{3,4,2,1,0:T(8,128)} collective-permute-done((f32[1,8,2,128,32]{3,4,2,1,0:T(8,128)}, f32[1,8,2,128,32]{3,4,2,1,0:T(8,128)}, u32[]{:S(2)}, u32[]{:S(2)}) %collective-permute-start.5) | collective-permute-done | bytes 262176 | tf_op jit(solution)/shard_map/ppermute | solution.py:30
  90.2 6.1 %collective-permute-done.6 = f32[4,2,128,32]{2,3,1,0:T(8,128)S(1)} collective-permute-done((f32[4,2,128,32]{2,3,1,0:T(8,128)S(1)}, f32[4,2,128,32]{2,3,1,0:T(8,128)S(1)}, u32[]{:S(2)}, u32[]{:S(2)}) %collective-permute-start.6) | collective-permute-done | bytes 131104 | tf_op jit(solution)/shard_map/ppermute | solution.py:15
  98.2 4.7 %collective-permute-done.7 = f32[2,2,128,32]{2,3,1,0:T(8,128)S(1)} collective-permute-done((f32[2,2,128,32]{2,3,1,0:T(8,128)S(1)}, f32[2,2,128,32]{2,3,1,0:T(8,128)S(1)}, u32[]{:S(2)}, u32[]{:S(2)}) %collective-permute-start.7) | collective-permute-done | bytes 65568 | tf_op jit(solution)/shard_map/ppermute | solution.py:15
  102.9 5.7 %collective-permute-start.8 = (f32[1,2,128,32]{2,3,1,0:T(8,128)S(1)}, f32[1,2,128,32]{2,3,1,0:T(8,128)S(1)}, u32[]{:S(2)}, u32[]{:S(2)}) collective-permute-start(f32[1,2,128,32]{2,3,1,0:T(8,128)S(1)} %slice.304), channel_id=1, source_target_pairs={{4,0},{8,4},{12,8},{16,12},{20,16},{24,20},{28,24},{32,28},{36,32}... | collective-permute-start | bytes 98312 | tf_op jit(solution)/shard_map/ppermute | solution.py:15
  108.7 3.2 %collective-permute-done.8 = f32[1,2,128,32]{2,3,1,0:T(8,128)S(1)} collective-permute-done((f32[1,2,128,32]{2,3,1,0:T(8,128)S(1)}, f32[1,2,128,32]{2,3,1,0:T(8,128)S(1)}, u32[]{:S(2)}, u32[]{:S(2)}) %collective-permute-start.8) | collective-permute-done | bytes 32800 | tf_op jit(solution)/shard_map/ppermute | solution.py:15
  122.6 2.6 %collective-permute-done.10 = bf16[16,5120]{1,0:T(8,128)(2,1)S(1)} collective-permute-done((bf16[16,5120]{1,0:T(8,128)(2,1)S(1)}, bf16[16,5120]{1,0:T(8,128)(2,1)S(1)}, u32[]{:S(2)}, u32[]{:S(2)}) %collective-permute-start.10) | collective-permute-done | bytes 163872 | tf_op jit(solution)/shard_map/ppermute | solution.py:30
  125.2 2.6 %collective-permute-done.11 = bf16[16,5120]{1,0:T(8,128)(2,1)S(1)} collective-permute-done((bf16[16,5120]{1,0:T(8,128)(2,1)S(1)}, bf16[16,5120]{1,0:T(8,128)(2,1)S(1)}, u32[]{:S(2)}, u32[]{:S(2)}) %collective-permute-start.11) | collective-permute-done | bytes 163872 | tf_op jit(solution)/shard_map/ppermute | solution.py:30
  128.3 5.4 %collective-permute-start.12 = (f32[32768]{0:T(1024)S(1)}, f32[32768]{0:T(1024)S(1)}, u32[]{:S(2)}, u32[]{:S(2)}) collective-permute-start(f32[32768]{0:T(1024)S(1)} %get-tuple-element.56), channel_id=1, source_target_pairs={{0,16},{4,20},{8,24},{12,28},{16,0},{20,4},{24,8},{28,12},{32,48},... | collective-permute-start | bytes 393224 | tf_op jit(solution)/shard_map/ppermute | solution.py:30
  138.2 3.5 %collective-permute-done.14 = f32[32768]{0:T(1024)S(1)} collective-permute-done((f32[32768]{0:T(1024)S(1)}, f32[32768]{0:T(1024)S(1)}, u32[]{:S(2)}, u32[]{:S(2)}) %collective-permute-start.14) | collective-permute-done | bytes 131104 | tf_op jit(solution)/shard_map/ppermute | solution.py:30
  143.9 10.4 %collective-permute-start.15 = (f32[20480]{0:T(1024)S(1)}, f32[20480]{0:T(1024)S(1)}, u32[]{:S(2)}, u32[]{:S(2)}) collective-permute-start(f32[20480]{0:T(1024)S(1)} %get-tuple-element.48), channel_id=1, source_target_pairs={{0,64},{4,68},{8,72},{12,76},{16,80},{20,84},{24,88},{28,92},{32,9... | collective-permute-start | bytes 245768 | tf_op jit(solution)/shard_map/ppermute | solution.py:30
  155.2 2.6 %collective-permute-start.17 = (f32[20480]{0:T(1024)S(1)}, f32[20480]{0:T(1024)S(1)}, u32[]{:S(2)}, u32[]{:S(2)}) collective-permute-start(f32[20480]{0:T(1024)S(1)} %get-tuple-element.50), channel_id=1, source_target_pairs={{0,192},{4,196},{8,200},{12,204},{16,208},{20,212},{24,216},{28,22... | collective-permute-start | bytes 245768 | tf_op jit(solution)/shard_map/ppermute | solution.py:30
  158.2 3.4 %collective-permute-done.16 = f32[20480]{0:T(1024)S(1)} collective-permute-done((f32[20480]{0:T(1024)S(1)}, f32[20480]{0:T(1024)S(1)}, u32[]{:S(2)}, u32[]{:S(2)}) %collective-permute-start.16) | collective-permute-done | bytes 81952 | tf_op jit(solution)/shard_map/ppermute | solution.py:30
  162.4 5.0 %collective-permute-start.21 = (f32[16,1024]{1,0:T(8,128)S(1)}, f32[16,1024]{1,0:T(8,128)S(1)}, u32[]{:S(2)}, u32[]{:S(2)}) collective-permute-start(f32[16,1024]{1,0:T(8,128)S(1)} %fusion.53), channel_id=1, source_target_pairs={{0,4},{4,0},{8,12},{12,8},{16,20},{20,16},{24,28},{28,24},{32,36},... | collective-permute-start | bytes 196616 | tf_op jit(solution)/shard_map/ppermute | solution.py:30
  170.1 2.5 %collective-permute-start.20 = (f32[1,64,2,32]{1,3,2,0:T(8,128)S(1)}, f32[1,64,2,32]{1,3,2,0:T(8,128)S(1)}, u32[]{:S(2)}, u32[]{:S(2)}) collective-permute-start(f32[1,64,2,32]{1,3,2,0:T(8,128)S(1)} %add_add_fusion), channel_id=1, source_target_pairs={{0,3},{1,2},{2,1},{3,0},{4,7},{5,6},{6,5},{7,4},{8,11},{9,10},{10,... | collective-permute-start | bytes 49160 | tf_op jit(solution)/shard_map/ppermute | solution.py:30
  172.9 2.3 %collective-permute-start.23 = (f32[16,1024]{1,0:T(8,128)S(1)}, f32[16,1024]{1,0:T(8,128)S(1)}, u32[]{:S(2)}, u32[]{:S(2)}) collective-permute-start(f32[16,1024]{1,0:T(8,128)S(1)} %fusion.53), channel_id=1, source_target_pairs={{0,12},{4,8},{8,4},{12,0},{16,28},{20,24},{24,20},{28,16},{32,44},... | collective-permute-start | bytes 196616 | tf_op jit(solution)/shard_map/ppermute | solution.py:30
  (169 shorter events, 49.8 us)
Async XLA Ops:
  5.1 7.2 %collective-permute-start = (bf16[1,2,128,384]{2,3,0,1:T(8,128)(2,1)S(1)}, bf16[1,2,128,384]{2,3,0,1:T(8,128)(2,1)S(1)}, u32[]{:S(2)}, u32[]{:S(2)}) collective-permute-start(bf16[1,2,128,384]{2,3,0,1:T(8,128)(2,1)S(1)} %maximum_bitcast_fusion.4), channel_id=1, source_target_pairs={{0,4},{4,8},{8,12},{12,16},{16,20},{20,24},{24,28},{28,32},{32,36}... | collective-permute-start | bytes 589832 | tf_op jit(solution)/shard_map/ppermute | solution.py:15
  12.3 10.4 %collective-permute-start.1 = (bf16[2,2,128,384]{2,3,0,1:T(8,128)(2,1)S(1)}, bf16[2,2,128,384]{2,3,0,1:T(8,128)(2,1)S(1)}, u32[]{:S(2)}, u32[]{:S(2)}) collective-permute-start(bf16[2,2,128,384]{2,3,0,1:T(8,128)(2,1)S(1)} %pad_maximum_fusion.2), channel_id=1, source_target_pairs={{0,8},{4,12},{8,16},{12,20},{16,24},{20,28},{24,32},{28,36},{32,40... | collective-permute-start | bytes 1179656 | tf_op jit(solution)/shard_map/ppermute | solution.py:15
  22.7 19.6 %collective-permute-start.2 = (bf16[4,2,128,384]{2,3,0,1:T(8,128)(2,1)S(1)}, bf16[4,2,128,384]{2,3,0,1:T(8,128)(2,1)S(1)}, u32[]{:S(2)}, u32[]{:S(2)}) collective-permute-start(bf16[4,2,128,384]{2,3,0,1:T(8,128)(2,1)S(1)} %pad_maximum_fusion.1), channel_id=1, source_target_pairs={{0,16},{4,20},{8,24},{12,28},{16,32},{20,36},{24,40},{28,44},{32,4... | collective-permute-start | bytes 2359304 | tf_op jit(solution)/shard_map/ppermute | solution.py:15
  70.3 5.5 %collective-permute-start.3 = (f32[1,8,2,128,32]{3,4,2,1,0:T(8,128)}, f32[1,8,2,128,32]{3,4,2,1,0:T(8,128)}, u32[]{:S(2)}, u32[]{:S(2)}) collective-permute-start(f32[1,8,2,128,32]{3,4,2,1,0:T(8,128)} %bitcast.139), channel_id=1, source_target_pairs={{0,1},{1,0},{2,3},{3,2},{4,5},{5,4},{6,7},{7,6},{8,9},{9,8},{10,11... | collective-permute-start | bytes 786440 | tf_op jit(solution)/shard_map/ppermute | solution.py:30
  72.2 10.4 %collective-permute-start.4 = (f32[1,8,2,128,32]{3,4,2,1,0:T(8,128)}, f32[1,8,2,128,32]{3,4,2,1,0:T(8,128)}, u32[]{:S(2)}, u32[]{:S(2)}) collective-permute-start(f32[1,8,2,128,32]{3,4,2,1,0:T(8,128)} %bitcast.138), channel_id=1, source_target_pairs={{0,2},{1,3},{2,0},{3,1},{4,6},{5,7},{6,4},{7,5},{8,10},{9,11},{10,... | collective-permute-start | bytes 786440 | tf_op jit(solution)/shard_map/ppermute | solution.py:30
  75.4 11.7 %collective-permute-start.5 = (f32[1,8,2,128,32]{3,4,2,1,0:T(8,128)}, f32[1,8,2,128,32]{3,4,2,1,0:T(8,128)}, u32[]{:S(2)}, u32[]{:S(2)}) collective-permute-start(f32[1,8,2,128,32]{3,4,2,1,0:T(8,128)} %bitcast.137), channel_id=1, source_target_pairs={{0,3},{1,2},{2,1},{3,0},{4,7},{5,6},{6,5},{7,4},{8,11},{9,10},{10,... | collective-permute-start | bytes 786440 | tf_op jit(solution)/shard_map/ppermute | solution.py:30
  88.4 8.0 %collective-permute-start.6 = (f32[4,2,128,32]{2,3,1,0:T(8,128)S(1)}, f32[4,2,128,32]{2,3,1,0:T(8,128)S(1)}, u32[]{:S(2)}, u32[]{:S(2)}) collective-permute-start(f32[4,2,128,32]{2,3,1,0:T(8,128)S(1)} %slice_bitcast_fusion), channel_id=1, source_target_pairs={{16,0},{20,4},{24,8},{28,12},{32,16},{36,20},{40,24},{44,28},{48,3... | collective-permute-start | bytes 393224 | tf_op jit(solution)/shard_map/ppermute | solution.py:15
  96.4 6.5 %collective-permute-start.7 = (f32[2,2,128,32]{2,3,1,0:T(8,128)S(1)}, f32[2,2,128,32]{2,3,1,0:T(8,128)S(1)}, u32[]{:S(2)}, u32[]{:S(2)}) collective-permute-start(f32[2,2,128,32]{2,3,1,0:T(8,128)S(1)} %slice.302), channel_id=1, source_target_pairs={{8,0},{12,4},{16,8},{20,12},{24,16},{28,20},{32,24},{36,28},{40,32... | collective-permute-start | bytes 196616 | tf_op jit(solution)/shard_map/ppermute | solution.py:15
  102.9 9.1 %collective-permute-start.8 = (f32[1,2,128,32]{2,3,1,0:T(8,128)S(1)}, f32[1,2,128,32]{2,3,1,0:T(8,128)S(1)}, u32[]{:S(2)}, u32[]{:S(2)}) collective-permute-start(f32[1,2,128,32]{2,3,1,0:T(8,128)S(1)} %slice.304), channel_id=1, source_target_pairs={{4,0},{8,4},{12,8},{16,12},{20,16},{24,20},{28,24},{32,28},{36,32}... | collective-permute-start | bytes 98312 | tf_op jit(solution)/shard_map/ppermute | solution.py:15
  119.3 5.9 %collective-permute-start.10 = (bf16[16,5120]{1,0:T(8,128)(2,1)S(1)}, bf16[16,5120]{1,0:T(8,128)(2,1)S(1)}, u32[]{:S(2)}, u32[]{:S(2)}) collective-permute-start(bf16[16,5120]{1,0:T(8,128)(2,1)S(1)} %bitcast.157), channel_id=1, source_target_pairs={{0,8},{4,12},{8,0},{12,4},{16,24},{20,28},{24,16},{28,20},{32,40},... | collective-permute-start | bytes 491528 | tf_op jit(solution)/shard_map/ppermute | solution.py:30
  121.6 6.2 %collective-permute-start.11 = (bf16[16,5120]{1,0:T(8,128)(2,1)S(1)}, bf16[16,5120]{1,0:T(8,128)(2,1)S(1)}, u32[]{:S(2)}, u32[]{:S(2)}) collective-permute-start(bf16[16,5120]{1,0:T(8,128)(2,1)S(1)} %bitcast.158), channel_id=1, source_target_pairs={{0,12},{4,8},{8,4},{12,0},{16,28},{20,24},{24,20},{28,16},{32,44},... | collective-permute-start | bytes 491528 | tf_op jit(solution)/shard_map/ppermute | solution.py:30
  121.7 6.0 %collective-permute-start.9 = (bf16[16,5120]{1,0:T(8,128)(2,1)S(1)}, bf16[16,5120]{1,0:T(8,128)(2,1)S(1)}, u32[]{:S(2)}, u32[]{:S(2)}) collective-permute-start(bf16[16,5120]{1,0:T(8,128)(2,1)S(1)} %bitcast.159), channel_id=1, source_target_pairs={{0,4},{4,0},{8,12},{12,8},{16,20},{20,16},{24,28},{28,24},{32,36},... | collective-permute-start | bytes 491528 | tf_op jit(solution)/shard_map/ppermute | solution.py:30
  128.3 7.8 %collective-permute-start.12 = (f32[32768]{0:T(1024)S(1)}, f32[32768]{0:T(1024)S(1)}, u32[]{:S(2)}, u32[]{:S(2)}) collective-permute-start(f32[32768]{0:T(1024)S(1)} %get-tuple-element.56), channel_id=1, source_target_pairs={{0,16},{4,20},{8,24},{12,28},{16,0},{20,4},{24,8},{28,12},{32,48},... | collective-permute-start | bytes 393224 | tf_op jit(solution)/shard_map/ppermute | solution.py:30
  133.7 4.4 %collective-permute-start.13 = (f32[32768]{0:T(1024)S(1)}, f32[32768]{0:T(1024)S(1)}, u32[]{:S(2)}, u32[]{:S(2)}) collective-permute-start(f32[32768]{0:T(1024)S(1)} %get-tuple-element.57), channel_id=1, source_target_pairs={{0,32},{4,36},{8,40},{12,44},{16,48},{20,52},{24,56},{28,60},{32,0... | collective-permute-start | bytes 393224 | tf_op jit(solution)/shard_map/ppermute | solution.py:30
  135.5 6.2 %collective-permute-start.14 = (f32[32768]{0:T(1024)S(1)}, f32[32768]{0:T(1024)S(1)}, u32[]{:S(2)}, u32[]{:S(2)}) collective-permute-start(f32[32768]{0:T(1024)S(1)} %get-tuple-element.58), channel_id=1, source_target_pairs={{0,48},{4,52},{8,56},{12,60},{16,32},{20,36},{24,40},{28,44},{32,1... | collective-permute-start | bytes 393224 | tf_op jit(solution)/shard_map/ppermute | solution.py:30
  143.9 14.3 %collective-permute-start.15 = (f32[20480]{0:T(1024)S(1)}, f32[20480]{0:T(1024)S(1)}, u32[]{:S(2)}, u32[]{:S(2)}) collective-permute-start(f32[20480]{0:T(1024)S(1)} %get-tuple-element.48), channel_id=1, source_target_pairs={{0,64},{4,68},{8,72},{12,76},{16,80},{20,84},{24,88},{28,92},{32,9... | collective-permute-start | bytes 245768 | tf_op jit(solution)/shard_map/ppermute | solution.py:30
  154.4 7.2 %collective-permute-start.16 = (f32[20480]{0:T(1024)S(1)}, f32[20480]{0:T(1024)S(1)}, u32[]{:S(2)}, u32[]{:S(2)}) collective-permute-start(f32[20480]{0:T(1024)S(1)} %get-tuple-element.49), channel_id=1, source_target_pairs={{0,128},{4,132},{8,136},{12,140},{16,144},{20,148},{24,152},{28,15... | collective-permute-start | bytes 245768 | tf_op jit(solution)/shard_map/ppermute | solution.py:30
  155.2 6.4 %collective-permute-start.17 = (f32[20480]{0:T(1024)S(1)}, f32[20480]{0:T(1024)S(1)}, u32[]{:S(2)}, u32[]{:S(2)}) collective-permute-start(f32[20480]{0:T(1024)S(1)} %get-tuple-element.50), channel_id=1, source_target_pairs={{0,192},{4,196},{8,200},{12,204},{16,208},{20,212},{24,216},{28,22... | collective-permute-start | bytes 245768 | tf_op jit(solution)/shard_map/ppermute | solution.py:30
  162.4 15.0 %collective-permute-start.21 = (f32[16,1024]{1,0:T(8,128)S(1)}, f32[16,1024]{1,0:T(8,128)S(1)}, u32[]{:S(2)}, u32[]{:S(2)}) collective-permute-start(f32[16,1024]{1,0:T(8,128)S(1)} %fusion.53), channel_id=1, source_target_pairs={{0,4},{4,0},{8,12},{12,8},{16,20},{20,16},{24,28},{28,24},{32,36},... | collective-permute-start | bytes 196616 | tf_op jit(solution)/shard_map/ppermute | solution.py:30
  167.3 10.0 %collective-permute-start.22 = (f32[16,1024]{1,0:T(8,128)S(1)}, f32[16,1024]{1,0:T(8,128)S(1)}, u32[]{:S(2)}, u32[]{:S(2)}) collective-permute-start(f32[16,1024]{1,0:T(8,128)S(1)} %fusion.53), channel_id=1, source_target_pairs={{0,8},{4,12},{8,0},{12,4},{16,24},{20,28},{24,16},{28,20},{32,40},... | collective-permute-start | bytes 196616 | tf_op jit(solution)/shard_map/ppermute | solution.py:30
  168.7 4.2 %collective-permute-start.18 = (f32[1,64,2,32]{1,3,2,0:T(8,128)S(1)}, f32[1,64,2,32]{1,3,2,0:T(8,128)S(1)}, u32[]{:S(2)}, u32[]{:S(2)}) collective-permute-start(f32[1,64,2,32]{1,3,2,0:T(8,128)S(1)} %add_add_fusion), channel_id=1, source_target_pairs={{0,1},{1,0},{2,3},{3,2},{4,5},{5,4},{6,7},{7,6},{8,9},{9,8},{10,11... | collective-permute-start | bytes 49160 | tf_op jit(solution)/shard_map/ppermute | solution.py:30
  168.8 6.5 %collective-permute-start.19 = (f32[1,64,2,32]{1,3,2,0:T(8,128)S(1)}, f32[1,64,2,32]{1,3,2,0:T(8,128)S(1)}, u32[]{:S(2)}, u32[]{:S(2)}) collective-permute-start(f32[1,64,2,32]{1,3,2,0:T(8,128)S(1)} %add_add_fusion), channel_id=1, source_target_pairs={{0,2},{1,3},{2,0},{3,1},{4,6},{5,7},{6,4},{7,5},{8,10},{9,11},{10,... | collective-permute-start | bytes 49160 | tf_op jit(solution)/shard_map/ppermute | solution.py:30
  170.1 5.1 %collective-permute-start.20 = (f32[1,64,2,32]{1,3,2,0:T(8,128)S(1)}, f32[1,64,2,32]{1,3,2,0:T(8,128)S(1)}, u32[]{:S(2)}, u32[]{:S(2)}) collective-permute-start(f32[1,64,2,32]{1,3,2,0:T(8,128)S(1)} %add_add_fusion), channel_id=1, source_target_pairs={{0,3},{1,2},{2,1},{3,0},{4,7},{5,6},{6,5},{7,4},{8,11},{9,10},{10,... | collective-permute-start | bytes 49160 | tf_op jit(solution)/shard_map/ppermute | solution.py:30
  172.9 5.2 %collective-permute-start.23 = (f32[16,1024]{1,0:T(8,128)S(1)}, f32[16,1024]{1,0:T(8,128)S(1)}, u32[]{:S(2)}, u32[]{:S(2)}) collective-permute-start(f32[16,1024]{1,0:T(8,128)S(1)} %fusion.53), channel_id=1, source_target_pairs={{0,12},{4,8},{8,4},{12,0},{16,28},{20,24},{24,20},{28,16},{32,44},... | collective-permute-start | bytes 196616 | tf_op jit(solution)/shard_map/ppermute | solution.py:30
  (9 other events, 87.0 us)

commit v13 on v10

--- a/solution.py
+++ b/solution.py
@@ -186,7 +186,7 @@
     reach = span // 2
     while reach >= 1:
         give = contrib[reach : 2 * reach]
-        if reach == span // 2:
+        if reach >= span // 4:
             give = give.astype(jnp.bfloat16)
         contrib = contrib[:reach] + passed_along(give, "wide", -reach).astype(jnp.float32)
         reach //= 2

time: 169 us -> 169 us (level)
  waiting for transfers between devices: 65.4 us -> 60 us
  other arithmetic: 4.5 us -> 7.36 us
    ppermute x6, waiting for transfers between devices: 43.3 us -> 38.5 us  [passed_along(): return lax.ppermute(array, axis, pairs)]
    add x3, other arithmetic: 0.22 us -> 2.28 us  [on_device(): contrib[:reach] + passed_along(give, 'wide', -reach).astype(jnp.float32)]
    unnamed x20 -> x22, local copies, waits for them, and re-layouts: 3.27 us -> 4.05 us
  transfers between devices with their start and end apart: 24 -> 24, of which waited for: 15 -> 16; matrix products, arithmetic and copies ran while one was open for 3% -> 3% of each run, Pallas kernels for 0% -> 0%
where the time goes in v13:
time: 169 us; the launch traced here: 168 us
  waiting for transfers between devices  60 us (36%)
  starting transfers between devices  57.3 us (34%)
  Pallas kernels  19.5 us (12%)
  local copies, waits for them, and re-layouts  17.7 us (10%)
  other arithmetic  7.36 us (4%)
  matrix products  4.04 us (2%)
  between operations  2.19 us (1%)
    ppermute x6, waiting for transfers between devices, passed_along(): return lax.ppermute(array, axis, pairs)  38.5 us
    ppermute x18, starting transfers between devices, xor_partner(): return lax.ppermute(array, axis, [(i, i ^ mask) for i in range(devices)])  34.8 us
    ppermute x6, starting transfers between devices, passed_along(): return lax.ppermute(array, axis, pairs)  22.4 us
    ppermute x18, waiting for transfers between devices, xor_partner(): return lax.ppermute(array, axis, [(i, i ^ mask) for i in range(devices)])  21.5 us
    pallas_call x1, Pallas kernels, attention_grads(): pl.pallas_call(attention_body, grid_spec=grid_spec, out_shape=[jax.ShapeD...  19.5 us
    unnamed x22, local copies, waits for them, and re-layouts  4.05 us
  transfers between devices with their start and end apart: 24, of which 16 were waited for; matrix products, arithmetic and copies ran while one was open for 3% of the time, Pallas kernels for 0%

profile of v13, /device:TPU:1, one launch (start us, length us, event | category | flops | bytes accessed | tf_op | source)
XLA Modules:
  0.0 168.0 jit_solution(5790805157925843481)
XLA Ops:
  1.6 4.6 %collective-permute-start = (bf16[1,2,128,256]{3,2,1,0:T(8,128)(2,1)S(1)}, bf16[1,2,128,256]{3,2,1,0:T(8,128)(2,1)S(1)}, u32[]{:S(2)}, u32[]{:S(2)}) collective-permute-start(bf16[1,2,128,256]{3,2,1,0:T(8,128)(2,1)S(1)} %maximum_bitcast_fusion), channel_id=1, source_target_pairs={{0,4},{4,8},{8,12},{12,16},{16,20},{20,24},{24,28},{28,32},{32,36}... | collective-permute-start | bytes 393224 | tf_op jit(solution)/shard_map/ppermute | solution.py:15
  6.2 1.9 %collective-permute-done = bf16[1,2,128,256]{3,2,1,0:T(8,128)(2,1)S(1)} collective-permute-done((bf16[1,2,128,256]{3,2,1,0:T(8,128)(2,1)S(1)}, bf16[1,2,128,256]{3,2,1,0:T(8,128)(2,1)S(1)}, u32[]{:S(2)}, u32[]{:S(2)}) %collective-permute-start) | collective-permute-done | bytes 131104 | tf_op jit(solution)/shard_map/ppermute | solution.py:15
  8.2 3.2 %collective-permute-start.1 = (bf16[2,2,128,256]{3,2,1,0:T(8,128)(2,1)S(1)}, bf16[2,2,128,256]{3,2,1,0:T(8,128)(2,1)S(1)}, u32[]{:S(2)}, u32[]{:S(2)}) collective-permute-start(bf16[2,2,128,256]{3,2,1,0:T(8,128)(2,1)S(1)} %pad_maximum_fusion.3), channel_id=1, source_target_pairs={{0,8},{4,12},{8,16},{12,20},{16,24},{20,28},{24,32},{28,36},{32,40... | collective-permute-start | bytes 786440 | tf_op jit(solution)/shard_map/ppermute | solution.py:15
  11.4 4.4 %collective-permute-done.1 = bf16[2,2,128,256]{3,2,1,0:T(8,128)(2,1)S(1)} collective-permute-done((bf16[2,2,128,256]{3,2,1,0:T(8,128)(2,1)S(1)}, bf16[2,2,128,256]{3,2,1,0:T(8,128)(2,1)S(1)}, u32[]{:S(2)}, u32[]{:S(2)}) %collective-permute-start.1) | collective-permute-done | bytes 262176 | tf_op jit(solution)/shard_map/ppermute | solution.py:15
  15.8 5.2 %collective-permute-start.2 = (bf16[4,2,128,256]{3,2,1,0:T(8,128)(2,1)S(1)}, bf16[4,2,128,256]{3,2,1,0:T(8,128)(2,1)S(1)}, u32[]{:S(2)}, u32[]{:S(2)}) collective-permute-start(bf16[4,2,128,256]{3,2,1,0:T(8,128)(2,1)S(1)} %pad_maximum_fusion.2), channel_id=1, source_target_pairs={{0,16},{4,20},{8,24},{12,28},{16,32},{20,36},{24,40},{28,44},{32,4... | collective-permute-start | bytes 1572872 | tf_op jit(solution)/shard_map/ppermute | solution.py:15
  22.6 7.3 %collective-permute-done.2 = bf16[4,2,128,256]{3,2,1,0:T(8,128)(2,1)S(1)} collective-permute-done((bf16[4,2,128,256]{3,2,1,0:T(8,128)(2,1)S(1)}, bf16[4,2,128,256]{3,2,1,0:T(8,128)(2,1)S(1)}, u32[]{:S(2)}, u32[]{:S(2)}) %collective-permute-start.2) | collective-permute-done | bytes 524320 | tf_op jit(solution)/shard_map/ppermute | solution.py:15
  31.0 19.5 %shard_map.129 = (f32[1024,256]{1,0:T(8,128)}, f32[1024,256]{1,0:T(8,128)}) custom-call(s32[1]{0:T(128)} %bitcast.1.pos_ref, bf16[512,1024]{1,0:T(8,128)(2,1)} %q_ref.1, bf16[512,1024]{1,0:T(8,128)(2,1)} %do_ref.1, bf16[1024,256]{1,0:T(8,128)(2,1)} %bitcast.116, bf16[1024,256]{1,0:T(8,128)(2,1)} %bitcast.115), custom_call_target="tpu_custom_call" | custom-call | tf_op jit(solution)/shard_map/pallas_call | solution.py:146
  54.2 13.6 %collective-permute-done.3 = bf16[4,2,128,256]{3,2,1,0:T(8,128)(2,1)} collective-permute-done((bf16[4,2,128,256]{3,2,1,0:T(8,128)(2,1)}, bf16[4,2,128,256]{3,2,1,0:T(8,128)(2,1)}, u32[]{:S(2)}, u32[]{:S(2)}) %collective-permute-start.3) | collective-permute-done | bytes 524320 | tf_op jit(solution)/shard_map/ppermute | solution.py:15
  71.4 5.7 %collective-permute-done.4 = bf16[2,2,128,256]{3,2,1,0:T(8,128)(2,1)S(1)} collective-permute-done((bf16[2,2,128,256]{3,2,1,0:T(8,128)(2,1)S(1)}, bf16[2,2,128,256]{3,2,1,0:T(8,128)(2,1)S(1)}, u32[]{:S(2)}, u32[]{:S(2)}) %collective-permute-start.4) | collective-permute-done | bytes 262176 | tf_op jit(solution)/shard_map/ppermute | solution.py:15
  78.2 6.9 %collective-permute-start.5 = (f32[1,2,128,256]{3,2,1,0:T(8,128)S(1)}, f32[1,2,128,256]{3,2,1,0:T(8,128)S(1)}, u32[]{:S(2)}, u32[]{:S(2)}) collective-permute-start(f32[1,2,128,256]{3,2,1,0:T(8,128)S(1)} %slice.285), channel_id=1, source_target_pairs={{4,0},{8,4},{12,8},{16,12},{20,16},{24,20},{28,24},{32,28},{36,32}... | collective-permute-start | bytes 786440 | tf_op jit(solution)/shard_map/ppermute | solution.py:15
  85.3 5.6 %collective-permute-done.5 = f32[1,2,128,256]{3,2,1,0:T(8,128)S(1)} collective-permute-done((f32[1,2,128,256]{3,2,1,0:T(8,128)S(1)}, f32[1,2,128,256]{3,2,1,0:T(8,128)S(1)}, u32[]{:S(2)}, u32[]{:S(2)}) %collective-permute-start.5) | collective-permute-done | bytes 262176 | tf_op jit(solution)/shard_map/ppermute | solution.py:15
  95.1 2.5 %collective-permute-start.7 = (f32[1,128,64]{1,2,0:T(8,128)S(1)}, f32[1,128,64]{1,2,0:T(8,128)S(1)}, u32[]{:S(2)}, u32[]{:S(2)}) collective-permute-start(f32[1,128,64]{1,2,0:T(8,128)S(1)} %get-tuple-element.45), channel_id=1, source_target_pairs={{0,2},{1,3},{2,0},{3,1},{4,6},{5,7},{6,4},{7,5},{8,10},{9,11},{10,... | collective-permute-start | bytes 98312 | tf_op jit(solution)/shard_map/ppermute | solution.py:30
  99.4 2.2 %collective-permute-done.8 = f32[1,128,64]{1,2,0:T(8,128)S(1)} collective-permute-done((f32[1,128,64]{1,2,0:T(8,128)S(1)}, f32[1,128,64]{1,2,0:T(8,128)S(1)}, u32[]{:S(2)}, u32[]{:S(2)}) %collective-permute-start.8) | collective-permute-done | bytes 32800 | tf_op jit(solution)/shard_map/ppermute | solution.py:30
  112.0 3.4 %collective-permute-done.10 = bf16[16,5120]{1,0:T(8,128)(2,1)S(1)} collective-permute-done((bf16[16,5120]{1,0:T(8,128)(2,1)S(1)}, bf16[16,5120]{1,0:T(8,128)(2,1)S(1)}, u32[]{:S(2)}, u32[]{:S(2)}) %collective-permute-start.10) | collective-permute-done | bytes 163872 | tf_op jit(solution)/shard_map/ppermute | solution.py:30
  115.4 3.5 %collective-permute-done.11 = bf16[16,5120]{1,0:T(8,128)(2,1)S(1)} collective-permute-done((bf16[16,5120]{1,0:T(8,128)(2,1)S(1)}, bf16[16,5120]{1,0:T(8,128)(2,1)S(1)}, u32[]{:S(2)}, u32[]{:S(2)}) %collective-permute-start.11) | collective-permute-done | bytes 163872 | tf_op jit(solution)/shard_map/ppermute | solution.py:30
  119.5 5.5 %collective-permute-start.12 = (f32[32768]{0:T(1024)S(1)}, f32[32768]{0:T(1024)S(1)}, u32[]{:S(2)}, u32[]{:S(2)}) collective-permute-start(f32[32768]{0:T(1024)S(1)} %get-tuple-element.55), channel_id=1, source_target_pairs={{0,16},{4,20},{8,24},{12,28},{16,0},{20,4},{24,8},{28,12},{32,48},... | collective-permute-start | bytes 393224 | tf_op jit(solution)/shard_map/ppermute | solution.py:30
  130.0 3.3 %collective-permute-done.14 = f32[32768]{0:T(1024)S(1)} collective-permute-done((f32[32768]{0:T(1024)S(1)}, f32[32768]{0:T(1024)S(1)}, u32[]{:S(2)}, u32[]{:S(2)}) %collective-permute-start.14) | collective-permute-done | bytes 131104 | tf_op jit(solution)/shard_map/ppermute | solution.py:30
  135.6 7.9 %collective-permute-start.15 = (f32[20480]{0:T(1024)S(1)}, f32[20480]{0:T(1024)S(1)}, u32[]{:S(2)}, u32[]{:S(2)}) collective-permute-start(f32[20480]{0:T(1024)S(1)} %get-tuple-element.47), channel_id=1, source_target_pairs={{0,64},{4,68},{8,72},{12,76},{16,80},{20,84},{24,88},{28,92},{32,9... | collective-permute-start | bytes 245768 | tf_op jit(solution)/shard_map/ppermute | solution.py:30
  143.5 3.4 %collective-permute-start.17 = (f32[20480]{0:T(1024)S(1)}, f32[20480]{0:T(1024)S(1)}, u32[]{:S(2)}, u32[]{:S(2)}) collective-permute-start(f32[20480]{0:T(1024)S(1)} %get-tuple-element.49), channel_id=1, source_target_pairs={{0,192},{4,196},{8,200},{12,204},{16,208},{20,212},{24,216},{28,22... | collective-permute-start | bytes 245768 | tf_op jit(solution)/shard_map/ppermute | solution.py:30
  147.3 2.1 %collective-permute-done.15 = f32[20480]{0:T(1024)S(1)} collective-permute-done((f32[20480]{0:T(1024)S(1)}, f32[20480]{0:T(1024)S(1)}, u32[]{:S(2)}, u32[]{:S(2)}) %collective-permute-start.15) | collective-permute-done | bytes 81952 | tf_op jit(solution)/shard_map/ppermute | solution.py:30
  149.4 2.1 %collective-permute-done.16 = f32[20480]{0:T(1024)S(1)} collective-permute-done((f32[20480]{0:T(1024)S(1)}, f32[20480]{0:T(1024)S(1)}, u32[]{:S(2)}, u32[]{:S(2)}) %collective-permute-start.16) | collective-permute-done | bytes 81952 | tf_op jit(solution)/shard_map/ppermute | solution.py:30
  152.3 3.2 %collective-permute-start.21 = (f32[16,1024]{1,0:T(8,128)S(1)}, f32[16,1024]{1,0:T(8,128)S(1)}, u32[]{:S(2)}, u32[]{:S(2)}) collective-permute-start(f32[16,1024]{1,0:T(8,128)S(1)} %fusion.40), channel_id=1, source_target_pairs={{0,4},{4,0},{8,12},{12,8},{16,20},{20,16},{24,28},{28,24},{32,36},... | collective-permute-start | bytes 196616 | tf_op jit(solution)/shard_map/ppermute | solution.py:30
  158.4 2.0 %collective-permute-start.20 = (f32[1,64,2,32]{1,3,2,0:T(8,128)S(1)}, f32[1,64,2,32]{1,3,2,0:T(8,128)S(1)}, u32[]{:S(2)}, u32[]{:S(2)}) collective-permute-start(f32[1,64,2,32]{1,3,2,0:T(8,128)S(1)} %add_add_fusion), channel_id=1, source_target_pairs={{0,3},{1,2},{2,1},{3,0},{4,7},{5,6},{6,5},{7,4},{8,11},{9,10},{10,... | collective-permute-start | bytes 49160 | tf_op jit(solution)/shard_map/ppermute | solution.py:30
  160.7 2.7 %collective-permute-start.23 = (f32[16,1024]{1,0:T(8,128)S(1)}, f32[16,1024]{1,0:T(8,128)S(1)}, u32[]{:S(2)}, u32[]{:S(2)}) collective-permute-start(f32[16,1024]{1,0:T(8,128)S(1)} %fusion.40), channel_id=1, source_target_pairs={{0,12},{4,8},{8,4},{12,0},{16,28},{20,24},{24,20},{28,16},{32,44},... | collective-permute-start | bytes 196616 | tf_op jit(solution)/shard_map/ppermute | solution.py:30
  (154 shorter events, 44.3 us)
Async XLA Ops:
  1.6 6.5 %collective-permute-start = (bf16[1,2,128,256]{3,2,1,0:T(8,128)(2,1)S(1)}, bf16[1,2,128,256]{3,2,1,0:T(8,128)(2,1)S(1)}, u32[]{:S(2)}, u32[]{:S(2)}) collective-permute-start(bf16[1,2,128,256]{3,2,1,0:T(8,128)(2,1)S(1)} %maximum_bitcast_fusion), channel_id=1, source_target_pairs={{0,4},{4,8},{8,12},{12,16},{16,20},{20,24},{24,28},{28,32},{32,36}... | collective-permute-start | bytes 393224 | tf_op jit(solution)/shard_map/ppermute | solution.py:15
  8.2 7.6 %collective-permute-start.1 = (bf16[2,2,128,256]{3,2,1,0:T(8,128)(2,1)S(1)}, bf16[2,2,128,256]{3,2,1,0:T(8,128)(2,1)S(1)}, u32[]{:S(2)}, u32[]{:S(2)}) collective-permute-start(bf16[2,2,128,256]{3,2,1,0:T(8,128)(2,1)S(1)} %pad_maximum_fusion.3), channel_id=1, source_target_pairs={{0,8},{4,12},{8,16},{12,20},{16,24},{20,28},{24,32},{28,36},{32,40... | collective-permute-start | bytes 786440 | tf_op jit(solution)/shard_map/ppermute | solution.py:15
  15.8 14.0 %collective-permute-start.2 = (bf16[4,2,128,256]{3,2,1,0:T(8,128)(2,1)S(1)}, bf16[4,2,128,256]{3,2,1,0:T(8,128)(2,1)S(1)}, u32[]{:S(2)}, u32[]{:S(2)}) collective-permute-start(bf16[4,2,128,256]{3,2,1,0:T(8,128)(2,1)S(1)} %pad_maximum_fusion.2), channel_id=1, source_target_pairs={{0,16},{4,20},{8,24},{12,28},{16,32},{20,36},{24,40},{28,44},{32,4... | collective-permute-start | bytes 1572872 | tf_op jit(solution)/shard_map/ppermute | solution.py:15
  52.9 14.9 %collective-permute-start.3 = (bf16[4,2,128,256]{3,2,1,0:T(8,128)(2,1)}, bf16[4,2,128,256]{3,2,1,0:T(8,128)(2,1)}, u32[]{:S(2)}, u32[]{:S(2)}) collective-permute-start(bf16[4,2,128,256]{3,2,1,0:T(8,128)(2,1)} %fusion.2), channel_id=1, source_target_pairs={{16,0},{20,4},{24,8},{28,12},{32,16},{36,20},{40,24},{44,28},{48,3... | collective-permute-start | bytes 1572872 | tf_op jit(solution)/shard_map/ppermute | solution.py:15
  70.0 7.1 %collective-permute-start.4 = (bf16[2,2,128,256]{3,2,1,0:T(8,128)(2,1)S(1)}, bf16[2,2,128,256]{3,2,1,0:T(8,128)(2,1)S(1)}, u32[]{:S(2)}, u32[]{:S(2)}) collective-permute-start(bf16[2,2,128,256]{3,2,1,0:T(8,128)(2,1)S(1)} %slice.359), channel_id=1, source_target_pairs={{8,0},{12,4},{16,8},{20,12},{24,16},{28,20},{32,24},{36,28},{40,32... | collective-permute-start | bytes 786440 | tf_op jit(solution)/shard_map/ppermute | solution.py:15
  78.2 12.6 %collective-permute-start.5 = (f32[1,2,128,256]{3,2,1,0:T(8,128)S(1)}, f32[1,2,128,256]{3,2,1,0:T(8,128)S(1)}, u32[]{:S(2)}, u32[]{:S(2)}) collective-permute-start(f32[1,2,128,256]{3,2,1,0:T(8,128)S(1)} %slice.285), channel_id=1, source_target_pairs={{4,0},{8,4},{12,8},{16,12},{20,16},{24,20},{28,24},{32,28},{36,32}... | collective-permute-start | bytes 786440 | tf_op jit(solution)/shard_map/ppermute | solution.py:15
  93.8 4.1 %collective-permute-start.6 = (f32[1,128,64]{1,2,0:T(8,128)S(1)}, f32[1,128,64]{1,2,0:T(8,128)S(1)}, u32[]{:S(2)}, u32[]{:S(2)}) collective-permute-start(f32[1,128,64]{1,2,0:T(8,128)S(1)} %get-tuple-element.44), channel_id=1, source_target_pairs={{0,1},{1,0},{2,3},{3,2},{4,5},{5,4},{6,7},{7,6},{8,9},{9,8},{10,11... | collective-permute-start | bytes 98312 | tf_op jit(solution)/shard_map/ppermute | solution.py:30
  95.1 4.3 %collective-permute-start.7 = (f32[1,128,64]{1,2,0:T(8,128)S(1)}, f32[1,128,64]{1,2,0:T(8,128)S(1)}, u32[]{:S(2)}, u32[]{:S(2)}) collective-permute-start(f32[1,128,64]{1,2,0:T(8,128)S(1)} %get-tuple-element.45), channel_id=1, source_target_pairs={{0,2},{1,3},{2,0},{3,1},{4,6},{5,7},{6,4},{7,5},{8,10},{9,11},{10,... | collective-permute-start | bytes 98312 | tf_op jit(solution)/shard_map/ppermute | solution.py:30
  97.6 4.0 %collective-permute-start.8 = (f32[1,128,64]{1,2,0:T(8,128)S(1)}, f32[1,128,64]{1,2,0:T(8,128)S(1)}, u32[]{:S(2)}, u32[]{:S(2)}) collective-permute-start(f32[1,128,64]{1,2,0:T(8,128)S(1)} %get-tuple-element.46), channel_id=1, source_target_pairs={{0,3},{1,2},{2,1},{3,0},{4,7},{5,6},{6,5},{7,4},{8,11},{9,10},{10,... | collective-permute-start | bytes 98312 | tf_op jit(solution)/shard_map/ppermute | solution.py:30
  108.9 6.5 %collective-permute-start.10 = (bf16[16,5120]{1,0:T(8,128)(2,1)S(1)}, bf16[16,5120]{1,0:T(8,128)(2,1)S(1)}, u32[]{:S(2)}, u32[]{:S(2)}) collective-permute-start(bf16[16,5120]{1,0:T(8,128)(2,1)S(1)} %bitcast.123), channel_id=1, source_target_pairs={{0,8},{4,12},{8,0},{12,4},{16,24},{20,28},{24,16},{28,20},{32,40},... | collective-permute-start | bytes 491528 | tf_op jit(solution)/shard_map/ppermute | solution.py:30
  110.8 8.1 %collective-permute-start.11 = (bf16[16,5120]{1,0:T(8,128)(2,1)S(1)}, bf16[16,5120]{1,0:T(8,128)(2,1)S(1)}, u32[]{:S(2)}, u32[]{:S(2)}) collective-permute-start(bf16[16,5120]{1,0:T(8,128)(2,1)S(1)} %bitcast.124), channel_id=1, source_target_pairs={{0,12},{4,8},{8,4},{12,0},{16,28},{20,24},{24,20},{28,16},{32,44},... | collective-permute-start | bytes 491528 | tf_op jit(solution)/shard_map/ppermute | solution.py:30
  111.0 8.0 %collective-permute-start.9 = (bf16[16,5120]{1,0:T(8,128)(2,1)S(1)}, bf16[16,5120]{1,0:T(8,128)(2,1)S(1)}, u32[]{:S(2)}, u32[]{:S(2)}) collective-permute-start(bf16[16,5120]{1,0:T(8,128)(2,1)S(1)} %bitcast.125), channel_id=1, source_target_pairs={{0,4},{4,0},{8,12},{12,8},{16,20},{20,16},{24,28},{28,24},{32,36},... | collective-permute-start | bytes 491528 | tf_op jit(solution)/shard_map/ppermute | solution.py:30
  119.5 9.1 %collective-permute-start.12 = (f32[32768]{0:T(1024)S(1)}, f32[32768]{0:T(1024)S(1)}, u32[]{:S(2)}, u32[]{:S(2)}) collective-permute-start(f32[32768]{0:T(1024)S(1)} %get-tuple-element.55), channel_id=1, source_target_pairs={{0,16},{4,20},{8,24},{12,28},{16,0},{20,4},{24,8},{28,12},{32,48},... | collective-permute-start | bytes 393224 | tf_op jit(solution)/shard_map/ppermute | solution.py:30
  125.0 4.9 %collective-permute-start.13 = (f32[32768]{0:T(1024)S(1)}, f32[32768]{0:T(1024)S(1)}, u32[]{:S(2)}, u32[]{:S(2)}) collective-permute-start(f32[32768]{0:T(1024)S(1)} %get-tuple-element.56), channel_id=1, source_target_pairs={{0,32},{4,36},{8,40},{12,44},{16,48},{20,52},{24,56},{28,60},{32,0... | collective-permute-start | bytes 393224 | tf_op jit(solution)/shard_map/ppermute | solution.py:30
  126.8 6.6 %collective-permute-start.14 = (f32[32768]{0:T(1024)S(1)}, f32[32768]{0:T(1024)S(1)}, u32[]{:S(2)}, u32[]{:S(2)}) collective-permute-start(f32[32768]{0:T(1024)S(1)} %get-tuple-element.57), channel_id=1, source_target_pairs={{0,48},{4,52},{8,56},{12,60},{16,32},{20,36},{24,40},{28,44},{32,1... | collective-permute-start | bytes 393224 | tf_op jit(solution)/shard_map/ppermute | solution.py:30
  135.6 13.8 %collective-permute-start.15 = (f32[20480]{0:T(1024)S(1)}, f32[20480]{0:T(1024)S(1)}, u32[]{:S(2)}, u32[]{:S(2)}) collective-permute-start(f32[20480]{0:T(1024)S(1)} %get-tuple-element.47), channel_id=1, source_target_pairs={{0,64},{4,68},{8,72},{12,76},{16,80},{20,84},{24,88},{28,92},{32,9... | collective-permute-start | bytes 245768 | tf_op jit(solution)/shard_map/ppermute | solution.py:30
  143.5 8.0 %collective-permute-start.16 = (f32[20480]{0:T(1024)S(1)}, f32[20480]{0:T(1024)S(1)}, u32[]{:S(2)}, u32[]{:S(2)}) collective-permute-start(f32[20480]{0:T(1024)S(1)} %get-tuple-element.48), channel_id=1, source_target_pairs={{0,128},{4,132},{8,136},{12,140},{16,144},{20,148},{24,152},{28,15... | collective-permute-start | bytes 245768 | tf_op jit(solution)/shard_map/ppermute | solution.py:30
  143.5 8.0 %collective-permute-start.17 = (f32[20480]{0:T(1024)S(1)}, f32[20480]{0:T(1024)S(1)}, u32[]{:S(2)}, u32[]{:S(2)}) collective-permute-start(f32[20480]{0:T(1024)S(1)} %get-tuple-element.49), channel_id=1, source_target_pairs={{0,192},{4,196},{8,200},{12,204},{16,208},{20,212},{24,216},{28,22... | collective-permute-start | bytes 245768 | tf_op jit(solution)/shard_map/ppermute | solution.py:30
  152.3 13.2 %collective-permute-start.21 = (f32[16,1024]{1,0:T(8,128)S(1)}, f32[16,1024]{1,0:T(8,128)S(1)}, u32[]{:S(2)}, u32[]{:S(2)}) collective-permute-start(f32[16,1024]{1,0:T(8,128)S(1)} %fusion.40), channel_id=1, source_target_pairs={{0,4},{4,0},{8,12},{12,8},{16,20},{20,16},{24,28},{28,24},{32,36},... | collective-permute-start | bytes 196616 | tf_op jit(solution)/shard_map/ppermute | solution.py:30
  155.4 10.0 %collective-permute-start.22 = (f32[16,1024]{1,0:T(8,128)S(1)}, f32[16,1024]{1,0:T(8,128)S(1)}, u32[]{:S(2)}, u32[]{:S(2)}) collective-permute-start(f32[16,1024]{1,0:T(8,128)S(1)} %fusion.40), channel_id=1, source_target_pairs={{0,8},{4,12},{8,0},{12,4},{16,24},{20,28},{24,16},{28,20},{32,40},... | collective-permute-start | bytes 196616 | tf_op jit(solution)/shard_map/ppermute | solution.py:30
  156.4 4.2 %collective-permute-start.18 = (f32[1,64,2,32]{1,3,2,0:T(8,128)S(1)}, f32[1,64,2,32]{1,3,2,0:T(8,128)S(1)}, u32[]{:S(2)}, u32[]{:S(2)}) collective-permute-start(f32[1,64,2,32]{1,3,2,0:T(8,128)S(1)} %add_add_fusion), channel_id=1, source_target_pairs={{0,1},{1,0},{2,3},{3,2},{4,5},{5,4},{6,7},{7,6},{8,9},{9,8},{10,11... | collective-permute-start | bytes 49160 | tf_op jit(solution)/shard_map/ppermute | solution.py:30
  156.5 6.8 %collective-permute-start.19 = (f32[1,64,2,32]{1,3,2,0:T(8,128)S(1)}, f32[1,64,2,32]{1,3,2,0:T(8,128)S(1)}, u32[]{:S(2)}, u32[]{:S(2)}) collective-permute-start(f32[1,64,2,32]{1,3,2,0:T(8,128)S(1)} %add_add_fusion), channel_id=1, source_target_pairs={{0,2},{1,3},{2,0},{3,1},{4,6},{5,7},{6,4},{7,5},{8,10},{9,11},{10,... | collective-permute-start | bytes 49160 | tf_op jit(solution)/shard_map/ppermute | solution.py:30
  158.4 5.0 %collective-permute-start.20 = (f32[1,64,2,32]{1,3,2,0:T(8,128)S(1)}, f32[1,64,2,32]{1,3,2,0:T(8,128)S(1)}, u32[]{:S(2)}, u32[]{:S(2)}) collective-permute-start(f32[1,64,2,32]{1,3,2,0:T(8,128)S(1)} %add_add_fusion), channel_id=1, source_target_pairs={{0,3},{1,2},{2,1},{3,0},{4,7},{5,6},{6,5},{7,4},{8,11},{9,10},{10,... | collective-permute-start | bytes 49160 | tf_op jit(solution)/shard_map/ppermute | solution.py:30
  160.7 5.0 %collective-permute-start.23 = (f32[16,1024]{1,0:T(8,128)S(1)}, f32[16,1024]{1,0:T(8,128)S(1)}, u32[]{:S(2)}, u32[]{:S(2)}) collective-permute-start(f32[16,1024]{1,0:T(8,128)S(1)} %fusion.40), channel_id=1, source_target_pairs={{0,12},{4,8},{8,4},{12,0},{16,28},{20,24},{24,20},{28,16},{32,44},... | collective-permute-start | bytes 196616 | tf_op jit(solution)/shard_map/ppermute | solution.py:30
  (7 other events, 136.8 us)

commit v14 on v10

--- a/solution.py
+++ b/solution.py
@@ -94,7 +94,7 @@
     return y
 
 
-def attention_body(pos_ref, q_ref, do_ref, k_ref, v_ref, dk_ref, dv_ref):
+def attention_body(pos_ref, q_ref, do_ref, k_ref, v_ref, out_ref):
     m = pl.program_id(1)
     scale = HEAD_SIZE ** (-0.5)
     q = q_ref[...]
@@ -113,22 +113,31 @@
     dk = lax.dot_general(dscore, q, (((0,), (0,)), ((), ())), preferred_element_type=jnp.float32)
     dv = lax.dot_general(prob_b, do, (((0,), (0,)), ((), ())), preferred_element_type=jnp.float32)
 
+    blocks, _, rows, width = out_ref.shape
+    dk = dk.reshape(blocks, rows, width)
+    dv = dv.reshape(blocks, rows, width)
+
     @pl.when(m == 0)
     def _():
-        dk_ref[...] = dk
-        dv_ref[...] = dv
-
-    @pl.when(m > 0)
+        out_ref[:, 0] = dk
+        out_ref[:, 1] = dv
+
+    @pl.when((m > 0) & (m < Q_PER_KV - 1))
     def _():
-        dk_ref[...] += dk
-        dv_ref[...] += dv
-
-
-def attention_grads(position, queries, out_grad, keys, values):
+        out_ref[:, 0] += dk
+        out_ref[:, 1] += dv
+
+    @pl.when(m == Q_PER_KV - 1)
+    def _():
+        out_ref[:, 0] = (out_ref[:, 0] + dk) * scale
+        out_ref[:, 1] += dv
+
+
+def attention_grads(position, queries, out_grad, keys, values, span):
     tokens = queries.shape[0]
     window_rows, cols = keys.shape
     heads = cols // HEAD_SIZE
-    scale = HEAD_SIZE ** (-0.5)
+    rows = window_rows // span
     grid_spec = pltpu.PrefetchScalarGridSpec(
         num_scalar_prefetch=1,
         grid=(heads, Q_PER_KV),
@@ -138,18 +147,14 @@
             pl.BlockSpec((window_rows, HEAD_SIZE), lambda g, m, p: (0, g)),
             pl.BlockSpec((window_rows, HEAD_SIZE), lambda g, m, p: (0, g)),
         ],
-        out_specs=[
-            pl.BlockSpec((window_rows, HEAD_SIZE), lambda g, m, p: (0, g)),
-            pl.BlockSpec((window_rows, HEAD_SIZE), lambda g, m, p: (0, g)),
-        ],
-    )
-    dk, dv = pl.pallas_call(
+        out_specs=pl.BlockSpec((span, 2, rows, HEAD_SIZE), lambda g, m, p: (0, 0, 0, g)),
+    )
+    return pl.pallas_call(
         attention_body,
         grid_spec=grid_spec,
-        out_shape=[jax.ShapeDtypeStruct((window_rows, cols), jnp.float32)] * 2,
+        out_shape=jax.ShapeDtypeStruct((span, 2, rows, cols), jnp.float32),
         compiler_params=pltpu.CompilerParams(dimension_semantics=("arbitrary", "arbitrary")),
     )(position.reshape(1).astype(jnp.int32), queries, out_grad, keys, values)
-    return dk * scale, dv
 
 
 def on_device(
@@ -181,8 +186,7 @@
         reach *= 2
     keys = window[:, 0].reshape(span * rows, cols)
     values = window[:, 1].reshape(span * rows, cols)
-    dkey, dval = attention_grads(position, queries, out_grad, keys, values)
-    contrib = jnp.stack([dkey.reshape(span, rows, cols), dval.reshape(span, rows, cols)], 1)
+    contrib = attention_grads(position, queries, out_grad, keys, values, span)
     reach = span // 2
     while reach >= 1:
         give = contrib[reach : 2 * reach]

time: 169 us -> 170 us (level)
  no operation moved by 1% of the time
where the time goes in v14:
time: 170 us
  waiting for transfers between devices  64.7 us (38%)
  starting transfers between devices  57 us (34%)
  Pallas kernels  19.5 us (11%)
  local copies, waits for them, and re-layouts  18.1 us (11%)
  other arithmetic  4.26 us (3%)
  matrix products  4.07 us (2%)
  between operations  2.18 us (1%)
    ppermute x6, waiting for transfers between devices, passed_along(): return lax.ppermute(array, axis, pairs)  42.6 us
    ppermute x18, starting transfers between devices, xor_partner(): return lax.ppermute(array, axis, [(i, i ^ mask) for i in range(devices)])  34.9 us
    ppermute x6, starting transfers between devices, passed_along(): return lax.ppermute(array, axis, pairs)  22.2 us
    ppermute x18, waiting for transfers between devices, xor_partner(): return lax.ppermute(array, axis, [(i, i ^ mask) for i in range(devices)])  22.1 us
    pallas_call x1, Pallas kernels, attention_grads(): pl.pallas_call(attention_body, grid_spec=grid_spec, out_shape=jax.ShapeDt...  19.5 us
  transfers between devices with their start and end apart: 24, of which 15 were waited for; matrix products, arithmetic and copies ran while one was open for 3% of the time, Pallas kernels for 0%

profile of v14, /device:TPU:1, one launch (start us, length us, event | category | flops | bytes accessed | tf_op | source)
XLA Modules:
  0.0 169.8 jit_solution(2624170523236181720)
XLA Ops:
  1.6 4.6 %collective-permute-start = (bf16[1,2,128,256]{3,2,1,0:T(8,128)(2,1)S(1)}, bf16[1,2,128,256]{3,2,1,0:T(8,128)(2,1)S(1)}, u32[]{:S(2)}, u32[]{:S(2)}) collective-permute-start(bf16[1,2,128,256]{3,2,1,0:T(8,128)(2,1)S(1)} %maximum_bitcast_fusion), channel_id=1, source_target_pairs={{0,4},{4,8},{8,12},{12,16},{16,20},{20,24},{24,28},{28,32},{32,36}... | collective-permute-start | bytes 393224 | tf_op jit(solution)/shard_map/ppermute | solution.py:15
  8.2 3.2 %collective-permute-start.1 = (bf16[2,2,128,256]{3,2,1,0:T(8,128)(2,1)S(1)}, bf16[2,2,128,256]{3,2,1,0:T(8,128)(2,1)S(1)}, u32[]{:S(2)}, u32[]{:S(2)}) collective-permute-start(bf16[2,2,128,256]{3,2,1,0:T(8,128)(2,1)S(1)} %pad_maximum_fusion.2), channel_id=1, source_target_pairs={{0,8},{4,12},{8,16},{12,20},{16,24},{20,28},{24,32},{28,36},{32,40... | collective-permute-start | bytes 786440 | tf_op jit(solution)/shard_map/ppermute | solution.py:15
  11.4 4.4 %collective-permute-done.1 = bf16[2,2,128,256]{3,2,1,0:T(8,128)(2,1)S(1)} collective-permute-done((bf16[2,2,128,256]{3,2,1,0:T(8,128)(2,1)S(1)}, bf16[2,2,128,256]{3,2,1,0:T(8,128)(2,1)S(1)}, u32[]{:S(2)}, u32[]{:S(2)}) %collective-permute-start.1) | collective-permute-done | bytes 262176 | tf_op jit(solution)/shard_map/ppermute | solution.py:15
  15.8 5.2 %collective-permute-start.2 = (bf16[4,2,128,256]{3,2,1,0:T(8,128)(2,1)S(1)}, bf16[4,2,128,256]{3,2,1,0:T(8,128)(2,1)S(1)}, u32[]{:S(2)}, u32[]{:S(2)}) collective-permute-start(bf16[4,2,128,256]{3,2,1,0:T(8,128)(2,1)S(1)} %pad_maximum_fusion.1), channel_id=1, source_target_pairs={{0,16},{4,20},{8,24},{12,28},{16,32},{20,36},{24,40},{28,44},{32,4... | collective-permute-start | bytes 1572872 | tf_op jit(solution)/shard_map/ppermute | solution.py:15
  22.6 7.3 %collective-permute-done.2 = bf16[4,2,128,256]{3,2,1,0:T(8,128)(2,1)S(1)} collective-permute-done((bf16[4,2,128,256]{3,2,1,0:T(8,128)(2,1)S(1)}, bf16[4,2,128,256]{3,2,1,0:T(8,128)(2,1)S(1)}, u32[]{:S(2)}, u32[]{:S(2)}) %collective-permute-start.2) | collective-permute-done | bytes 524320 | tf_op jit(solution)/shard_map/ppermute | solution.py:15
  31.0 19.5 %shard_map.129 = f32[8,2,128,256]{3,2,1,0:T(8,128)} custom-call(s32[1]{0:T(128)} %bitcast.1.pos_ref, bf16[512,1024]{1,0:T(8,128)(2,1)} %q_ref.1, bf16[512,1024]{1,0:T(8,128)(2,1)} %do_ref.1, bf16[1024,256]{1,0:T(8,128)(2,1)} %bitcast.106, bf16[1024,256]{1,0:T(8,128)(2,1)} %bitcast.105), custom_call_target="tpu_custom_call" | custom-call | tf_op jit(solution)/shard_map/pallas_call | solution.py:152
  53.1 13.3 %collective-permute-done.3 = bf16[4,2,128,256]{3,2,1,0:T(8,128)(2,1)S(1)} collective-permute-done((bf16[4,2,128,256]{3,2,1,0:T(8,128)(2,1)S(1)}, bf16[4,2,128,256]{3,2,1,0:T(8,128)(2,1)S(1)}, u32[]{:S(2)}, u32[]{:S(2)}) %collective-permute-start.3) | collective-permute-done | bytes 524320 | tf_op jit(solution)/shard_map/ppermute | solution.py:15
  69.3 10.1 %collective-permute-done.4 = f32[2,2,128,256]{3,2,1,0:T(8,128)S(1)} collective-permute-done((f32[2,2,128,256]{3,2,1,0:T(8,128)S(1)}, f32[2,2,128,256]{3,2,1,0:T(8,128)S(1)}, u32[]{:S(2)}, u32[]{:S(2)}) %collective-permute-start.4) | collective-permute-done | bytes 524320 | tf_op jit(solution)/shard_map/ppermute | solution.py:15
  79.5 6.6 %collective-permute-start.5 = (f32[1,2,128,256]{3,2,1,0:T(8,128)S(1)}, f32[1,2,128,256]{3,2,1,0:T(8,128)S(1)}, u32[]{:S(2)}, u32[]{:S(2)}) collective-permute-start(f32[1,2,128,256]{3,2,1,0:T(8,128)S(1)} %slice.284), channel_id=1, source_target_pairs={{4,0},{8,4},{12,8},{16,12},{20,16},{24,20},{28,24},{32,28},{36,32}... | collective-permute-start | bytes 786440 | tf_op jit(solution)/shard_map/ppermute | solution.py:15
  86.2 5.6 %collective-permute-done.5 = f32[1,2,128,256]{3,2,1,0:T(8,128)S(1)} collective-permute-done((f32[1,2,128,256]{3,2,1,0:T(8,128)S(1)}, f32[1,2,128,256]{3,2,1,0:T(8,128)S(1)}, u32[]{:S(2)}, u32[]{:S(2)}) %collective-permute-start.5) | collective-permute-done | bytes 262176 | tf_op jit(solution)/shard_map/ppermute | solution.py:15
  91.9 1.9 %convolution_bitcast_fusion.1 = f32[1,128,256]{2,1,0:T(8,128)S(1)} fusion(bf16[128,4096]{1,0:T(8,128)(2,1)S(1)} %copy-done, bf16[4096,128]{1,0:T(8,128)(2,1)} %param.20, bf16[1,2,128,256]{3,2,1,0:T(8,128)(2,1)S(1)} %slice_add_fusion.2), kind=kOutput, calls=%fused_computation.5 | convolution fusion | flops 142622720 | bytes 2293760 | tf_op jit(solution)/shard_map/dot_general | solution.py:215
  96.3 2.4 %collective-permute-start.7 = (f32[1,128,64]{1,2,0:T(8,128)S(1)}, f32[1,128,64]{1,2,0:T(8,128)S(1)}, u32[]{:S(2)}, u32[]{:S(2)}) collective-permute-start(f32[1,128,64]{1,2,0:T(8,128)S(1)} %get-tuple-element.41), channel_id=1, source_target_pairs={{0,2},{1,3},{2,0},{3,1},{4,6},{5,7},{6,4},{7,5},{8,10},{9,11},{10,... | collective-permute-start | bytes 98312 | tf_op jit(solution)/shard_map/ppermute | solution.py:30
  100.6 2.1 %collective-permute-done.8 = f32[1,128,64]{1,2,0:T(8,128)S(1)} collective-permute-done((f32[1,128,64]{1,2,0:T(8,128)S(1)}, f32[1,128,64]{1,2,0:T(8,128)S(1)}, u32[]{:S(2)}, u32[]{:S(2)}) %collective-permute-start.8) | collective-permute-done | bytes 32800 | tf_op jit(solution)/shard_map/ppermute | solution.py:30
  110.1 2.0 %collective-permute-start.10 = (bf16[16,5120]{1,0:T(8,128)(2,1)S(1)}, bf16[16,5120]{1,0:T(8,128)(2,1)S(1)}, u32[]{:S(2)}, u32[]{:S(2)}) collective-permute-start(bf16[16,5120]{1,0:T(8,128)(2,1)S(1)} %bitcast.113), channel_id=1, source_target_pairs={{0,8},{4,12},{8,0},{12,4},{16,24},{20,28},{24,16},{28,20},{32,40},... | collective-permute-start | bytes 491528 | tf_op jit(solution)/shard_map/ppermute | solution.py:30
  113.3 3.3 %collective-permute-done.10 = bf16[16,5120]{1,0:T(8,128)(2,1)S(1)} collective-permute-done((bf16[16,5120]{1,0:T(8,128)(2,1)S(1)}, bf16[16,5120]{1,0:T(8,128)(2,1)S(1)}, u32[]{:S(2)}, u32[]{:S(2)}) %collective-permute-start.10) | collective-permute-done | bytes 163872 | tf_op jit(solution)/shard_map/ppermute | solution.py:30
  116.7 3.5 %collective-permute-done.11 = bf16[16,5120]{1,0:T(8,128)(2,1)S(1)} collective-permute-done((bf16[16,5120]{1,0:T(8,128)(2,1)S(1)}, bf16[16,5120]{1,0:T(8,128)(2,1)S(1)}, u32[]{:S(2)}, u32[]{:S(2)}) %collective-permute-start.11) | collective-permute-done | bytes 163872 | tf_op jit(solution)/shard_map/ppermute | solution.py:30
  120.8 5.3 %collective-permute-start.12 = (f32[32768]{0:T(1024)S(1)}, f32[32768]{0:T(1024)S(1)}, u32[]{:S(2)}, u32[]{:S(2)}) collective-permute-start(f32[32768]{0:T(1024)S(1)} %get-tuple-element.51), channel_id=1, source_target_pairs={{0,16},{4,20},{8,24},{12,28},{16,0},{20,4},{24,8},{28,12},{32,48},... | collective-permute-start | bytes 393224 | tf_op jit(solution)/shard_map/ppermute | solution.py:30
  131.1 3.3 %collective-permute-done.14 = f32[32768]{0:T(1024)S(1)} collective-permute-done((f32[32768]{0:T(1024)S(1)}, f32[32768]{0:T(1024)S(1)}, u32[]{:S(2)}, u32[]{:S(2)}) %collective-permute-start.14) | collective-permute-done | bytes 131104 | tf_op jit(solution)/shard_map/ppermute | solution.py:30
  136.6 7.9 %collective-permute-start.15 = (f32[20480]{0:T(1024)S(1)}, f32[20480]{0:T(1024)S(1)}, u32[]{:S(2)}, u32[]{:S(2)}) collective-permute-start(f32[20480]{0:T(1024)S(1)} %get-tuple-element.43), channel_id=1, source_target_pairs={{0,64},{4,68},{8,72},{12,76},{16,80},{20,84},{24,88},{28,92},{32,9... | collective-permute-start | bytes 245768 | tf_op jit(solution)/shard_map/ppermute | solution.py:30
  144.7 3.3 %collective-permute-start.17 = (f32[20480]{0:T(1024)S(1)}, f32[20480]{0:T(1024)S(1)}, u32[]{:S(2)}, u32[]{:S(2)}) collective-permute-start(f32[20480]{0:T(1024)S(1)} %get-tuple-element.45), channel_id=1, source_target_pairs={{0,192},{4,196},{8,200},{12,204},{16,208},{20,212},{24,216},{28,22... | collective-permute-start | bytes 245768 | tf_op jit(solution)/shard_map/ppermute | solution.py:30
  148.4 4.3 %collective-permute-done.16 = f32[20480]{0:T(1024)S(1)} collective-permute-done((f32[20480]{0:T(1024)S(1)}, f32[20480]{0:T(1024)S(1)}, u32[]{:S(2)}, u32[]{:S(2)}) %collective-permute-start.16) | collective-permute-done | bytes 81952 | tf_op jit(solution)/shard_map/ppermute | solution.py:30
  153.5 3.2 %collective-permute-start.21 = (f32[16,1024]{1,0:T(8,128)S(1)}, f32[16,1024]{1,0:T(8,128)S(1)}, u32[]{:S(2)}, u32[]{:S(2)}) collective-permute-start(f32[16,1024]{1,0:T(8,128)S(1)} %fusion.37), channel_id=1, source_target_pairs={{0,4},{4,0},{8,12},{12,8},{16,20},{20,16},{24,28},{28,24},{32,36},... | collective-permute-start | bytes 196616 | tf_op jit(solution)/shard_map/ppermute | solution.py:30
  159.7 2.2 %collective-permute-start.20 = (f32[1,64,2,32]{1,3,2,0:T(8,128)S(1)}, f32[1,64,2,32]{1,3,2,0:T(8,128)S(1)}, u32[]{:S(2)}, u32[]{:S(2)}) collective-permute-start(f32[1,64,2,32]{1,3,2,0:T(8,128)S(1)} %add_add_fusion), channel_id=1, source_target_pairs={{0,3},{1,2},{2,1},{3,0},{4,7},{5,6},{6,5},{7,4},{8,11},{9,10},{10,... | collective-permute-start | bytes 49160 | tf_op jit(solution)/shard_map/ppermute | solution.py:30
  162.2 2.4 %collective-permute-start.23 = (f32[16,1024]{1,0:T(8,128)S(1)}, f32[16,1024]{1,0:T(8,128)S(1)}, u32[]{:S(2)}, u32[]{:S(2)}) collective-permute-start(f32[16,1024]{1,0:T(8,128)S(1)} %fusion.37), channel_id=1, source_target_pairs={{0,12},{4,8},{8,4},{12,0},{16,28},{20,24},{24,20},{28,16},{32,44},... | collective-permute-start | bytes 196616 | tf_op jit(solution)/shard_map/ppermute | solution.py:30
  (149 shorter events, 40.5 us)
Async XLA Ops:
  1.6 6.5 %collective-permute-start = (bf16[1,2,128,256]{3,2,1,0:T(8,128)(2,1)S(1)}, bf16[1,2,128,256]{3,2,1,0:T(8,128)(2,1)S(1)}, u32[]{:S(2)}, u32[]{:S(2)}) collective-permute-start(bf16[1,2,128,256]{3,2,1,0:T(8,128)(2,1)S(1)} %maximum_bitcast_fusion), channel_id=1, source_target_pairs={{0,4},{4,8},{8,12},{12,16},{16,20},{20,24},{24,28},{28,32},{32,36}... | collective-permute-start | bytes 393224 | tf_op jit(solution)/shard_map/ppermute | solution.py:15
  8.2 7.6 %collective-permute-start.1 = (bf16[2,2,128,256]{3,2,1,0:T(8,128)(2,1)S(1)}, bf16[2,2,128,256]{3,2,1,0:T(8,128)(2,1)S(1)}, u32[]{:S(2)}, u32[]{:S(2)}) collective-permute-start(bf16[2,2,128,256]{3,2,1,0:T(8,128)(2,1)S(1)} %pad_maximum_fusion.2), channel_id=1, source_target_pairs={{0,8},{4,12},{8,16},{12,20},{16,24},{20,28},{24,32},{28,36},{32,40... | collective-permute-start | bytes 786440 | tf_op jit(solution)/shard_map/ppermute | solution.py:15
  15.8 14.0 %collective-permute-start.2 = (bf16[4,2,128,256]{3,2,1,0:T(8,128)(2,1)S(1)}, bf16[4,2,128,256]{3,2,1,0:T(8,128)(2,1)S(1)}, u32[]{:S(2)}, u32[]{:S(2)}) collective-permute-start(bf16[4,2,128,256]{3,2,1,0:T(8,128)(2,1)S(1)} %pad_maximum_fusion.1), channel_id=1, source_target_pairs={{0,16},{4,20},{8,24},{12,28},{16,32},{20,36},{24,40},{28,44},{32,4... | collective-permute-start | bytes 1572872 | tf_op jit(solution)/shard_map/ppermute | solution.py:15
  51.8 14.6 %collective-permute-start.3 = (bf16[4,2,128,256]{3,2,1,0:T(8,128)(2,1)S(1)}, bf16[4,2,128,256]{3,2,1,0:T(8,128)(2,1)S(1)}, u32[]{:S(2)}, u32[]{:S(2)}) collective-permute-start(bf16[4,2,128,256]{3,2,1,0:T(8,128)(2,1)S(1)} %slice.351), channel_id=1, source_target_pairs={{16,0},{20,4},{24,8},{28,12},{32,16},{36,20},{40,24},{44,28},{48,3... | collective-permute-start | bytes 1572872 | tf_op jit(solution)/shard_map/ppermute | solution.py:15
  67.9 11.5 %collective-permute-start.4 = (f32[2,2,128,256]{3,2,1,0:T(8,128)S(1)}, f32[2,2,128,256]{3,2,1,0:T(8,128)S(1)}, u32[]{:S(2)}, u32[]{:S(2)}) collective-permute-start(f32[2,2,128,256]{3,2,1,0:T(8,128)S(1)} %slice.282), channel_id=1, source_target_pairs={{8,0},{12,4},{16,8},{20,12},{24,16},{28,20},{32,24},{36,28},{40,32... | collective-permute-start | bytes 1572872 | tf_op jit(solution)/shard_map/ppermute | solution.py:15
  79.5 12.3 %collective-permute-start.5 = (f32[1,2,128,256]{3,2,1,0:T(8,128)S(1)}, f32[1,2,128,256]{3,2,1,0:T(8,128)S(1)}, u32[]{:S(2)}, u32[]{:S(2)}) collective-permute-start(f32[1,2,128,256]{3,2,1,0:T(8,128)S(1)} %slice.284), channel_id=1, source_target_pairs={{4,0},{8,4},{12,8},{16,12},{20,16},{24,20},{28,24},{32,28},{36,32}... | collective-permute-start | bytes 786440 | tf_op jit(solution)/shard_map/ppermute | solution.py:15
  95.0 4.1 %collective-permute-start.6 = (f32[1,128,64]{1,2,0:T(8,128)S(1)}, f32[1,128,64]{1,2,0:T(8,128)S(1)}, u32[]{:S(2)}, u32[]{:S(2)}) collective-permute-start(f32[1,128,64]{1,2,0:T(8,128)S(1)} %get-tuple-element.40), channel_id=1, source_target_pairs={{0,1},{1,0},{2,3},{3,2},{4,5},{5,4},{6,7},{7,6},{8,9},{9,8},{10,11... | collective-permute-start | bytes 98312 | tf_op jit(solution)/shard_map/ppermute | solution.py:30
  96.3 4.3 %collective-permute-start.7 = (f32[1,128,64]{1,2,0:T(8,128)S(1)}, f32[1,128,64]{1,2,0:T(8,128)S(1)}, u32[]{:S(2)}, u32[]{:S(2)}) collective-permute-start(f32[1,128,64]{1,2,0:T(8,128)S(1)} %get-tuple-element.41), channel_id=1, source_target_pairs={{0,2},{1,3},{2,0},{3,1},{4,6},{5,7},{6,4},{7,5},{8,10},{9,11},{10,... | collective-permute-start | bytes 98312 | tf_op jit(solution)/shard_map/ppermute | solution.py:30
  98.8 4.0 %collective-permute-start.8 = (f32[1,128,64]{1,2,0:T(8,128)S(1)}, f32[1,128,64]{1,2,0:T(8,128)S(1)}, u32[]{:S(2)}, u32[]{:S(2)}) collective-permute-start(f32[1,128,64]{1,2,0:T(8,128)S(1)} %get-tuple-element.42), channel_id=1, source_target_pairs={{0,3},{1,2},{2,1},{3,0},{4,7},{5,6},{6,5},{7,4},{8,11},{9,10},{10,... | collective-permute-start | bytes 98312 | tf_op jit(solution)/shard_map/ppermute | solution.py:30
  110.1 6.6 %collective-permute-start.10 = (bf16[16,5120]{1,0:T(8,128)(2,1)S(1)}, bf16[16,5120]{1,0:T(8,128)(2,1)S(1)}, u32[]{:S(2)}, u32[]{:S(2)}) collective-permute-start(bf16[16,5120]{1,0:T(8,128)(2,1)S(1)} %bitcast.113), channel_id=1, source_target_pairs={{0,8},{4,12},{8,0},{12,4},{16,24},{20,28},{24,16},{28,20},{32,40},... | collective-permute-start | bytes 491528 | tf_op jit(solution)/shard_map/ppermute | solution.py:30
  112.2 8.0 %collective-permute-start.11 = (bf16[16,5120]{1,0:T(8,128)(2,1)S(1)}, bf16[16,5120]{1,0:T(8,128)(2,1)S(1)}, u32[]{:S(2)}, u32[]{:S(2)}) collective-permute-start(bf16[16,5120]{1,0:T(8,128)(2,1)S(1)} %bitcast.114), channel_id=1, source_target_pairs={{0,12},{4,8},{8,4},{12,0},{16,28},{20,24},{24,20},{28,16},{32,44},... | collective-permute-start | bytes 491528 | tf_op jit(solution)/shard_map/ppermute | solution.py:30
  112.3 7.9 %collective-permute-start.9 = (bf16[16,5120]{1,0:T(8,128)(2,1)S(1)}, bf16[16,5120]{1,0:T(8,128)(2,1)S(1)}, u32[]{:S(2)}, u32[]{:S(2)}) collective-permute-start(bf16[16,5120]{1,0:T(8,128)(2,1)S(1)} %bitcast.115), channel_id=1, source_target_pairs={{0,4},{4,0},{8,12},{12,8},{16,20},{20,16},{24,28},{28,24},{32,36},... | collective-permute-start | bytes 491528 | tf_op jit(solution)/shard_map/ppermute | solution.py:30
  120.8 8.9 %collective-permute-start.12 = (f32[32768]{0:T(1024)S(1)}, f32[32768]{0:T(1024)S(1)}, u32[]{:S(2)}, u32[]{:S(2)}) collective-permute-start(f32[32768]{0:T(1024)S(1)} %get-tuple-element.51), channel_id=1, source_target_pairs={{0,16},{4,20},{8,24},{12,28},{16,0},{20,4},{24,8},{28,12},{32,48},... | collective-permute-start | bytes 393224 | tf_op jit(solution)/shard_map/ppermute | solution.py:30
  126.1 4.9 %collective-permute-start.13 = (f32[32768]{0:T(1024)S(1)}, f32[32768]{0:T(1024)S(1)}, u32[]{:S(2)}, u32[]{:S(2)}) collective-permute-start(f32[32768]{0:T(1024)S(1)} %get-tuple-element.52), channel_id=1, source_target_pairs={{0,32},{4,36},{8,40},{12,44},{16,48},{20,52},{24,56},{28,60},{32,0... | collective-permute-start | bytes 393224 | tf_op jit(solution)/shard_map/ppermute | solution.py:30
  127.8 6.6 %collective-permute-start.14 = (f32[32768]{0:T(1024)S(1)}, f32[32768]{0:T(1024)S(1)}, u32[]{:S(2)}, u32[]{:S(2)}) collective-permute-start(f32[32768]{0:T(1024)S(1)} %get-tuple-element.53), channel_id=1, source_target_pairs={{0,48},{4,52},{8,56},{12,60},{16,32},{20,36},{24,40},{28,44},{32,1... | collective-permute-start | bytes 393224 | tf_op jit(solution)/shard_map/ppermute | solution.py:30
  136.6 11.7 %collective-permute-start.15 = (f32[20480]{0:T(1024)S(1)}, f32[20480]{0:T(1024)S(1)}, u32[]{:S(2)}, u32[]{:S(2)}) collective-permute-start(f32[20480]{0:T(1024)S(1)} %get-tuple-element.43), channel_id=1, source_target_pairs={{0,64},{4,68},{8,72},{12,76},{16,80},{20,84},{24,88},{28,92},{32,9... | collective-permute-start | bytes 245768 | tf_op jit(solution)/shard_map/ppermute | solution.py:30
  144.6 8.1 %collective-permute-start.16 = (f32[20480]{0:T(1024)S(1)}, f32[20480]{0:T(1024)S(1)}, u32[]{:S(2)}, u32[]{:S(2)}) collective-permute-start(f32[20480]{0:T(1024)S(1)} %get-tuple-element.44), channel_id=1, source_target_pairs={{0,128},{4,132},{8,136},{12,140},{16,144},{20,148},{24,152},{28,15... | collective-permute-start | bytes 245768 | tf_op jit(solution)/shard_map/ppermute | solution.py:30
  144.7 8.0 %collective-permute-start.17 = (f32[20480]{0:T(1024)S(1)}, f32[20480]{0:T(1024)S(1)}, u32[]{:S(2)}, u32[]{:S(2)}) collective-permute-start(f32[20480]{0:T(1024)S(1)} %get-tuple-element.45), channel_id=1, source_target_pairs={{0,192},{4,196},{8,200},{12,204},{16,208},{20,212},{24,216},{28,22... | collective-permute-start | bytes 245768 | tf_op jit(solution)/shard_map/ppermute | solution.py:30
  153.5 13.2 %collective-permute-start.21 = (f32[16,1024]{1,0:T(8,128)S(1)}, f32[16,1024]{1,0:T(8,128)S(1)}, u32[]{:S(2)}, u32[]{:S(2)}) collective-permute-start(f32[16,1024]{1,0:T(8,128)S(1)} %fusion.37), channel_id=1, source_target_pairs={{0,4},{4,0},{8,12},{12,8},{16,20},{20,16},{24,28},{28,24},{32,36},... | collective-permute-start | bytes 196616 | tf_op jit(solution)/shard_map/ppermute | solution.py:30
  156.7 10.0 %collective-permute-start.22 = (f32[16,1024]{1,0:T(8,128)S(1)}, f32[16,1024]{1,0:T(8,128)S(1)}, u32[]{:S(2)}, u32[]{:S(2)}) collective-permute-start(f32[16,1024]{1,0:T(8,128)S(1)} %fusion.37), channel_id=1, source_target_pairs={{0,8},{4,12},{8,0},{12,4},{16,24},{20,28},{24,16},{28,20},{32,40},... | collective-permute-start | bytes 196616 | tf_op jit(solution)/shard_map/ppermute | solution.py:30
  157.9 4.2 %collective-permute-start.18 = (f32[1,64,2,32]{1,3,2,0:T(8,128)S(1)}, f32[1,64,2,32]{1,3,2,0:T(8,128)S(1)}, u32[]{:S(2)}, u32[]{:S(2)}) collective-permute-start(f32[1,64,2,32]{1,3,2,0:T(8,128)S(1)} %add_add_fusion), channel_id=1, source_target_pairs={{0,1},{1,0},{2,3},{3,2},{4,5},{5,4},{6,7},{7,6},{8,9},{9,8},{10,11... | collective-permute-start | bytes 49160 | tf_op jit(solution)/shard_map/ppermute | solution.py:30
  158.0 6.5 %collective-permute-start.19 = (f32[1,64,2,32]{1,3,2,0:T(8,128)S(1)}, f32[1,64,2,32]{1,3,2,0:T(8,128)S(1)}, u32[]{:S(2)}, u32[]{:S(2)}) collective-permute-start(f32[1,64,2,32]{1,3,2,0:T(8,128)S(1)} %add_add_fusion), channel_id=1, source_target_pairs={{0,2},{1,3},{2,0},{3,1},{4,6},{5,7},{6,4},{7,5},{8,10},{9,11},{10,... | collective-permute-start | bytes 49160 | tf_op jit(solution)/shard_map/ppermute | solution.py:30
  159.7 4.9 %collective-permute-start.20 = (f32[1,64,2,32]{1,3,2,0:T(8,128)S(1)}, f32[1,64,2,32]{1,3,2,0:T(8,128)S(1)}, u32[]{:S(2)}, u32[]{:S(2)}) collective-permute-start(f32[1,64,2,32]{1,3,2,0:T(8,128)S(1)} %add_add_fusion), channel_id=1, source_target_pairs={{0,3},{1,2},{2,1},{3,0},{4,7},{5,6},{6,5},{7,4},{8,11},{9,10},{10,... | collective-permute-start | bytes 49160 | tf_op jit(solution)/shard_map/ppermute | solution.py:30
  162.2 5.3 %collective-permute-start.23 = (f32[16,1024]{1,0:T(8,128)S(1)}, f32[16,1024]{1,0:T(8,128)S(1)}, u32[]{:S(2)}, u32[]{:S(2)}) collective-permute-start(f32[16,1024]{1,0:T(8,128)S(1)} %fusion.37), channel_id=1, source_target_pairs={{0,12},{4,8},{8,4},{12,0},{16,28},{20,24},{24,20},{28,16},{32,44},... | collective-permute-start | bytes 196616 | tf_op jit(solution)/shard_map/ppermute | solution.py:30
  (5 other events, 115.4 us)

commit v15 on v13

--- a/solution.py
+++ b/solution.py
@@ -175,22 +175,18 @@
     first = jnp.max(jnp.where(starts <= stretch, starts, 0))
     position = stretch - first
     window = jnp.stack([mem_key, memory_values])[None]
-    reach = 1
-    while reach < span:
-        window = jnp.concatenate([window, passed_along(window, "wide", reach)], 0)
-        reach *= 2
+    half = span // 2
+    window = jnp.concatenate([window] + [passed_along(window, "wide", by) for by in range(1, half)], 0)
+    window = jnp.concatenate([window, passed_along(window, "wide", half)], 0)
     keys = window[:, 0].reshape(span * rows, cols)
     values = window[:, 1].reshape(span * rows, cols)
     dkey, dval = attention_grads(position, queries, out_grad, keys, values)
     contrib = jnp.stack([dkey.reshape(span, rows, cols), dval.reshape(span, rows, cols)], 1)
-    reach = span // 2
-    while reach >= 1:
-        give = contrib[reach : 2 * reach]
-        if reach >= span // 4:
-            give = give.astype(jnp.bfloat16)
-        contrib = contrib[:reach] + passed_along(give, "wide", -reach).astype(jnp.float32)
-        reach //= 2
+    give = contrib[half:].astype(jnp.bfloat16)
+    contrib = contrib[:half] + passed_along(give, "wide", -half).astype(jnp.float32)
     total = contrib[0]
+    for by in range(1, half):
+        total = total + passed_along(contrib[by], "wide", -by)
     key_grad = total[0].astype(jnp.bfloat16)
     value_grad = total[1].astype(jnp.bfloat16)
     u_key = jnp.dot(enc_rows, key_down, preferred_element_type=jnp.float32).astype(jnp.bfloat16)

time: 169 us -> 175 us (1.036)
  starting transfers between devices: 57.3 us -> 62.7 us
  local copies, waits for them, and re-layouts: 17.7 us -> 20 us
    ppermute x6 -> x8, waiting for transfers between devices: 38.5 us -> 35.1 us  [passed_along(): return lax.ppermute(array, axis, pairs)]
    ppermute x18, starting transfers between devices: 34.8 us -> 38.1 us  [xor_partner(): return lax.ppermute(array, axis, [(i, i ^ mask) for i in range(devices)])]
    ppermute x18, waiting for transfers between devices: 21.5 us -> 23.8 us  [xor_partner(): return lax.ppermute(array, axis, [(i, i ^ mask) for i in range(devices)])]
    ppermute x6 -> x8, starting transfers between devices: 22.4 us -> 24.6 us  [passed_along(): return lax.ppermute(array, axis, pairs)]
    unnamed x22 -> x37, local copies, waits for them, and re-layouts: 4.05 us -> 4.92 us
  transfers between devices with their start and end apart: 24 -> 26, of which waited for: 16 -> 18; matrix products, arithmetic and copies ran while one was open for 3% -> 4% of each run, Pallas kernels for 0% -> 0%
where the time goes in v15:
time: 175 us; the launch traced here: 174 us
  starting transfers between devices  62.7 us (36%)
  waiting for transfers between devices  58.9 us (34%)
  local copies, waits for them, and re-layouts  20 us (11%)
  Pallas kernels  19.5 us (11%)
  other arithmetic  8.14 us (5%)
  matrix products  2.78 us (2%)
  between operations  2.23 us (1%)
    ppermute x18, starting transfers between devices, xor_partner(): return lax.ppermute(array, axis, [(i, i ^ mask) for i in range(devices)])  38.1 us
    ppermute x8, waiting for transfers between devices, passed_along(): return lax.ppermute(array, axis, pairs)  35.1 us
    ppermute x8, starting transfers between devices, passed_along(): return lax.ppermute(array, axis, pairs)  24.6 us
    ppermute x18, waiting for transfers between devices, xor_partner(): return lax.ppermute(array, axis, [(i, i ^ mask) for i in range(devices)])  23.8 us
    pallas_call x1, Pallas kernels, attention_grads(): pl.pallas_call(attention_body, grid_spec=grid_spec, out_shape=[jax.ShapeD...  19.5 us
    unnamed x37, local copies, waits for them, and re-layouts  4.92 us
  transfers between devices with their start and end apart: 26, of which 18 were waited for; matrix products, arithmetic and copies ran while one was open for 4% of the time, Pallas kernels for 0%

profile of v15, /device:TPU:1, one launch (start us, length us, event | category | flops | bytes accessed | tf_op | source)
XLA Modules:
  0.0 174.3 jit_solution(12845363210433108303)
XLA Ops:
  1.7 4.6 %collective-permute-start = (bf16[1,2,128,256]{3,2,1,0:T(8,128)(2,1)S(1)}, bf16[1,2,128,256]{3,2,1,0:T(8,128)(2,1)S(1)}, u32[]{:S(2)}, u32[]{:S(2)}) collective-permute-start(bf16[1,2,128,256]{3,2,1,0:T(8,128)(2,1)S(1)} %maximum_bitcast_fusion), channel_id=1, source_target_pairs={{0,4},{4,8},{8,12},{12,16},{16,20},{20,24},{24,28},{28,32},{32,36}... | collective-permute-start | bytes 393224 | tf_op jit(solution)/shard_map/ppermute | solution.py:15
  6.3 3.2 %collective-permute-start.1 = (bf16[1,2,128,256]{3,2,1,0:T(8,128)(2,1)S(1)}, bf16[1,2,128,256]{3,2,1,0:T(8,128)(2,1)S(1)}, u32[]{:S(2)}, u32[]{:S(2)}) collective-permute-start(bf16[1,2,128,256]{3,2,1,0:T(8,128)(2,1)S(1)} %maximum_bitcast_fusion), channel_id=1, source_target_pairs={{0,8},{4,12},{8,16},{12,20},{16,24},{20,28},{24,32},{28,36},{32,40... | collective-permute-start | bytes 393224 | tf_op jit(solution)/shard_map/ppermute | solution.py:15
  9.5 3.5 %collective-permute-start.2 = (bf16[1,2,128,256]{3,2,1,0:T(8,128)(2,1)S(1)}, bf16[1,2,128,256]{3,2,1,0:T(8,128)(2,1)S(1)}, u32[]{:S(2)}, u32[]{:S(2)}) collective-permute-start(bf16[1,2,128,256]{3,2,1,0:T(8,128)(2,1)S(1)} %maximum_bitcast_fusion), channel_id=1, source_target_pairs={{0,12},{4,16},{8,20},{12,24},{16,28},{20,32},{24,36},{28,40},{32,4... | collective-permute-start | bytes 393224 | tf_op jit(solution)/shard_map/ppermute | solution.py:15
  13.9 2.4 %collective-permute-done.2 = bf16[1,2,128,256]{3,2,1,0:T(8,128)(2,1)S(1)} collective-permute-done((bf16[1,2,128,256]{3,2,1,0:T(8,128)(2,1)S(1)}, bf16[1,2,128,256]{3,2,1,0:T(8,128)(2,1)S(1)}, u32[]{:S(2)}, u32[]{:S(2)}) %collective-permute-start.2) | collective-permute-done | bytes 131104 | tf_op jit(solution)/shard_map/ppermute | solution.py:15
  16.4 5.6 %collective-permute-start.3 = (bf16[4,2,128,256]{3,2,1,0:T(8,128)(2,1)S(1)}, bf16[4,2,128,256]{3,2,1,0:T(8,128)(2,1)S(1)}, u32[]{:S(2)}, u32[]{:S(2)}) collective-permute-start(bf16[4,2,128,256]{3,2,1,0:T(8,128)(2,1)S(1)} %pad_maximum_fusion.1), channel_id=1, source_target_pairs={{0,16},{4,20},{8,24},{12,28},{16,32},{20,36},{24,40},{28,44},{32,4... | collective-permute-start | bytes 1572872 | tf_op jit(solution)/shard_map/ppermute | solution.py:15
  23.4 9.4 %collective-permute-done.3 = bf16[4,2,128,256]{3,2,1,0:T(8,128)(2,1)S(1)} collective-permute-done((bf16[4,2,128,256]{3,2,1,0:T(8,128)(2,1)S(1)}, bf16[4,2,128,256]{3,2,1,0:T(8,128)(2,1)S(1)}, u32[]{:S(2)}, u32[]{:S(2)}) %collective-permute-start.3) | collective-permute-done | bytes 524320 | tf_op jit(solution)/shard_map/ppermute | solution.py:15
  33.8 19.5 %shard_map.129 = (f32[1024,256]{1,0:T(8,128)}, f32[1024,256]{1,0:T(8,128)}) custom-call(s32[1]{0:T(128)} %bitcast.1.pos_ref, bf16[512,1024]{1,0:T(8,128)(2,1)} %q_ref.1, bf16[512,1024]{1,0:T(8,128)(2,1)} %do_ref.1, bf16[1024,256]{1,0:T(8,128)(2,1)} %bitcast.130, bf16[1024,256]{1,0:T(8,128)(2,1)} %bitcast.129), custom_call_target="tpu_custom_call" | custom-call | tf_op jit(solution)/shard_map/pallas_call | solution.py:146
  58.1 14.5 %collective-permute-done.4 = bf16[4,2,128,256]{3,2,1,0:T(8,128)(2,1)} collective-permute-done((bf16[4,2,128,256]{3,2,1,0:T(8,128)(2,1)}, bf16[4,2,128,256]{3,2,1,0:T(8,128)(2,1)}, u32[]{:S(2)}, u32[]{:S(2)}) %collective-permute-start.4) | collective-permute-done | bytes 524320 | tf_op jit(solution)/shard_map/ppermute | solution.py:15
  75.5 3.8 %collective-permute-start.5 = (f32[2,128,256]{2,1,0:T(8,128)}, f32[2,128,256]{2,1,0:T(8,128)S(1)}, u32[]{:S(2)}, u32[]{:S(2)}) collective-permute-start(f32[2,128,256]{2,1,0:T(8,128)} %get-tuple-element.26), channel_id=1, source_target_pairs={{4,0},{8,4},{12,8},{16,12},{20,16},{24,20},{28,24},{32,28},{36,32}... | collective-permute-start | bytes 786440 | tf_op jit(solution)/shard_map/ppermute | solution.py:15
  83.4 5.8 %collective-permute-done.6 = f32[2,128,256]{2,1,0:T(8,128)S(1)} collective-permute-done((f32[2,128,256]{2,1,0:T(8,128)S(1)}, f32[2,128,256]{2,1,0:T(8,128)S(1)}, u32[]{:S(2)}, u32[]{:S(2)}) %collective-permute-start.6) | collective-permute-done | bytes 262176 | tf_op jit(solution)/shard_map/ppermute | solution.py:15
  94.4 2.6 %collective-permute-start.10 = (f32[1,128,64]{1,2,0:T(8,128)S(1)}, f32[1,128,64]{1,2,0:T(8,128)S(1)}, u32[]{:S(2)}, u32[]{:S(2)}) collective-permute-start(f32[1,128,64]{1,2,0:T(8,128)S(1)} %get-tuple-element.49), channel_id=1, source_target_pairs={{0,3},{1,2},{2,1},{3,0},{4,7},{5,6},{6,5},{7,4},{8,11},{9,10},{10,... | collective-permute-start | bytes 98312 | tf_op jit(solution)/shard_map/ppermute | solution.py:30
  104.4 1.9 %concatenate.39 = f32[16,4,4096]{2,1,0:T(4,128)} reshape(f32[4096,64]{1,0:T(8,128)S(1)} %copy.55) | data formatting | bytes 2097152 | tf_op jit(solution)/shard_map/concatenate | solution.py:52
  108.6 6.2 %collective-permute-start.11 = (bf16[16,5120]{1,0:T(8,128)(2,1)S(1)}, bf16[16,5120]{1,0:T(8,128)(2,1)S(1)}, u32[]{:S(2)}, u32[]{:S(2)}) collective-permute-start(bf16[16,5120]{1,0:T(8,128)(2,1)S(1)} %bitcast.141), channel_id=1, source_target_pairs={{0,4},{4,0},{8,12},{12,8},{16,20},{20,16},{24,28},{28,24},{32,36},... | collective-permute-start | bytes 491528 | tf_op jit(solution)/shard_map/ppermute | solution.py:30
  114.9 3.6 %collective-permute-start.12 = (bf16[16,5120]{1,0:T(8,128)(2,1)S(1)}, bf16[16,5120]{1,0:T(8,128)(2,1)S(1)}, u32[]{:S(2)}, u32[]{:S(2)}) collective-permute-start(bf16[16,5120]{1,0:T(8,128)(2,1)S(1)} %bitcast.142), channel_id=1, source_target_pairs={{0,8},{4,12},{8,0},{12,4},{16,24},{20,28},{24,16},{28,20},{32,40},... | collective-permute-start | bytes 491528 | tf_op jit(solution)/shard_map/ppermute | solution.py:30
  119.2 3.9 %collective-permute-done.12 = bf16[16,5120]{1,0:T(8,128)(2,1)S(1)} collective-permute-done((bf16[16,5120]{1,0:T(8,128)(2,1)S(1)}, bf16[16,5120]{1,0:T(8,128)(2,1)S(1)}, u32[]{:S(2)}, u32[]{:S(2)}) %collective-permute-start.12) | collective-permute-done | bytes 163872 | tf_op jit(solution)/shard_map/ppermute | solution.py:30
  123.0 3.5 %collective-permute-done.13 = bf16[16,5120]{1,0:T(8,128)(2,1)S(1)} collective-permute-done((bf16[16,5120]{1,0:T(8,128)(2,1)S(1)}, bf16[16,5120]{1,0:T(8,128)(2,1)S(1)}, u32[]{:S(2)}, u32[]{:S(2)}) %collective-permute-start.13) | collective-permute-done | bytes 163872 | tf_op jit(solution)/shard_map/ppermute | solution.py:30
  127.1 5.5 %collective-permute-start.14 = (f32[32768]{0:T(1024)S(1)}, f32[32768]{0:T(1024)S(1)}, u32[]{:S(2)}, u32[]{:S(2)}) collective-permute-start(f32[32768]{0:T(1024)S(1)} %get-tuple-element.58), channel_id=1, source_target_pairs={{0,16},{4,20},{8,24},{12,28},{16,0},{20,4},{24,8},{28,12},{32,48},... | collective-permute-start | bytes 393224 | tf_op jit(solution)/shard_map/ppermute | solution.py:30
  134.3 1.9 %collective-permute-done.14 = f32[32768]{0:T(1024)S(1)} collective-permute-done((f32[32768]{0:T(1024)S(1)}, f32[32768]{0:T(1024)S(1)}, u32[]{:S(2)}, u32[]{:S(2)}) %collective-permute-start.14) | collective-permute-done | bytes 131104 | tf_op jit(solution)/shard_map/ppermute | solution.py:30
  137.7 3.3 %collective-permute-done.16 = f32[32768]{0:T(1024)S(1)} collective-permute-done((f32[32768]{0:T(1024)S(1)}, f32[32768]{0:T(1024)S(1)}, u32[]{:S(2)}, u32[]{:S(2)}) %collective-permute-start.16) | collective-permute-done | bytes 131104 | tf_op jit(solution)/shard_map/ppermute | solution.py:30
  143.3 5.0 %collective-permute-start.17 = (f32[20480]{0:T(1024)S(1)}, f32[20480]{0:T(1024)S(1)}, u32[]{:S(2)}, u32[]{:S(2)}) collective-permute-start(f32[20480]{0:T(1024)S(1)} %get-tuple-element.50), channel_id=1, source_target_pairs={{0,64},{4,68},{8,72},{12,76},{16,80},{20,84},{24,88},{28,92},{32,9... | collective-permute-start | bytes 245768 | tf_op jit(solution)/shard_map/ppermute | solution.py:30
  148.3 2.3 %collective-permute-start.18 = (f32[20480]{0:T(1024)S(1)}, f32[20480]{0:T(1024)S(1)}, u32[]{:S(2)}, u32[]{:S(2)}) collective-permute-start(f32[20480]{0:T(1024)S(1)} %get-tuple-element.51), channel_id=1, source_target_pairs={{0,128},{4,132},{8,136},{12,140},{16,144},{20,148},{24,152},{28,15... | collective-permute-start | bytes 245768 | tf_op jit(solution)/shard_map/ppermute | solution.py:30
  152.1 3.5 %collective-permute-done.18 = f32[20480]{0:T(1024)S(1)} collective-permute-done((f32[20480]{0:T(1024)S(1)}, f32[20480]{0:T(1024)S(1)}, u32[]{:S(2)}, u32[]{:S(2)}) %collective-permute-start.18) | collective-permute-done | bytes 81952 | tf_op jit(solution)/shard_map/ppermute | solution.py:30
  155.6 2.3 %collective-permute-done.19 = f32[20480]{0:T(1024)S(1)} collective-permute-done((f32[20480]{0:T(1024)S(1)}, f32[20480]{0:T(1024)S(1)}, u32[]{:S(2)}, u32[]{:S(2)}) %collective-permute-start.19) | collective-permute-done | bytes 81952 | tf_op jit(solution)/shard_map/ppermute | solution.py:30
  158.7 2.0 %collective-permute-start.23 = (f32[16,1024]{1,0:T(8,128)S(1)}, f32[16,1024]{1,0:T(8,128)S(1)}, u32[]{:S(2)}, u32[]{:S(2)}) collective-permute-start(f32[16,1024]{1,0:T(8,128)S(1)} %fusion.43), channel_id=1, source_target_pairs={{0,4},{4,0},{8,12},{12,8},{16,20},{20,16},{24,28},{28,24},{32,36},... | collective-permute-start | bytes 196616 | tf_op jit(solution)/shard_map/ppermute | solution.py:30
  (171 shorter events, 52.5 us)
Async XLA Ops:
  1.7 12.3 %collective-permute-start = (bf16[1,2,128,256]{3,2,1,0:T(8,128)(2,1)S(1)}, bf16[1,2,128,256]{3,2,1,0:T(8,128)(2,1)S(1)}, u32[]{:S(2)}, u32[]{:S(2)}) collective-permute-start(bf16[1,2,128,256]{3,2,1,0:T(8,128)(2,1)S(1)} %maximum_bitcast_fusion), channel_id=1, source_target_pairs={{0,4},{4,8},{8,12},{12,16},{16,20},{20,24},{24,28},{28,32},{32,36}... | collective-permute-start | bytes 393224 | tf_op jit(solution)/shard_map/ppermute | solution.py:15
  6.3 7.7 %collective-permute-start.1 = (bf16[1,2,128,256]{3,2,1,0:T(8,128)(2,1)S(1)}, bf16[1,2,128,256]{3,2,1,0:T(8,128)(2,1)S(1)}, u32[]{:S(2)}, u32[]{:S(2)}) collective-permute-start(bf16[1,2,128,256]{3,2,1,0:T(8,128)(2,1)S(1)} %maximum_bitcast_fusion), channel_id=1, source_target_pairs={{0,8},{4,12},{8,16},{12,20},{16,24},{20,28},{24,32},{28,36},{32,40... | collective-permute-start | bytes 393224 | tf_op jit(solution)/shard_map/ppermute | solution.py:15
  9.5 6.8 %collective-permute-start.2 = (bf16[1,2,128,256]{3,2,1,0:T(8,128)(2,1)S(1)}, bf16[1,2,128,256]{3,2,1,0:T(8,128)(2,1)S(1)}, u32[]{:S(2)}, u32[]{:S(2)}) collective-permute-start(bf16[1,2,128,256]{3,2,1,0:T(8,128)(2,1)S(1)} %maximum_bitcast_fusion), channel_id=1, source_target_pairs={{0,12},{4,16},{8,20},{12,24},{16,28},{20,32},{24,36},{28,40},{32,4... | collective-permute-start | bytes 393224 | tf_op jit(solution)/shard_map/ppermute | solution.py:15
  16.4 16.4 %collective-permute-start.3 = (bf16[4,2,128,256]{3,2,1,0:T(8,128)(2,1)S(1)}, bf16[4,2,128,256]{3,2,1,0:T(8,128)(2,1)S(1)}, u32[]{:S(2)}, u32[]{:S(2)}) collective-permute-start(bf16[4,2,128,256]{3,2,1,0:T(8,128)(2,1)S(1)} %pad_maximum_fusion.1), channel_id=1, source_target_pairs={{0,16},{4,20},{8,24},{12,28},{16,32},{20,36},{24,40},{28,44},{32,4... | collective-permute-start | bytes 1572872 | tf_op jit(solution)/shard_map/ppermute | solution.py:15
  55.7 16.9 %collective-permute-start.4 = (bf16[4,2,128,256]{3,2,1,0:T(8,128)(2,1)}, bf16[4,2,128,256]{3,2,1,0:T(8,128)(2,1)}, u32[]{:S(2)}, u32[]{:S(2)}) collective-permute-start(bf16[4,2,128,256]{3,2,1,0:T(8,128)(2,1)} %fusion.2), channel_id=1, source_target_pairs={{16,0},{20,4},{24,8},{28,12},{32,16},{36,20},{40,24},{44,28},{48,3... | collective-permute-start | bytes 1572872 | tf_op jit(solution)/shard_map/ppermute | solution.py:15
  75.5 7.9 %collective-permute-start.5 = (f32[2,128,256]{2,1,0:T(8,128)}, f32[2,128,256]{2,1,0:T(8,128)S(1)}, u32[]{:S(2)}, u32[]{:S(2)}) collective-permute-start(f32[2,128,256]{2,1,0:T(8,128)} %get-tuple-element.26), channel_id=1, source_target_pairs={{4,0},{8,4},{12,8},{16,12},{20,16},{24,20},{28,24},{32,28},{36,32}... | collective-permute-start | bytes 786440 | tf_op jit(solution)/shard_map/ppermute | solution.py:15
  79.3 9.9 %collective-permute-start.6 = (f32[2,128,256]{2,1,0:T(8,128)S(1)}, f32[2,128,256]{2,1,0:T(8,128)S(1)}, u32[]{:S(2)}, u32[]{:S(2)}) collective-permute-start(f32[2,128,256]{2,1,0:T(8,128)S(1)} %get-tuple-element.28), channel_id=1, source_target_pairs={{8,0},{12,4},{16,8},{20,12},{24,16},{28,20},{32,24},{36,28},{40,32... | collective-permute-start | bytes 786440 | tf_op jit(solution)/shard_map/ppermute | solution.py:15
  80.6 10.3 %collective-permute-start.7 = (f32[2,128,256]{2,1,0:T(8,128)S(1)}, f32[2,128,256]{2,1,0:T(8,128)S(1)}, u32[]{:S(2)}, u32[]{:S(2)}) collective-permute-start(f32[2,128,256]{2,1,0:T(8,128)S(1)} %get-tuple-element.27), channel_id=1, source_target_pairs={{12,0},{16,4},{20,8},{24,12},{28,16},{32,20},{36,24},{40,28},{44,3... | collective-permute-start | bytes 786440 | tf_op jit(solution)/shard_map/ppermute | solution.py:15
  94.4 4.1 %collective-permute-start.10 = (f32[1,128,64]{1,2,0:T(8,128)S(1)}, f32[1,128,64]{1,2,0:T(8,128)S(1)}, u32[]{:S(2)}, u32[]{:S(2)}) collective-permute-start(f32[1,128,64]{1,2,0:T(8,128)S(1)} %get-tuple-element.49), channel_id=1, source_target_pairs={{0,3},{1,2},{2,1},{3,0},{4,7},{5,6},{6,5},{7,4},{8,11},{9,10},{10,... | collective-permute-start | bytes 98312 | tf_op jit(solution)/shard_map/ppermute | solution.py:30
  97.0 4.3 %collective-permute-start.9 = (f32[1,128,64]{1,2,0:T(8,128)S(1)}, f32[1,128,64]{1,2,0:T(8,128)S(1)}, u32[]{:S(2)}, u32[]{:S(2)}) collective-permute-start(f32[1,128,64]{1,2,0:T(8,128)S(1)} %get-tuple-element.48), channel_id=1, source_target_pairs={{0,2},{1,3},{2,0},{3,1},{4,6},{5,7},{6,4},{7,5},{8,10},{9,11},{10,... | collective-permute-start | bytes 98312 | tf_op jit(solution)/shard_map/ppermute | solution.py:30
  108.6 10.5 %collective-permute-start.11 = (bf16[16,5120]{1,0:T(8,128)(2,1)S(1)}, bf16[16,5120]{1,0:T(8,128)(2,1)S(1)}, u32[]{:S(2)}, u32[]{:S(2)}) collective-permute-start(bf16[16,5120]{1,0:T(8,128)(2,1)S(1)} %bitcast.141), channel_id=1, source_target_pairs={{0,4},{4,0},{8,12},{12,8},{16,20},{20,16},{24,28},{28,24},{32,36},... | collective-permute-start | bytes 491528 | tf_op jit(solution)/shard_map/ppermute | solution.py:30
  114.9 8.2 %collective-permute-start.12 = (bf16[16,5120]{1,0:T(8,128)(2,1)S(1)}, bf16[16,5120]{1,0:T(8,128)(2,1)S(1)}, u32[]{:S(2)}, u32[]{:S(2)}) collective-permute-start(bf16[16,5120]{1,0:T(8,128)(2,1)S(1)} %bitcast.142), channel_id=1, source_target_pairs={{0,8},{4,12},{8,0},{12,4},{16,24},{20,28},{24,16},{28,20},{32,40},... | collective-permute-start | bytes 491528 | tf_op jit(solution)/shard_map/ppermute | solution.py:30
  118.5 8.0 %collective-permute-start.13 = (bf16[16,5120]{1,0:T(8,128)(2,1)S(1)}, bf16[16,5120]{1,0:T(8,128)(2,1)S(1)}, u32[]{:S(2)}, u32[]{:S(2)}) collective-permute-start(bf16[16,5120]{1,0:T(8,128)(2,1)S(1)} %bitcast.143), channel_id=1, source_target_pairs={{0,12},{4,8},{8,4},{12,0},{16,28},{20,24},{24,20},{28,16},{32,44},... | collective-permute-start | bytes 491528 | tf_op jit(solution)/shard_map/ppermute | solution.py:30
  127.1 9.1 %collective-permute-start.14 = (f32[32768]{0:T(1024)S(1)}, f32[32768]{0:T(1024)S(1)}, u32[]{:S(2)}, u32[]{:S(2)}) collective-permute-start(f32[32768]{0:T(1024)S(1)} %get-tuple-element.58), channel_id=1, source_target_pairs={{0,16},{4,20},{8,24},{12,28},{16,0},{20,4},{24,8},{28,12},{32,48},... | collective-permute-start | bytes 393224 | tf_op jit(solution)/shard_map/ppermute | solution.py:30
  132.6 5.0 %collective-permute-start.15 = (f32[32768]{0:T(1024)S(1)}, f32[32768]{0:T(1024)S(1)}, u32[]{:S(2)}, u32[]{:S(2)}) collective-permute-start(f32[32768]{0:T(1024)S(1)} %get-tuple-element.59), channel_id=1, source_target_pairs={{0,32},{4,36},{8,40},{12,44},{16,48},{20,52},{24,56},{28,60},{32,0... | collective-permute-start | bytes 393224 | tf_op jit(solution)/shard_map/ppermute | solution.py:30
  134.3 6.7 %collective-permute-start.16 = (f32[32768]{0:T(1024)S(1)}, f32[32768]{0:T(1024)S(1)}, u32[]{:S(2)}, u32[]{:S(2)}) collective-permute-start(f32[32768]{0:T(1024)S(1)} %get-tuple-element.60), channel_id=1, source_target_pairs={{0,48},{4,52},{8,56},{12,60},{16,32},{20,36},{24,40},{28,44},{32,1... | collective-permute-start | bytes 393224 | tf_op jit(solution)/shard_map/ppermute | solution.py:30
  143.3 8.8 %collective-permute-start.17 = (f32[20480]{0:T(1024)S(1)}, f32[20480]{0:T(1024)S(1)}, u32[]{:S(2)}, u32[]{:S(2)}) collective-permute-start(f32[20480]{0:T(1024)S(1)} %get-tuple-element.50), channel_id=1, source_target_pairs={{0,64},{4,68},{8,72},{12,76},{16,80},{20,84},{24,88},{28,92},{32,9... | collective-permute-start | bytes 245768 | tf_op jit(solution)/shard_map/ppermute | solution.py:30
  148.3 7.3 %collective-permute-start.18 = (f32[20480]{0:T(1024)S(1)}, f32[20480]{0:T(1024)S(1)}, u32[]{:S(2)}, u32[]{:S(2)}) collective-permute-start(f32[20480]{0:T(1024)S(1)} %get-tuple-element.51), channel_id=1, source_target_pairs={{0,128},{4,132},{8,136},{12,140},{16,144},{20,148},{24,152},{28,15... | collective-permute-start | bytes 245768 | tf_op jit(solution)/shard_map/ppermute | solution.py:30
  150.5 7.4 %collective-permute-start.19 = (f32[20480]{0:T(1024)S(1)}, f32[20480]{0:T(1024)S(1)}, u32[]{:S(2)}, u32[]{:S(2)}) collective-permute-start(f32[20480]{0:T(1024)S(1)} %get-tuple-element.52), channel_id=1, source_target_pairs={{0,192},{4,196},{8,200},{12,204},{16,208},{20,212},{24,216},{28,22... | collective-permute-start | bytes 245768 | tf_op jit(solution)/shard_map/ppermute | solution.py:30
  158.7 12.7 %collective-permute-start.23 = (f32[16,1024]{1,0:T(8,128)S(1)}, f32[16,1024]{1,0:T(8,128)S(1)}, u32[]{:S(2)}, u32[]{:S(2)}) collective-permute-start(f32[16,1024]{1,0:T(8,128)S(1)} %fusion.43), channel_id=1, source_target_pairs={{0,4},{4,0},{8,12},{12,8},{16,20},{20,16},{24,28},{28,24},{32,36},... | collective-permute-start | bytes 196616 | tf_op jit(solution)/shard_map/ppermute | solution.py:30
  160.7 10.8 %collective-permute-start.24 = (f32[16,1024]{1,0:T(8,128)S(1)}, f32[16,1024]{1,0:T(8,128)S(1)}, u32[]{:S(2)}, u32[]{:S(2)}) collective-permute-start(f32[16,1024]{1,0:T(8,128)S(1)} %fusion.43), channel_id=1, source_target_pairs={{0,8},{4,12},{8,0},{12,4},{16,24},{20,28},{24,16},{28,20},{32,40},... | collective-permute-start | bytes 196616 | tf_op jit(solution)/shard_map/ppermute | solution.py:30
  163.1 4.4 %collective-permute-start.20 = (f32[1,64,2,32]{1,3,2,0:T(8,128)S(1)}, f32[1,64,2,32]{1,3,2,0:T(8,128)S(1)}, u32[]{:S(2)}, u32[]{:S(2)}) collective-permute-start(f32[1,64,2,32]{1,3,2,0:T(8,128)S(1)} %add_add_fusion), channel_id=1, source_target_pairs={{0,1},{1,0},{2,3},{3,2},{4,5},{5,4},{6,7},{7,6},{8,9},{9,8},{10,11... | collective-permute-start | bytes 49160 | tf_op jit(solution)/shard_map/ppermute | solution.py:30
  164.7 4.3 %collective-permute-start.21 = (f32[1,64,2,32]{1,3,2,0:T(8,128)S(1)}, f32[1,64,2,32]{1,3,2,0:T(8,128)S(1)}, u32[]{:S(2)}, u32[]{:S(2)}) collective-permute-start(f32[1,64,2,32]{1,3,2,0:T(8,128)S(1)} %add_add_fusion), channel_id=1, source_target_pairs={{0,2},{1,3},{2,0},{3,1},{4,6},{5,7},{6,4},{7,5},{8,10},{9,11},{10,... | collective-permute-start | bytes 49160 | tf_op jit(solution)/shard_map/ppermute | solution.py:30
  167.5 4.4 %collective-permute-start.25 = (f32[16,1024]{1,0:T(8,128)S(1)}, f32[16,1024]{1,0:T(8,128)S(1)}, u32[]{:S(2)}, u32[]{:S(2)}) collective-permute-start(f32[16,1024]{1,0:T(8,128)S(1)} %fusion.43), channel_id=1, source_target_pairs={{0,12},{4,8},{8,4},{12,0},{16,28},{20,24},{24,20},{28,16},{32,44},... | collective-permute-start | bytes 196616 | tf_op jit(solution)/shard_map/ppermute | solution.py:30
  (15 other events, 216.2 us)

commit v16 on v10

--- a/solution.py
+++ b/solution.py
@@ -19,7 +19,7 @@
     steps = []
     low = 1
     while low < devices:
-        radix = 4 if devices % (low * 4) == 0 else 2
+        radix = 4 if devices % (low * 4) == 0 and devices > 4 else 2
         steps.append((low, radix))
         low *= radix
     return steps

time: 169 us -> 173 us (1.024)
  other arithmetic: 4.5 us -> 6.53 us
    ppermute x18 -> x16, starting transfers between devices: 34.8 us -> 33.9 us  [xor_partner(): return lax.ppermute(array, axis, [(i, i ^ mask) for i in range(devices)])]
    ppermute x18 -> x16, waiting for transfers between devices: 22.1 us -> 22.7 us  [xor_partner(): return lax.ppermute(array, axis, [(i, i ^ mask) for i in range(devices)])]
  transfers between devices with their start and end apart: 24 -> 22, of which waited for: 15 -> 16; matrix products, arithmetic and copies ran while one was open for 3% -> 5% of each run, Pallas kernels for 0% -> 0%
where the time goes in v16:
time: 173 us; the launch traced here: 172 us
  waiting for transfers between devices  65.7 us (38%)
  starting transfers between devices  56.2 us (32%)
  Pallas kernels  19.5 us (11%)
  local copies, waits for them, and re-layouts  17.5 us (10%)
  other arithmetic  6.53 us (4%)
  matrix products  4 us (2%)
  between operations  2.23 us (1%)
    ppermute x6, waiting for transfers between devices, passed_along(): return lax.ppermute(array, axis, pairs)  43 us
    ppermute x16, starting transfers between devices, xor_partner(): return lax.ppermute(array, axis, [(i, i ^ mask) for i in range(devices)])  33.9 us
    ppermute x16, waiting for transfers between devices, xor_partner(): return lax.ppermute(array, axis, [(i, i ^ mask) for i in range(devices)])  22.7 us
    ppermute x6, starting transfers between devices, passed_along(): return lax.ppermute(array, axis, pairs)  22.3 us
    pallas_call x1, Pallas kernels, attention_grads(): pl.pallas_call(attention_body, grid_spec=grid_spec, out_shape=[jax.ShapeD...  19.5 us
  transfers between devices with their start and end apart: 22, of which 16 were waited for; matrix products, arithmetic and copies ran while one was open for 5% of the time, Pallas kernels for 0%

profile of v16, /device:TPU:1, one launch (start us, length us, event | category | flops | bytes accessed | tf_op | source)
XLA Modules:
  0.0 171.6 jit_solution(11648329893388603086)
XLA Ops:
  1.6 4.6 %collective-permute-start = (bf16[1,2,128,256]{3,2,1,0:T(8,128)(2,1)S(1)}, bf16[1,2,128,256]{3,2,1,0:T(8,128)(2,1)S(1)}, u32[]{:S(2)}, u32[]{:S(2)}) collective-permute-start(bf16[1,2,128,256]{3,2,1,0:T(8,128)(2,1)S(1)} %maximum_bitcast_fusion), channel_id=1, source_target_pairs={{0,4},{4,8},{8,12},{12,16},{16,20},{20,24},{24,28},{28,32},{32,36}... | collective-permute-start | bytes 393224 | tf_op jit(solution)/shard_map/ppermute | solution.py:15
  6.2 1.9 %collective-permute-done = bf16[1,2,128,256]{3,2,1,0:T(8,128)(2,1)S(1)} collective-permute-done((bf16[1,2,128,256]{3,2,1,0:T(8,128)(2,1)S(1)}, bf16[1,2,128,256]{3,2,1,0:T(8,128)(2,1)S(1)}, u32[]{:S(2)}, u32[]{:S(2)}) %collective-permute-start) | collective-permute-done | bytes 131104 | tf_op jit(solution)/shard_map/ppermute | solution.py:15
  8.2 3.2 %collective-permute-start.1 = (bf16[2,2,128,256]{3,2,1,0:T(8,128)(2,1)S(1)}, bf16[2,2,128,256]{3,2,1,0:T(8,128)(2,1)S(1)}, u32[]{:S(2)}, u32[]{:S(2)}) collective-permute-start(bf16[2,2,128,256]{3,2,1,0:T(8,128)(2,1)S(1)} %pad_maximum_fusion.3), channel_id=1, source_target_pairs={{0,8},{4,12},{8,16},{12,20},{16,24},{20,28},{24,32},{28,36},{32,40... | collective-permute-start | bytes 786440 | tf_op jit(solution)/shard_map/ppermute | solution.py:15
  11.4 4.4 %collective-permute-done.1 = bf16[2,2,128,256]{3,2,1,0:T(8,128)(2,1)S(1)} collective-permute-done((bf16[2,2,128,256]{3,2,1,0:T(8,128)(2,1)S(1)}, bf16[2,2,128,256]{3,2,1,0:T(8,128)(2,1)S(1)}, u32[]{:S(2)}, u32[]{:S(2)}) %collective-permute-start.1) | collective-permute-done | bytes 262176 | tf_op jit(solution)/shard_map/ppermute | solution.py:15
  15.8 5.2 %collective-permute-start.2 = (bf16[4,2,128,256]{3,2,1,0:T(8,128)(2,1)S(1)}, bf16[4,2,128,256]{3,2,1,0:T(8,128)(2,1)S(1)}, u32[]{:S(2)}, u32[]{:S(2)}) collective-permute-start(bf16[4,2,128,256]{3,2,1,0:T(8,128)(2,1)S(1)} %pad_maximum_fusion.2), channel_id=1, source_target_pairs={{0,16},{4,20},{8,24},{12,28},{16,32},{20,36},{24,40},{28,44},{32,4... | collective-permute-start | bytes 1572872 | tf_op jit(solution)/shard_map/ppermute | solution.py:15
  22.6 7.3 %collective-permute-done.2 = bf16[4,2,128,256]{3,2,1,0:T(8,128)(2,1)S(1)} collective-permute-done((bf16[4,2,128,256]{3,2,1,0:T(8,128)(2,1)S(1)}, bf16[4,2,128,256]{3,2,1,0:T(8,128)(2,1)S(1)}, u32[]{:S(2)}, u32[]{:S(2)}) %collective-permute-start.2) | collective-permute-done | bytes 524320 | tf_op jit(solution)/shard_map/ppermute | solution.py:15
  31.0 19.5 %shard_map.129 = (f32[1024,256]{1,0:T(8,128)}, f32[1024,256]{1,0:T(8,128)}) custom-call(s32[1]{0:T(128)} %bitcast.1.pos_ref, bf16[512,1024]{1,0:T(8,128)(2,1)} %q_ref.1, bf16[512,1024]{1,0:T(8,128)(2,1)} %do_ref.1, bf16[1024,256]{1,0:T(8,128)(2,1)} %bitcast.126, bf16[1024,256]{1,0:T(8,128)(2,1)} %bitcast.125), custom_call_target="tpu_custom_call" | custom-call | tf_op jit(solution)/shard_map/pallas_call | solution.py:146
  54.3 13.5 %collective-permute-done.3 = bf16[4,2,128,256]{3,2,1,0:T(8,128)(2,1)} collective-permute-done((bf16[4,2,128,256]{3,2,1,0:T(8,128)(2,1)}, bf16[4,2,128,256]{3,2,1,0:T(8,128)(2,1)}, u32[]{:S(2)}, u32[]{:S(2)}) %collective-permute-start.3) | collective-permute-done | bytes 524320 | tf_op jit(solution)/shard_map/ppermute | solution.py:15
  70.4 10.1 %collective-permute-done.4 = f32[2,2,128,256]{3,2,1,0:T(8,128)S(1)} collective-permute-done((f32[2,2,128,256]{3,2,1,0:T(8,128)S(1)}, f32[2,2,128,256]{3,2,1,0:T(8,128)S(1)}, u32[]{:S(2)}, u32[]{:S(2)}) %collective-permute-start.4) | collective-permute-done | bytes 524320 | tf_op jit(solution)/shard_map/ppermute | solution.py:15
  80.7 6.7 %collective-permute-start.5 = (f32[1,2,128,256]{3,2,1,0:T(8,128)S(1)}, f32[1,2,128,256]{3,2,1,0:T(8,128)S(1)}, u32[]{:S(2)}, u32[]{:S(2)}) collective-permute-start(f32[1,2,128,256]{3,2,1,0:T(8,128)S(1)} %slice.286), channel_id=1, source_target_pairs={{4,0},{8,4},{12,8},{16,12},{20,16},{24,20},{28,24},{32,28},{36,32}... | collective-permute-start | bytes 786440 | tf_op jit(solution)/shard_map/ppermute | solution.py:15
  87.6 5.8 %collective-permute-done.5 = f32[1,2,128,256]{3,2,1,0:T(8,128)S(1)} collective-permute-done((f32[1,2,128,256]{3,2,1,0:T(8,128)S(1)}, f32[1,2,128,256]{3,2,1,0:T(8,128)S(1)}, u32[]{:S(2)}, u32[]{:S(2)}) %collective-permute-start.5) | collective-permute-done | bytes 262176 | tf_op jit(solution)/shard_map/ppermute | solution.py:15
  95.7 1.9 %convolution_bitcast_fusion.2 = f32[1,128,256]{2,1,0:T(8,128)S(1)} fusion(bf16[128,4096]{1,0:T(8,128)(2,1)S(1)} %copy-done, bf16[4096,128]{1,0:T(8,128)(2,1)} %param.18, bf16[1,2,128,256]{3,2,1,0:T(8,128)(2,1)S(1)} %slice_add_fusion.1), kind=kOutput, calls=%fused_computation.9 | convolution fusion | flops 142622720 | bytes 2293760 | tf_op jit(solution)/shard_map/dot_general | solution.py:210
  97.6 2.5 %collective-permute-start.7 = (f32[1,128,64]{1,2,0:T(8,128)S(1)}, f32[1,128,64]{1,2,0:T(8,128)S(1)}, u32[]{:S(2)}, u32[]{:S(2)}) collective-permute-start(f32[1,128,64]{1,2,0:T(8,128)S(1)} %constant_dynamic-slice_fusion.9), channel_id=1, source_target_pairs={{0,2},{1,3},{2,0},{3,1},{4,6},{5,7},{6,4},{7,5},{8,10},{9,11},{10,... | collective-permute-start | bytes 98312 | tf_op jit(solution)/shard_map/ppermute | solution.py:30
  103.2 1.8 %copy.50 = f32[4096,64]{1,0:T(8,128)S(1)} copy(f32[4096,64]{0,1:T(8,128)} %convolution_bitcast_fusion) | data formatting | bytes 2097152 | tf_op jit(solution)/shard_map/dot_general | solution.py:212
  105.1 1.8 %concatenate.44 = f32[16,4,4096]{2,1,0:T(4,128)} reshape(f32[4096,64]{1,0:T(8,128)S(1)} %copy.50) | data formatting | bytes 2097152 | tf_op jit(solution)/shard_map/concatenate | solution.py:52
  112.2 3.7 %collective-permute-done.10 = bf16[16,5120]{1,0:T(8,128)(2,1)S(1)} collective-permute-done((bf16[16,5120]{1,0:T(8,128)(2,1)S(1)}, bf16[16,5120]{1,0:T(8,128)(2,1)S(1)}, u32[]{:S(2)}, u32[]{:S(2)}) %collective-permute-start.10) | collective-permute-done | bytes 163872 | tf_op jit(solution)/shard_map/ppermute | solution.py:30
  115.9 3.2 %collective-permute-done.9 = bf16[16,5120]{1,0:T(8,128)(2,1)S(1)} collective-permute-done((bf16[16,5120]{1,0:T(8,128)(2,1)S(1)}, bf16[16,5120]{1,0:T(8,128)(2,1)S(1)}, u32[]{:S(2)}, u32[]{:S(2)}) %collective-permute-start.9) | collective-permute-done | bytes 163872 | tf_op jit(solution)/shard_map/ppermute | solution.py:30
  119.7 4.2 %collective-permute-start.11 = (f32[32768]{0:T(1024)S(1)}, f32[32768]{0:T(1024)S(1)}, u32[]{:S(2)}, u32[]{:S(2)}) collective-permute-start(f32[32768]{0:T(1024)S(1)} %get-tuple-element.52), channel_id=1, source_target_pairs={{0,16},{4,20},{8,24},{12,28},{16,0},{20,4},{24,8},{28,12},{32,48},... | collective-permute-start | bytes 393224 | tf_op jit(solution)/shard_map/ppermute | solution.py:30
  128.2 3.8 %collective-permute-done.13 = f32[32768]{0:T(1024)S(1)} collective-permute-done((f32[32768]{0:T(1024)S(1)}, f32[32768]{0:T(1024)S(1)}, u32[]{:S(2)}, u32[]{:S(2)}) %collective-permute-start.13) | collective-permute-done | bytes 131104 | tf_op jit(solution)/shard_map/ppermute | solution.py:30
  134.2 8.7 %collective-permute-start.14 = (f32[20480]{0:T(1024)S(1)}, f32[20480]{0:T(1024)S(1)}, u32[]{:S(2)}, u32[]{:S(2)}) collective-permute-start(f32[20480]{0:T(1024)S(1)} %get-tuple-element.44), channel_id=1, source_target_pairs={{0,64},{4,68},{8,72},{12,76},{16,80},{20,84},{24,88},{28,92},{32,9... | collective-permute-start | bytes 245768 | tf_op jit(solution)/shard_map/ppermute | solution.py:30
  143.9 2.3 %collective-permute-start.16 = (f32[20480]{0:T(1024)S(1)}, f32[20480]{0:T(1024)S(1)}, u32[]{:S(2)}, u32[]{:S(2)}) collective-permute-start(f32[20480]{0:T(1024)S(1)} %get-tuple-element.46), channel_id=1, source_target_pairs={{0,192},{4,196},{8,200},{12,204},{16,208},{20,212},{24,216},{28,22... | collective-permute-start | bytes 245768 | tf_op jit(solution)/shard_map/ppermute | solution.py:30
  146.7 3.5 %collective-permute-done.15 = f32[20480]{0:T(1024)S(1)} collective-permute-done((f32[20480]{0:T(1024)S(1)}, f32[20480]{0:T(1024)S(1)}, u32[]{:S(2)}, u32[]{:S(2)}) %collective-permute-start.15) | collective-permute-done | bytes 81952 | tf_op jit(solution)/shard_map/ppermute | solution.py:30
  152.2 3.8 %collective-permute-start.19 = (f32[16,1024]{1,0:T(8,128)S(1)}, f32[16,1024]{1,0:T(8,128)S(1)}, u32[]{:S(2)}, u32[]{:S(2)}) collective-permute-start(f32[16,1024]{1,0:T(8,128)S(1)} %fusion.32), channel_id=1, source_target_pairs={{0,4},{4,0},{8,12},{12,8},{16,20},{20,16},{24,28},{28,24},{32,36},... | collective-permute-start | bytes 196616 | tf_op jit(solution)/shard_map/ppermute | solution.py:30
  158.9 2.9 %collective-permute-start.17 = (f32[1,64,2,32]{1,3,2,0:T(8,128)S(1)}, f32[1,64,2,32]{1,3,2,0:T(8,128)S(1)}, u32[]{:S(2)}, u32[]{:S(2)}) collective-permute-start(f32[1,64,2,32]{1,3,2,0:T(8,128)S(1)} %add_add_fusion), channel_id=1, source_target_pairs={{0,2},{1,3},{2,0},{3,1},{4,6},{5,7},{6,4},{7,5},{8,10},{9,11},{10,... | collective-permute-start | bytes 49160 | tf_op jit(solution)/shard_map/ppermute | solution.py:30
  (162 shorter events, 43.1 us)
Async XLA Ops:
  0.6 94.4 %copy-start = (bf16[128,4096]{1,0:T(8,128)(2,1)S(1)}, bf16[128,4096]{1,0:T(8,128)(2,1)}, u32[]{:S(2)}) copy-start(bf16[128,4096]{1,0:T(8,128)(2,1)} %param.17) | copy-start | bytes 3145732
  1.6 6.5 %collective-permute-start = (bf16[1,2,128,256]{3,2,1,0:T(8,128)(2,1)S(1)}, bf16[1,2,128,256]{3,2,1,0:T(8,128)(2,1)S(1)}, u32[]{:S(2)}, u32[]{:S(2)}) collective-permute-start(bf16[1,2,128,256]{3,2,1,0:T(8,128)(2,1)S(1)} %maximum_bitcast_fusion), channel_id=1, source_target_pairs={{0,4},{4,8},{8,12},{12,16},{16,20},{20,24},{24,28},{28,32},{32,36}... | collective-permute-start | bytes 393224 | tf_op jit(solution)/shard_map/ppermute | solution.py:15
  8.2 7.6 %collective-permute-start.1 = (bf16[2,2,128,256]{3,2,1,0:T(8,128)(2,1)S(1)}, bf16[2,2,128,256]{3,2,1,0:T(8,128)(2,1)S(1)}, u32[]{:S(2)}, u32[]{:S(2)}) collective-permute-start(bf16[2,2,128,256]{3,2,1,0:T(8,128)(2,1)S(1)} %pad_maximum_fusion.3), channel_id=1, source_target_pairs={{0,8},{4,12},{8,16},{12,20},{16,24},{20,28},{24,32},{28,36},{32,40... | collective-permute-start | bytes 786440 | tf_op jit(solution)/shard_map/ppermute | solution.py:15
  15.8 14.0 %collective-permute-start.2 = (bf16[4,2,128,256]{3,2,1,0:T(8,128)(2,1)S(1)}, bf16[4,2,128,256]{3,2,1,0:T(8,128)(2,1)S(1)}, u32[]{:S(2)}, u32[]{:S(2)}) collective-permute-start(bf16[4,2,128,256]{3,2,1,0:T(8,128)(2,1)S(1)} %pad_maximum_fusion.2), channel_id=1, source_target_pairs={{0,16},{4,20},{8,24},{12,28},{16,32},{20,36},{24,40},{28,44},{32,4... | collective-permute-start | bytes 1572872 | tf_op jit(solution)/shard_map/ppermute | solution.py:15
  52.9 14.9 %collective-permute-start.3 = (bf16[4,2,128,256]{3,2,1,0:T(8,128)(2,1)}, bf16[4,2,128,256]{3,2,1,0:T(8,128)(2,1)}, u32[]{:S(2)}, u32[]{:S(2)}) collective-permute-start(bf16[4,2,128,256]{3,2,1,0:T(8,128)(2,1)} %fusion.2), channel_id=1, source_target_pairs={{16,0},{20,4},{24,8},{28,12},{32,16},{36,20},{40,24},{44,28},{48,3... | collective-permute-start | bytes 1572872 | tf_op jit(solution)/shard_map/ppermute | solution.py:15
  69.0 11.5 %collective-permute-start.4 = (f32[2,2,128,256]{3,2,1,0:T(8,128)S(1)}, f32[2,2,128,256]{3,2,1,0:T(8,128)S(1)}, u32[]{:S(2)}, u32[]{:S(2)}) collective-permute-start(f32[2,2,128,256]{3,2,1,0:T(8,128)S(1)} %slice.284), channel_id=1, source_target_pairs={{8,0},{12,4},{16,8},{20,12},{24,16},{28,20},{32,24},{36,28},{40,32... | collective-permute-start | bytes 1572872 | tf_op jit(solution)/shard_map/ppermute | solution.py:15
  70.4 23.1 %copy-start.4 = (bf16[128,256]{1,0:T(8,128)(2,1)S(1)}, bf16[128,256]{1,0:T(8,128)(2,1)}, u32[]{:S(2)}) copy-start(bf16[128,256]{1,0:T(8,128)(2,1)} %param.19) | copy-start | bytes 196612
  80.7 12.6 %collective-permute-start.5 = (f32[1,2,128,256]{3,2,1,0:T(8,128)S(1)}, f32[1,2,128,256]{3,2,1,0:T(8,128)S(1)}, u32[]{:S(2)}, u32[]{:S(2)}) collective-permute-start(f32[1,2,128,256]{3,2,1,0:T(8,128)S(1)} %slice.286), channel_id=1, source_target_pairs={{4,0},{8,4},{12,8},{16,12},{20,16},{24,20},{28,24},{32,28},{36,32}... | collective-permute-start | bytes 786440 | tf_op jit(solution)/shard_map/ppermute | solution.py:15
  93.8 3.8 %collective-permute-start.6 = (f32[2,128,64]{1,2,0:T(8,128)S(1)}, f32[2,128,64]{1,2,0:T(8,128)S(1)}, u32[]{:S(2)}, u32[]{:S(2)}) collective-permute-start(f32[2,128,64]{1,2,0:T(8,128)S(1)} %dynamic-slice_bitcast_fusion), channel_id=1, source_target_pairs={{0,1},{1,0},{2,3},{3,2},{4,5},{5,4},{6,7},{7,6},{8,9},{9,8},{10,11... | collective-permute-start | bytes 196616 | tf_op jit(solution)/shard_map/ppermute | solution.py:30
  97.6 4.4 %collective-permute-start.7 = (f32[1,128,64]{1,2,0:T(8,128)S(1)}, f32[1,128,64]{1,2,0:T(8,128)S(1)}, u32[]{:S(2)}, u32[]{:S(2)}) collective-permute-start(f32[1,128,64]{1,2,0:T(8,128)S(1)} %constant_dynamic-slice_fusion.9), channel_id=1, source_target_pairs={{0,2},{1,3},{2,0},{3,1},{4,6},{5,7},{6,4},{7,5},{8,10},{9,11},{10,... | collective-permute-start | bytes 98312 | tf_op jit(solution)/shard_map/ppermute | solution.py:30
  109.3 6.6 %collective-permute-start.10 = (bf16[16,5120]{1,0:T(8,128)(2,1)S(1)}, bf16[16,5120]{1,0:T(8,128)(2,1)S(1)}, u32[]{:S(2)}, u32[]{:S(2)}) collective-permute-start(bf16[16,5120]{1,0:T(8,128)(2,1)S(1)} %bitcast.137), channel_id=1, source_target_pairs={{0,12},{4,8},{8,4},{12,0},{16,28},{20,24},{24,20},{28,16},{32,44},... | collective-permute-start | bytes 491528 | tf_op jit(solution)/shard_map/ppermute | solution.py:30
  110.8 5.1 %collective-permute-start.8 = (bf16[16,5120]{1,0:T(8,128)(2,1)S(1)}, bf16[16,5120]{1,0:T(8,128)(2,1)S(1)}, u32[]{:S(2)}, u32[]{:S(2)}) collective-permute-start(bf16[16,5120]{1,0:T(8,128)(2,1)S(1)} %bitcast.138), channel_id=1, source_target_pairs={{0,4},{4,0},{8,12},{12,8},{16,20},{20,16},{24,28},{28,24},{32,36},... | collective-permute-start | bytes 491528 | tf_op jit(solution)/shard_map/ppermute | solution.py:30
  111.7 7.4 %collective-permute-start.9 = (bf16[16,5120]{1,0:T(8,128)(2,1)S(1)}, bf16[16,5120]{1,0:T(8,128)(2,1)S(1)}, u32[]{:S(2)}, u32[]{:S(2)}) collective-permute-start(bf16[16,5120]{1,0:T(8,128)(2,1)S(1)} %bitcast.139), channel_id=1, source_target_pairs={{0,8},{4,12},{8,0},{12,4},{16,24},{20,28},{24,16},{28,20},{32,40},... | collective-permute-start | bytes 491528 | tf_op jit(solution)/shard_map/ppermute | solution.py:30
  119.7 6.9 %collective-permute-start.11 = (f32[32768]{0:T(1024)S(1)}, f32[32768]{0:T(1024)S(1)}, u32[]{:S(2)}, u32[]{:S(2)}) collective-permute-start(f32[32768]{0:T(1024)S(1)} %get-tuple-element.52), channel_id=1, source_target_pairs={{0,16},{4,20},{8,24},{12,28},{16,0},{20,4},{24,8},{28,12},{32,48},... | collective-permute-start | bytes 393224 | tf_op jit(solution)/shard_map/ppermute | solution.py:30
  124.0 4.1 %collective-permute-start.12 = (f32[32768]{0:T(1024)S(1)}, f32[32768]{0:T(1024)S(1)}, u32[]{:S(2)}, u32[]{:S(2)}) collective-permute-start(f32[32768]{0:T(1024)S(1)} %get-tuple-element.53), channel_id=1, source_target_pairs={{0,32},{4,36},{8,40},{12,44},{16,48},{20,52},{24,56},{28,60},{32,0... | collective-permute-start | bytes 393224 | tf_op jit(solution)/shard_map/ppermute | solution.py:30
  125.7 6.2 %collective-permute-start.13 = (f32[32768]{0:T(1024)S(1)}, f32[32768]{0:T(1024)S(1)}, u32[]{:S(2)}, u32[]{:S(2)}) collective-permute-start(f32[32768]{0:T(1024)S(1)} %get-tuple-element.54), channel_id=1, source_target_pairs={{0,48},{4,52},{8,56},{12,60},{16,32},{20,36},{24,40},{28,44},{32,1... | collective-permute-start | bytes 393224 | tf_op jit(solution)/shard_map/ppermute | solution.py:30
  134.2 12.5 %collective-permute-start.14 = (f32[20480]{0:T(1024)S(1)}, f32[20480]{0:T(1024)S(1)}, u32[]{:S(2)}, u32[]{:S(2)}) collective-permute-start(f32[20480]{0:T(1024)S(1)} %get-tuple-element.44), channel_id=1, source_target_pairs={{0,64},{4,68},{8,72},{12,76},{16,80},{20,84},{24,88},{28,92},{32,9... | collective-permute-start | bytes 245768 | tf_op jit(solution)/shard_map/ppermute | solution.py:30
  142.8 7.3 %collective-permute-start.15 = (f32[20480]{0:T(1024)S(1)}, f32[20480]{0:T(1024)S(1)}, u32[]{:S(2)}, u32[]{:S(2)}) collective-permute-start(f32[20480]{0:T(1024)S(1)} %get-tuple-element.45), channel_id=1, source_target_pairs={{0,128},{4,132},{8,136},{12,140},{16,144},{20,148},{24,152},{28,15... | collective-permute-start | bytes 245768 | tf_op jit(solution)/shard_map/ppermute | solution.py:30
  143.9 7.6 %collective-permute-start.16 = (f32[20480]{0:T(1024)S(1)}, f32[20480]{0:T(1024)S(1)}, u32[]{:S(2)}, u32[]{:S(2)}) collective-permute-start(f32[20480]{0:T(1024)S(1)} %get-tuple-element.46), channel_id=1, source_target_pairs={{0,192},{4,196},{8,200},{12,204},{16,208},{20,212},{24,216},{28,22... | collective-permute-start | bytes 245768 | tf_op jit(solution)/shard_map/ppermute | solution.py:30
  152.2 17.0 %collective-permute-start.19 = (f32[16,1024]{1,0:T(8,128)S(1)}, f32[16,1024]{1,0:T(8,128)S(1)}, u32[]{:S(2)}, u32[]{:S(2)}) collective-permute-start(f32[16,1024]{1,0:T(8,128)S(1)} %fusion.32), channel_id=1, source_target_pairs={{0,4},{4,0},{8,12},{12,8},{16,20},{20,16},{24,28},{28,24},{32,36},... | collective-permute-start | bytes 196616 | tf_op jit(solution)/shard_map/ppermute | solution.py:30
  156.0 13.3 %collective-permute-start.20 = (f32[16,1024]{1,0:T(8,128)S(1)}, f32[16,1024]{1,0:T(8,128)S(1)}, u32[]{:S(2)}, u32[]{:S(2)}) collective-permute-start(f32[16,1024]{1,0:T(8,128)S(1)} %fusion.32), channel_id=1, source_target_pairs={{0,8},{4,12},{8,0},{12,4},{16,24},{20,28},{24,16},{28,20},{32,40},... | collective-permute-start | bytes 196616 | tf_op jit(solution)/shard_map/ppermute | solution.py:30
  156.8 12.4 %collective-permute-start.21 = (f32[16,1024]{1,0:T(8,128)S(1)}, f32[16,1024]{1,0:T(8,128)S(1)}, u32[]{:S(2)}, u32[]{:S(2)}) collective-permute-start(f32[16,1024]{1,0:T(8,128)S(1)} %fusion.32), channel_id=1, source_target_pairs={{0,12},{4,8},{8,4},{12,0},{16,28},{20,24},{24,20},{28,16},{32,44},... | collective-permute-start | bytes 196616 | tf_op jit(solution)/shard_map/ppermute | solution.py:30
  158.9 4.4 %collective-permute-start.17 = (f32[1,64,2,32]{1,3,2,0:T(8,128)S(1)}, f32[1,64,2,32]{1,3,2,0:T(8,128)S(1)}, u32[]{:S(2)}, u32[]{:S(2)}) collective-permute-start(f32[1,64,2,32]{1,3,2,0:T(8,128)S(1)} %add_add_fusion), channel_id=1, source_target_pairs={{0,2},{1,3},{2,0},{3,1},{4,6},{5,7},{6,4},{7,5},{8,10},{9,11},{10,... | collective-permute-start | bytes 49160 | tf_op jit(solution)/shard_map/ppermute | solution.py:30
  163.9 3.1 %collective-permute-start.18 = (f32[2,64,2,32]{1,3,2,0:T(8,128)S(1)}, f32[2,64,2,32]{1,3,2,0:T(8,128)S(1)}, u32[]{:S(2)}, u32[]{:S(2)}) collective-permute-start(f32[2,64,2,32]{1,3,2,0:T(8,128)S(1)} %broadcast_select_fusion.2), channel_id=1, source_target_pairs={{0,1},{1,0},{2,3},{3,2},{4,5},{5,4},{6,7},{7,6},{8,9},{9,8},{10,11... | collective-permute-start | bytes 98312 | tf_op jit(solution)/shard_map/ppermute | solution.py:30
  (4 other events, 59.3 us)
